TPU v7x, 512 devices: a whole 4x4x16 slice. The times are simulated.
512 devices in a mesh: seq: 32 (over z, core), dp: 4 (over x), tensor: 4 (over y).
Axes of the slice: x: 4, y: 4, z: 16, core: 2. Of those that a mesh axis runs over, the one named last changes fastest.
Arguments:
- attention_queries: bfloat16 [4, 4096, 3584], P('dp', 'seq', 'tensor')
- attention_keys: bfloat16 [4, 4096, 512], P('dp', 'seq', 'tensor')
- attention_values: bfloat16 [4, 4096, 512], P('dp', 'seq', 'tensor')
- key_window_length: int32 [4], P('tensor'), may hold values from 128 to 512, as said below
- norm_gain: float32 [3584], P('tensor'), may hold values from 0.5 to 2
- spike_levels: int32 [3584], P('tensor'), may hold values from 1 to 4
- lin_queries: bfloat16 [4, 4096, 3584], P('dp', 'seq', 'tensor'), may hold values from -6 to 6
- lin_keys: bfloat16 [4, 4096, 3584], P('dp', 'seq', 'tensor'), may hold values from -6 to 6
- decay_logs: float32 [4, 28, 4096], P('dp', 'tensor', 'seq'), as said below
- cotangent: bfloat16 [4, 4096, 3584], P('dp', 'seq', 'tensor')
Outputs:
- layer_output: bfloat16 [4, 4096, 3584], P('dp', 'seq', 'tensor')
- query_grads: bfloat16 [4, 4096, 3584], P('dp', 'seq', 'tensor')
- key_gradient: bfloat16 [4, 4096, 512], P('dp', 'seq', 'tensor')
- value_gradient: bfloat16 [4, 4096, 512], P('dp', 'seq', 'tensor')
- gain_grads: float32 [3584], P('tensor')
Inputs may be any that keep to these rules, and one draw needn't show every extreme that they name: Key head g lets query t see positions j with t - key_window_length[g] < j <= t; some head has exactly 512. `decay_logs`: non-positive.
All inputs are finite; a program needn't handle non-finite values.
Results may differ from a plain program's by a relative error of at most 0.015.
Values may be sent and summed in bfloat16 or wider, within the bound.
No kernel may reach another device: no remote copies, remote signals or barrier semaphores. Data moves between devices by JAX's collectives and lax.ppermute only.
A program may use at most 128 MiB of HBM per device.

v0:
```python
import math

import jax
import jax.numpy as jnp
from jax import lax
from jax.sharding import PartitionSpec as P

HEAD_SIZE = 128
D = 3584
LONGEST_WINDOW = 512


precise = lax.Precision.HIGHEST
epsilon = 1e-06


def passed_along(block, axis, distance):
    devices = range(lax.axis_size(axis))
    route = [(i - distance, i) for i in devices if i - distance in devices]
    return lax.ppermute(block, axis, route)


def entering(value, axis, join, neutral, backward):
    count, mine = (lax.axis_size(axis), lax.axis_index(axis))
    pieces = jax.tree.map(lambda part: lax.all_gather(part, axis), value)
    if backward:
        pieces = jax.tree.map(lambda part: part[::-1], pieces)
        mine = count - 1 - mine
    running = jax.tree.map(
        lambda part, zero: jnp.full_like(part, 0) + jnp.asarray(zero, part.dtype), value, neutral
    )

    def turn(position, running):
        longer = join(running, jax.tree.map(lambda part: part[position], pieces))
        return jax.tree.map(lambda new, old: jnp.where(position < mine, new, old), longer, running)

    return lax.fori_loop(0, count - 1, turn, running)


def head_logits(query_rows, key_row_block, first_query, key_reach, scaling):
    block_rows = query_rows.shape[0]
    key_span = key_row_block.shape[0] - block_rows
    logits = (
        jnp.einsum("sd,kd->sk", query_rows, key_row_block, preferred_element_type=jnp.float32)
        * scaling
    )
    query_pos = first_query + jnp.arange(block_rows, dtype=jnp.int32)[:, None]
    key_pos = first_query - key_span + jnp.arange(key_row_block.shape[0], dtype=jnp.int32)[None, :]
    allowed = (key_pos >= 0) & (key_pos <= query_pos) & (key_pos > query_pos - key_reach)
    return jnp.where(allowed, logits, -jnp.inf)


def chain_states(earlier, later):
    return (earlier[0] * later[0], later[0][:, None, None] * earlier[1] + later[1])


def local(
    attention_queries,
    attention_keys,
    attention_values,
    key_window_length,
    norm_gain,
    spike_levels,
    lin_queries,
    lin_keys,
    decay_logs,
    cotangent,
):
    block_rows = attention_queries.shape[1]
    q_heads = attention_queries.shape[2] // HEAD_SIZE
    kv_heads = attention_keys.shape[2] // HEAD_SIZE
    head_groups = q_heads // kv_heads
    previous = (LONGEST_WINDOW + block_rows - 1) // block_rows
    key_span = previous * block_rows
    first_query = lax.axis_index("seq") * block_rows
    scaling = 1.0 / math.sqrt(HEAD_SIZE)
    own_pair = jnp.stack([attention_keys, attention_values])
    earlier_blocks = []
    moving = own_pair
    for distance in range(previous):
        moving = passed_along(moving, "seq", 1)
        earlier_blocks.append(moving)
    window_pair = jnp.concatenate(earlier_blocks[::-1] + [own_pair], axis=2)
    window_pair = window_pair.reshape(2, key_span + block_rows, kv_heads, HEAD_SIZE).transpose(
        0, 2, 1, 3
    )
    window_keys = window_pair[0]
    window_values = window_pair[1]
    head_queries = attention_queries[0].reshape(block_rows, q_heads, HEAD_SIZE).transpose(1, 0, 2)
    kv_of_head = jnp.arange(q_heads, dtype=jnp.int32) // head_groups

    def forward_head(operands):
        query_rows, kv_index = operands
        key_row_block = lax.dynamic_index_in_dim(window_keys, kv_index, 0, keepdims=False)
        value_rows = lax.dynamic_index_in_dim(window_values, kv_index, 0, keepdims=False)
        key_reach = lax.dynamic_index_in_dim(key_window_length, kv_index, 0, keepdims=False)
        logits = head_logits(query_rows, key_row_block, first_query, key_reach, scaling)
        row_max = jnp.max(logits, axis=-1)
        exponent = jnp.exp(logits - row_max[:, None])
        row_sum = jnp.sum(exponent, axis=-1)
        weights = (exponent / row_sum[:, None]).astype(jnp.bfloat16)
        head_output = jnp.dot(weights, value_rows, preferred_element_type=jnp.float32).astype(
            jnp.bfloat16
        )
        return (head_output, row_max, row_sum)

    heads_out, maxima, sums = lax.map(forward_head, (head_queries, kv_of_head))
    out_float = heads_out.astype(jnp.float32)
    square_sum = lax.psum(jnp.sum(out_float * out_float, axis=(0, 2)), "tensor")
    inverse = 1.0 / jnp.sqrt(square_sum / D + epsilon)
    normed = out_float * inverse[None, :, None]
    gain_rows = norm_gain.reshape(q_heads, HEAD_SIZE)[:, None, :]
    ceiling = spike_levels.astype(jnp.float32).reshape(q_heads, HEAD_SIZE)[:, None, :]
    bounded = jnp.tanh(normed * gain_rows / ceiling)
    spikes = (ceiling * bounded).astype(jnp.bfloat16)
    membrane_queries = lin_queries[0].reshape(block_rows, q_heads, HEAD_SIZE).transpose(1, 0, 2)
    membrane_keys = lin_keys[0].reshape(block_rows, q_heads, HEAD_SIZE).transpose(1, 0, 2)
    cumulative = jnp.cumsum(decay_logs[0], axis=1)
    lower_mask = jnp.arange(block_rows)[:, None] >= jnp.arange(block_rows)[None, :]
    gaps = jnp.where(lower_mask[None], cumulative[:, :, None] - cumulative[:, None, :], 0.0)
    products = jnp.einsum(
        "hsd,htd->hst", membrane_queries, membrane_keys, preferred_element_type=jnp.float32
    )
    decayed = jnp.where(lower_mask[None], jnp.exp(gaps), 0.0) * products
    spike_float = spikes.astype(jnp.float32)
    query_float = membrane_queries.astype(jnp.float32)
    key_float = membrane_keys.astype(jnp.float32)
    block_decay = jnp.exp(cumulative[:, -1])
    tail_decay = jnp.exp(cumulative[:, -1:] - cumulative)
    local_state = jnp.einsum(
        "hsd,hse->hde", key_float * tail_decay[..., None], spike_float, precision=precise
    )
    identity = (jnp.ones_like(block_decay), jnp.zeros_like(local_state))
    decay_before, state_in = entering(
        (block_decay, local_state), "seq", chain_states, identity, False
    )
    carried = jnp.einsum("hsd,hde->hse", query_float, state_in, precision=precise)
    membrane = (
        jnp.einsum("hst,htd->hsd", decayed, spike_float, precision=precise)
        + jnp.exp(cumulative)[..., None] * carried
    )
    scale_out = 1.0 / jnp.sqrt(jnp.mean(membrane * membrane, axis=-1) + epsilon)
    unit_out = membrane * scale_out[..., None]
    layer_output = (
        unit_out.astype(jnp.bfloat16).transpose(1, 0, 2).reshape(1, block_rows, q_heads * HEAD_SIZE)
    )
    incoming = (
        cotangent[0].reshape(block_rows, q_heads, HEAD_SIZE).transpose(1, 0, 2).astype(jnp.float32)
    )
    membrane_grad = scale_out[..., None] * (
        incoming - unit_out * jnp.mean(incoming * unit_out, axis=-1, keepdims=True)
    )
    head_part = jnp.einsum(
        "hsd,hse->hde",
        query_float * jnp.exp(cumulative)[..., None],
        membrane_grad,
        precision=precise,
    )
    decay_after, state_after = entering(
        (block_decay, head_part), "seq", chain_states, identity, True
    )
    later_part = jnp.einsum("htd,hde->hte", key_float, state_after, precision=precise)
    spike_grad = (
        jnp.einsum("hst,hsd->htd", decayed, membrane_grad, precision=precise)
        + tail_decay[..., None] * later_part
    )
    level_grad = spike_grad * (1.0 - bounded * bounded)
    gain_part = jnp.sum(level_grad * normed, axis=1).reshape(q_heads * HEAD_SIZE)
    gain_grads = lax.psum(gain_part, ("seq", "dp"))
    normed_grad = level_grad * gain_rows
    slope_sum = lax.psum(jnp.sum(normed_grad * normed, axis=(0, 2)), "tensor")
    output_gradient = (
        inverse[None, :, None] * (normed_grad - normed * (slope_sum / D)[None, :, None])
    ).astype(jnp.bfloat16)

    def backward_head(operands):
        query_rows, grad_rows, row_max, row_sum, kv_index = operands
        key_row_block = lax.dynamic_index_in_dim(window_keys, kv_index, 0, keepdims=False)
        value_rows = lax.dynamic_index_in_dim(window_values, kv_index, 0, keepdims=False)
        key_reach = lax.dynamic_index_in_dim(key_window_length, kv_index, 0, keepdims=False)
        logits = head_logits(query_rows, key_row_block, first_query, key_reach, scaling)
        probs = jnp.exp(logits - row_max[:, None]) / row_sum[:, None]
        weights = probs.astype(jnp.bfloat16)
        prob_grad = jnp.einsum(
            "sd,kd->sk", grad_rows, value_rows, preferred_element_type=jnp.float32
        )
        row_delta = jnp.sum(probs * prob_grad, axis=-1, keepdims=True)
        logit_grad = (probs * (prob_grad - row_delta) * scaling).astype(jnp.bfloat16)
        query_grad = jnp.dot(logit_grad, key_row_block, preferred_element_type=jnp.float32)
        key_part = jnp.einsum(
            "sk,sd->kd", logit_grad, query_rows, preferred_element_type=jnp.float32
        )
        value_part = jnp.einsum("sk,sd->kd", weights, grad_rows, preferred_element_type=jnp.float32)
        return (query_grad, key_part, value_part)

    query_parts, key_parts, value_parts = lax.map(
        backward_head, (head_queries, output_gradient, maxima, sums, kv_of_head)
    )
    key_sum = key_parts.reshape(kv_heads, head_groups, key_span + block_rows, HEAD_SIZE).sum(axis=1)
    value_sum = value_parts.reshape(kv_heads, head_groups, key_span + block_rows, HEAD_SIZE).sum(
        axis=1
    )
    pair_grads = jnp.stack([key_sum, value_sum])
    own_grads = pair_grads[:, :, key_span:]
    carried_grads = jnp.zeros_like(own_grads)
    for distance in range(previous, 0, -1):
        offset = (previous - distance) * block_rows
        carried_grads = passed_along(
            carried_grads + pair_grads[:, :, offset : offset + block_rows], "seq", -1
        )
    total_grads = own_grads + carried_grads
    query_grads = (
        query_parts.astype(jnp.bfloat16)
        .transpose(1, 0, 2)
        .reshape(1, block_rows, q_heads * HEAD_SIZE)
    )
    key_gradient = (
        total_grads[0]
        .astype(jnp.bfloat16)
        .transpose(1, 0, 2)
        .reshape(1, block_rows, kv_heads * HEAD_SIZE)
    )
    value_gradient = (
        total_grads[1]
        .astype(jnp.bfloat16)
        .transpose(1, 0, 2)
        .reshape(1, block_rows, kv_heads * HEAD_SIZE)
    )
    return (layer_output, query_grads, key_gradient, value_gradient, gain_grads)


def solution(mesh):
    placed = (
        P("dp", "seq", "tensor"),
        P("dp", "seq", "tensor"),
        P("dp", "seq", "tensor"),
        P("tensor"),
        P("tensor"),
        P("tensor"),
        P("dp", "seq", "tensor"),
        P("dp", "seq", "tensor"),
        P("dp", "tensor", "seq"),
        P("dp", "seq", "tensor"),
    )
    return jax.shard_map(
        local,
        mesh=mesh,
        in_specs=placed,
        out_specs=(
            P("dp", "seq", "tensor"),
            P("dp", "seq", "tensor"),
            P("dp", "seq", "tensor"),
            P("dp", "seq", "tensor"),
            P("tensor"),
        ),
        check_vma=False,
    )
```

profile of v0, /device:TPU:1, one launch (start us, length us, event | category | flops | bytes accessed | tf_op | source)
XLA Modules:
  0.0 717.0 jit_solution(11965284962167923408)
XLA Ops:
  8.0 4.9 collective-permute-start
  13.9 3.0 collective-permute-done
  16.8 1.9 collective-permute-start.1
  20.1 4.3 collective-permute-start.2
  25.6 4.3 collective-permute-start.3
  33.9 28.6 %while.62 = (s32[]{:T(128)}, bf16[7,128,128]{2,1,0:T(8,128)(2,1)S(1)}, f32[7,128]{1,0:T(8,128)}, f32[7,128]{1,0:T(8,128)}, s32[]{:T(128)}, /*index=5*/s32[]{:T(1...) while((s32[]{:T(128)}, ...), condition=%wide.region_4.5_spmd, body=%wide.region_1.4_spmd.sunk | while | flops 42944384 | bytes 1391389 | solution.py:107
  62.7 8.6 %psum.21 = f32[128]{0:T(128)S(1)} all-reduce(f32[128]{0:T(128)S(1)} %fusion.52), channel_id=1, replica_groups=mesh['seq'=32,'dp'=4,'tensor'=4] {'tensor'}, use_global_device_ids=true, to_apply=%region_6.7 | all-reduce | flops 128 | bytes 1024 | tf_op jit(solution)/shard_map/psum | solution.py:109
  74.8 56.0 %all-reduce = f32[224]{0:T(256)S(1)} all-reduce(f32[224]{0:T(256)S(1)} %dynamic-update-slice), channel_id=2, replica_groups=mesh['seq'=32,'dp'=4,'tensor'=4] {'seq'}, use_global_device_ids=true, to_apply=%add | all-reduce | flops 224 | bytes 1792
  131.7 45.4 %all-gather.6.cloned.1.call-done = f32[224,128,128]{2,1,0:T(8,128)} async-done(((f32[7,128,128]{2,1,0:T(8,128)}), f32[224,128,128]{2,1,0:T(8,128)}) %all-gather.6.cloned.1.call-update) | async-done | bytes 14680080 | tf_op jit(solution)/shard_map/all_gather | solution.py:25
  177.1 36.8 %while.64 = (s32[]{:T(128)}, f32[7,128,128]{2,1,0:T(8,128)S(1)}, s32[]{:T(128)}, f32[32,7]{1,0:T(8,128)S(1)}, f32[32,7,128,128]{3,2,1,0:T(8,128)}, /*index=5*/s32[]{:T(128)}, s32[]{:T(128)}) while((s32[]{:T(128)}, f32[7,128,128]{2,1,0:T(8,128)S(1)}, s32[]{:T(128)}, f32[32,7]{1,0:T(8,128)S(1)}, f32[32,7,128,128]{3,2,1,0:T(8,128)}, ...), condition=%wide.region_8.9_spmd.clone, body=%wide.region_7.8_spmd.clone.sunk | while | flops 458756 | bytes 1376453 | solution.py:37
  216.8 1.9 fusion.56
  219.3 93.6 %all-gather.8.cloned.1.call-done = f32[224,128,128]{2,1,0:T(8,128)} async-done(((f32[7,128,128]{2,1,0:T(8,128)}), f32[224,128,128]{2,1,0:T(8,128)}) %all-gather.8.cloned.1.call-update) | async-done | bytes 14680080 | tf_op jit(solution)/shard_map/all_gather | solution.py:25
  312.9 13.1 %rev.7 = f32[32,7,128,128]{3,2,1,0:T(8,128)} reverse(f32[32,7,128,128]{3,2,1,0:T(8,128)} %bitcast.189), dimensions={0} | reverse | bytes 29360128 | tf_op jit(solution)/shard_map/rev | solution.py:27
  326.0 57.7 %while.65 = (s32[]{:T(128)}, f32[7,128,128]{2,1,0:T(8,128)S(1)}, s32[]{:T(128)}, f32[32,7]{1,0:T(8,128)}, f32[32,7,128,128]{3,2,1,0:T(8,128)}, /*index=5*/s32[]{:T(128)}, s32[]{:T(128)}) while((s32[]{:T(128)}, f32[7,128,128]{2,1,0:T(8,128)S(1)}, s32[]{:T(128)}, f32[32,7]{1,0:T(8,128)}, f32[32,7,128,128]{3,2,1,0:T(8,128)}, ...), condition=%wide.region_12.13_spmd.clone, body=%wide.region_11.12_spmd.clone.sunk | while | flops 458756 | bytes 1376453 | solution.py:37
  385.1 3.7 fusion.51
  388.8 8.4 %psum.22 = f32[128]{0:T(128)S(1)} all-reduce(f32[128]{0:T(128)S(1)} %get-tuple-element.606), channel_id=1, replica_groups=mesh['seq'=32,'dp'=4,'tensor'=4] {'tensor'}, use_global_device_ids=true, to_apply=%region_14.15 | all-reduce | flops 128 | bytes 1024 | tf_op jit(solution)/shard_map/psum | solution.py:171
  398.4 39.9 %while.63 = (s32[]{:T(128)}, bf16[7,128,128]{1,2,0:T(8,128)(2,1)}, f32[7,640,128]{2,1,0:T(8,128)}, f32[7,640,128]{2,1,0:T(8,128)S(1)}, s32[]{:T(128)}, /*index=5...) while((s32[]{:T(128)}, bf16[7,128,128]{1,2,0:T(8,128)(2,1)}, ...), condition=%wide.region_17.18_spmd, body=%wide.region_15.17_spmd.sunk | while | flops 106088448 | bytes 3815853 | solution.py:196
  402.4 1.7 fusion.121
  408.1 1.8 fusion.121
  413.9 1.7 fusion.121
  419.6 1.7 fusion.121
  425.3 1.7 fusion.121
  436.6 1.7 fusion.121
  438.5 1.8 reduce_sum.91
  440.4 4.3 collective-permute-start.4
  444.7 2.1 collective-permute-done.4
  446.9 1.9 collective-permute-start.5
  448.8 4.4 collective-permute-done.5
  453.2 1.9 collective-permute-start.6
  455.1 4.4 collective-permute-done.6
  459.5 1.9 collective-permute-start.7
  463.2 246.4 %psum.23 = f32[896]{0:T(1024)} all-reduce(f32[896]{0:T(1024)S(1)} %bitcast.224), channel_id=1, replica_groups=mesh['seq'=32,'dp'=4,'tensor'=4] {'seq','dp'}, use_global_device_ids=true, to_apply=%region_21.22 | all-reduce | flops 896 | bytes 7168 | tf_op jit(solution)/shard_map/psum | solution.py:169
  (339 shorter events, 171.2 us)
Async XLA Ops:
  7.2 169.9 %all-gather.6.cloned.1.call-start = ((), (), s32[]{:S(2)}) async-start(), calls=%async_computation | async-start | bytes 15138816 | tf_op jit(solution)/shard_map/all_gather | solution.py:25
  8.0 8.9 %collective-permute-start = (bf16[2,1,128,128]{3,2,1,0:T(8,128)(2,1)S(1)}, bf16[2,1,128,128]{3,2,1,0:T(8,128)(2,1)S(1)}, u32[]{:S(2)}, u32[]{:S(2)}) collective-permute-start(bf16[2,1,128,128]{3,2,1,0:T(8,128)(2,1)S(1)} %pad_maximum_fusion.1), channel_id=1, source_target_pairs={{0,16},{16,32},{32,48},{48,64},{64,80},{80,96},{96,112},{112,128},... | collective-permute-start | bytes 196616 | tf_op jit(solution)/shard_map/ppermute | solution.py:20
  16.8 3.2 collective-permute-start.1
  20.1 5.6 collective-permute-start.2
  24.4 46.9 %copy-start.11 = (f32[7,128]{1,0:T(8,128)}, f32[7,128]{1,0:T(8,128)S(1)}, u32[]{:S(2)}) copy-start(f32[7,128]{1,0:T(8,128)S(1)} %get-tuple-element.695) | copy-start | bytes 10756
  25.6 7.4 %collective-permute-start.3 = (bf16[2,1,128,128]{3,2,1,0:T(8,128)(2,1)S(1)}, bf16[2,1,128,128]{3,2,1,0:T(8,128)(2,1)S(1)}, u32[]{:S(2)}, u32[]{:S(2)}) collective-permute-start(bf16[2,1,128,128]{3,2,1,0:T(8,128)(2,1)S(1)} %collective-permute-done.2), channel_id=1, source_target_pairs={{0,16},{16,32},{32,48},{48,64},{64,80},{80,96},{96,112},{112,128},... | collective-permute-start | bytes 196616 | tf_op jit(solution)/shard_map/ppermute | solution.py:20
  30.6 183.8 %copy-start.13 = (f32[7,128]{1,0:T(8,128)}, f32[7,128]{1,0:T(8,128)S(1)}, u32[]{:S(2)}) copy-start(f32[7,128]{1,0:T(8,128)S(1)} %convert_bitcast_fusion) | copy-start | bytes 10756
  33.0 98.3 %copy-start.5 = (bf16[1,128,896]{1,2,0:T(8,128)(2,1)}, bf16[1,128,896]{1,2,0:T(8,128)(2,1)S(1)}, u32[]{:S(2)}) copy-start(bf16[1,128,896]{1,2,0:T(8,128)(2,1)S(1)} %copy.51) | copy-start | bytes 688132
  33.9 37.3 %copy-start.12 = (f32[896]{0:T(1024)S(1)}, f32[896]{0:T(1024)}, u32[]{:S(2)}) copy-start(f32[896]{0:T(1024)} %param.22) | copy-start | bytes 10756
  62.5 68.4 %copy-start.6 = (bf16[7,128,128]{2,1,0:T(8,128)(2,1)}, bf16[7,128,128]{2,1,0:T(8,128)(2,1)S(1)}, u32[]{:S(2)}) copy-start(bf16[7,128,128]{2,1,0:T(8,128)(2,1)S(1)} %get-tuple-element.1047) | copy-start | bytes 688132
  62.5 151.9 %copy-start.3 = (bf16[7,128,128]{2,1,0:T(8,128)(2,1)}, bf16[7,128,128]{2,1,0:T(8,128)(2,1)S(1)}, u32[]{:S(2)}) copy-start(bf16[7,128,128]{2,1,0:T(8,128)(2,1)S(1)} %get-tuple-element.500) | copy-start | bytes 688132
  62.5 68.4 %copy-start.8 = (bf16[1,128,896]{2,1,0:T(8,128)(2,1)S(1)}, bf16[1,128,896]{2,1,0:T(8,128)(2,1)}, u32[]{:S(2)}) copy-start(bf16[1,128,896]{2,1,0:T(8,128)(2,1)} %param.24) | copy-start | bytes 688132
  62.5 68.6 %copy-start.10 = (bf16[1,128,896]{2,1,0:T(8,128)(2,1)S(1)}, bf16[1,128,896]{2,1,0:T(8,128)(2,1)}, u32[]{:S(2)}) copy-start(bf16[1,128,896]{2,1,0:T(8,128)(2,1)} %param.27) | copy-start | bytes 688132
  71.3 143.2 %copy-start.15 = (f32[128]{0:T(128)}, f32[128]{0:T(128)S(1)}, u32[]{:S(2)}) copy-start(f32[128]{0:T(128)S(1)} %add_rsqrt_fusion.1) | copy-start | bytes 1540
  72.6 240.3 %all-gather.8.cloned.1.call-start = ((), (), s32[]{:S(2)}) async-start(), calls=%async_computation.1 | async-start | bytes 15138816 | tf_op jit(solution)/shard_map/all_gather | solution.py:25
  131.6 82.8 %copy-start.16 = (f32[7,128,128]{2,1,0:T(8,128)}, f32[7,128,128]{2,1,0:T(8,128)S(1)}, u32[]{:S(2)}) copy-start(f32[7,128,128]{2,1,0:T(8,128)S(1)} %convolution_multiply_fusion.3) | copy-start | bytes 1376260
  214.4 0.8 copy-start
  216.7 2.6 copy-start.2
  385.1 12.1 %copy-start.4 = (bf16[7,128,128]{2,1,0:T(8,128)(2,1)S(1)}, bf16[7,128,128]{2,1,0:T(8,128)(2,1)}, u32[]{:S(2)}) copy-start(bf16[7,128,128]{2,1,0:T(8,128)(2,1)} %copy-done.3) | copy-start | bytes 688132
  440.3 21.1 %copy-start.1 = (f32[7,128,128]{2,1,0:T(8,128)S(1)}, f32[7,128,128]{2,1,0:T(8,128)}, u32[]{:S(2)}) copy-start(f32[7,128,128]{2,1,0:T(8,128)} %copy-done) | copy-start | bytes 1376260
  440.3 21.1 %copy-start.7 = (f32[7,128,128]{1,2,0:T(8,128)S(1)}, f32[7,128,128]{1,2,0:T(8,128)}, u32[]{:S(2)}) copy-start(f32[7,128,128]{1,2,0:T(8,128)} %get-tuple-element.696) | copy-start | bytes 1376260
  440.3 22.0 %copy-start.9 = (bf16[7,128,128]{1,2,0:T(8,128)(2,1)S(1)}, bf16[7,128,128]{1,2,0:T(8,128)(2,1)}, u32[]{:S(2)}) copy-start(bf16[7,128,128]{1,2,0:T(8,128)(2,1)} %get-tuple-element.505) | copy-start | bytes 688132
  440.3 22.8 %copy-start.14 = (f32[7,128]{1,0:T(8,128)S(1)}, f32[7,128]{1,0:T(8,128)}, u32[]{:S(2)}) copy-start(f32[7,128]{1,0:T(8,128)} %get-tuple-element.605) | copy-start | bytes 10756
  440.4 6.5 collective-permute-start.4
  446.9 6.3 collective-permute-start.5
  453.2 6.3 collective-permute-start.6
  459.5 250.1 %collective-permute-start.7 = (f32[2,1,128,128]{3,2,1,0:T(8,128)S(1)}, f32[2,1,128,128]{3,2,1,0:T(8,128)S(1)}, u32[]{:S(2)}, u32[]{:S(2)}) collective-permute-start(f32[2,1,128,128]{3,2,1,0:T(8,128)S(1)} %fusion.72), channel_id=1, source_target_pairs={{16,0},{32,16},{48,32},{64,48},{80,64},{96,80},{112,96},{128,112},... | collective-permute-start | bytes 393224 | tf_op jit(solution)/shard_map/ppermute | solution.py:20
Sparse Core Ops, SparseCore 0:
  72.7 104.3 all-gather.5
  218.8 94.0 all-gather.7
where the time goes:
time: 727 us; the launch traced here: 717 us
  blocking collectives  319 us (44%)
  waiting for transfers between devices  155 us (21%)
  other arithmetic  88.5 us (12%)
  local copies, waits for them, and re-layouts  67 us (9%)
  matrix products  44.1 us (6%)
  starting transfers between devices  25.5 us (4%)
  between operations  15.1 us (2%)
    psum x1, blocking collectives, local(): gain_grads = lax.psum(gain_part, ('seq', 'dp'))  246 us
    all_gather x2, waiting for transfers between devices, entering(): pieces = jax.tree.map(lambda part: lax.all_gather(part, axis), value)  139 us
    select_n x62, other arithmetic, turn(): jnp.where(position < mine, new, old)  70.8 us
    unnamed x1, blocking collectives  56 us
    ppermute x8, starting transfers between devices, passed_along(): return lax.ppermute(block, axis, route)  25.4 us
    mul x62, local copies, waits for them, and re-layouts, chain_states(): later[0][:, None, None] * earlier[1] + later[1]  21.9 us
    dynamic_update_slice x14, local copies, waits for them, and re-layouts, local(): heads_out, maxima, sums = lax.map(forward_head, (head_queries, kv_of_head))  18.1 us
    ppermute x8, waiting for transfers between devices, passed_along(): return lax.ppermute(block, axis, route)  16.2 us
  transfers between devices with their start and end apart: 10, of which 8 were waited for; matrix products, arithmetic and copies ran while one was open for 1% of the time, Pallas kernels for 0%

commit v1 on v0

--- a/solution.py
+++ b/solution.py
@@ -22,19 +22,40 @@
 
 def entering(value, axis, join, neutral, backward):
     count, mine = (lax.axis_size(axis), lax.axis_index(axis))
-    pieces = jax.tree.map(lambda part: lax.all_gather(part, axis), value)
     if backward:
-        pieces = jax.tree.map(lambda part: part[::-1], pieces)
         mine = count - 1 - mine
-    running = jax.tree.map(
+    before = jax.tree.map(
         lambda part, zero: jnp.full_like(part, 0) + jnp.asarray(zero, part.dtype), value, neutral
     )
-
-    def turn(position, running):
-        longer = join(running, jax.tree.map(lambda part: part[position], pieces))
-        return jax.tree.map(lambda new, old: jnp.where(position < mine, new, old), longer, running)
-
-    return lax.fori_loop(0, count - 1, turn, running)
+    covered = value
+    distance = 1
+    while distance < count:
+        moved = passed_along(covered, axis, -distance if backward else distance)
+        present = mine >= distance
+        before = jax.tree.map(
+            lambda new, old: jnp.where(present, new, old), join(moved, before), before
+        )
+        if 2 * distance < count:
+            covered = jax.tree.map(
+                lambda new, old: jnp.where(present, new, old), join(moved, covered), covered
+            )
+        distance *= 2
+    return before
+
+
+def summed(value, axes):
+    for axis in axes:
+        count = lax.axis_size(axis)
+        if count & (count - 1):
+            value = lax.psum(value, axis)
+            continue
+        distance = 1
+        while distance < count:
+            value = value + lax.ppermute(
+                value, axis, [(i, i ^ distance) for i in range(count)]
+            )
+            distance *= 2
+    return value
 
 
 def head_logits(query_rows, key_row_block, first_query, key_reach, scaling):
@@ -75,12 +96,8 @@
     first_query = lax.axis_index("seq") * block_rows
     scaling = 1.0 / math.sqrt(HEAD_SIZE)
     own_pair = jnp.stack([attention_keys, attention_values])
-    earlier_blocks = []
-    moving = own_pair
-    for distance in range(previous):
-        moving = passed_along(moving, "seq", 1)
-        earlier_blocks.append(moving)
-    window_pair = jnp.concatenate(earlier_blocks[::-1] + [own_pair], axis=2)
+    earlier_blocks = [passed_along(own_pair, "seq", distance) for distance in range(previous, 0, -1)]
+    window_pair = jnp.concatenate(earlier_blocks + [own_pair], axis=2)
     window_pair = window_pair.reshape(2, key_span + block_rows, kv_heads, HEAD_SIZE).transpose(
         0, 2, 1, 3
     )
@@ -106,7 +123,7 @@
 
     heads_out, maxima, sums = lax.map(forward_head, (head_queries, kv_of_head))
     out_float = heads_out.astype(jnp.float32)
-    square_sum = lax.psum(jnp.sum(out_float * out_float, axis=(0, 2)), "tensor")
+    square_sum = summed(jnp.sum(out_float * out_float, axis=(0, 2)), ("tensor",))
     inverse = 1.0 / jnp.sqrt(square_sum / D + epsilon)
     normed = out_float * inverse[None, :, None]
     gain_rows = norm_gain.reshape(q_heads, HEAD_SIZE)[:, None, :]
@@ -166,9 +183,9 @@
     )
     level_grad = spike_grad * (1.0 - bounded * bounded)
     gain_part = jnp.sum(level_grad * normed, axis=1).reshape(q_heads * HEAD_SIZE)
-    gain_grads = lax.psum(gain_part, ("seq", "dp"))
+    gain_grads = summed(gain_part, ("seq", "dp"))
     normed_grad = level_grad * gain_rows
-    slope_sum = lax.psum(jnp.sum(normed_grad * normed, axis=(0, 2)), "tensor")
+    slope_sum = summed(jnp.sum(normed_grad * normed, axis=(0, 2)), ("tensor",))
     output_gradient = (
         inverse[None, :, None] * (normed_grad - normed * (slope_sum / D)[None, :, None])
     ).astype(jnp.bfloat16)
@@ -202,13 +219,12 @@
     )
     pair_grads = jnp.stack([key_sum, value_sum])
     own_grads = pair_grads[:, :, key_span:]
-    carried_grads = jnp.zeros_like(own_grads)
+    total_grads = own_grads
     for distance in range(previous, 0, -1):
         offset = (previous - distance) * block_rows
-        carried_grads = passed_along(
-            carried_grads + pair_grads[:, :, offset : offset + block_rows], "seq", -1
-        )
-    total_grads = own_grads + carried_grads
+        total_grads = total_grads + passed_along(
+            pair_grads[:, :, offset : offset + block_rows], "seq", -distance
+        )
     query_grads = (
         query_parts.astype(jnp.bfloat16)
         .transpose(1, 0, 2)

time: 727 us -> 467 us (0.64)
  blocking collectives: 319 us -> 0 us
  starting transfers between devices: 25.5 us -> 197 us
  other arithmetic: 88.5 us -> 24.4 us
  local copies, waits for them, and re-layouts: 67 us -> 31.7 us
  between operations: 15.1 us -> 1.72 us
    psum x3 -> x0, blocking collectives: 263 us -> none  [the longest x1 246 us: local(): gain_grads = lax.psum(gain_part, ('seq', 'dp'))]
    all_gather x2 -> x0, waiting for transfers between devices: 139 us -> none  [entering(): pieces = jax.tree.map(lambda part: lax.all_gather(part, axis), value)]
    ppermute x8 -> x26, waiting for transfers between devices: 16.2 us -> 155 us  [passed_along(): return lax.ppermute(block, axis, route)]
    ppermute x8 -> x26, starting transfers between devices: 25.4 us -> 128 us  [passed_along(): return lax.ppermute(block, axis, route)]
    ppermute x0 -> x11, starting transfers between devices: none -> 69.2 us  [summed(): lax.ppermute(value, axis, [(i, i ^ distance) for i in range(count)])]
    select_n x62 -> x15, other arithmetic: 70.8 us -> 6.64 us  [entering(): jnp.where(present, new, old)]
    unnamed x1 -> x0, blocking collectives: 56 us -> none
    mul x62 -> x0, local copies, waits for them, and re-layouts: 21.9 us -> none  [chain_states(): later[0][:, None, None] * earlier[1] + later[1]]
  transfers between devices with their start and end apart: 10 -> 37, of which waited for: 8 -> 19; matrix products, arithmetic and copies ran while one was open for 1% -> 12% of each run, Pallas kernels for 0% -> 0%
where the time goes in v1:
time: 467 us; the launch traced here: 459 us
  starting transfers between devices  197 us (42%)
  waiting for transfers between devices  162 us (35%)
  matrix products  41.9 us (9%)
  local copies, waits for them, and re-layouts  31.7 us (7%)
  other arithmetic  24.4 us (5%)
    ppermute x26, waiting for transfers between devices, passed_along(): return lax.ppermute(block, axis, route)  155 us
    ppermute x26, starting transfers between devices, passed_along(): return lax.ppermute(block, axis, route)  128 us
    ppermute x11, starting transfers between devices, summed(): lax.ppermute(value, axis, [(i, i ^ distance) for i in range(count)])  69.2 us
    dynamic_update_slice x14, local copies, waits for them, and re-layouts, local(): heads_out, maxima, sums = lax.map(forward_head, (head_queries, kv_of_head))  18.1 us
    dot_general x7, matrix products, backward_head(): jnp.einsum('sk,sd->kd', logit_grad, query_rows, preferred_element_type=jn...  12.1 us
    dot_general x14, matrix products, head_logits(): jnp.einsum('sd,kd->sk', query_rows, key_row_block, preferred_element_type...  10 us
  transfers between devices with their start and end apart: 37, of which 19 were waited for; matrix products, arithmetic and copies ran while one was open for 12% of the time, Pallas kernels for 0%

profile of v1, /device:TPU:1, one launch (start us, length us, event | category | flops | bytes accessed | tf_op | source)
XLA Modules:
  0.0 459.5 jit_solution(14355289726234212632)
XLA Ops:
  1.4 4.9 %collective-permute-start.3 = (bf16[2,1,128,128]{3,2,1,0:T(8,128)(2,1)S(1)}, bf16[2,1,128,128]{3,2,1,0:T(8,128)(2,1)S(1)}, u32[]{:S(2)}, u32[]{:S(2)}) collective-permute-start(bf16[2,1,128,128]{3,2,1,0:T(8,128)(2,1)S(1)} %pad_maximum_fusion.1), channel_id=1, source_target_pairs={{0,16},{16,32},{32,48},{48,64},{64,80},{80,96},{96,112},{112,128},... | collective-permute-start | bytes 196616 | tf_op jit(solution)/shard_map/ppermute | solution.py:20
  6.3 3.5 collective-permute-start.2
  9.9 3.6 collective-permute-start.1
  13.4 6.1 %collective-permute-start = (bf16[2,1,128,128]{3,2,1,0:T(8,128)(2,1)S(1)}, bf16[2,1,128,128]{3,2,1,0:T(8,128)(2,1)S(1)}, u32[]{:S(2)}, u32[]{:S(2)}) collective-permute-start(bf16[2,1,128,128]{3,2,1,0:T(8,128)(2,1)S(1)} %pad_maximum_fusion.1), channel_id=1, source_target_pairs={{0,64},{16,80},{32,96},{48,112},{64,128},{80,144},{96,160},{112,17... | collective-permute-start | bytes 196616 | tf_op jit(solution)/shard_map/ppermute | solution.py:20
  23.0 28.7 %while.34 = (s32[]{:T(128)}, bf16[7,128,128]{2,1,0:T(8,128)(2,1)S(1)}, f32[7,128]{1,0:T(8,128)}, f32[7,128]{1,0:T(8,128)}, s32[]{:T(128)}, /*index=5*/s32[]{:T(1...) while((s32[]{:T(128)}, ...), condition=%wide.region_4.5_spmd, body=%wide.region_1.4_spmd.sunk | while | flops 42944384 | bytes 1391389 | solution.py:124
  56.1 4.8 %collective-permute-start.5 = (f32[128]{0:T(128)S(1)}, f32[128]{0:T(128)S(1)}, u32[]{:S(2)}, u32[]{:S(2)}) collective-permute-start(f32[128]{0:T(128)S(1)} %add.229), channel_id=1, source_target_pairs={{0,2},{1,3},{2,0},{3,1},{4,6},{5,7},{6,4},{7,5},{8,10},{9,11},{10,... | collective-permute-start | bytes 1544 | tf_op jit(solution)/shard_map/ppermute | solution.py:54
  62.5 6.5 %collective-permute-start.10 = (f32[7,128,128]{2,1,0:T(8,128)S(1)}, f32[7,128,128]{2,1,0:T(8,128)S(1)}, u32[]{:S(2)}, u32[]{:S(2)}) collective-permute-start(f32[7,128,128]{2,1,0:T(8,128)S(1)} %fusion.68), channel_id=1, source_target_pairs={{0,16},{16,32},{32,48},{48,64},{64,80},{80,96},{96,112},{112,128},... | collective-permute-start | bytes 1376264 | tf_op jit(solution)/shard_map/ppermute | solution.py:20
  69.0 5.4 %collective-permute-done.10 = f32[7,128,128]{2,1,0:T(8,128)S(1)} collective-permute-done((f32[7,128,128]{2,1,0:T(8,128)S(1)}, f32[7,128,128]{2,1,0:T(8,128)S(1)}, u32[]{:S(2)}, u32[]{:S(2)}) %collective-permute-start.10) | collective-permute-done | bytes 458784 | tf_op jit(solution)/shard_map/ppermute | solution.py:20
  74.5 3.9 collective-permute-start.11
  81.2 3.7 collective-permute-start.6
  88.3 6.6 %collective-permute-start.12 = (f32[7,128,128]{2,1,0:T(8,128)S(1)}, f32[7,128,128]{2,1,0:T(8,128)S(1)}, u32[]{:S(2)}, u32[]{:S(2)}) collective-permute-start(f32[7,128,128]{2,1,0:T(8,128)S(1)} %add_select_fusion.14), channel_id=1, source_target_pairs={{0,64},{16,80},{32,96},{48,112},{64,128},{80,144},{96,160},{112,17... | collective-permute-start | bytes 1376264 | tf_op jit(solution)/shard_map/ppermute | solution.py:20
  98.4 5.8 %collective-permute-done.7 = f32[7]{0:T(128)S(1)} collective-permute-done((f32[7]{0:T(128)S(1)}, f32[7]{0:T(128)S(1)}, u32[]{:S(2)}, u32[]{:S(2)}) %collective-permute-start.7) | collective-permute-done | bytes 60 | tf_op jit(solution)/shard_map/ppermute | solution.py:20
  104.9 13.8 %collective-permute-start.13 = (f32[7,128,128]{2,1,0:T(8,128)S(1)}, f32[7,128,128]{2,1,0:T(8,128)S(1)}, u32[]{:S(2)}, u32[]{:S(2)}) collective-permute-start(f32[7,128,128]{2,1,0:T(8,128)S(1)} %add_select_fusion.13), channel_id=1, source_target_pairs={{0,128},{16,144},{32,160},{48,176},{64,192},{80,208},{96,224},{112... | collective-permute-start | bytes 1376264 | tf_op jit(solution)/shard_map/ppermute | solution.py:20
  120.9 4.4 collective-permute-start.8
  126.3 32.5 %collective-permute-start.14 = (f32[7,128,128]{2,1,0:T(8,128)S(1)}, f32[7,128,128]{2,1,0:T(8,128)S(1)}, u32[]{:S(2)}, u32[]{:S(2)}) collective-permute-start(f32[7,128,128]{2,1,0:T(8,128)S(1)} %add_select_fusion.12), channel_id=1, source_target_pairs={{0,256},{16,272},{32,288},{48,304},{64,320},{80,336},{96,352},{112... | collective-permute-start | bytes 1376264 | tf_op jit(solution)/shard_map/ppermute | solution.py:20
  160.4 7.5 %collective-permute-done.9 = f32[7]{0:T(128)S(1)} collective-permute-done((f32[7]{0:T(128)S(1)}, f32[7]{0:T(128)S(1)}, u32[]{:S(2)}, u32[]{:S(2)}) %collective-permute-start.9) | collective-permute-done | bytes 60 | tf_op jit(solution)/shard_map/ppermute | solution.py:20
  172.0 12.5 %collective-permute-start.19 = (f32[7,128,128]{2,1,0:T(8,128)S(1)}, f32[7,128,128]{2,1,0:T(8,128)S(1)}, u32[]{:S(2)}, u32[]{:S(2)}) collective-permute-start(f32[7,128,128]{2,1,0:T(8,128)S(1)} %fusion.60), channel_id=1, source_target_pairs={{16,0},{32,16},{48,32},{64,48},{80,64},{96,80},{112,96},{128,112},... | collective-permute-start | bytes 1376264 | tf_op jit(solution)/shard_map/ppermute | solution.py:20
  184.6 36.9 %collective-permute-done.19 = f32[7,128,128]{2,1,0:T(8,128)S(1)} collective-permute-done((f32[7,128,128]{2,1,0:T(8,128)S(1)}, f32[7,128,128]{2,1,0:T(8,128)S(1)}, u32[]{:S(2)}, u32[]{:S(2)}) %collective-permute-start.19) | collective-permute-done | bytes 458784 | tf_op jit(solution)/shard_map/ppermute | solution.py:20
  222.9 11.5 %collective-permute-done.20 = f32[7,128,128]{2,1,0:T(8,128)S(1)} collective-permute-done((f32[7,128,128]{2,1,0:T(8,128)S(1)}, f32[7,128,128]{2,1,0:T(8,128)S(1)}, u32[]{:S(2)}, u32[]{:S(2)}) %collective-permute-start.20) | collective-permute-done | bytes 458784 | tf_op jit(solution)/shard_map/ppermute | solution.py:20
  237.7 3.7 collective-permute-done.16
  242.6 12.2 %collective-permute-done.21 = f32[7,128,128]{2,1,0:T(8,128)S(1)} collective-permute-done((f32[7,128,128]{2,1,0:T(8,128)S(1)}, f32[7,128,128]{2,1,0:T(8,128)S(1)}, u32[]{:S(2)}, u32[]{:S(2)}) %collective-permute-start.21) | collective-permute-done | bytes 458784 | tf_op jit(solution)/shard_map/ppermute | solution.py:20
  258.3 9.9 %collective-permute-done.17 = f32[7]{0:T(128)S(1)} collective-permute-done((f32[7]{0:T(128)}, f32[7]{0:T(128)S(1)}, u32[]{:S(2)}, u32[]{:S(2)}) %collective-permute-start.17) | collective-permute-done | bytes 60 | tf_op jit(solution)/shard_map/ppermute | solution.py:20
  269.4 33.5 %collective-permute-done.22 = f32[7,128,128]{2,1,0:T(8,128)S(1)} collective-permute-done((f32[7,128,128]{2,1,0:T(8,128)}, f32[7,128,128]{2,1,0:T(8,128)S(1)}, u32[]{:S(2)}, u32[]{:S(2)}) %collective-permute-start.22) | collective-permute-done | bytes 458784 | tf_op jit(solution)/shard_map/ppermute | solution.py:20
  307.6 13.3 %collective-permute-done.18 = f32[7]{0:T(128)S(1)} collective-permute-done((f32[7]{0:T(128)}, f32[7]{0:T(128)S(1)}, u32[]{:S(2)}, u32[]{:S(2)}) %collective-permute-start.18) | collective-permute-done | bytes 60 | tf_op jit(solution)/shard_map/ppermute | solution.py:20
  321.6 10.9 %collective-permute-done.23 = f32[7,128,128]{2,1,0:T(8,128)} collective-permute-done((f32[7,128,128]{2,1,0:T(8,128)}, f32[7,128,128]{2,1,0:T(8,128)}, u32[]{:S(2)}, u32[]{:S(2)}) %collective-permute-start.23) | collective-permute-done | bytes 458784 | tf_op jit(solution)/shard_map/ppermute | solution.py:20
  336.2 4.3 collective-permute-start.30
  341.3 27.4 %collective-permute-start.31 = (f32[896]{0:T(1024)S(1)}, f32[896]{0:T(1024)S(1)}, u32[]{:S(2)}, u32[]{:S(2)}) collective-permute-start(f32[896]{0:T(1024)S(1)} %bitcast_add_fusion.1), channel_id=1, source_target_pairs={{0,32},{16,48},{32,0},{48,16},{64,96},{80,112},{96,64},{112,80},{1... | collective-permute-start | bytes 10760 | tf_op jit(solution)/shard_map/ppermute | solution.py:54
  373.0 4.8 %collective-permute-start.25 = (f32[128]{0:T(128)S(1)}, f32[128]{0:T(128)S(1)}, u32[]{:S(2)}, u32[]{:S(2)}) collective-permute-start(f32[128]{0:T(128)S(1)} %add.254), channel_id=1, source_target_pairs={{0,2},{1,3},{2,0},{3,1},{4,6},{5,7},{6,4},{7,5},{8,10},{9,11},{10,... | collective-permute-start | bytes 1544 | tf_op jit(solution)/shard_map/ppermute | solution.py:54
  383.2 10.2 %collective-permute-start.33 = (f32[896]{0:T(1024)S(1)}, f32[896]{0:T(1024)S(1)}, u32[]{:S(2)}, u32[]{:S(2)}) collective-permute-start(f32[896]{0:T(1024)S(1)} %add.262), channel_id=1, source_target_pairs={{0,128},{16,144},{32,160},{48,176},{64,192},{80,208},{96,224},{112... | collective-permute-start | bytes 10760 | tf_op jit(solution)/shard_map/ppermute | solution.py:54
  396.5 39.9 %while.35 = (s32[]{:T(128)}, bf16[7,128,128]{1,2,0:T(8,128)(2,1)}, f32[7,640,128]{2,1,0:T(8,128)}, f32[7,640,128]{2,1,0:T(8,128)S(1)}, s32[]{:T(128)}, /*index=5...) while((s32[]{:T(128)}, bf16[7,128,128]{1,2,0:T(8,128)(2,1)}, ...), condition=%wide.region_11.12_spmd, body=%wide.region_9.11_spmd.sunk | while | flops 106088448 | bytes 3815853 | solution.py:213
  444.2 5.4 %collective-permute-start.29 = (f32[2,1,128,128]{3,2,1,0:T(8,128)S(1)}, f32[2,1,128,128]{3,2,1,0:T(8,128)S(1)}, u32[]{:S(2)}, u32[]{:S(2)}) collective-permute-start(f32[2,1,128,128]{3,2,1,0:T(8,128)S(1)} %get-tuple-element.421), channel_id=1, source_target_pairs={{16,0},{32,16},{48,32},{64,48},{80,64},{96,80},{112,96},{128,112},... | collective-permute-start | bytes 393224 | tf_op jit(solution)/shard_map/ppermute | solution.py:20
  450.9 4.4 collective-permute-start.36
  (309 shorter events, 143.5 us)
Async XLA Ops:
  1.4 20.7 %collective-permute-start.3 = (bf16[2,1,128,128]{3,2,1,0:T(8,128)(2,1)S(1)}, bf16[2,1,128,128]{3,2,1,0:T(8,128)(2,1)S(1)}, u32[]{:S(2)}, u32[]{:S(2)}) collective-permute-start(bf16[2,1,128,128]{3,2,1,0:T(8,128)(2,1)S(1)} %pad_maximum_fusion.1), channel_id=1, source_target_pairs={{0,16},{16,32},{32,48},{48,64},{64,80},{80,96},{96,112},{112,128},... | collective-permute-start | bytes 196616 | tf_op jit(solution)/shard_map/ppermute | solution.py:20
  6.3 15.8 %collective-permute-start.2 = (bf16[2,1,128,128]{3,2,1,0:T(8,128)(2,1)S(1)}, bf16[2,1,128,128]{3,2,1,0:T(8,128)(2,1)S(1)}, u32[]{:S(2)}, u32[]{:S(2)}) collective-permute-start(bf16[2,1,128,128]{3,2,1,0:T(8,128)(2,1)S(1)} %pad_maximum_fusion.1), channel_id=1, source_target_pairs={{0,32},{16,48},{32,64},{48,80},{64,96},{80,112},{96,128},{112,144}... | collective-permute-start | bytes 196616 | tf_op jit(solution)/shard_map/ppermute | solution.py:20
  9.9 12.2 %collective-permute-start.1 = (bf16[2,1,128,128]{3,2,1,0:T(8,128)(2,1)S(1)}, bf16[2,1,128,128]{3,2,1,0:T(8,128)(2,1)S(1)}, u32[]{:S(2)}, u32[]{:S(2)}) collective-permute-start(bf16[2,1,128,128]{3,2,1,0:T(8,128)(2,1)S(1)} %pad_maximum_fusion.1), channel_id=1, source_target_pairs={{0,48},{16,64},{32,80},{48,96},{64,112},{80,128},{96,144},{112,160... | collective-permute-start | bytes 196616 | tf_op jit(solution)/shard_map/ppermute | solution.py:20
  13.4 8.6 %collective-permute-start = (bf16[2,1,128,128]{3,2,1,0:T(8,128)(2,1)S(1)}, bf16[2,1,128,128]{3,2,1,0:T(8,128)(2,1)S(1)}, u32[]{:S(2)}, u32[]{:S(2)}) collective-permute-start(bf16[2,1,128,128]{3,2,1,0:T(8,128)(2,1)S(1)} %pad_maximum_fusion.1), channel_id=1, source_target_pairs={{0,64},{16,80},{32,96},{48,112},{64,128},{80,144},{96,160},{112,17... | collective-permute-start | bytes 196616 | tf_op jit(solution)/shard_map/ppermute | solution.py:20
  56.1 5.8 %collective-permute-start.5 = (f32[128]{0:T(128)S(1)}, f32[128]{0:T(128)S(1)}, u32[]{:S(2)}, u32[]{:S(2)}) collective-permute-start(f32[128]{0:T(128)S(1)} %add.229), channel_id=1, source_target_pairs={{0,2},{1,3},{2,0},{3,1},{4,6},{5,7},{6,4},{7,5},{8,10},{9,11},{10,... | collective-permute-start | bytes 1544 | tf_op jit(solution)/shard_map/ppermute | solution.py:54
  62.5 11.9 %collective-permute-start.10 = (f32[7,128,128]{2,1,0:T(8,128)S(1)}, f32[7,128,128]{2,1,0:T(8,128)S(1)}, u32[]{:S(2)}, u32[]{:S(2)}) collective-permute-start(f32[7,128,128]{2,1,0:T(8,128)S(1)} %fusion.68), channel_id=1, source_target_pairs={{0,16},{16,32},{32,48},{48,64},{64,80},{80,96},{96,112},{112,128},... | collective-permute-start | bytes 1376264 | tf_op jit(solution)/shard_map/ppermute | solution.py:20
  74.5 13.6 %collective-permute-start.11 = (f32[7,128,128]{2,1,0:T(8,128)S(1)}, f32[7,128,128]{2,1,0:T(8,128)S(1)}, u32[]{:S(2)}, u32[]{:S(2)}) collective-permute-start(f32[7,128,128]{2,1,0:T(8,128)S(1)} %add_select_fusion.15), channel_id=1, source_target_pairs={{0,32},{16,48},{32,64},{48,80},{64,96},{80,112},{96,128},{112,144}... | collective-permute-start | bytes 1376264 | tf_op jit(solution)/shard_map/ppermute | solution.py:20
  78.4 6.6 %collective-permute-start.15 = (f32[7]{0:T(128)S(1)}, f32[7]{0:T(128)S(1)}, u32[]{:S(2)}, u32[]{:S(2)}) collective-permute-start(f32[7]{0:T(128)S(1)} %exp.44), channel_id=1, source_target_pairs={{16,0},{32,16},{48,32},{64,48},{80,64},{96,80},{112,96},{128,112},... | collective-permute-start | bytes 92 | tf_op jit(solution)/shard_map/ppermute | solution.py:20
  81.2 6.4 %collective-permute-start.6 = (f32[7]{0:T(128)S(1)}, f32[7]{0:T(128)S(1)}, u32[]{:S(2)}, u32[]{:S(2)}) collective-permute-start(f32[7]{0:T(128)S(1)} %exp.44), channel_id=1, source_target_pairs={{0,16},{16,32},{32,48},{48,64},{64,80},{80,96},{96,112},{112,128},... | collective-permute-start | bytes 92 | tf_op jit(solution)/shard_map/ppermute | solution.py:20
  88.3 15.9 %collective-permute-start.12 = (f32[7,128,128]{2,1,0:T(8,128)S(1)}, f32[7,128,128]{2,1,0:T(8,128)S(1)}, u32[]{:S(2)}, u32[]{:S(2)}) collective-permute-start(f32[7,128,128]{2,1,0:T(8,128)S(1)} %add_select_fusion.14), channel_id=1, source_target_pairs={{0,64},{16,80},{32,96},{48,112},{64,128},{80,144},{96,160},{112,17... | collective-permute-start | bytes 1376264 | tf_op jit(solution)/shard_map/ppermute | solution.py:20
  94.9 9.3 %collective-permute-start.7 = (f32[7]{0:T(128)S(1)}, f32[7]{0:T(128)S(1)}, u32[]{:S(2)}, u32[]{:S(2)}) collective-permute-start(f32[7]{0:T(128)S(1)} %get-tuple-element.433), channel_id=1, source_target_pairs={{0,32},{16,48},{32,64},{48,80},{64,96},{80,112},{96,128},{112,144}... | collective-permute-start | bytes 92 | tf_op jit(solution)/shard_map/ppermute | solution.py:20
  104.9 21.2 %collective-permute-start.13 = (f32[7,128,128]{2,1,0:T(8,128)S(1)}, f32[7,128,128]{2,1,0:T(8,128)S(1)}, u32[]{:S(2)}, u32[]{:S(2)}) collective-permute-start(f32[7,128,128]{2,1,0:T(8,128)S(1)} %add_select_fusion.13), channel_id=1, source_target_pairs={{0,128},{16,144},{32,160},{48,176},{64,192},{80,208},{96,224},{112... | collective-permute-start | bytes 1376264 | tf_op jit(solution)/shard_map/ppermute | solution.py:20
  126.3 41.6 %collective-permute-start.14 = (f32[7,128,128]{2,1,0:T(8,128)S(1)}, f32[7,128,128]{2,1,0:T(8,128)S(1)}, u32[]{:S(2)}, u32[]{:S(2)}) collective-permute-start(f32[7,128,128]{2,1,0:T(8,128)S(1)} %add_select_fusion.12), channel_id=1, source_target_pairs={{0,256},{16,272},{32,288},{48,304},{64,320},{80,336},{96,352},{112... | collective-permute-start | bytes 1376264 | tf_op jit(solution)/shard_map/ppermute | solution.py:20
  159.1 8.7 %collective-permute-start.9 = (f32[7]{0:T(128)S(1)}, f32[7]{0:T(128)S(1)}, u32[]{:S(2)}, u32[]{:S(2)}) collective-permute-start(f32[7]{0:T(128)S(1)} %broadcast_select_fusion.12), channel_id=1, source_target_pairs={{0,128},{16,144},{32,160},{48,176},{64,192},{80,208},{96,224},{112... | collective-permute-start | bytes 92 | tf_op jit(solution)/shard_map/ppermute | solution.py:20
  172.0 49.4 %collective-permute-start.19 = (f32[7,128,128]{2,1,0:T(8,128)S(1)}, f32[7,128,128]{2,1,0:T(8,128)S(1)}, u32[]{:S(2)}, u32[]{:S(2)}) collective-permute-start(f32[7,128,128]{2,1,0:T(8,128)S(1)} %fusion.60), channel_id=1, source_target_pairs={{16,0},{32,16},{48,32},{64,48},{80,64},{96,80},{112,96},{128,112},... | collective-permute-start | bytes 1376264 | tf_op jit(solution)/shard_map/ppermute | solution.py:20
  221.6 12.8 %collective-permute-start.20 = (f32[7,128,128]{2,1,0:T(8,128)S(1)}, f32[7,128,128]{2,1,0:T(8,128)S(1)}, u32[]{:S(2)}, u32[]{:S(2)}) collective-permute-start(f32[7,128,128]{2,1,0:T(8,128)S(1)} %add_select_fusion.7), channel_id=1, source_target_pairs={{32,0},{48,16},{64,32},{80,48},{96,64},{112,80},{128,96},{144,112}... | collective-permute-start | bytes 1376264 | tf_op jit(solution)/shard_map/ppermute | solution.py:20
  235.1 19.7 %collective-permute-start.21 = (f32[7,128,128]{2,1,0:T(8,128)S(1)}, f32[7,128,128]{2,1,0:T(8,128)S(1)}, u32[]{:S(2)}, u32[]{:S(2)}) collective-permute-start(f32[7,128,128]{2,1,0:T(8,128)S(1)} %add_select_fusion.6), channel_id=1, source_target_pairs={{64,0},{80,16},{96,32},{112,48},{128,64},{144,80},{160,96},{176,11... | collective-permute-start | bytes 1376264 | tf_op jit(solution)/shard_map/ppermute | solution.py:20
  255.7 47.2 %collective-permute-start.22 = (f32[7,128,128]{2,1,0:T(8,128)}, f32[7,128,128]{2,1,0:T(8,128)S(1)}, u32[]{:S(2)}, u32[]{:S(2)}) collective-permute-start(f32[7,128,128]{2,1,0:T(8,128)} %add_select_fusion.5), channel_id=1, source_target_pairs={{128,0},{144,16},{160,32},{176,48},{192,64},{208,80},{224,96},{240... | collective-permute-start | bytes 1376264 | tf_op jit(solution)/shard_map/ppermute | solution.py:20
  257.0 11.2 %collective-permute-start.17 = (f32[7]{0:T(128)}, f32[7]{0:T(128)S(1)}, u32[]{:S(2)}, u32[]{:S(2)}) collective-permute-start(f32[7]{0:T(128)} %copy-done.11), channel_id=1, source_target_pairs={{64,0},{80,16},{96,32},{112,48},{128,64},{144,80},{160,96},{176,11... | collective-permute-start | bytes 92 | tf_op jit(solution)/shard_map/ppermute | solution.py:20
  304.8 27.7 %collective-permute-start.23 = (f32[7,128,128]{2,1,0:T(8,128)}, f32[7,128,128]{2,1,0:T(8,128)}, u32[]{:S(2)}, u32[]{:S(2)}) collective-permute-start(f32[7,128,128]{2,1,0:T(8,128)} %add_select_fusion.4), channel_id=1, source_target_pairs={{256,0},{272,16},{288,32},{304,48},{320,64},{336,80},{352,96},{368... | collective-permute-start | bytes 1376264 | tf_op jit(solution)/shard_map/ppermute | solution.py:20
  306.2 14.8 %collective-permute-start.18 = (f32[7]{0:T(128)}, f32[7]{0:T(128)S(1)}, u32[]{:S(2)}, u32[]{:S(2)}) collective-permute-start(f32[7]{0:T(128)} %copy-done.21), channel_id=1, source_target_pairs={{128,0},{144,16},{160,32},{176,48},{192,64},{208,80},{224,96},{240... | collective-permute-start | bytes 92 | tf_op jit(solution)/shard_map/ppermute | solution.py:20
  341.3 36.6 %collective-permute-start.31 = (f32[896]{0:T(1024)S(1)}, f32[896]{0:T(1024)S(1)}, u32[]{:S(2)}, u32[]{:S(2)}) collective-permute-start(f32[896]{0:T(1024)S(1)} %bitcast_add_fusion.1), channel_id=1, source_target_pairs={{0,32},{16,48},{32,0},{48,16},{64,96},{80,112},{96,64},{112,80},{1... | collective-permute-start | bytes 10760 | tf_op jit(solution)/shard_map/ppermute | solution.py:54
  373.0 6.8 %collective-permute-start.25 = (f32[128]{0:T(128)S(1)}, f32[128]{0:T(128)S(1)}, u32[]{:S(2)}, u32[]{:S(2)}) collective-permute-start(f32[128]{0:T(128)S(1)} %add.254), channel_id=1, source_target_pairs={{0,2},{1,3},{2,0},{3,1},{4,6},{5,7},{6,4},{7,5},{8,10},{9,11},{10,... | collective-permute-start | bytes 1544 | tf_op jit(solution)/shard_map/ppermute | solution.py:54
  377.9 5.3 %collective-permute-start.32 = (f32[896]{0:T(1024)S(1)}, f32[896]{0:T(1024)S(1)}, u32[]{:S(2)}, u32[]{:S(2)}) collective-permute-start(f32[896]{0:T(1024)S(1)} %add.261), channel_id=1, source_target_pairs={{0,64},{16,80},{32,96},{48,112},{64,0},{80,16},{96,32},{112,48},{1... | collective-permute-start | bytes 10760 | tf_op jit(solution)/shard_map/ppermute | solution.py:54
  383.2 11.4 %collective-permute-start.33 = (f32[896]{0:T(1024)S(1)}, f32[896]{0:T(1024)S(1)}, u32[]{:S(2)}, u32[]{:S(2)}) collective-permute-start(f32[896]{0:T(1024)S(1)} %add.262), channel_id=1, source_target_pairs={{0,128},{16,144},{32,160},{48,176},{64,192},{80,208},{96,224},{112... | collective-permute-start | bytes 10760 | tf_op jit(solution)/shard_map/ppermute | solution.py:54
  394.6 43.8 %collective-permute-start.34 = (f32[896]{0:T(1024)S(1)}, f32[896]{0:T(1024)S(1)}, u32[]{:S(2)}, u32[]{:S(2)}) collective-permute-start(f32[896]{0:T(1024)S(1)} %add.263), channel_id=1, source_target_pairs={{0,256},{16,272},{32,288},{48,304},{64,320},{80,336},{96,352},{112... | collective-permute-start | bytes 10760 | tf_op jit(solution)/shard_map/ppermute | solution.py:54
  438.4 12.5 %collective-permute-start.35 = (f32[896]{0:T(1024)S(1)}, f32[896]{0:T(1024)S(1)}, u32[]{:S(2)}, u32[]{:S(2)}) collective-permute-start(f32[896]{0:T(1024)S(1)} %add.264), channel_id=1, source_target_pairs={{0,4},{4,0},{8,12},{12,8},{1,5},{5,1},{9,13},{13,9},{2,6},{6,2},{1... | collective-permute-start | bytes 10760 | tf_op jit(solution)/shard_map/ppermute | solution.py:54
  441.6 16.1 %collective-permute-start.26 = (f32[2,1,128,128]{3,2,1,0:T(8,128)S(1)}, f32[2,1,128,128]{3,2,1,0:T(8,128)S(1)}, u32[]{:S(2)}, u32[]{:S(2)}) collective-permute-start(f32[2,1,128,128]{3,2,1,0:T(8,128)S(1)} %get-tuple-element.419), channel_id=1, source_target_pairs={{64,0},{80,16},{96,32},{112,48},{128,64},{144,80},{160,96},{176,11... | collective-permute-start | bytes 393224 | tf_op jit(solution)/shard_map/ppermute | solution.py:20
  442.9 14.8 %collective-permute-start.27 = (f32[2,1,128,128]{3,2,1,0:T(8,128)S(1)}, f32[2,1,128,128]{3,2,1,0:T(8,128)S(1)}, u32[]{:S(2)}, u32[]{:S(2)}) collective-permute-start(f32[2,1,128,128]{3,2,1,0:T(8,128)S(1)} %get-tuple-element.420), channel_id=1, source_target_pairs={{48,0},{64,16},{80,32},{96,48},{112,64},{128,80},{144,96},{160,112... | collective-permute-start | bytes 393224 | tf_op jit(solution)/shard_map/ppermute | solution.py:20
  444.2 13.5 %collective-permute-start.29 = (f32[2,1,128,128]{3,2,1,0:T(8,128)S(1)}, f32[2,1,128,128]{3,2,1,0:T(8,128)S(1)}, u32[]{:S(2)}, u32[]{:S(2)}) collective-permute-start(f32[2,1,128,128]{3,2,1,0:T(8,128)S(1)} %get-tuple-element.421), channel_id=1, source_target_pairs={{16,0},{32,16},{48,32},{64,48},{80,64},{96,80},{112,96},{128,112},... | collective-permute-start | bytes 393224 | tf_op jit(solution)/shard_map/ppermute | solution.py:20
  449.6 9.2 %collective-permute-start.28 = (f32[2,1,128,128]{3,2,1,0:T(8,128)S(1)}, f32[2,1,128,128]{3,2,1,0:T(8,128)S(1)}, u32[]{:S(2)}, u32[]{:S(2)}) collective-permute-start(f32[2,1,128,128]{3,2,1,0:T(8,128)S(1)} %get-tuple-element.422), channel_id=1, source_target_pairs={{32,0},{48,16},{64,32},{80,48},{96,64},{112,80},{128,96},{144,112}... | collective-permute-start | bytes 393224 | tf_op jit(solution)/shard_map/ppermute | solution.py:20
  450.9 6.1 %collective-permute-start.36 = (f32[896]{0:T(1024)S(1)}, f32[896]{0:T(1024)S(1)}, u32[]{:S(2)}, u32[]{:S(2)}) collective-permute-start(f32[896]{0:T(1024)S(1)} %add.265), channel_id=1, source_target_pairs={{0,8},{4,12},{8,0},{12,4},{1,9},{5,13},{9,1},{13,5},{2,10},{6,14},... | collective-permute-start | bytes 10760 | tf_op jit(solution)/shard_map/ppermute | solution.py:54
  (39 other events, 1180.6 us)

commit v2 on v1

v2 whole, which is shorter than its diff:
```python
import math

import jax
import jax.numpy as jnp
from jax import lax
from jax.sharding import PartitionSpec as P

HEAD_SIZE = 128
D = 3584
LONGEST_WINDOW = 512
HEAD_SPLITS = 2


precise = lax.Precision.HIGHEST
epsilon = 1e-06


def passed_along(block, axis, distance):
    devices = range(lax.axis_size(axis))
    route = [(i - distance, i) for i in devices if i - distance in devices]
    return lax.ppermute(block, axis, route)


def chain_states(earlier, later):
    return (earlier[0] * later[0], later[0][:, None, None] * earlier[1] + later[1])


def picked(flag, new, old):
    return jax.tree.map(lambda a, b: jnp.where(flag, a, b), new, old)


def moved_on(value, axis, pairs):
    return lax.ppermute(value, axis, pairs)


def entering(value, axis, backward):
    count, index = (lax.axis_size(axis), lax.axis_index(axis))
    place = count - 1 - index if backward else index
    spot = (lambda p: count - 1 - p) if backward else (lambda p: p)
    identity = (jnp.ones_like(value[0]), jnp.zeros_like(value[1]))
    if count % 2:
        before, covered, distance = identity, value, 1
        while distance < count:
            moved = moved_on(
                covered, axis, [(spot(p), spot(p + distance)) for p in range(count - distance)]
            )
            present = place >= distance
            before = picked(present, chain_states(moved, before), before)
            covered = picked(present, chain_states(moved, covered), covered)
            distance *= 2
        return before[1]
    lead = place % 2 == 1
    first = moved_on(value, axis, [(spot(p), spot(p + 1)) for p in range(0, count, 2)])
    covered = chain_states(first, value)
    before = identity
    distance = 2
    while distance < count:
        moved = moved_on(
            covered,
            axis,
            [(spot(p), spot(p + distance)) for p in range(1, count - distance, 2)],
        )
        present = place >= distance
        before = picked(present, chain_states(moved, before), before)
        if 2 * distance < count:
            covered = picked(present, chain_states(moved, covered), covered)
        distance *= 2
    handed = moved_on(before[1], axis, [(spot(p), spot(p - 1)) for p in range(1, count, 2)])
    own_lead = chain_states(before, first)[1]
    return jnp.where(lead, own_lead, handed)


def summed(value, axes):
    for axis in axes:
        count = lax.axis_size(axis)
        if count & (count - 1):
            value = lax.psum(value, axis)
            continue
        distance = 1
        while distance < count:
            value = value + lax.ppermute(value, axis, [(i, i ^ distance) for i in range(count)])
            distance *= 2
    return value


def local(
    attention_queries,
    attention_keys,
    attention_values,
    key_window_length,
    norm_gain,
    spike_levels,
    lin_queries,
    lin_keys,
    decay_logs,
    cotangent,
):
    block_rows = attention_queries.shape[1]
    q_heads = attention_queries.shape[2] // HEAD_SIZE
    kv_heads = attention_keys.shape[2] // HEAD_SIZE
    head_groups = q_heads // kv_heads
    previous = (LONGEST_WINDOW + block_rows - 1) // block_rows
    key_span = previous * block_rows
    window = key_span + block_rows
    first_query = lax.axis_index("seq") * block_rows
    scaling = 1.0 / math.sqrt(HEAD_SIZE)
    own_pair = jnp.stack([attention_keys, attention_values])
    earlier_blocks = [passed_along(own_pair, "seq", distance) for distance in range(previous, 0, -1)]
    window_pair = jnp.concatenate(earlier_blocks + [own_pair], axis=2)
    window_pair = window_pair.reshape(2, window, kv_heads, HEAD_SIZE).transpose(0, 2, 1, 3)
    window_keys = window_pair[0]
    window_values = window_pair[1]
    head_queries = attention_queries[0].reshape(block_rows, q_heads, HEAD_SIZE).transpose(1, 0, 2)
    group_queries = head_queries.reshape(kv_heads, head_groups, block_rows, HEAD_SIZE)

    query_pos = first_query + jnp.arange(block_rows, dtype=jnp.int32)[:, None]
    key_pos = first_query - key_span + jnp.arange(window, dtype=jnp.int32)[None, :]
    reach = key_window_length[:, None, None, None]
    allowed = (
        (key_pos >= 0)[None, None]
        & (key_pos <= query_pos)[None, None]
        & (key_pos[None, None] > query_pos[None, None] - reach)
    )
    logits = (
        jnp.einsum(
            "gjsd,gkd->gjsk", group_queries, window_keys, preferred_element_type=jnp.float32
        )
        * scaling
    )
    logits = jnp.where(allowed, logits, -jnp.inf)
    row_max = jnp.max(logits, axis=-1, keepdims=True)
    exponent = jnp.exp(logits - row_max)
    row_sum = jnp.sum(exponent, axis=-1, keepdims=True)
    probs = exponent / row_sum
    weights = probs.astype(jnp.bfloat16)
    heads_out = (
        jnp.einsum("gjsk,gkd->gjsd", weights, window_values, preferred_element_type=jnp.float32)
        .astype(jnp.bfloat16)
        .reshape(q_heads, block_rows, HEAD_SIZE)
    )

    out_float = heads_out.astype(jnp.float32)
    square_sum = summed(jnp.sum(out_float * out_float, axis=(0, 2)), ("tensor",))
    inverse = 1.0 / jnp.sqrt(square_sum / D + epsilon)
    normed = out_float * inverse[None, :, None]
    gain_rows = norm_gain.reshape(q_heads, HEAD_SIZE)[:, None, :]
    ceiling = spike_levels.astype(jnp.float32).reshape(q_heads, HEAD_SIZE)[:, None, :]
    bounded = jnp.tanh(normed * gain_rows / ceiling)
    spikes = (ceiling * bounded).astype(jnp.bfloat16)
    membrane_queries = lin_queries[0].reshape(block_rows, q_heads, HEAD_SIZE).transpose(1, 0, 2)
    membrane_keys = lin_keys[0].reshape(block_rows, q_heads, HEAD_SIZE).transpose(1, 0, 2)
    cumulative = jnp.cumsum(decay_logs[0], axis=1)
    lower_mask = jnp.arange(block_rows)[:, None] >= jnp.arange(block_rows)[None, :]
    gaps = jnp.where(lower_mask[None], cumulative[:, :, None] - cumulative[:, None, :], 0.0)
    products = jnp.einsum(
        "hsd,htd->hst", membrane_queries, membrane_keys, preferred_element_type=jnp.float32
    )
    decayed = jnp.where(lower_mask[None], jnp.exp(gaps), 0.0) * products
    spike_float = spikes.astype(jnp.float32)
    query_float = membrane_queries.astype(jnp.float32)
    key_float = membrane_keys.astype(jnp.float32)
    block_decay = jnp.exp(cumulative[:, -1])
    tail_decay = jnp.exp(cumulative[:, -1:] - cumulative)
    head_decay = jnp.exp(cumulative)
    local_state = jnp.einsum(
        "hsd,hse->hde", key_float * tail_decay[..., None], spike_float, precision=precise
    )
    incoming = (
        cotangent[0].reshape(block_rows, q_heads, HEAD_SIZE).transpose(1, 0, 2).astype(jnp.float32)
    )

    splits = min(HEAD_SPLITS, q_heads)
    bounds = [q_heads * part // splits for part in range(splits + 1)]
    unit_parts, grad_parts = [], []
    for low, high in zip(bounds[:-1], bounds[1:]):
        part = slice(low, high)
        state_in = entering((block_decay[part], local_state[part]), "seq", False)
        carried = jnp.einsum("hsd,hde->hse", query_float[part], state_in, precision=precise)
        membrane = (
            jnp.einsum("hst,htd->hsd", decayed[part], spike_float[part], precision=precise)
            + head_decay[part][..., None] * carried
        )
        scale_out = 1.0 / jnp.sqrt(jnp.mean(membrane * membrane, axis=-1) + epsilon)
        unit_out = membrane * scale_out[..., None]
        membrane_grad = scale_out[..., None] * (
            incoming[part] - unit_out * jnp.mean(incoming[part] * unit_out, axis=-1, keepdims=True)
        )
        head_part = jnp.einsum(
            "hsd,hse->hde",
            query_float[part] * head_decay[part][..., None],
            membrane_grad,
            precision=precise,
        )
        state_after = entering((block_decay[part], head_part), "seq", True)
        later_part = jnp.einsum("htd,hde->hte", key_float[part], state_after, precision=precise)
        spike_grad = (
            jnp.einsum("hst,hsd->htd", decayed[part], membrane_grad, precision=precise)
            + tail_decay[part][..., None] * later_part
        )
        unit_parts.append(unit_out)
        grad_parts.append(spike_grad)
    unit_out = jnp.concatenate(unit_parts, axis=0)
    spike_grad = jnp.concatenate(grad_parts, axis=0)
    layer_output = (
        unit_out.astype(jnp.bfloat16).transpose(1, 0, 2).reshape(1, block_rows, q_heads * HEAD_SIZE)
    )
    level_grad = spike_grad * (1.0 - bounded * bounded)
    gain_part = jnp.sum(level_grad * normed, axis=1).reshape(q_heads * HEAD_SIZE)
    gain_grads = summed(gain_part, ("seq", "dp"))
    normed_grad = level_grad * gain_rows
    slope_sum = summed(jnp.sum(normed_grad * normed, axis=(0, 2)), ("tensor",))
    output_gradient = (
        inverse[None, :, None] * (normed_grad - normed * (slope_sum / D)[None, :, None])
    ).astype(jnp.bfloat16)

    grad_rows = output_gradient.reshape(kv_heads, head_groups, block_rows, HEAD_SIZE)
    prob_grad = jnp.einsum(
        "gjsd,gkd->gjsk", grad_rows, window_values, preferred_element_type=jnp.float32
    )
    row_delta = jnp.sum(probs * prob_grad, axis=-1, keepdims=True)
    logit_grad = (probs * (prob_grad - row_delta) * scaling).astype(jnp.bfloat16)
    query_parts = jnp.einsum(
        "gjsk,gkd->gjsd", logit_grad, window_keys, preferred_element_type=jnp.float32
    ).reshape(q_heads, block_rows, HEAD_SIZE)
    key_sum = jnp.einsum(
        "gjsk,gjsd->gkd", logit_grad, group_queries, preferred_element_type=jnp.float32
    )
    value_sum = jnp.einsum(
        "gjsk,gjsd->gkd", weights, grad_rows, preferred_element_type=jnp.float32
    )
    pair_grads = jnp.stack([key_sum, value_sum])
    total_grads = pair_grads[:, :, key_span:]
    for distance in range(previous, 0, -1):
        offset = (previous - distance) * block_rows
        total_grads = total_grads + passed_along(
            pair_grads[:, :, offset : offset + block_rows], "seq", -distance
        )
    query_grads = (
        query_parts.astype(jnp.bfloat16)
        .transpose(1, 0, 2)
        .reshape(1, block_rows, q_heads * HEAD_SIZE)
    )
    key_gradient = (
        total_grads[0]
        .astype(jnp.bfloat16)
        .transpose(1, 0, 2)
        .reshape(1, block_rows, kv_heads * HEAD_SIZE)
    )
    value_gradient = (
        total_grads[1]
        .astype(jnp.bfloat16)
        .transpose(1, 0, 2)
        .reshape(1, block_rows, kv_heads * HEAD_SIZE)
    )
    return (layer_output, query_grads, key_gradient, value_gradient, gain_grads)


def solution(mesh):
    placed = (
        P("dp", "seq", "tensor"),
        P("dp", "seq", "tensor"),
        P("dp", "seq", "tensor"),
        P("tensor"),
        P("tensor"),
        P("tensor"),
        P("dp", "seq", "tensor"),
        P("dp", "seq", "tensor"),
        P("dp", "tensor", "seq"),
        P("dp", "seq", "tensor"),
    )
    return jax.shard_map(
        local,
        mesh=mesh,
        in_specs=placed,
        out_specs=(
            P("dp", "seq", "tensor"),
            P("dp", "seq", "tensor"),
            P("dp", "seq", "tensor"),
            P("dp", "seq", "tensor"),
            P("tensor"),
        ),
        check_vma=False,
    )
```

time: 467 us -> 327 us (0.70); the launches traced: 459 us -> 326 us
  waiting for transfers between devices: 162 us -> 105 us
  matrix products: 41.9 us -> 16.9 us
  local copies, waits for them, and re-layouts: 31.7 us -> 7.18 us
  other arithmetic: 24.4 us -> 7.67 us
  starting transfers between devices: 197 us -> 187 us
    ppermute x26 -> x8, waiting for transfers between devices: 155 us -> 4.56 us  [passed_along(): return lax.ppermute(block, axis, route)]
    ppermute x0 -> x40, starting transfers between devices: none -> 110 us  [moved_on(): return lax.ppermute(value, axis, pairs)]
    ppermute x26 -> x8, starting transfers between devices: 128 us -> 25.4 us  [passed_along(): return lax.ppermute(block, axis, route)]
    ppermute x0 -> x40, waiting for transfers between devices: none -> 80.8 us  [moved_on(): return lax.ppermute(value, axis, pairs)]
    dot_general x54 -> x15, matrix products: 41.1 us -> 13.7 us  [the longest x1 3.14 us: local(): jnp.einsum('gjsk,gkd->gjsd', logit_grad, window_keys, preferred_element_t...]
    dynamic_update_slice x14 -> x0, local copies, waits for them, and re-layouts: 18.1 us -> none  [local(): heads_out, maxima, sums = lax.map(forward_head, (head_queries, kv_of_head))]
    ppermute x11, starting transfers between devices: 69.2 us -> 51.4 us  [summed(): lax.ppermute(value, axis, [(i, i ^ distance) for i in range(count)])]
    ppermute x11, waiting for transfers between devices: 7 us -> 19.3 us  [summed(): lax.ppermute(value, axis, [(i, i ^ distance) for i in range(count)])]
  transfers between devices with their start and end apart: 37 -> 59, of which waited for: 19 -> 18; matrix products, arithmetic and copies ran while one was open for 12% -> 9% of each run, Pallas kernels for 0% -> 0%
where the time goes in v2:
time: 327 us; the launch traced here: 326 us
  starting transfers between devices  187 us (57%)
  waiting for transfers between devices  105 us (32%)
  matrix products  16.9 us (5%)
  other arithmetic  7.67 us (2%)
  local copies, waits for them, and re-layouts  7.18 us (2%)
    ppermute x40, starting transfers between devices, moved_on(): return lax.ppermute(value, axis, pairs)  110 us
    ppermute x40, waiting for transfers between devices, moved_on(): return lax.ppermute(value, axis, pairs)  80.8 us
    ppermute x11, starting transfers between devices, summed(): lax.ppermute(value, axis, [(i, i ^ distance) for i in range(count)])  51.4 us
    ppermute x8, starting transfers between devices, passed_along(): return lax.ppermute(block, axis, route)  25.4 us
    ppermute x11, waiting for transfers between devices, summed(): lax.ppermute(value, axis, [(i, i ^ distance) for i in range(count)])  19.3 us
  transfers between devices with their start and end apart: 59, of which 18 were waited for; matrix products, arithmetic and copies ran while one was open for 9% of the time, Pallas kernels for 0%

profile of v2, /device:TPU:1, one launch (start us, length us, event | category | flops | bytes accessed | tf_op | source)
XLA Modules:
  0.0 325.7 jit_solution(2575967044445407217)
XLA Ops:
  1.5 5.7 %collective-permute-start = (bf16[2,1,128,128]{3,2,1,0:T(8,128)(2,1)S(1)}, bf16[2,1,128,128]{3,2,1,0:T(8,128)(2,1)S(1)}, u32[]{:S(2)}, u32[]{:S(2)}) collective-permute-start(bf16[2,1,128,128]{3,2,1,0:T(8,128)(2,1)S(1)} %pad_maximum_fusion.2), channel_id=1, source_target_pairs={{0,64},{16,80},{32,96},{48,112},{64,128},{80,144},{96,160},{112,17... | collective-permute-start | bytes 196616 | tf_op jit(solution)/shard_map/ppermute | solution.py:21
  7.2 7.0 %collective-permute-start.1 = (bf16[2,1,128,128]{3,2,1,0:T(8,128)(2,1)S(1)}, bf16[2,1,128,128]{3,2,1,0:T(8,128)(2,1)S(1)}, u32[]{:S(2)}, u32[]{:S(2)}) collective-permute-start(bf16[2,1,128,128]{3,2,1,0:T(8,128)(2,1)S(1)} %pad_maximum_fusion.2), channel_id=1, source_target_pairs={{0,48},{16,64},{32,80},{48,96},{64,112},{80,128},{96,144},{112,160... | collective-permute-start | bytes 196616 | tf_op jit(solution)/shard_map/ppermute | solution.py:21
  14.1 3.5 %collective-permute-start.2 = (bf16[2,1,128,128]{3,2,1,0:T(8,128)(2,1)S(1)}, bf16[2,1,128,128]{3,2,1,0:T(8,128)(2,1)S(1)}, u32[]{:S(2)}, u32[]{:S(2)}) collective-permute-start(bf16[2,1,128,128]{3,2,1,0:T(8,128)(2,1)S(1)} %pad_maximum_fusion.2), channel_id=1, source_target_pairs={{0,32},{16,48},{32,64},{48,80},{64,96},{80,112},{96,128},{112,144}... | collective-permute-start | bytes 196616 | tf_op jit(solution)/shard_map/ppermute | solution.py:21
  37.6 3.5 %collective-permute-start.7 = (f32[3]{0:T(128)S(1)}, f32[3]{0:T(128)S(1)}, u32[]{:S(2)}, u32[]{:S(2)}) collective-permute-start(f32[3]{0:T(128)S(1)} %get-tuple-element.42), channel_id=1, source_target_pairs={{16,48},{48,80},{80,112},{112,144},{144,176},{176,208},{208,240},{... | collective-permute-start | bytes 44 | tf_op jit(solution)/shard_map/ppermute | solution.py:33
  42.5 3.6 %collective-permute-start.17 = (f32[4]{0:T(128)S(1)}, f32[4]{0:T(128)S(1)}, u32[]{:S(2)}, u32[]{:S(2)}) collective-permute-start(f32[4]{0:T(128)S(1)} %get-tuple-element.44), channel_id=1, source_target_pairs={{16,48},{48,80},{80,112},{112,144},{144,176},{176,208},{208,240},{... | collective-permute-start | bytes 56 | tf_op jit(solution)/shard_map/ppermute | solution.py:33
  47.5 6.1 %collective-permute-start.8 = (f32[3]{0:T(128)S(1)}, f32[3]{0:T(128)S(1)}, u32[]{:S(2)}, u32[]{:S(2)}) collective-permute-start(f32[3]{0:T(128)S(1)} %broadcast_select_fusion.16), channel_id=1, source_target_pairs={{16,80},{48,112},{80,144},{112,176},{144,208},{176,240},{208,272},... | collective-permute-start | bytes 44 | tf_op jit(solution)/shard_map/ppermute | solution.py:33
  54.3 6.5 %collective-permute-start.18 = (f32[4]{0:T(128)S(1)}, f32[4]{0:T(128)S(1)}, u32[]{:S(2)}, u32[]{:S(2)}) collective-permute-start(f32[4]{0:T(128)S(1)} %broadcast_select_fusion.11), channel_id=1, source_target_pairs={{16,80},{48,112},{80,144},{112,176},{144,208},{176,240},{208,272},... | collective-permute-start | bytes 56 | tf_op jit(solution)/shard_map/ppermute | solution.py:33
  65.1 3.2 collective-permute-start.4
  68.3 4.0 %collective-permute-start.9 = (f32[3]{0:T(128)S(1)}, f32[3]{0:T(128)S(1)}, u32[]{:S(2)}, u32[]{:S(2)}) collective-permute-start(f32[3]{0:T(128)S(1)} %broadcast_select_fusion.18), channel_id=1, source_target_pairs={{16,144},{48,176},{80,208},{112,240},{144,272},{176,304},{208,336}... | collective-permute-start | bytes 44 | tf_op jit(solution)/shard_map/ppermute | solution.py:33
  72.4 4.5 %collective-permute-start.5 = (f32[128]{0:T(128)S(1)}, f32[128]{0:T(128)S(1)}, u32[]{:S(2)}, u32[]{:S(2)}) collective-permute-start(f32[128]{0:T(128)S(1)} %add.228), channel_id=1, source_target_pairs={{0,2},{1,3},{2,0},{3,1},{4,6},{5,7},{6,4},{7,5},{8,10},{9,11},{10,... | collective-permute-start | bytes 1544 | tf_op jit(solution)/shard_map/ppermute | solution.py:81
  89.9 4.1 %collective-permute-start.12 = (f32[3,128,128]{2,1,0:T(8,128)S(1)}, f32[3,128,128]{2,1,0:T(8,128)S(1)}, u32[]{:S(2)}, u32[]{:S(2)}) collective-permute-start(f32[3,128,128]{2,1,0:T(8,128)S(1)} %add_select_fusion.23), channel_id=1, source_target_pairs={{16,80},{48,112},{80,144},{112,176},{144,208},{176,240},{208,272},... | collective-permute-start | bytes 589832 | tf_op jit(solution)/shard_map/ppermute | solution.py:33
  94.1 3.4 %collective-permute-start.22 = (f32[4,128,128]{2,1,0:T(8,128)S(1)}, f32[4,128,128]{2,1,0:T(8,128)S(1)}, u32[]{:S(2)}, u32[]{:S(2)}) collective-permute-start(f32[4,128,128]{2,1,0:T(8,128)S(1)} %add_select_fusion.11), channel_id=1, source_target_pairs={{16,80},{48,112},{80,144},{112,176},{144,208},{176,240},{208,272},... | collective-permute-start | bytes 786440 | tf_op jit(solution)/shard_map/ppermute | solution.py:33
  98.0 6.6 %collective-permute-start.13 = (f32[3,128,128]{2,1,0:T(8,128)S(1)}, f32[3,128,128]{2,1,0:T(8,128)S(1)}, u32[]{:S(2)}, u32[]{:S(2)}) collective-permute-start(f32[3,128,128]{2,1,0:T(8,128)S(1)} %add_select_fusion.22), channel_id=1, source_target_pairs={{16,144},{48,176},{80,208},{112,240},{144,272},{176,304},{208,336}... | collective-permute-start | bytes 589832 | tf_op jit(solution)/shard_map/ppermute | solution.py:33
  104.7 10.1 %collective-permute-start.23 = (f32[4,128,128]{2,1,0:T(8,128)S(1)}, f32[4,128,128]{2,1,0:T(8,128)S(1)}, u32[]{:S(2)}, u32[]{:S(2)}) collective-permute-start(f32[4,128,128]{2,1,0:T(8,128)S(1)} %add_select_fusion.10), channel_id=1, source_target_pairs={{16,144},{48,176},{80,208},{112,240},{144,272},{176,304},{208,336}... | collective-permute-start | bytes 786440 | tf_op jit(solution)/shard_map/ppermute | solution.py:33
  114.9 15.3 %collective-permute-start.14 = (f32[3,128,128]{2,1,0:T(8,128)S(1)}, f32[3,128,128]{2,1,0:T(8,128)S(1)}, u32[]{:S(2)}, u32[]{:S(2)}) collective-permute-start(f32[3,128,128]{2,1,0:T(8,128)S(1)} %add_select_fusion.21), channel_id=1, source_target_pairs={{16,272},{48,304},{80,336},{112,368},{144,400},{176,432},{208,464}... | collective-permute-start | bytes 589832 | tf_op jit(solution)/shard_map/ppermute | solution.py:33
  134.4 12.6 %collective-permute-start.24 = (f32[4,128,128]{2,1,0:T(8,128)S(1)}, f32[4,128,128]{2,1,0:T(8,128)S(1)}, u32[]{:S(2)}, u32[]{:S(2)}) collective-permute-start(f32[4,128,128]{2,1,0:T(8,128)S(1)} %add_select_fusion.9), channel_id=1, source_target_pairs={{16,272},{48,304},{80,336},{112,368},{144,400},{176,432},{208,464}... | collective-permute-start | bytes 786440 | tf_op jit(solution)/shard_map/ppermute | solution.py:33
  168.1 57.2 %collective-permute-done.35 = f32[3,128,128]{2,1,0:T(8,128)S(1)} collective-permute-done((f32[3,128,128]{2,1,0:T(8,128)S(1)}, f32[3,128,128]{2,1,0:T(8,128)S(1)}, u32[]{:S(2)}, u32[]{:S(2)}) %collective-permute-start.35) | collective-permute-done | bytes 196640 | tf_op jit(solution)/shard_map/ppermute | solution.py:33
  225.7 10.9 %collective-permute-done.45 = f32[4,128,128]{2,1,0:T(8,128)S(1)} collective-permute-done((f32[4,128,128]{2,1,0:T(8,128)S(1)}, f32[4,128,128]{2,1,0:T(8,128)S(1)}, u32[]{:S(2)}, u32[]{:S(2)}) %collective-permute-start.45) | collective-permute-done | bytes 262176 | tf_op jit(solution)/shard_map/ppermute | solution.py:33
  237.6 6.6 %collective-permute-start.46 = (f32[128]{0:T(128)S(1)}, f32[128]{0:T(128)S(1)}, u32[]{:S(2)}, u32[]{:S(2)}) collective-permute-start(f32[128]{0:T(128)S(1)} %get-tuple-element.16), channel_id=1, source_target_pairs={{0,1},{1,0},{2,3},{3,2},{4,5},{5,4},{6,7},{7,6},{8,9},{9,8},{10,11... | collective-permute-start | bytes 1544 | tf_op jit(solution)/shard_map/ppermute | solution.py:81
  245.1 5.5 %collective-permute-start.47 = (f32[128]{0:T(128)S(1)}, f32[128]{0:T(128)S(1)}, u32[]{:S(2)}, u32[]{:S(2)}) collective-permute-start(f32[128]{0:T(128)S(1)} %add.274), channel_id=1, source_target_pairs={{0,2},{1,3},{2,0},{3,1},{4,6},{5,7},{6,4},{7,5},{8,10},{9,11},{10,... | collective-permute-start | bytes 1544 | tf_op jit(solution)/shard_map/ppermute | solution.py:81
  251.5 3.2 collective-permute-start.52
  255.5 4.3 %collective-permute-start.53 = (f32[896]{0:T(1024)S(1)}, f32[896]{0:T(1024)S(1)}, u32[]{:S(2)}, u32[]{:S(2)}) collective-permute-start(f32[896]{0:T(1024)S(1)} %bitcast_add_fusion), channel_id=1, source_target_pairs={{0,32},{16,48},{32,0},{48,16},{64,96},{80,112},{96,64},{112,80},{1... | collective-permute-start | bytes 10760 | tf_op jit(solution)/shard_map/ppermute | solution.py:81
  266.0 2.9 collective-permute-start.55
  270.2 4.1 %collective-permute-done.55 = f32[896]{0:T(1024)S(1)} collective-permute-done((f32[896]{0:T(1024)S(1)}, f32[896]{0:T(1024)S(1)}, u32[]{:S(2)}, u32[]{:S(2)}) %collective-permute-start.55) | collective-permute-done | bytes 3616 | tf_op jit(solution)/shard_map/ppermute | solution.py:81
  274.3 11.8 %collective-permute-start.56 = (f32[896]{0:T(1024)S(1)}, f32[896]{0:T(1024)S(1)}, u32[]{:S(2)}, u32[]{:S(2)}) collective-permute-start(f32[896]{0:T(1024)S(1)} %add.283), channel_id=1, source_target_pairs={{0,256},{16,272},{32,288},{48,304},{64,320},{80,336},{96,352},{112... | collective-permute-start | bytes 10760 | tf_op jit(solution)/shard_map/ppermute | solution.py:81
  286.1 3.1 fusion.16
  289.2 9.9 %collective-permute-done.56 = f32[896]{0:T(1024)S(1)} collective-permute-done((f32[896]{0:T(1024)S(1)}, f32[896]{0:T(1024)S(1)}, u32[]{:S(2)}, u32[]{:S(2)}) %collective-permute-start.56) | collective-permute-done | bytes 3616 | tf_op jit(solution)/shard_map/ppermute | solution.py:81
  299.2 3.1 collective-permute-start.57
  303.1 3.4 %collective-permute-start.51 = (f32[2,1,128,128]{3,2,1,0:T(8,128)}, f32[2,1,128,128]{3,2,1,0:T(8,128)}, u32[]{:S(2)}, u32[]{:S(2)}) collective-permute-start(f32[2,1,128,128]{3,2,1,0:T(8,128)} %get-tuple-element.31), channel_id=1, source_target_pairs={{16,0},{32,16},{48,32},{64,48},{80,64},{96,80},{112,96},{128,112},... | collective-permute-start | bytes 393224 | tf_op jit(solution)/shard_map/ppermute | solution.py:21
  310.4 4.3 %collective-permute-start.58 = (f32[896]{0:T(1024)S(1)}, f32[896]{0:T(1024)S(1)}, u32[]{:S(2)}, u32[]{:S(2)}) collective-permute-start(f32[896]{0:T(1024)S(1)} %add.285), channel_id=1, source_target_pairs={{0,8},{4,12},{8,0},{12,4},{1,9},{5,13},{9,1},{13,5},{2,10},{6,14},... | collective-permute-start | bytes 10760 | tf_op jit(solution)/shard_map/ppermute | solution.py:81
  314.8 3.1 fusion.12
  320.5 3.5 %collective-permute-done.48 = f32[2,1,128,128]{3,2,1,0:T(8,128)} collective-permute-done((f32[2,1,128,128]{3,2,1,0:T(8,128)}, f32[2,1,128,128]{3,2,1,0:T(8,128)}, u32[]{:S(2)}, u32[]{:S(2)}) %collective-permute-start.48) | collective-permute-done | bytes 131104 | tf_op jit(solution)/shard_map/ppermute | solution.py:21
  (205 shorter events, 86.3 us)
Async XLA Ops:
  1.5 52.1 %collective-permute-start = (bf16[2,1,128,128]{3,2,1,0:T(8,128)(2,1)S(1)}, bf16[2,1,128,128]{3,2,1,0:T(8,128)(2,1)S(1)}, u32[]{:S(2)}, u32[]{:S(2)}) collective-permute-start(bf16[2,1,128,128]{3,2,1,0:T(8,128)(2,1)S(1)} %pad_maximum_fusion.2), channel_id=1, source_target_pairs={{0,64},{16,80},{32,96},{48,112},{64,128},{80,144},{96,160},{112,17... | collective-permute-start | bytes 196616 | tf_op jit(solution)/shard_map/ppermute | solution.py:21
  7.2 47.1 %collective-permute-start.1 = (bf16[2,1,128,128]{3,2,1,0:T(8,128)(2,1)S(1)}, bf16[2,1,128,128]{3,2,1,0:T(8,128)(2,1)S(1)}, u32[]{:S(2)}, u32[]{:S(2)}) collective-permute-start(bf16[2,1,128,128]{3,2,1,0:T(8,128)(2,1)S(1)} %pad_maximum_fusion.2), channel_id=1, source_target_pairs={{0,48},{16,64},{32,80},{48,96},{64,112},{80,128},{96,144},{112,160... | collective-permute-start | bytes 196616 | tf_op jit(solution)/shard_map/ppermute | solution.py:21
  14.1 46.7 %collective-permute-start.2 = (bf16[2,1,128,128]{3,2,1,0:T(8,128)(2,1)S(1)}, bf16[2,1,128,128]{3,2,1,0:T(8,128)(2,1)S(1)}, u32[]{:S(2)}, u32[]{:S(2)}) collective-permute-start(bf16[2,1,128,128]{3,2,1,0:T(8,128)(2,1)S(1)} %pad_maximum_fusion.2), channel_id=1, source_target_pairs={{0,32},{16,48},{32,64},{48,80},{64,96},{80,112},{96,128},{112,144}... | collective-permute-start | bytes 196616 | tf_op jit(solution)/shard_map/ppermute | solution.py:21
  17.7 43.8 %collective-permute-start.3 = (bf16[2,1,128,128]{3,2,1,0:T(8,128)(2,1)S(1)}, bf16[2,1,128,128]{3,2,1,0:T(8,128)(2,1)S(1)}, u32[]{:S(2)}, u32[]{:S(2)}) collective-permute-start(bf16[2,1,128,128]{3,2,1,0:T(8,128)(2,1)S(1)} %pad_maximum_fusion.2), channel_id=1, source_target_pairs={{0,16},{16,32},{32,48},{48,64},{64,80},{80,96},{96,112},{112,128},... | collective-permute-start | bytes 196616 | tf_op jit(solution)/shard_map/ppermute | solution.py:21
  20.8 7.8 %collective-permute-start.26 = (f32[3]{0:T(128)S(1)}, f32[3]{0:T(128)S(1)}, u32[]{:S(2)}, u32[]{:S(2)}) collective-permute-start(f32[3]{0:T(128)S(1)} %bitcast.153), channel_id=1, source_target_pairs={{496,480},{464,448},{432,416},{400,384},{368,352},{336,320},{304,2... | collective-permute-start | bytes 44 | tf_op jit(solution)/shard_map/ppermute | solution.py:33
  47.5 20.8 %collective-permute-start.8 = (f32[3]{0:T(128)S(1)}, f32[3]{0:T(128)S(1)}, u32[]{:S(2)}, u32[]{:S(2)}) collective-permute-start(f32[3]{0:T(128)S(1)} %broadcast_select_fusion.16), channel_id=1, source_target_pairs={{16,80},{48,112},{80,144},{112,176},{144,208},{176,240},{208,272},... | collective-permute-start | bytes 44 | tf_op jit(solution)/shard_map/ppermute | solution.py:33
  53.6 102.8 %collective-permute-start.28 = (f32[3]{0:T(128)S(1)}, f32[3]{0:T(128)S(1)}, u32[]{:S(2)}, u32[]{:S(2)}) collective-permute-start(f32[3]{0:T(128)S(1)} %broadcast_select_fusion.6), channel_id=1, source_target_pairs={{480,416},{448,384},{416,352},{384,320},{352,288},{320,256},{288,2... | collective-permute-start | bytes 44 | tf_op jit(solution)/shard_map/ppermute | solution.py:33
  54.3 22.6 %collective-permute-start.18 = (f32[4]{0:T(128)S(1)}, f32[4]{0:T(128)S(1)}, u32[]{:S(2)}, u32[]{:S(2)}) collective-permute-start(f32[4]{0:T(128)S(1)} %broadcast_select_fusion.11), channel_id=1, source_target_pairs={{16,80},{48,112},{80,144},{112,176},{144,208},{176,240},{208,272},... | collective-permute-start | bytes 56 | tf_op jit(solution)/shard_map/ppermute | solution.py:33
  60.8 97.9 %collective-permute-start.38 = (f32[4]{0:T(128)S(1)}, f32[4]{0:T(128)S(1)}, u32[]{:S(2)}, u32[]{:S(2)}) collective-permute-start(f32[4]{0:T(128)S(1)} %broadcast_select_fusion.1), channel_id=1, source_target_pairs={{480,416},{448,384},{416,352},{384,320},{352,288},{320,256},{288,2... | collective-permute-start | bytes 56 | tf_op jit(solution)/shard_map/ppermute | solution.py:33
  65.1 7.3 %collective-permute-start.4 = (f32[128]{0:T(128)S(1)}, f32[128]{0:T(128)S(1)}, u32[]{:S(2)}, u32[]{:S(2)}) collective-permute-start(f32[128]{0:T(128)S(1)} %get-tuple-element.47), channel_id=1, source_target_pairs={{0,1},{1,0},{2,3},{3,2},{4,5},{5,4},{6,7},{7,6},{8,9},{9,8},{10,11... | collective-permute-start | bytes 1544 | tf_op jit(solution)/shard_map/ppermute | solution.py:81
  68.3 13.7 %collective-permute-start.9 = (f32[3]{0:T(128)S(1)}, f32[3]{0:T(128)S(1)}, u32[]{:S(2)}, u32[]{:S(2)}) collective-permute-start(f32[3]{0:T(128)S(1)} %broadcast_select_fusion.18), channel_id=1, source_target_pairs={{16,144},{48,176},{80,208},{112,240},{144,272},{176,304},{208,336}... | collective-permute-start | bytes 44 | tf_op jit(solution)/shard_map/ppermute | solution.py:33
  72.4 7.3 %collective-permute-start.5 = (f32[128]{0:T(128)S(1)}, f32[128]{0:T(128)S(1)}, u32[]{:S(2)}, u32[]{:S(2)}) collective-permute-start(f32[128]{0:T(128)S(1)} %add.228), channel_id=1, source_target_pairs={{0,2},{1,3},{2,0},{3,1},{4,6},{5,7},{6,4},{7,5},{8,10},{9,11},{10,... | collective-permute-start | bytes 1544 | tf_op jit(solution)/shard_map/ppermute | solution.py:81
  76.9 12.8 %collective-permute-start.19 = (f32[4]{0:T(128)S(1)}, f32[4]{0:T(128)S(1)}, u32[]{:S(2)}, u32[]{:S(2)}) collective-permute-start(f32[4]{0:T(128)S(1)} %broadcast_select_fusion.13), channel_id=1, source_target_pairs={{16,144},{48,176},{80,208},{112,240},{144,272},{176,304},{208,336}... | collective-permute-start | bytes 56 | tf_op jit(solution)/shard_map/ppermute | solution.py:33
  89.9 8.0 %collective-permute-start.12 = (f32[3,128,128]{2,1,0:T(8,128)S(1)}, f32[3,128,128]{2,1,0:T(8,128)S(1)}, u32[]{:S(2)}, u32[]{:S(2)}) collective-permute-start(f32[3,128,128]{2,1,0:T(8,128)S(1)} %add_select_fusion.23), channel_id=1, source_target_pairs={{16,80},{48,112},{80,144},{112,176},{144,208},{176,240},{208,272},... | collective-permute-start | bytes 589832 | tf_op jit(solution)/shard_map/ppermute | solution.py:33
  94.1 10.5 %collective-permute-start.22 = (f32[4,128,128]{2,1,0:T(8,128)S(1)}, f32[4,128,128]{2,1,0:T(8,128)S(1)}, u32[]{:S(2)}, u32[]{:S(2)}) collective-permute-start(f32[4,128,128]{2,1,0:T(8,128)S(1)} %add_select_fusion.11), channel_id=1, source_target_pairs={{16,80},{48,112},{80,144},{112,176},{144,208},{176,240},{208,272},... | collective-permute-start | bytes 786440 | tf_op jit(solution)/shard_map/ppermute | solution.py:33
  98.0 16.8 %collective-permute-start.13 = (f32[3,128,128]{2,1,0:T(8,128)S(1)}, f32[3,128,128]{2,1,0:T(8,128)S(1)}, u32[]{:S(2)}, u32[]{:S(2)}) collective-permute-start(f32[3,128,128]{2,1,0:T(8,128)S(1)} %add_select_fusion.22), channel_id=1, source_target_pairs={{16,144},{48,176},{80,208},{112,240},{144,272},{176,304},{208,336}... | collective-permute-start | bytes 589832 | tf_op jit(solution)/shard_map/ppermute | solution.py:33
  104.7 29.6 %collective-permute-start.23 = (f32[4,128,128]{2,1,0:T(8,128)S(1)}, f32[4,128,128]{2,1,0:T(8,128)S(1)}, u32[]{:S(2)}, u32[]{:S(2)}) collective-permute-start(f32[4,128,128]{2,1,0:T(8,128)S(1)} %add_select_fusion.10), channel_id=1, source_target_pairs={{16,144},{48,176},{80,208},{112,240},{144,272},{176,304},{208,336}... | collective-permute-start | bytes 786440 | tf_op jit(solution)/shard_map/ppermute | solution.py:33
  114.9 17.9 %collective-permute-start.14 = (f32[3,128,128]{2,1,0:T(8,128)S(1)}, f32[3,128,128]{2,1,0:T(8,128)S(1)}, u32[]{:S(2)}, u32[]{:S(2)}) collective-permute-start(f32[3,128,128]{2,1,0:T(8,128)S(1)} %add_select_fusion.21), channel_id=1, source_target_pairs={{16,272},{48,304},{80,336},{112,368},{144,400},{176,432},{208,464}... | collective-permute-start | bytes 589832 | tf_op jit(solution)/shard_map/ppermute | solution.py:33
  132.9 14.1 %collective-permute-start.15 = (f32[3,128,128]{2,1,0:T(8,128)S(1)}, f32[3,128,128]{2,1,0:T(8,128)S(1)}, u32[]{:S(2)}, u32[]{:S(2)}) collective-permute-start(f32[3,128,128]{2,1,0:T(8,128)S(1)} %add_select_fusion.18), channel_id=1, source_target_pairs={{16,0},{48,32},{80,64},{112,96},{144,128},{176,160},{208,192},{240... | collective-permute-start | bytes 589832 | tf_op jit(solution)/shard_map/ppermute | solution.py:33
  134.4 15.9 %collective-permute-start.24 = (f32[4,128,128]{2,1,0:T(8,128)S(1)}, f32[4,128,128]{2,1,0:T(8,128)S(1)}, u32[]{:S(2)}, u32[]{:S(2)}) collective-permute-start(f32[4,128,128]{2,1,0:T(8,128)S(1)} %add_select_fusion.9), channel_id=1, source_target_pairs={{16,272},{48,304},{80,336},{112,368},{144,400},{176,432},{208,464}... | collective-permute-start | bytes 786440 | tf_op jit(solution)/shard_map/ppermute | solution.py:33
  164.8 60.5 %collective-permute-start.35 = (f32[3,128,128]{2,1,0:T(8,128)S(1)}, f32[3,128,128]{2,1,0:T(8,128)S(1)}, u32[]{:S(2)}, u32[]{:S(2)}) collective-permute-start(f32[3,128,128]{2,1,0:T(8,128)S(1)} %add_select_fusion.12), channel_id=1, source_target_pairs={{480,496},{448,464},{416,432},{384,400},{352,368},{320,336},{288,3... | collective-permute-start | bytes 589832 | tf_op jit(solution)/shard_map/ppermute | solution.py:33
  166.4 70.2 %collective-permute-start.45 = (f32[4,128,128]{2,1,0:T(8,128)S(1)}, f32[4,128,128]{2,1,0:T(8,128)S(1)}, u32[]{:S(2)}, u32[]{:S(2)}) collective-permute-start(f32[4,128,128]{2,1,0:T(8,128)S(1)} %add_select_fusion), channel_id=1, source_target_pairs={{480,496},{448,464},{416,432},{384,400},{352,368},{320,336},{288,3... | collective-permute-start | bytes 786440 | tf_op jit(solution)/shard_map/ppermute | solution.py:33
  237.6 7.6 %collective-permute-start.46 = (f32[128]{0:T(128)S(1)}, f32[128]{0:T(128)S(1)}, u32[]{:S(2)}, u32[]{:S(2)}) collective-permute-start(f32[128]{0:T(128)S(1)} %get-tuple-element.16), channel_id=1, source_target_pairs={{0,1},{1,0},{2,3},{3,2},{4,5},{5,4},{6,7},{7,6},{8,9},{9,8},{10,11... | collective-permute-start | bytes 1544 | tf_op jit(solution)/shard_map/ppermute | solution.py:81
  245.1 9.6 %collective-permute-start.47 = (f32[128]{0:T(128)S(1)}, f32[128]{0:T(128)S(1)}, u32[]{:S(2)}, u32[]{:S(2)}) collective-permute-start(f32[128]{0:T(128)S(1)} %add.274), channel_id=1, source_target_pairs={{0,2},{1,3},{2,0},{3,1},{4,6},{5,7},{6,4},{7,5},{8,10},{9,11},{10,... | collective-permute-start | bytes 1544 | tf_op jit(solution)/shard_map/ppermute | solution.py:81
  266.0 8.2 %collective-permute-start.55 = (f32[896]{0:T(1024)S(1)}, f32[896]{0:T(1024)S(1)}, u32[]{:S(2)}, u32[]{:S(2)}) collective-permute-start(f32[896]{0:T(1024)S(1)} %add.282), channel_id=1, source_target_pairs={{0,128},{16,144},{32,160},{48,176},{64,192},{80,208},{96,224},{112... | collective-permute-start | bytes 10760 | tf_op jit(solution)/shard_map/ppermute | solution.py:81
  274.3 24.9 %collective-permute-start.56 = (f32[896]{0:T(1024)S(1)}, f32[896]{0:T(1024)S(1)}, u32[]{:S(2)}, u32[]{:S(2)}) collective-permute-start(f32[896]{0:T(1024)S(1)} %add.283), channel_id=1, source_target_pairs={{0,256},{16,272},{32,288},{48,304},{64,320},{80,336},{96,352},{112... | collective-permute-start | bytes 10760 | tf_op jit(solution)/shard_map/ppermute | solution.py:81
  299.2 11.3 %collective-permute-start.57 = (f32[896]{0:T(1024)S(1)}, f32[896]{0:T(1024)S(1)}, u32[]{:S(2)}, u32[]{:S(2)}) collective-permute-start(f32[896]{0:T(1024)S(1)} %add.284), channel_id=1, source_target_pairs={{0,4},{4,0},{8,12},{12,8},{1,5},{5,1},{9,13},{13,9},{2,6},{6,2},{1... | collective-permute-start | bytes 10760 | tf_op jit(solution)/shard_map/ppermute | solution.py:81
  303.1 16.3 %collective-permute-start.51 = (f32[2,1,128,128]{3,2,1,0:T(8,128)}, f32[2,1,128,128]{3,2,1,0:T(8,128)}, u32[]{:S(2)}, u32[]{:S(2)}) collective-permute-start(f32[2,1,128,128]{3,2,1,0:T(8,128)} %get-tuple-element.31), channel_id=1, source_target_pairs={{16,0},{32,16},{48,32},{64,48},{80,64},{96,80},{112,96},{128,112},... | collective-permute-start | bytes 393224 | tf_op jit(solution)/shard_map/ppermute | solution.py:21
  306.5 12.9 %collective-permute-start.50 = (f32[2,1,128,128]{3,2,1,0:T(8,128)}, f32[2,1,128,128]{3,2,1,0:T(8,128)}, u32[]{:S(2)}, u32[]{:S(2)}) collective-permute-start(f32[2,1,128,128]{3,2,1,0:T(8,128)} %get-tuple-element.32), channel_id=1, source_target_pairs={{32,0},{48,16},{64,32},{80,48},{96,64},{112,80},{128,96},{144,112}... | collective-permute-start | bytes 393224 | tf_op jit(solution)/shard_map/ppermute | solution.py:21
  307.8 12.6 %collective-permute-start.49 = (f32[2,1,128,128]{3,2,1,0:T(8,128)}, f32[2,1,128,128]{3,2,1,0:T(8,128)}, u32[]{:S(2)}, u32[]{:S(2)}) collective-permute-start(f32[2,1,128,128]{3,2,1,0:T(8,128)} %get-tuple-element.30), channel_id=1, source_target_pairs={{48,0},{64,16},{80,32},{96,48},{112,64},{128,80},{144,96},{160,112... | collective-permute-start | bytes 393224 | tf_op jit(solution)/shard_map/ppermute | solution.py:21
  309.1 14.8 %collective-permute-start.48 = (f32[2,1,128,128]{3,2,1,0:T(8,128)}, f32[2,1,128,128]{3,2,1,0:T(8,128)}, u32[]{:S(2)}, u32[]{:S(2)}) collective-permute-start(f32[2,1,128,128]{3,2,1,0:T(8,128)} %get-tuple-element.29), channel_id=1, source_target_pairs={{64,0},{80,16},{96,32},{112,48},{128,64},{144,80},{160,96},{176,11... | collective-permute-start | bytes 393224 | tf_op jit(solution)/shard_map/ppermute | solution.py:21
  310.4 8.3 %collective-permute-start.58 = (f32[896]{0:T(1024)S(1)}, f32[896]{0:T(1024)S(1)}, u32[]{:S(2)}, u32[]{:S(2)}) collective-permute-start(f32[896]{0:T(1024)S(1)} %add.285), channel_id=1, source_target_pairs={{0,8},{4,12},{8,0},{12,4},{1,9},{5,13},{9,1},{13,5},{2,10},{6,14},... | collective-permute-start | bytes 10760 | tf_op jit(solution)/shard_map/ppermute | solution.py:81
  (32 other events, 229.8 us)

commit v3 on v2

--- a/solution.py
+++ b/solution.py
@@ -22,22 +22,28 @@
 
 
 def chain_states(earlier, later):
-    return (earlier[0] * later[0], later[0][:, None, None] * earlier[1] + later[1])
+    rows = later.shape[1] - 8
+    is_state = jnp.arange(later.shape[1])[None, :, None] < rows
+    return jnp.where(is_state, later[:, rows : rows + 1, :1] * earlier + later, earlier * later)
 
 
 def picked(flag, new, old):
-    return jax.tree.map(lambda a, b: jnp.where(flag, a, b), new, old)
+    return jnp.where(flag, new, old)
 
 
 def moved_on(value, axis, pairs):
     return lax.ppermute(value, axis, pairs)
 
 
-def entering(value, axis, backward):
+def entering(decay, state, axis, backward):
     count, index = (lax.axis_size(axis), lax.axis_index(axis))
     place = count - 1 - index if backward else index
     spot = (lambda p: count - 1 - p) if backward else (lambda p: p)
-    identity = (jnp.ones_like(value[0]), jnp.zeros_like(value[1]))
+    rows = state.shape[1]
+    value = jnp.concatenate(
+        [state, jnp.broadcast_to(decay[:, None, None], (state.shape[0], 8, state.shape[2]))], axis=1
+    )
+    identity = jnp.concatenate([jnp.zeros_like(state), jnp.ones_like(value[:, rows:])], axis=1)
     if count % 2:
         before, covered, distance = identity, value, 1
         while distance < count:
@@ -48,7 +54,7 @@
             before = picked(present, chain_states(moved, before), before)
             covered = picked(present, chain_states(moved, covered), covered)
             distance *= 2
-        return before[1]
+        return before[:, :rows]
     lead = place % 2 == 1
     first = moved_on(value, axis, [(spot(p), spot(p + 1)) for p in range(0, count, 2)])
     covered = chain_states(first, value)
@@ -65,8 +71,8 @@
         if 2 * distance < count:
             covered = picked(present, chain_states(moved, covered), covered)
         distance *= 2
-    handed = moved_on(before[1], axis, [(spot(p), spot(p - 1)) for p in range(1, count, 2)])
-    own_lead = chain_states(before, first)[1]
+    handed = moved_on(before[:, :rows], axis, [(spot(p), spot(p - 1)) for p in range(1, count, 2)])
+    own_lead = chain_states(before, first)[:, :rows]
     return jnp.where(lead, own_lead, handed)
 
 
@@ -171,10 +177,14 @@
 
     splits = min(HEAD_SPLITS, q_heads)
     bounds = [q_heads * part // splits for part in range(splits + 1)]
-    unit_parts, grad_parts = [], []
+    unit_parts, grad_parts, gain_parts = [], [], []
+    state_in = None
     for low, high in zip(bounds[:-1], bounds[1:]):
         part = slice(low, high)
-        state_in = entering((block_decay[part], local_state[part]), "seq", False)
+        part_state = local_state[part]
+        if state_in is not None:
+            part_state, _ = lax.optimization_barrier((part_state, state_in))
+        state_in = entering(block_decay[part], part_state, "seq", False)
         carried = jnp.einsum("hsd,hde->hse", query_float[part], state_in, precision=precise)
         membrane = (
             jnp.einsum("hst,htd->hsd", decayed[part], spike_float[part], precision=precise)
@@ -191,22 +201,23 @@
             membrane_grad,
             precision=precise,
         )
-        state_after = entering((block_decay[part], head_part), "seq", True)
+        state_after = entering(block_decay[part], head_part, "seq", True)
         later_part = jnp.einsum("htd,hde->hte", key_float[part], state_after, precision=precise)
         spike_grad = (
             jnp.einsum("hst,hsd->htd", decayed[part], membrane_grad, precision=precise)
             + tail_decay[part][..., None] * later_part
         )
+        part_level = spike_grad * (1.0 - bounded[part] * bounded[part])
+        part_gain = jnp.sum(part_level * normed[part], axis=1).reshape((high - low) * HEAD_SIZE)
+        gain_parts.append(jnp.sum(lax.all_gather(part_gain, ("seq", "dp")), axis=0))
         unit_parts.append(unit_out)
-        grad_parts.append(spike_grad)
+        grad_parts.append(part_level)
     unit_out = jnp.concatenate(unit_parts, axis=0)
-    spike_grad = jnp.concatenate(grad_parts, axis=0)
+    level_grad = jnp.concatenate(grad_parts, axis=0)
+    gain_grads = jnp.concatenate(gain_parts, axis=0)
     layer_output = (
         unit_out.astype(jnp.bfloat16).transpose(1, 0, 2).reshape(1, block_rows, q_heads * HEAD_SIZE)
     )
-    level_grad = spike_grad * (1.0 - bounded * bounded)
-    gain_part = jnp.sum(level_grad * normed, axis=1).reshape(q_heads * HEAD_SIZE)
-    gain_grads = summed(gain_part, ("seq", "dp"))
     normed_grad = level_grad * gain_rows
     slope_sum = summed(jnp.sum(normed_grad * normed, axis=(0, 2)), ("tensor",))
     output_gradient = (

time: 327 us -> 605 us (1.85)
  blocking collectives: 0 us -> 364 us
  starting transfers between devices: 187 us -> 132 us
  waiting for transfers between devices: 105 us -> 61.1 us
  other arithmetic: 7.67 us -> 16.3 us
    all_gather x0 -> x2, blocking collectives: none -> 364 us  [local(): gain_parts.append(jnp.sum(lax.all_gather(part_gain, ('seq', 'dp')), axis=0))]
    ppermute x11 -> x4, starting transfers between devices: 51.4 us -> 15.9 us  [summed(): lax.ppermute(value, axis, [(i, i ^ distance) for i in range(count)])]
    ppermute x40 -> x24, waiting for transfers between devices: 80.8 us -> 49.7 us  [moved_on(): return lax.ppermute(value, axis, pairs)]
    ppermute x40 -> x24, starting transfers between devices: 110 us -> 89.5 us  [moved_on(): return lax.ppermute(value, axis, pairs)]
    ppermute x11 -> x4, waiting for transfers between devices: 19.3 us -> 1.98 us  [summed(): lax.ppermute(value, axis, [(i, i ^ distance) for i in range(count)])]
  transfers between devices with their start and end apart: 59 -> 36, of which waited for: 18 -> 17; matrix products, arithmetic and copies ran while one was open for 9% -> 4% of each run, Pallas kernels for 0% -> 0%
where the time goes in v3:
time: 605 us; the launch traced here: 604 us
  blocking collectives  364 us (60%)
  starting transfers between devices  132 us (22%)
  waiting for transfers between devices  61.1 us (10%)
  matrix products  18.1 us (3%)
  other arithmetic  16.3 us (3%)
  local copies, waits for them, and re-layouts  10.3 us (2%)
    all_gather x2, blocking collectives, local(): gain_parts.append(jnp.sum(lax.all_gather(part_gain, ('seq', 'dp')), axis=0))  364 us
    ppermute x24, starting transfers between devices, moved_on(): return lax.ppermute(value, axis, pairs)  89.5 us
    ppermute x24, waiting for transfers between devices, moved_on(): return lax.ppermute(value, axis, pairs)  49.7 us
    ppermute x8, starting transfers between devices, passed_along(): return lax.ppermute(block, axis, route)  26.6 us
    ppermute x4, starting transfers between devices, summed(): lax.ppermute(value, axis, [(i, i ^ distance) for i in range(count)])  15.9 us
  transfers between devices with their start and end apart: 36, of which 17 were waited for; matrix products, arithmetic and copies ran while one was open for 4% of the time, Pallas kernels for 0%

profile of v3, /device:TPU:1, one launch (start us, length us, event | category | flops | bytes accessed | tf_op | source)
XLA Modules:
  0.0 603.6 jit_solution(6367092681350200356)
XLA Ops:
  1.4 5.7 collective-permute-start
  7.1 7.0 %collective-permute-start.1 = (bf16[2,1,128,128]{3,2,1,0:T(8,128)(2,1)S(1)}, bf16[2,1,128,128]{3,2,1,0:T(8,128)(2,1)S(1)}, u32[]{:S(2)}, u32[]{:S(2)}) collective-permute-start(bf16[2,1,128,128]{3,2,1,0:T(8,128)(2,1)S(1)} %pad_maximum_fusion.6), channel_id=1, source_target_pairs={{0,48},{16,64},{32,80},{48,96},{64,112},{80,128},{96,144},{112,160... | collective-permute-start | bytes 196616 | tf_op jit(solution)/shard_map/ppermute | solution.py:21
  14.1 3.5 collective-permute-start.2
  28.1 3.2 collective-permute-start.4
  32.4 4.8 collective-permute-start.5
  40.9 3.4 collective-permute-done.6
  45.1 4.2 collective-permute-start.7
  52.9 6.1 %collective-permute-start.8 = (f32[3,136,128]{2,1,0:T(8,128)S(1)}, f32[3,136,128]{2,1,0:T(8,128)S(1)}, u32[]{:S(2)}, u32[]{:S(2)}) collective-permute-start(f32[3,136,128]{2,1,0:T(8,128)S(1)} %get-tuple-element.53), channel_id=1, source_target_pairs={{16,80},{48,112},{80,144},{112,176},{144,208},{176,240},{208,272},... | collective-permute-start | bytes 626696 | tf_op jit(solution)/shard_map/ppermute | solution.py:35
  59.3 2.5 collective-permute-done.8
  61.9 11.5 %collective-permute-start.9 = (f32[3,136,128]{2,1,0:T(8,128)S(1)}, f32[3,136,128]{2,1,0:T(8,128)S(1)}, u32[]{:S(2)}, u32[]{:S(2)}) collective-permute-start(f32[3,136,128]{2,1,0:T(8,128)S(1)} %get-tuple-element.51), channel_id=1, source_target_pairs={{16,144},{48,176},{80,208},{112,240},{144,272},{176,304},{208,336}... | collective-permute-start | bytes 626696 | tf_op jit(solution)/shard_map/ppermute | solution.py:35
  73.7 2.5 collective-permute-done.9
  76.3 12.7 %collective-permute-start.10 = (f32[3,136,128]{2,1,0:T(8,128)S(1)}, f32[3,136,128]{2,1,0:T(8,128)S(1)}, u32[]{:S(2)}, u32[]{:S(2)}) collective-permute-start(f32[3,136,128]{2,1,0:T(8,128)S(1)} %get-tuple-element.49), channel_id=1, source_target_pairs={{16,272},{48,304},{80,336},{112,368},{144,400},{176,432},{208,464}... | collective-permute-start | bytes 626696 | tf_op jit(solution)/shard_map/ppermute | solution.py:35
  97.5 3.1 collective-permute-start.18
  100.6 4.2 collective-permute-start.13
  105.5 2.8 collective-permute-done.13
  108.5 3.8 collective-permute-start.14
  113.4 2.4 collective-permute-done.14
  116.0 13.7 %collective-permute-start.15 = (f32[4,136,128]{2,1,0:T(8,128)S(1)}, f32[4,136,128]{2,1,0:T(8,128)S(1)}, u32[]{:S(2)}, u32[]{:S(2)}) collective-permute-start(f32[4,136,128]{2,1,0:T(8,128)S(1)} %get-tuple-element.37), channel_id=1, source_target_pairs={{16,144},{48,176},{80,208},{112,240},{144,272},{176,304},{208,336}... | collective-permute-start | bytes 835592 | tf_op jit(solution)/shard_map/ppermute | solution.py:35
  130.1 3.1 collective-permute-done.15
  133.4 12.9 %collective-permute-start.16 = (f32[4,136,128]{2,1,0:T(8,128)S(1)}, f32[4,136,128]{2,1,0:T(8,128)S(1)}, u32[]{:S(2)}, u32[]{:S(2)}) collective-permute-start(f32[4,136,128]{2,1,0:T(8,128)S(1)} %get-tuple-element.35), channel_id=1, source_target_pairs={{16,272},{48,304},{80,336},{112,368},{144,400},{176,432},{208,464}... | collective-permute-start | bytes 835592 | tf_op jit(solution)/shard_map/ppermute | solution.py:35
  146.7 3.1 collective-permute-done.16
  154.3 2.3 collective-permute-start.24
  163.9 25.3 %collective-permute-done.23 = f32[3,128,128]{2,1,0:T(8,128)S(1)} collective-permute-done((f32[3,128,128]{2,1,0:T(8,128)S(1)}, f32[3,128,128]{2,1,0:T(8,128)S(1)}, u32[]{:S(2)}, u32[]{:S(2)}) %collective-permute-start.23) | collective-permute-done | bytes 196640 | tf_op jit(solution)/shard_map/ppermute | solution.py:35
  193.2 189.9 %all-gather = f32[128,1,384]{2,1,0:T(1,128)S(1)} all-gather(f32[1,1,384]{2,1,0:T(1,128)S(1)} %reshape.322), channel_id=1, replica_groups=mesh['seq'=32,'dp'=4,'tensor'=4] {'seq','dp'}, dimensions={0}, use_global_device_ids=true | all-gather | bytes 198144 | tf_op jit(solution)/shard_map/all_gather | solution.py:212
  390.2 3.3 collective-permute-start.30
  393.5 173.7 %all-gather.1 = f32[128,1,512]{2,1,0:T(1,128)S(1)} all-gather(f32[1,1,512]{2,1,0:T(1,128)S(1)} %bitcast.160), channel_id=1, replica_groups=mesh['seq'=32,'dp'=4,'tensor'=4] {'seq','dp'}, dimensions={0}, use_global_device_ids=true | all-gather | bytes 264192 | tf_op jit(solution)/shard_map/all_gather | solution.py:212
  567.5 4.5 collective-permute-start.31
  576.0 3.1 fusion.16
  580.0 4.6 collective-permute-start.35
  588.5 3.1 fusion.12
  592.5 3.7 collective-permute-done.33
  596.2 5.7 collective-permute-done.32
  (204 shorter events, 65.7 us)
Async XLA Ops:
  1.4 22.2 %collective-permute-start = (bf16[2,1,128,128]{3,2,1,0:T(8,128)(2,1)S(1)}, bf16[2,1,128,128]{3,2,1,0:T(8,128)(2,1)S(1)}, u32[]{:S(2)}, u32[]{:S(2)}) collective-permute-start(bf16[2,1,128,128]{3,2,1,0:T(8,128)(2,1)S(1)} %pad_maximum_fusion.6), channel_id=1, source_target_pairs={{0,64},{16,80},{32,96},{48,112},{64,128},{80,144},{96,160},{112,17... | collective-permute-start | bytes 196616 | tf_op jit(solution)/shard_map/ppermute | solution.py:21
  7.1 16.5 %collective-permute-start.1 = (bf16[2,1,128,128]{3,2,1,0:T(8,128)(2,1)S(1)}, bf16[2,1,128,128]{3,2,1,0:T(8,128)(2,1)S(1)}, u32[]{:S(2)}, u32[]{:S(2)}) collective-permute-start(bf16[2,1,128,128]{3,2,1,0:T(8,128)(2,1)S(1)} %pad_maximum_fusion.6), channel_id=1, source_target_pairs={{0,48},{16,64},{32,80},{48,96},{64,112},{80,128},{96,144},{112,160... | collective-permute-start | bytes 196616 | tf_op jit(solution)/shard_map/ppermute | solution.py:21
  14.1 9.6 %collective-permute-start.2 = (bf16[2,1,128,128]{3,2,1,0:T(8,128)(2,1)S(1)}, bf16[2,1,128,128]{3,2,1,0:T(8,128)(2,1)S(1)}, u32[]{:S(2)}, u32[]{:S(2)}) collective-permute-start(bf16[2,1,128,128]{3,2,1,0:T(8,128)(2,1)S(1)} %pad_maximum_fusion.6), channel_id=1, source_target_pairs={{0,32},{16,48},{32,64},{48,80},{64,96},{80,112},{96,128},{112,144}... | collective-permute-start | bytes 196616 | tf_op jit(solution)/shard_map/ppermute | solution.py:21
  17.6 6.0 %collective-permute-start.3 = (bf16[2,1,128,128]{3,2,1,0:T(8,128)(2,1)S(1)}, bf16[2,1,128,128]{3,2,1,0:T(8,128)(2,1)S(1)}, u32[]{:S(2)}, u32[]{:S(2)}) collective-permute-start(bf16[2,1,128,128]{3,2,1,0:T(8,128)(2,1)S(1)} %pad_maximum_fusion.6), channel_id=1, source_target_pairs={{0,16},{16,32},{32,48},{48,64},{64,80},{80,96},{96,112},{112,128},... | collective-permute-start | bytes 196616 | tf_op jit(solution)/shard_map/ppermute | solution.py:21
  28.1 4.3 collective-permute-start.4
  32.4 5.8 collective-permute-start.5
  39.3 5.0 collective-permute-start.6
  45.1 6.6 %collective-permute-start.7 = (f32[3,136,128]{2,1,0:T(8,128)}, f32[3,136,128]{2,1,0:T(8,128)}, u32[]{:S(2)}, u32[]{:S(2)}) collective-permute-start(f32[3,136,128]{2,1,0:T(8,128)} %multiply_select_fusion.3), channel_id=1, source_target_pairs={{16,48},{48,80},{80,112},{112,144},{144,176},{176,208},{208,240},{... | collective-permute-start | bytes 626696 | tf_op jit(solution)/shard_map/ppermute | solution.py:35
  52.9 8.8 %collective-permute-start.8 = (f32[3,136,128]{2,1,0:T(8,128)S(1)}, f32[3,136,128]{2,1,0:T(8,128)S(1)}, u32[]{:S(2)}, u32[]{:S(2)}) collective-permute-start(f32[3,136,128]{2,1,0:T(8,128)S(1)} %get-tuple-element.53), channel_id=1, source_target_pairs={{16,80},{48,112},{80,144},{112,176},{144,208},{176,240},{208,272},... | collective-permute-start | bytes 626696 | tf_op jit(solution)/shard_map/ppermute | solution.py:35
  61.9 14.3 %collective-permute-start.9 = (f32[3,136,128]{2,1,0:T(8,128)S(1)}, f32[3,136,128]{2,1,0:T(8,128)S(1)}, u32[]{:S(2)}, u32[]{:S(2)}) collective-permute-start(f32[3,136,128]{2,1,0:T(8,128)S(1)} %get-tuple-element.51), channel_id=1, source_target_pairs={{16,144},{48,176},{80,208},{112,240},{144,272},{176,304},{208,336}... | collective-permute-start | bytes 626696 | tf_op jit(solution)/shard_map/ppermute | solution.py:35
  76.3 15.4 %collective-permute-start.10 = (f32[3,136,128]{2,1,0:T(8,128)S(1)}, f32[3,136,128]{2,1,0:T(8,128)S(1)}, u32[]{:S(2)}, u32[]{:S(2)}) collective-permute-start(f32[3,136,128]{2,1,0:T(8,128)S(1)} %get-tuple-element.49), channel_id=1, source_target_pairs={{16,272},{48,304},{80,336},{112,368},{144,400},{176,432},{208,464}... | collective-permute-start | bytes 626696 | tf_op jit(solution)/shard_map/ppermute | solution.py:35
  94.5 6.1 %collective-permute-start.12 = (f32[4,136,128]{2,1,0:T(8,128)S(1)}, f32[4,136,128]{2,1,0:T(8,128)S(1)}, u32[]{:S(2)}, u32[]{:S(2)}) collective-permute-start(f32[4,136,128]{2,1,0:T(8,128)S(1)} %pad_maximum_fusion.1), channel_id=1, source_target_pairs={{0,16},{32,48},{64,80},{96,112},{128,144},{160,176},{192,208},{224... | collective-permute-start | bytes 835592 | tf_op jit(solution)/shard_map/ppermute | solution.py:35
  97.5 14.9 %collective-permute-start.18 = (f32[3,136,128]{2,1,0:T(8,128)S(1)}, f32[3,136,128]{2,1,0:T(8,128)S(1)}, u32[]{:S(2)}, u32[]{:S(2)}) collective-permute-start(f32[3,136,128]{2,1,0:T(8,128)S(1)} %pad_maximum_fusion.2), channel_id=1, source_target_pairs={{496,480},{464,448},{432,416},{400,384},{368,352},{336,320},{304,2... | collective-permute-start | bytes 626696 | tf_op jit(solution)/shard_map/ppermute | solution.py:35
  100.6 7.7 %collective-permute-start.13 = (f32[4,136,128]{2,1,0:T(8,128)S(1)}, f32[4,136,128]{2,1,0:T(8,128)S(1)}, u32[]{:S(2)}, u32[]{:S(2)}) collective-permute-start(f32[4,136,128]{2,1,0:T(8,128)S(1)} %multiply_select_fusion.1), channel_id=1, source_target_pairs={{16,48},{48,80},{80,112},{112,144},{144,176},{176,208},{208,240},{... | collective-permute-start | bytes 835592 | tf_op jit(solution)/shard_map/ppermute | solution.py:35
  108.5 7.3 %collective-permute-start.14 = (f32[4,136,128]{2,1,0:T(8,128)S(1)}, f32[4,136,128]{2,1,0:T(8,128)S(1)}, u32[]{:S(2)}, u32[]{:S(2)}) collective-permute-start(f32[4,136,128]{2,1,0:T(8,128)S(1)} %get-tuple-element.39), channel_id=1, source_target_pairs={{16,80},{48,112},{80,144},{112,176},{144,208},{176,240},{208,272},... | collective-permute-start | bytes 835592 | tf_op jit(solution)/shard_map/ppermute | solution.py:35
  112.5 38.8 %collective-permute-start.19 = (f32[3,136,128]{2,1,0:T(8,128)S(1)}, f32[3,136,128]{2,1,0:T(8,128)S(1)}, u32[]{:S(2)}, u32[]{:S(2)}) collective-permute-start(f32[3,136,128]{2,1,0:T(8,128)S(1)} %multiply_select_fusion.2), channel_id=1, source_target_pairs={{480,448},{448,416},{416,384},{384,352},{352,320},{320,288},{288,2... | collective-permute-start | bytes 626696 | tf_op jit(solution)/shard_map/ppermute | solution.py:35
  116.0 17.2 %collective-permute-start.15 = (f32[4,136,128]{2,1,0:T(8,128)S(1)}, f32[4,136,128]{2,1,0:T(8,128)S(1)}, u32[]{:S(2)}, u32[]{:S(2)}) collective-permute-start(f32[4,136,128]{2,1,0:T(8,128)S(1)} %get-tuple-element.37), channel_id=1, source_target_pairs={{16,144},{48,176},{80,208},{112,240},{144,272},{176,304},{208,336}... | collective-permute-start | bytes 835592 | tf_op jit(solution)/shard_map/ppermute | solution.py:35
  133.4 16.4 %collective-permute-start.16 = (f32[4,136,128]{2,1,0:T(8,128)S(1)}, f32[4,136,128]{2,1,0:T(8,128)S(1)}, u32[]{:S(2)}, u32[]{:S(2)}) collective-permute-start(f32[4,136,128]{2,1,0:T(8,128)S(1)} %get-tuple-element.35), channel_id=1, source_target_pairs={{16,272},{48,304},{80,336},{112,368},{144,400},{176,432},{208,464}... | collective-permute-start | bytes 835592 | tf_op jit(solution)/shard_map/ppermute | solution.py:35
  149.9 2.4 collective-permute-start.17
  151.5 5.1 collective-permute-start.20
  154.3 3.6 collective-permute-start.24
  159.9 2.4 collective-permute-start.26
  160.8 28.4 %collective-permute-start.23 = (f32[3,128,128]{2,1,0:T(8,128)S(1)}, f32[3,128,128]{2,1,0:T(8,128)S(1)}, u32[]{:S(2)}, u32[]{:S(2)}) collective-permute-start(f32[3,128,128]{2,1,0:T(8,128)S(1)} %slice.339), channel_id=1, source_target_pairs={{480,496},{448,464},{416,432},{384,400},{352,368},{320,336},{288,3... | collective-permute-start | bytes 589832 | tf_op jit(solution)/shard_map/ppermute | solution.py:35
  162.5 27.3 %collective-permute-start.27 = (f32[4,136,128]{2,1,0:T(8,128)S(1)}, f32[4,136,128]{2,1,0:T(8,128)}, u32[]{:S(2)}, u32[]{:S(2)}) collective-permute-start(f32[4,136,128]{2,1,0:T(8,128)S(1)} %get-tuple-element.31), channel_id=1, source_target_pairs={{480,352},{448,320},{416,288},{384,256},{352,224},{320,192},{288,1... | collective-permute-start | bytes 835592 | tf_op jit(solution)/shard_map/ppermute | solution.py:35
  191.6 193.4 %collective-permute-start.28 = (f32[4,136,128]{2,1,0:T(8,128)}, f32[4,136,128]{2,1,0:T(8,128)}, u32[]{:S(2)}, u32[]{:S(2)}) collective-permute-start(f32[4,136,128]{2,1,0:T(8,128)} %get-tuple-element.29), channel_id=1, source_target_pairs={{480,224},{448,192},{416,160},{384,128},{352,96},{320,64},{288,32}... | collective-permute-start | bytes 835592 | tf_op jit(solution)/shard_map/ppermute | solution.py:35
  386.2 3.4 collective-permute-start.29
  390.2 177.3 %collective-permute-start.30 = (f32[128]{0:T(128)S(1)}, f32[128]{0:T(128)S(1)}, u32[]{:S(2)}, u32[]{:S(2)}) collective-permute-start(f32[128]{0:T(128)S(1)} %multiply_reduce_fusion.1), channel_id=1, source_target_pairs={{0,1},{1,0},{2,3},{3,2},{4,5},{5,4},{6,7},{7,6},{8,9},{9,8},{10,11... | collective-permute-start | bytes 1544 | tf_op jit(solution)/shard_map/ppermute | solution.py:87
  567.5 5.8 collective-permute-start.31
  580.0 12.5 %collective-permute-start.35 = (f32[2,1,128,128]{3,2,1,0:T(8,128)}, f32[2,1,128,128]{3,2,1,0:T(8,128)}, u32[]{:S(2)}, u32[]{:S(2)}) collective-permute-start(f32[2,1,128,128]{3,2,1,0:T(8,128)} %get-tuple-element.27), channel_id=1, source_target_pairs={{16,0},{32,16},{48,32},{64,48},{80,64},{96,80},{112,96},{128,112},... | collective-permute-start | bytes 393224 | tf_op jit(solution)/shard_map/ppermute | solution.py:21
  584.6 7.9 %collective-permute-start.34 = (f32[2,1,128,128]{3,2,1,0:T(8,128)}, f32[2,1,128,128]{3,2,1,0:T(8,128)}, u32[]{:S(2)}, u32[]{:S(2)}) collective-permute-start(f32[2,1,128,128]{3,2,1,0:T(8,128)} %get-tuple-element.28), channel_id=1, source_target_pairs={{32,0},{48,16},{64,32},{80,48},{96,64},{112,80},{128,96},{144,112}... | collective-permute-start | bytes 393224 | tf_op jit(solution)/shard_map/ppermute | solution.py:21
  585.9 10.3 %collective-permute-start.33 = (f32[2,1,128,128]{3,2,1,0:T(8,128)}, f32[2,1,128,128]{3,2,1,0:T(8,128)}, u32[]{:S(2)}, u32[]{:S(2)}) collective-permute-start(f32[2,1,128,128]{3,2,1,0:T(8,128)} %get-tuple-element.26), channel_id=1, source_target_pairs={{48,0},{64,16},{80,32},{96,48},{112,64},{128,80},{144,96},{160,112... | collective-permute-start | bytes 393224 | tf_op jit(solution)/shard_map/ppermute | solution.py:21
  587.2 14.7 %collective-permute-start.32 = (f32[2,1,128,128]{3,2,1,0:T(8,128)}, f32[2,1,128,128]{3,2,1,0:T(8,128)}, u32[]{:S(2)}, u32[]{:S(2)}) collective-permute-start(f32[2,1,128,128]{3,2,1,0:T(8,128)} %get-tuple-element.25), channel_id=1, source_target_pairs={{64,0},{80,16},{96,32},{112,48},{128,64},{144,80},{160,96},{176,11... | collective-permute-start | bytes 393224 | tf_op jit(solution)/shard_map/ppermute | solution.py:21
  (18 other events, 919.0 us)

commit v4 on v3

--- a/solution.py
+++ b/solution.py
@@ -61,11 +61,12 @@
     before = identity
     distance = 2
     while distance < count:
+        sent = covered.astype(jnp.bfloat16) if distance >= 4 else covered
         moved = moved_on(
-            covered,
+            sent,
             axis,
             [(spot(p), spot(p + distance)) for p in range(1, count - distance, 2)],
-        )
+        ).astype(jnp.float32)
         present = place >= distance
         before = picked(present, chain_states(moved, before), before)
         if 2 * distance < count:
@@ -178,13 +179,9 @@
     splits = min(HEAD_SPLITS, q_heads)
     bounds = [q_heads * part // splits for part in range(splits + 1)]
     unit_parts, grad_parts, gain_parts = [], [], []
-    state_in = None
     for low, high in zip(bounds[:-1], bounds[1:]):
         part = slice(low, high)
-        part_state = local_state[part]
-        if state_in is not None:
-            part_state, _ = lax.optimization_barrier((part_state, state_in))
-        state_in = entering(block_decay[part], part_state, "seq", False)
+        state_in = entering(block_decay[part], local_state[part], "seq", False)
         carried = jnp.einsum("hsd,hde->hse", query_float[part], state_in, precision=precise)
         membrane = (
             jnp.einsum("hst,htd->hsd", decayed[part], spike_float[part], precision=precise)
@@ -209,12 +206,12 @@
         )
         part_level = spike_grad * (1.0 - bounded[part] * bounded[part])
         part_gain = jnp.sum(part_level * normed[part], axis=1).reshape((high - low) * HEAD_SIZE)
-        gain_parts.append(jnp.sum(lax.all_gather(part_gain, ("seq", "dp")), axis=0))
+        gain_parts.append(part_gain)
         unit_parts.append(unit_out)
         grad_parts.append(part_level)
     unit_out = jnp.concatenate(unit_parts, axis=0)
     level_grad = jnp.concatenate(grad_parts, axis=0)
-    gain_grads = jnp.concatenate(gain_parts, axis=0)
+    gain_grads = summed(jnp.concatenate(gain_parts, axis=0), ("seq", "dp"))
     layer_output = (
         unit_out.astype(jnp.bfloat16).transpose(1, 0, 2).reshape(1, block_rows, q_heads * HEAD_SIZE)
     )

time: 605 us -> 263 us (0.43)
  blocking collectives: 364 us -> 0 us
  waiting for transfers between devices: 61.1 us -> 81.8 us
  starting transfers between devices: 132 us -> 140 us
  other arithmetic: 16.3 us -> 8.42 us
    all_gather x2 -> x0, blocking collectives: 364 us -> none  [local(): gain_parts.append(jnp.sum(lax.all_gather(part_gain, ('seq', 'dp')), axis=0))]
    ppermute x4 -> x11, starting transfers between devices: 15.9 us -> 44.8 us  [summed(): lax.ppermute(value, axis, [(i, i ^ distance) for i in range(count)])]
    ppermute x24, starting transfers between devices: 89.5 us -> 66.9 us  [moved_on(): return lax.ppermute(value, axis, pairs)]
    ppermute x4 -> x11, waiting for transfers between devices: 1.98 us -> 14.5 us  [summed(): lax.ppermute(value, axis, [(i, i ^ distance) for i in range(count)])]
    ppermute x24, waiting for transfers between devices: 49.7 us -> 61.9 us  [moved_on(): return lax.ppermute(value, axis, pairs)]
  transfers between devices with their start and end apart: 36 -> 43, of which waited for: 17 -> 16; matrix products, arithmetic and copies ran while one was open for 4% -> 11% of each run, Pallas kernels for 0% -> 0%
where the time goes in v4:
time: 263 us; the launch traced here: 261 us
  starting transfers between devices  140 us (53%)
  waiting for transfers between devices  81.8 us (31%)
  matrix products  18.2 us (7%)
  local copies, waits for them, and re-layouts  10.6 us (4%)
  other arithmetic  8.42 us (3%)
    ppermute x24, starting transfers between devices, moved_on(): return lax.ppermute(value, axis, pairs)  66.9 us
    ppermute x24, waiting for transfers between devices, moved_on(): return lax.ppermute(value, axis, pairs)  61.9 us
    ppermute x11, starting transfers between devices, summed(): lax.ppermute(value, axis, [(i, i ^ distance) for i in range(count)])  44.8 us
    ppermute x8, starting transfers between devices, passed_along(): return lax.ppermute(block, axis, route)  28.6 us
    ppermute x11, waiting for transfers between devices, summed(): lax.ppermute(value, axis, [(i, i ^ distance) for i in range(count)])  14.5 us
    unnamed x22, local copies, waits for them, and re-layouts  5.77 us
    ppermute x8, waiting for transfers between devices, passed_along(): return lax.ppermute(block, axis, route)  5.36 us
  transfers between devices with their start and end apart: 43, of which 16 were waited for; matrix products, arithmetic and copies ran while one was open for 11% of the time, Pallas kernels for 0%

profile of v4, /device:TPU:1, one launch (start us, length us, event | category | flops | bytes accessed | tf_op | source)
XLA Modules:
  0.0 261.4 jit_solution(14401124785531287439)
XLA Ops:
  1.4 5.7 %collective-permute-start = (bf16[2,1,128,128]{3,2,1,0:T(8,128)(2,1)S(1)}, bf16[2,1,128,128]{3,2,1,0:T(8,128)(2,1)S(1)}, u32[]{:S(2)}, u32[]{:S(2)}) collective-permute-start(bf16[2,1,128,128]{3,2,1,0:T(8,128)(2,1)S(1)} %pad_maximum_fusion.6), channel_id=1, source_target_pairs={{0,64},{16,80},{32,96},{48,112},{64,128},{80,144},{96,160},{112,17... | collective-permute-start | bytes 196616 | tf_op jit(solution)/shard_map/ppermute | solution.py:21
  7.1 7.0 %collective-permute-start.1 = (bf16[2,1,128,128]{3,2,1,0:T(8,128)(2,1)S(1)}, bf16[2,1,128,128]{3,2,1,0:T(8,128)(2,1)S(1)}, u32[]{:S(2)}, u32[]{:S(2)}) collective-permute-start(bf16[2,1,128,128]{3,2,1,0:T(8,128)(2,1)S(1)} %pad_maximum_fusion.6), channel_id=1, source_target_pairs={{0,48},{16,64},{32,80},{48,96},{64,112},{80,128},{96,144},{112,160... | collective-permute-start | bytes 196616 | tf_op jit(solution)/shard_map/ppermute | solution.py:21
  14.1 3.5 %collective-permute-start.2 = (bf16[2,1,128,128]{3,2,1,0:T(8,128)(2,1)S(1)}, bf16[2,1,128,128]{3,2,1,0:T(8,128)(2,1)S(1)}, u32[]{:S(2)}, u32[]{:S(2)}) collective-permute-start(bf16[2,1,128,128]{3,2,1,0:T(8,128)(2,1)S(1)} %pad_maximum_fusion.6), channel_id=1, source_target_pairs={{0,32},{16,48},{32,64},{48,80},{64,96},{80,112},{96,128},{112,144}... | collective-permute-start | bytes 196616 | tf_op jit(solution)/shard_map/ppermute | solution.py:21
  26.7 2.2 fusion.198
  30.3 3.2 %collective-permute-start.4 = (f32[128]{0:T(128)S(1)}, f32[128]{0:T(128)S(1)}, u32[]{:S(2)}, u32[]{:S(2)}) collective-permute-start(f32[128]{0:T(128)S(1)} %get-tuple-element.64), channel_id=1, source_target_pairs={{0,1},{1,0},{2,3},{3,2},{4,5},{5,4},{6,7},{7,6},{8,9},{9,8},{10,11... | collective-permute-start | bytes 1544 | tf_op jit(solution)/shard_map/ppermute | solution.py:88
  34.6 4.8 %collective-permute-start.5 = (f32[128]{0:T(128)S(1)}, f32[128]{0:T(128)S(1)}, u32[]{:S(2)}, u32[]{:S(2)}) collective-permute-start(f32[128]{0:T(128)S(1)} %add.242), channel_id=1, source_target_pairs={{0,2},{1,3},{2,0},{3,1},{4,6},{5,7},{6,4},{7,5},{8,10},{9,11},{10,... | collective-permute-start | bytes 1544 | tf_op jit(solution)/shard_map/ppermute | solution.py:88
  45.0 3.4 %collective-permute-done.6 = f32[3,136,128]{2,1,0:T(8,128)S(1)} collective-permute-done((f32[3,136,128]{2,1,0:T(8,128)S(1)}, f32[3,136,128]{2,1,0:T(8,128)S(1)}, u32[]{:S(2)}, u32[]{:S(2)}) %collective-permute-start.6) | collective-permute-done | bytes 208928 | tf_op jit(solution)/shard_map/ppermute | solution.py:35
  48.5 3.6 %collective-permute-start.7 = (f32[3,136,128]{2,1,0:T(8,128)S(1)}, f32[3,136,128]{2,1,0:T(8,128)S(1)}, u32[]{:S(2)}, u32[]{:S(2)}) collective-permute-start(f32[3,136,128]{2,1,0:T(8,128)S(1)} %multiply_select_fusion.3), channel_id=1, source_target_pairs={{16,48},{48,80},{80,112},{112,144},{144,176},{176,208},{208,240},{... | collective-permute-start | bytes 626696 | tf_op jit(solution)/shard_map/ppermute | solution.py:35
  52.3 3.6 %collective-permute-start.13 = (f32[4,136,128]{2,1,0:T(8,128)S(1)}, f32[4,136,128]{2,1,0:T(8,128)S(1)}, u32[]{:S(2)}, u32[]{:S(2)}) collective-permute-start(f32[4,136,128]{2,1,0:T(8,128)S(1)} %multiply_select_fusion.1), channel_id=1, source_target_pairs={{16,48},{48,80},{80,112},{112,144},{144,176},{176,208},{208,240},{... | collective-permute-start | bytes 835592 | tf_op jit(solution)/shard_map/ppermute | solution.py:35
  56.3 5.2 %collective-permute-start.8 = (bf16[3,136,128]{2,1,0:T(8,128)(2,1)S(1)}, bf16[3,136,128]{2,1,0:T(8,128)(2,1)S(1)}, u32[]{:S(2)}, u32[]{:S(2)}) collective-permute-start(bf16[3,136,128]{2,1,0:T(8,128)(2,1)S(1)} %get-tuple-element.25), channel_id=1, source_target_pairs={{16,80},{48,112},{80,144},{112,176},{144,208},{176,240},{208,272},... | collective-permute-start | bytes 313352 | tf_op jit(solution)/shard_map/ppermute | solution.py:35
  63.4 9.7 %collective-permute-start.9 = (bf16[3,136,128]{2,1,0:T(8,128)(2,1)S(1)}, bf16[3,136,128]{2,1,0:T(8,128)(2,1)S(1)}, u32[]{:S(2)}, u32[]{:S(2)}) collective-permute-start(bf16[3,136,128]{2,1,0:T(8,128)(2,1)S(1)} %get-tuple-element.23), channel_id=1, source_target_pairs={{16,144},{48,176},{80,208},{112,240},{144,272},{176,304},{208,336}... | collective-permute-start | bytes 313352 | tf_op jit(solution)/shard_map/ppermute | solution.py:35
  75.2 11.6 %collective-permute-start.10 = (bf16[3,136,128]{2,1,0:T(8,128)(2,1)S(1)}, bf16[3,136,128]{2,1,0:T(8,128)(2,1)S(1)}, u32[]{:S(2)}, u32[]{:S(2)}) collective-permute-start(bf16[3,136,128]{2,1,0:T(8,128)(2,1)S(1)} %get-tuple-element.55), channel_id=1, source_target_pairs={{16,272},{48,304},{80,336},{112,368},{144,400},{176,432},{208,464}... | collective-permute-start | bytes 313352 | tf_op jit(solution)/shard_map/ppermute | solution.py:35
  87.1 4.0 %collective-permute-start.15 = (bf16[4,136,128]{2,1,0:T(8,128)(2,1)S(1)}, bf16[4,136,128]{2,1,0:T(8,128)(2,1)S(1)}, u32[]{:S(2)}, u32[]{:S(2)}) collective-permute-start(bf16[4,136,128]{2,1,0:T(8,128)(2,1)S(1)} %get-tuple-element.27), channel_id=1, source_target_pairs={{16,144},{48,176},{80,208},{112,240},{144,272},{176,304},{208,336}... | collective-permute-start | bytes 417800 | tf_op jit(solution)/shard_map/ppermute | solution.py:35
  93.3 11.1 %collective-permute-start.16 = (bf16[4,136,128]{2,1,0:T(8,128)(2,1)S(1)}, bf16[4,136,128]{2,1,0:T(8,128)(2,1)S(1)}, u32[]{:S(2)}, u32[]{:S(2)}) collective-permute-start(bf16[4,136,128]{2,1,0:T(8,128)(2,1)S(1)} %get-tuple-element.49), channel_id=1, source_target_pairs={{16,272},{48,304},{80,336},{112,368},{144,400},{176,432},{208,464}... | collective-permute-start | bytes 417800 | tf_op jit(solution)/shard_map/ppermute | solution.py:35
  111.4 2.3 collective-permute-start.24
  124.7 42.3 %collective-permute-done.23 = f32[3,128,128]{2,1,0:T(8,128)S(1)} collective-permute-done((f32[3,128,128]{2,1,0:T(8,128)S(1)}, f32[3,128,128]{2,1,0:T(8,128)S(1)}, u32[]{:S(2)}, u32[]{:S(2)}) %collective-permute-start.23) | collective-permute-done | bytes 196640 | tf_op jit(solution)/shard_map/ppermute | solution.py:35
  167.4 14.2 %collective-permute-done.29 = f32[4,128,128]{2,1,0:T(8,128)S(1)} collective-permute-done((f32[4,128,128]{2,1,0:T(8,128)S(1)}, f32[4,128,128]{2,1,0:T(8,128)S(1)}, u32[]{:S(2)}, u32[]{:S(2)}) %collective-permute-start.29) | collective-permute-done | bytes 262176 | tf_op jit(solution)/shard_map/ppermute | solution.py:35
  182.2 3.2 %collective-permute-start.30 = (f32[128]{0:T(128)S(1)}, f32[128]{0:T(128)S(1)}, u32[]{:S(2)}, u32[]{:S(2)}) collective-permute-start(f32[128]{0:T(128)S(1)} %multiply_reduce_fusion.1), channel_id=1, source_target_pairs={{0,1},{1,0},{2,3},{3,2},{4,5},{5,4},{6,7},{7,6},{8,9},{9,8},{10,11... | collective-permute-start | bytes 1544 | tf_op jit(solution)/shard_map/ppermute | solution.py:88
  186.5 4.8 %collective-permute-start.31 = (f32[128]{0:T(128)S(1)}, f32[128]{0:T(128)S(1)}, u32[]{:S(2)}, u32[]{:S(2)}) collective-permute-start(f32[128]{0:T(128)S(1)} %add.292), channel_id=1, source_target_pairs={{0,2},{1,3},{2,0},{3,1},{4,6},{5,7},{6,4},{7,5},{8,10},{9,11},{10,... | collective-permute-start | bytes 1544 | tf_op jit(solution)/shard_map/ppermute | solution.py:88
  191.3 3.5 %collective-permute-start.36 = (f32[896]{0:T(1024)S(1)}, f32[896]{0:T(1024)S(1)}, u32[]{:S(2)}, u32[]{:S(2)}) collective-permute-start(f32[896]{0:T(1024)S(1)} %pad_maximum_fusion.7), channel_id=1, source_target_pairs={{0,16},{16,0},{32,48},{48,32},{64,80},{80,64},{96,112},{112,96},{1... | collective-permute-start | bytes 10760 | tf_op jit(solution)/shard_map/ppermute | solution.py:88
  197.7 2.3 collective-permute-done.37
  199.9 8.7 %collective-permute-start.38 = (f32[896]{0:T(1024)S(1)}, f32[896]{0:T(1024)S(1)}, u32[]{:S(2)}, u32[]{:S(2)}) collective-permute-start(f32[896]{0:T(1024)S(1)} %add.299), channel_id=1, source_target_pairs={{0,64},{16,80},{32,96},{48,112},{64,0},{80,16},{96,32},{112,48},{1... | collective-permute-start | bytes 10760 | tf_op jit(solution)/shard_map/ppermute | solution.py:88
  209.6 5.3 %collective-permute-start.39 = (f32[896]{0:T(1024)S(1)}, f32[896]{0:T(1024)S(1)}, u32[]{:S(2)}, u32[]{:S(2)}) collective-permute-start(f32[896]{0:T(1024)S(1)} %add.300), channel_id=1, source_target_pairs={{0,128},{16,144},{32,160},{48,176},{64,192},{80,208},{96,224},{112... | collective-permute-start | bytes 10760 | tf_op jit(solution)/shard_map/ppermute | solution.py:88
  214.9 2.1 convolution_bitcast_fusion
  219.8 3.1 %fusion.16 = f32[1,1,640,128]{3,2,1,0:T(8,128)S(1)} fusion(bf16[7,128,128]{1,2,0:T(8,128)(2,1)S(1)} %bitcast.150, f32[7,128,640]{1,2,0:T(8,128)S(1)} %fusion.136, f32[7,128,640]{1,2,0:T(8,128)} %get-tuple-element.63, f32[7,128]{1,0:T(8,128)S(1)} %get-tuple-element.62), kind=kOutput, calls=%fused_computation.14 | convolution fusion | flops 150816256 | bytes 5148160 | tf_op jit(solution)/shard_map/gjsk,gjsd->gkd/dot_general | solution.py:233
  222.9 8.1 %collective-permute-done.40 = f32[896]{0:T(1024)S(1)} collective-permute-done((f32[896]{0:T(1024)S(1)}, f32[896]{0:T(1024)S(1)}, u32[]{:S(2)}, u32[]{:S(2)}) %collective-permute-start.40) | collective-permute-done | bytes 3616 | tf_op jit(solution)/shard_map/ppermute | solution.py:88
  230.9 3.1 %collective-permute-start.41 = (f32[896]{0:T(1024)S(1)}, f32[896]{0:T(1024)S(1)}, u32[]{:S(2)}, u32[]{:S(2)}) collective-permute-start(f32[896]{0:T(1024)S(1)} %add.302), channel_id=1, source_target_pairs={{0,4},{4,0},{8,12},{12,8},{1,5},{5,1},{9,13},{13,9},{2,6},{6,2},{1... | collective-permute-start | bytes 10760 | tf_op jit(solution)/shard_map/ppermute | solution.py:88
  234.9 6.6 %collective-permute-start.35 = (f32[2,1,128,128]{3,2,1,0:T(8,128)}, f32[2,1,128,128]{3,2,1,0:T(8,128)}, u32[]{:S(2)}, u32[]{:S(2)}) collective-permute-start(f32[2,1,128,128]{3,2,1,0:T(8,128)} %get-tuple-element.36), channel_id=1, source_target_pairs={{16,0},{32,16},{48,32},{64,48},{80,64},{96,80},{112,96},{128,112},... | collective-permute-start | bytes 393224 | tf_op jit(solution)/shard_map/ppermute | solution.py:21
  245.4 4.4 %collective-permute-start.42 = (f32[896]{0:T(1024)S(1)}, f32[896]{0:T(1024)S(1)}, u32[]{:S(2)}, u32[]{:S(2)}) collective-permute-start(f32[896]{0:T(1024)S(1)} %add.303), channel_id=1, source_target_pairs={{0,8},{4,12},{8,0},{12,4},{1,9},{5,13},{9,1},{13,5},{2,10},{6,14},... | collective-permute-start | bytes 10760 | tf_op jit(solution)/shard_map/ppermute | solution.py:88
  249.7 3.1 %fusion.12 = bf16[7,128,128]{1,2,0:T(8,128)(2,1)S(1)} fusion(f32[7,128,640]{1,2,0:T(8,128)S(1)} %fusion.136, bf16[2,1,640,128]{3,2,1,0:T(8,128)(2,1)S(1)} %constant_dynamic-update-slice_fusion, f32[7,128,640]{1,2,0:T(8,128)} %get-tuple-element.63, f32[7,128]{1,0:T(8,128)S(1)} %get-tuple-element.62), kind=kOutput, calls=%fused_computation.11 | convolution fusion | flops 150930944 | bytes 9576448 | tf_op jit(solution)/shard_map/gjsk,gkd->gjsd/dot_general | solution.py:230
  254.3 2.2 collective-permute-done.33
  256.5 3.1 %collective-permute-done.32 = f32[2,1,128,128]{3,2,1,0:T(8,128)} collective-permute-done((f32[2,1,128,128]{3,2,1,0:T(8,128)}, f32[2,1,128,128]{3,2,1,0:T(8,128)}, u32[]{:S(2)}, u32[]{:S(2)}) %collective-permute-start.32) | collective-permute-done | bytes 131104 | tf_op jit(solution)/shard_map/ppermute | solution.py:21
  (203 shorter events, 58.3 us)
Async XLA Ops:
  1.4 25.2 %collective-permute-start = (bf16[2,1,128,128]{3,2,1,0:T(8,128)(2,1)S(1)}, bf16[2,1,128,128]{3,2,1,0:T(8,128)(2,1)S(1)}, u32[]{:S(2)}, u32[]{:S(2)}) collective-permute-start(bf16[2,1,128,128]{3,2,1,0:T(8,128)(2,1)S(1)} %pad_maximum_fusion.6), channel_id=1, source_target_pairs={{0,64},{16,80},{32,96},{48,112},{64,128},{80,144},{96,160},{112,17... | collective-permute-start | bytes 196616 | tf_op jit(solution)/shard_map/ppermute | solution.py:21
  7.1 19.5 %collective-permute-start.1 = (bf16[2,1,128,128]{3,2,1,0:T(8,128)(2,1)S(1)}, bf16[2,1,128,128]{3,2,1,0:T(8,128)(2,1)S(1)}, u32[]{:S(2)}, u32[]{:S(2)}) collective-permute-start(bf16[2,1,128,128]{3,2,1,0:T(8,128)(2,1)S(1)} %pad_maximum_fusion.6), channel_id=1, source_target_pairs={{0,48},{16,64},{32,80},{48,96},{64,112},{80,128},{96,144},{112,160... | collective-permute-start | bytes 196616 | tf_op jit(solution)/shard_map/ppermute | solution.py:21
  14.1 12.5 %collective-permute-start.2 = (bf16[2,1,128,128]{3,2,1,0:T(8,128)(2,1)S(1)}, bf16[2,1,128,128]{3,2,1,0:T(8,128)(2,1)S(1)}, u32[]{:S(2)}, u32[]{:S(2)}) collective-permute-start(bf16[2,1,128,128]{3,2,1,0:T(8,128)(2,1)S(1)} %pad_maximum_fusion.6), channel_id=1, source_target_pairs={{0,32},{16,48},{32,64},{48,80},{64,96},{80,112},{96,128},{112,144}... | collective-permute-start | bytes 196616 | tf_op jit(solution)/shard_map/ppermute | solution.py:21
  17.6 9.0 %collective-permute-start.3 = (bf16[2,1,128,128]{3,2,1,0:T(8,128)(2,1)S(1)}, bf16[2,1,128,128]{3,2,1,0:T(8,128)(2,1)S(1)}, u32[]{:S(2)}, u32[]{:S(2)}) collective-permute-start(bf16[2,1,128,128]{3,2,1,0:T(8,128)(2,1)S(1)} %pad_maximum_fusion.6), channel_id=1, source_target_pairs={{0,16},{16,32},{32,48},{48,64},{64,80},{80,96},{96,112},{112,128},... | collective-permute-start | bytes 196616 | tf_op jit(solution)/shard_map/ppermute | solution.py:21
  30.3 4.3 %collective-permute-start.4 = (f32[128]{0:T(128)S(1)}, f32[128]{0:T(128)S(1)}, u32[]{:S(2)}, u32[]{:S(2)}) collective-permute-start(f32[128]{0:T(128)S(1)} %get-tuple-element.64), channel_id=1, source_target_pairs={{0,1},{1,0},{2,3},{3,2},{4,5},{5,4},{6,7},{7,6},{8,9},{9,8},{10,11... | collective-permute-start | bytes 1544 | tf_op jit(solution)/shard_map/ppermute | solution.py:88
  34.6 5.8 %collective-permute-start.5 = (f32[128]{0:T(128)S(1)}, f32[128]{0:T(128)S(1)}, u32[]{:S(2)}, u32[]{:S(2)}) collective-permute-start(f32[128]{0:T(128)S(1)} %add.242), channel_id=1, source_target_pairs={{0,2},{1,3},{2,0},{3,1},{4,6},{5,7},{6,4},{7,5},{8,10},{9,11},{10,... | collective-permute-start | bytes 1544 | tf_op jit(solution)/shard_map/ppermute | solution.py:88
  41.9 10.3 %collective-permute-start.12 = (f32[4,136,128]{2,1,0:T(8,128)S(1)}, f32[4,136,128]{2,1,0:T(8,128)S(1)}, u32[]{:S(2)}, u32[]{:S(2)}) collective-permute-start(f32[4,136,128]{2,1,0:T(8,128)S(1)} %pad_maximum_fusion.1), channel_id=1, source_target_pairs={{0,16},{32,48},{64,80},{96,112},{128,144},{160,176},{192,208},{224... | collective-permute-start | bytes 835592 | tf_op jit(solution)/shard_map/ppermute | solution.py:35
  43.3 5.0 %collective-permute-start.6 = (f32[3,136,128]{2,1,0:T(8,128)S(1)}, f32[3,136,128]{2,1,0:T(8,128)S(1)}, u32[]{:S(2)}, u32[]{:S(2)}) collective-permute-start(f32[3,136,128]{2,1,0:T(8,128)S(1)} %pad_maximum_fusion.3), channel_id=1, source_target_pairs={{0,16},{32,48},{64,80},{96,112},{128,144},{160,176},{192,208},{224... | collective-permute-start | bytes 626696 | tf_op jit(solution)/shard_map/ppermute | solution.py:35
  48.5 7.7 %collective-permute-start.7 = (f32[3,136,128]{2,1,0:T(8,128)S(1)}, f32[3,136,128]{2,1,0:T(8,128)S(1)}, u32[]{:S(2)}, u32[]{:S(2)}) collective-permute-start(f32[3,136,128]{2,1,0:T(8,128)S(1)} %multiply_select_fusion.3), channel_id=1, source_target_pairs={{16,48},{48,80},{80,112},{112,144},{144,176},{176,208},{208,240},{... | collective-permute-start | bytes 626696 | tf_op jit(solution)/shard_map/ppermute | solution.py:35
  52.3 20.9 %collective-permute-start.13 = (f32[4,136,128]{2,1,0:T(8,128)S(1)}, f32[4,136,128]{2,1,0:T(8,128)S(1)}, u32[]{:S(2)}, u32[]{:S(2)}) collective-permute-start(f32[4,136,128]{2,1,0:T(8,128)S(1)} %multiply_select_fusion.1), channel_id=1, source_target_pairs={{16,48},{48,80},{80,112},{112,144},{144,176},{176,208},{208,240},{... | collective-permute-start | bytes 835592 | tf_op jit(solution)/shard_map/ppermute | solution.py:35
  56.3 6.9 %collective-permute-start.8 = (bf16[3,136,128]{2,1,0:T(8,128)(2,1)S(1)}, bf16[3,136,128]{2,1,0:T(8,128)(2,1)S(1)}, u32[]{:S(2)}, u32[]{:S(2)}) collective-permute-start(bf16[3,136,128]{2,1,0:T(8,128)(2,1)S(1)} %get-tuple-element.25), channel_id=1, source_target_pairs={{16,80},{48,112},{80,144},{112,176},{144,208},{176,240},{208,272},... | collective-permute-start | bytes 313352 | tf_op jit(solution)/shard_map/ppermute | solution.py:35
  63.4 11.6 %collective-permute-start.9 = (bf16[3,136,128]{2,1,0:T(8,128)(2,1)S(1)}, bf16[3,136,128]{2,1,0:T(8,128)(2,1)S(1)}, u32[]{:S(2)}, u32[]{:S(2)}) collective-permute-start(bf16[3,136,128]{2,1,0:T(8,128)(2,1)S(1)} %get-tuple-element.23), channel_id=1, source_target_pairs={{16,144},{48,176},{80,208},{112,240},{144,272},{176,304},{208,336}... | collective-permute-start | bytes 313352 | tf_op jit(solution)/shard_map/ppermute | solution.py:35
  73.5 13.4 %collective-permute-start.14 = (bf16[4,136,128]{2,1,0:T(8,128)(2,1)S(1)}, bf16[4,136,128]{2,1,0:T(8,128)(2,1)S(1)}, u32[]{:S(2)}, u32[]{:S(2)}) collective-permute-start(bf16[4,136,128]{2,1,0:T(8,128)(2,1)S(1)} %get-tuple-element.29), channel_id=1, source_target_pairs={{16,80},{48,112},{80,144},{112,176},{144,208},{176,240},{208,272},... | collective-permute-start | bytes 417800 | tf_op jit(solution)/shard_map/ppermute | solution.py:35
  75.2 16.2 %collective-permute-start.10 = (bf16[3,136,128]{2,1,0:T(8,128)(2,1)S(1)}, bf16[3,136,128]{2,1,0:T(8,128)(2,1)S(1)}, u32[]{:S(2)}, u32[]{:S(2)}) collective-permute-start(bf16[3,136,128]{2,1,0:T(8,128)(2,1)S(1)} %get-tuple-element.55), channel_id=1, source_target_pairs={{16,272},{48,304},{80,336},{112,368},{144,400},{176,432},{208,464}... | collective-permute-start | bytes 313352 | tf_op jit(solution)/shard_map/ppermute | solution.py:35
  87.1 6.0 %collective-permute-start.15 = (bf16[4,136,128]{2,1,0:T(8,128)(2,1)S(1)}, bf16[4,136,128]{2,1,0:T(8,128)(2,1)S(1)}, u32[]{:S(2)}, u32[]{:S(2)}) collective-permute-start(bf16[4,136,128]{2,1,0:T(8,128)(2,1)S(1)} %get-tuple-element.27), channel_id=1, source_target_pairs={{16,144},{48,176},{80,208},{112,240},{144,272},{176,304},{208,336}... | collective-permute-start | bytes 417800 | tf_op jit(solution)/shard_map/ppermute | solution.py:35
  91.5 13.0 %collective-permute-start.11 = (f32[3,128,128]{2,1,0:T(8,128)S(1)}, f32[3,128,128]{2,1,0:T(8,128)S(1)}, u32[]{:S(2)}, u32[]{:S(2)}) collective-permute-start(f32[3,128,128]{2,1,0:T(8,128)S(1)} %slice.311), channel_id=1, source_target_pairs={{16,0},{48,32},{80,64},{112,96},{144,128},{176,160},{208,192},{240... | collective-permute-start | bytes 589832 | tf_op jit(solution)/shard_map/ppermute | solution.py:35
  93.3 14.2 %collective-permute-start.16 = (bf16[4,136,128]{2,1,0:T(8,128)(2,1)S(1)}, bf16[4,136,128]{2,1,0:T(8,128)(2,1)S(1)}, u32[]{:S(2)}, u32[]{:S(2)}) collective-permute-start(bf16[4,136,128]{2,1,0:T(8,128)(2,1)S(1)} %get-tuple-element.49), channel_id=1, source_target_pairs={{16,272},{48,304},{80,336},{112,368},{144,400},{176,432},{208,464}... | collective-permute-start | bytes 417800 | tf_op jit(solution)/shard_map/ppermute | solution.py:35
  109.1 5.2 %collective-permute-start.19 = (f32[3,136,128]{2,1,0:T(8,128)S(1)}, f32[3,136,128]{2,1,0:T(8,128)S(1)}, u32[]{:S(2)}, u32[]{:S(2)}) collective-permute-start(f32[3,136,128]{2,1,0:T(8,128)S(1)} %multiply_select_fusion.2), channel_id=1, source_target_pairs={{480,448},{448,416},{416,384},{384,352},{352,320},{320,288},{288,2... | collective-permute-start | bytes 626696 | tf_op jit(solution)/shard_map/ppermute | solution.py:35
  111.4 5.2 %collective-permute-start.24 = (f32[4,136,128]{2,1,0:T(8,128)S(1)}, f32[4,136,128]{2,1,0:T(8,128)S(1)}, u32[]{:S(2)}, u32[]{:S(2)}) collective-permute-start(f32[4,136,128]{2,1,0:T(8,128)S(1)} %pad_maximum_fusion), channel_id=1, source_target_pairs={{496,480},{464,448},{432,416},{400,384},{368,352},{336,320},{304,2... | collective-permute-start | bytes 835592 | tf_op jit(solution)/shard_map/ppermute | solution.py:35
  121.7 45.3 %collective-permute-start.23 = (f32[3,128,128]{2,1,0:T(8,128)S(1)}, f32[3,128,128]{2,1,0:T(8,128)S(1)}, u32[]{:S(2)}, u32[]{:S(2)}) collective-permute-start(f32[3,128,128]{2,1,0:T(8,128)S(1)} %slice.339), channel_id=1, source_target_pairs={{480,496},{448,464},{416,432},{384,400},{352,368},{320,336},{288,3... | collective-permute-start | bytes 589832 | tf_op jit(solution)/shard_map/ppermute | solution.py:35
  123.3 58.3 %collective-permute-start.29 = (f32[4,128,128]{2,1,0:T(8,128)S(1)}, f32[4,128,128]{2,1,0:T(8,128)S(1)}, u32[]{:S(2)}, u32[]{:S(2)}) collective-permute-start(f32[4,128,128]{2,1,0:T(8,128)S(1)} %slice.354), channel_id=1, source_target_pairs={{480,496},{448,464},{416,432},{384,400},{352,368},{320,336},{288,3... | collective-permute-start | bytes 786440 | tf_op jit(solution)/shard_map/ppermute | solution.py:35
  186.5 8.3 %collective-permute-start.31 = (f32[128]{0:T(128)S(1)}, f32[128]{0:T(128)S(1)}, u32[]{:S(2)}, u32[]{:S(2)}) collective-permute-start(f32[128]{0:T(128)S(1)} %add.292), channel_id=1, source_target_pairs={{0,2},{1,3},{2,0},{3,1},{4,6},{5,7},{6,4},{7,5},{8,10},{9,11},{10,... | collective-permute-start | bytes 1544 | tf_op jit(solution)/shard_map/ppermute | solution.py:88
  195.6 4.3 %collective-permute-start.37 = (f32[896]{0:T(1024)S(1)}, f32[896]{0:T(1024)S(1)}, u32[]{:S(2)}, u32[]{:S(2)}) collective-permute-start(f32[896]{0:T(1024)S(1)} %fusion.180), channel_id=1, source_target_pairs={{0,32},{16,48},{32,0},{48,16},{64,96},{80,112},{96,64},{112,80},{1... | collective-permute-start | bytes 10760 | tf_op jit(solution)/shard_map/ppermute | solution.py:88
  199.9 9.6 %collective-permute-start.38 = (f32[896]{0:T(1024)S(1)}, f32[896]{0:T(1024)S(1)}, u32[]{:S(2)}, u32[]{:S(2)}) collective-permute-start(f32[896]{0:T(1024)S(1)} %add.299), channel_id=1, source_target_pairs={{0,64},{16,80},{32,96},{48,112},{64,0},{80,16},{96,32},{112,48},{1... | collective-permute-start | bytes 10760 | tf_op jit(solution)/shard_map/ppermute | solution.py:88
  209.6 8.2 %collective-permute-start.39 = (f32[896]{0:T(1024)S(1)}, f32[896]{0:T(1024)S(1)}, u32[]{:S(2)}, u32[]{:S(2)}) collective-permute-start(f32[896]{0:T(1024)S(1)} %add.300), channel_id=1, source_target_pairs={{0,128},{16,144},{32,160},{48,176},{64,192},{80,208},{96,224},{112... | collective-permute-start | bytes 10760 | tf_op jit(solution)/shard_map/ppermute | solution.py:88
  217.8 13.1 %collective-permute-start.40 = (f32[896]{0:T(1024)S(1)}, f32[896]{0:T(1024)S(1)}, u32[]{:S(2)}, u32[]{:S(2)}) collective-permute-start(f32[896]{0:T(1024)S(1)} %add.301), channel_id=1, source_target_pairs={{0,256},{16,272},{32,288},{48,304},{64,320},{80,336},{96,352},{112... | collective-permute-start | bytes 10760 | tf_op jit(solution)/shard_map/ppermute | solution.py:88
  230.9 14.4 %collective-permute-start.41 = (f32[896]{0:T(1024)S(1)}, f32[896]{0:T(1024)S(1)}, u32[]{:S(2)}, u32[]{:S(2)}) collective-permute-start(f32[896]{0:T(1024)S(1)} %add.302), channel_id=1, source_target_pairs={{0,4},{4,0},{8,12},{12,8},{1,5},{5,1},{9,13},{13,9},{2,6},{6,2},{1... | collective-permute-start | bytes 10760 | tf_op jit(solution)/shard_map/ppermute | solution.py:88
  234.9 19.4 %collective-permute-start.35 = (f32[2,1,128,128]{3,2,1,0:T(8,128)}, f32[2,1,128,128]{3,2,1,0:T(8,128)}, u32[]{:S(2)}, u32[]{:S(2)}) collective-permute-start(f32[2,1,128,128]{3,2,1,0:T(8,128)} %get-tuple-element.36), channel_id=1, source_target_pairs={{16,0},{32,16},{48,32},{64,48},{80,64},{96,80},{112,96},{128,112},... | collective-permute-start | bytes 393224 | tf_op jit(solution)/shard_map/ppermute | solution.py:21
  241.5 12.9 %collective-permute-start.34 = (f32[2,1,128,128]{3,2,1,0:T(8,128)}, f32[2,1,128,128]{3,2,1,0:T(8,128)}, u32[]{:S(2)}, u32[]{:S(2)}) collective-permute-start(f32[2,1,128,128]{3,2,1,0:T(8,128)} %get-tuple-element.37), channel_id=1, source_target_pairs={{32,0},{48,16},{64,32},{80,48},{96,64},{112,80},{128,96},{144,112}... | collective-permute-start | bytes 393224 | tf_op jit(solution)/shard_map/ppermute | solution.py:21
  242.8 13.8 %collective-permute-start.33 = (f32[2,1,128,128]{3,2,1,0:T(8,128)}, f32[2,1,128,128]{3,2,1,0:T(8,128)}, u32[]{:S(2)}, u32[]{:S(2)}) collective-permute-start(f32[2,1,128,128]{3,2,1,0:T(8,128)} %get-tuple-element.35), channel_id=1, source_target_pairs={{48,0},{64,16},{80,32},{96,48},{112,64},{128,80},{144,96},{160,112... | collective-permute-start | bytes 393224 | tf_op jit(solution)/shard_map/ppermute | solution.py:21
  244.1 15.6 %collective-permute-start.32 = (f32[2,1,128,128]{3,2,1,0:T(8,128)}, f32[2,1,128,128]{3,2,1,0:T(8,128)}, u32[]{:S(2)}, u32[]{:S(2)}) collective-permute-start(f32[2,1,128,128]{3,2,1,0:T(8,128)} %get-tuple-element.34), channel_id=1, source_target_pairs={{64,0},{80,16},{96,32},{112,48},{128,64},{144,80},{160,96},{176,11... | collective-permute-start | bytes 393224 | tf_op jit(solution)/shard_map/ppermute | solution.py:21
  245.4 8.3 %collective-permute-start.42 = (f32[896]{0:T(1024)S(1)}, f32[896]{0:T(1024)S(1)}, u32[]{:S(2)}, u32[]{:S(2)}) collective-permute-start(f32[896]{0:T(1024)S(1)} %add.303), channel_id=1, source_target_pairs={{0,8},{4,12},{8,0},{12,4},{1,9},{5,13},{9,1},{13,5},{2,10},{6,14},... | collective-permute-start | bytes 10760 | tf_op jit(solution)/shard_map/ppermute | solution.py:88
  (17 other events, 71.8 us)

commit v5 on v4

--- a/solution.py
+++ b/solution.py
@@ -8,7 +8,7 @@
 HEAD_SIZE = 128
 D = 3584
 LONGEST_WINDOW = 512
-HEAD_SPLITS = 2
+HEAD_SPLITS = 1
 
 
 precise = lax.Precision.HIGHEST
@@ -77,16 +77,28 @@
     return jnp.where(lead, own_lead, handed)
 
 
+def xor_reduced(value, axis, offsets):
+    count = lax.axis_size(axis)
+    combos = [0]
+    for offset in offsets:
+        combos = combos + [c ^ offset for c in combos]
+    values = {0: value}
+    for c in combos[1:]:
+        values[c] = lax.ppermute(value, axis, [(i, i ^ c) for i in range(count)])
+    for offset in offsets:
+        values = {c: values[c] + values[c ^ offset] for c in values if not c & offset}
+    return values[0]
+
+
 def summed(value, axes):
     for axis in axes:
         count = lax.axis_size(axis)
         if count & (count - 1):
             value = lax.psum(value, axis)
             continue
-        distance = 1
-        while distance < count:
-            value = value + lax.ppermute(value, axis, [(i, i ^ distance) for i in range(count)])
-            distance *= 2
+        bits = [1 << k for k in range(count.bit_length() - 1)]
+        for low in range(0, len(bits), 3):
+            value = xor_reduced(value, axis, bits[low : low + 3])
     return value
 
 

time: 263 us -> 280 us (1.065)
  starting transfers between devices: 140 us -> 147 us
  other arithmetic: 8.42 us -> 13.2 us
  waiting for transfers between devices: 81.8 us -> 85.4 us
  matrix products: 18.2 us -> 21 us
    ppermute x11 -> x19, starting transfers between devices: 44.8 us -> 75.4 us  [xor_reduced(): values[c] = lax.ppermute(value, axis, [(i, i ^ c) for i in range(count)])]
    ppermute x24 -> x12, starting transfers between devices: 66.9 us -> 44.8 us  [moved_on(): return lax.ppermute(value, axis, pairs)]
    ppermute x11 -> x19, waiting for transfers between devices: 14.5 us -> 5.35 us  [xor_reduced(): values[c] = lax.ppermute(value, axis, [(i, i ^ c) for i in range(count)])]
    ppermute x8, waiting for transfers between devices: 5.36 us -> 13.7 us  [passed_along(): return lax.ppermute(block, axis, route)]
    convert_element_type x12 -> x6, other arithmetic: 2.08 us -> 7.14 us  [entering(): sent = covered.astype(jnp.bfloat16) if distance >= 4 else covered]
    ppermute x24 -> x12, waiting for transfers between devices: 61.9 us -> 66.4 us  [moved_on(): return lax.ppermute(value, axis, pairs)]
    unnamed x22 -> x92, local copies, waits for them, and re-layouts: 5.77 us -> 5.57 us
  transfers between devices with their start and end apart: 43 -> 39, of which waited for: 16 -> 13; matrix products, arithmetic and copies ran while one was open for 11% -> 7% of each run, Pallas kernels for 0% -> 0%
where the time goes in v5:
time: 280 us; the launch traced here: 278 us
  starting transfers between devices  147 us (52%)
  waiting for transfers between devices  85.4 us (30%)
  matrix products  21 us (8%)
  other arithmetic  13.2 us (5%)
  local copies, waits for them, and re-layouts  9.53 us (3%)
    ppermute x19, starting transfers between devices, xor_reduced(): values[c] = lax.ppermute(value, axis, [(i, i ^ c) for i in range(count)])  75.4 us
    ppermute x12, waiting for transfers between devices, moved_on(): return lax.ppermute(value, axis, pairs)  66.4 us
    ppermute x12, starting transfers between devices, moved_on(): return lax.ppermute(value, axis, pairs)  44.8 us
    ppermute x8, starting transfers between devices, passed_along(): return lax.ppermute(block, axis, route)  26.3 us
    ppermute x8, waiting for transfers between devices, passed_along(): return lax.ppermute(block, axis, route)  13.7 us
    convert_element_type x6, other arithmetic, entering(): sent = covered.astype(jnp.bfloat16) if distance >= 4 else covered  7.14 us
  transfers between devices with their start and end apart: 39, of which 13 were waited for; matrix products, arithmetic and copies ran while one was open for 7% of the time, Pallas kernels for 0%

profile of v5, /device:TPU:1, one launch (start us, length us, event | category | flops | bytes accessed | tf_op | source)
XLA Modules:
  0.0 278.2 jit_solution(7101916734578114811)
XLA Ops:
  1.4 5.7 %collective-permute-start = (bf16[2,1,128,128]{3,2,1,0:T(8,128)(2,1)S(1)}, bf16[2,1,128,128]{3,2,1,0:T(8,128)(2,1)S(1)}, u32[]{:S(2)}, u32[]{:S(2)}) collective-permute-start(bf16[2,1,128,128]{3,2,1,0:T(8,128)(2,1)S(1)} %pad_maximum_fusion.3), channel_id=1, source_target_pairs={{0,64},{16,80},{32,96},{48,112},{64,128},{80,144},{96,160},{112,17... | collective-permute-start | bytes 196616 | tf_op jit(solution)/shard_map/ppermute | solution.py:21
  7.1 7.0 %collective-permute-start.1 = (bf16[2,1,128,128]{3,2,1,0:T(8,128)(2,1)S(1)}, bf16[2,1,128,128]{3,2,1,0:T(8,128)(2,1)S(1)}, u32[]{:S(2)}, u32[]{:S(2)}) collective-permute-start(bf16[2,1,128,128]{3,2,1,0:T(8,128)(2,1)S(1)} %pad_maximum_fusion.3), channel_id=1, source_target_pairs={{0,48},{16,64},{32,80},{48,96},{64,112},{80,128},{96,144},{112,160... | collective-permute-start | bytes 196616 | tf_op jit(solution)/shard_map/ppermute | solution.py:21
  14.1 3.5 %collective-permute-start.2 = (bf16[2,1,128,128]{3,2,1,0:T(8,128)(2,1)S(1)}, bf16[2,1,128,128]{3,2,1,0:T(8,128)(2,1)S(1)}, u32[]{:S(2)}, u32[]{:S(2)}) collective-permute-start(bf16[2,1,128,128]{3,2,1,0:T(8,128)(2,1)S(1)} %pad_maximum_fusion.3), channel_id=1, source_target_pairs={{0,32},{16,48},{32,64},{48,80},{64,96},{80,112},{96,128},{112,144}... | collective-permute-start | bytes 196616 | tf_op jit(solution)/shard_map/ppermute | solution.py:21
  27.9 4.8 %collective-permute-start.5 = (f32[128]{0:T(128)S(1)}, f32[128]{0:T(128)S(1)}, u32[]{:S(2)}, u32[]{:S(2)}) collective-permute-start(f32[128]{0:T(128)S(1)} %get-tuple-element.48), channel_id=1, source_target_pairs={{0,2},{1,3},{2,0},{3,1},{4,6},{5,7},{6,4},{7,5},{8,10},{9,11},{10,... | collective-permute-start | bytes 1544 | tf_op jit(solution)/shard_map/ppermute | solution.py:87
  32.7 2.7 collective-permute-start.6
  42.0 3.5 %collective-permute-done.7 = f32[7,136,128]{2,1,0:T(8,128)S(1)} collective-permute-done((f32[7,136,128]{2,1,0:T(8,128)S(1)}, f32[7,136,128]{2,1,0:T(8,128)S(1)}, u32[]{:S(2)}, u32[]{:S(2)}) %collective-permute-start.7) | collective-permute-done | bytes 487456 | tf_op jit(solution)/shard_map/ppermute | solution.py:35
  45.7 3.6 %collective-permute-start.8 = (f32[7,136,128]{2,1,0:T(8,128)S(1)}, f32[7,136,128]{2,1,0:T(8,128)S(1)}, u32[]{:S(2)}, u32[]{:S(2)}) collective-permute-start(f32[7,136,128]{2,1,0:T(8,128)S(1)} %multiply_select_fusion.1), channel_id=1, source_target_pairs={{16,48},{48,80},{80,112},{112,144},{144,176},{176,208},{208,240},{... | collective-permute-start | bytes 1462280 | tf_op jit(solution)/shard_map/ppermute | solution.py:35
  49.4 5.5 %collective-permute-done.8 = f32[7,136,128]{2,1,0:T(8,128)S(1)} collective-permute-done((f32[7,136,128]{2,1,0:T(8,128)S(1)}, f32[7,136,128]{2,1,0:T(8,128)S(1)}, u32[]{:S(2)}, u32[]{:S(2)}) %collective-permute-start.8) | collective-permute-done | bytes 487456 | tf_op jit(solution)/shard_map/ppermute | solution.py:35
  56.0 6.8 %collective-permute-start.9 = (bf16[7,136,128]{2,1,0:T(8,128)(2,1)}, bf16[7,136,128]{2,1,0:T(8,128)(2,1)}, u32[]{:S(2)}, u32[]{:S(2)}) collective-permute-start(bf16[7,136,128]{2,1,0:T(8,128)(2,1)} %get-tuple-element.25), channel_id=1, source_target_pairs={{16,80},{48,112},{80,144},{112,176},{144,208},{176,240},{208,272},... | collective-permute-start | bytes 731144 | tf_op jit(solution)/shard_map/ppermute | solution.py:35
  63.0 2.5 collective-permute-done.9
  67.5 12.4 %collective-permute-start.10 = (bf16[7,136,128]{2,1,0:T(8,128)(2,1)}, bf16[7,136,128]{2,1,0:T(8,128)(2,1)}, u32[]{:S(2)}, u32[]{:S(2)}) collective-permute-start(bf16[7,136,128]{2,1,0:T(8,128)(2,1)} %get-tuple-element.23), channel_id=1, source_target_pairs={{16,144},{48,176},{80,208},{112,240},{144,272},{176,304},{208,336}... | collective-permute-start | bytes 731144 | tf_op jit(solution)/shard_map/ppermute | solution.py:35
  80.2 2.5 collective-permute-done.10
  83.9 12.6 %collective-permute-start.11 = (bf16[7,136,128]{2,1,0:T(8,128)(2,1)S(1)}, bf16[7,136,128]{2,1,0:T(8,128)(2,1)S(1)}, u32[]{:S(2)}, u32[]{:S(2)}) collective-permute-start(bf16[7,136,128]{2,1,0:T(8,128)(2,1)S(1)} %get-tuple-element.36), channel_id=1, source_target_pairs={{16,272},{48,304},{80,336},{112,368},{144,400},{176,432},{208,464}... | collective-permute-start | bytes 731144 | tf_op jit(solution)/shard_map/ppermute | solution.py:35
  120.8 50.2 %collective-permute-done.18 = f32[7,128,128]{2,1,0:T(8,128)} collective-permute-done((f32[7,128,128]{2,1,0:T(8,128)S(1)}, f32[7,128,128]{2,1,0:T(8,128)}, u32[]{:S(2)}, u32[]{:S(2)}) %collective-permute-start.18) | collective-permute-done | bytes 458784 | tf_op jit(solution)/shard_map/ppermute | solution.py:35
  171.0 2.7 multiply_reduce_fusion.1
  173.8 3.4 %collective-permute-start.20 = (f32[128]{0:T(128)S(1)}, f32[128]{0:T(128)S(1)}, u32[]{:S(2)}, u32[]{:S(2)}) collective-permute-start(f32[128]{0:T(128)S(1)} %get-tuple-element.16), channel_id=1, source_target_pairs={{0,2},{1,3},{2,0},{3,1},{4,6},{5,7},{6,4},{7,5},{8,10},{9,11},{10,... | collective-permute-start | bytes 1544 | tf_op jit(solution)/shard_map/ppermute | solution.py:87
  177.2 2.6 collective-permute-start.21
  183.3 12.2 %collective-permute-start.31 = (f32[896]{0:T(1024)}, f32[896]{0:T(1024)S(1)}, u32[]{:S(2)}, u32[]{:S(2)}) collective-permute-start(f32[896]{0:T(1024)} %bitcast.39), channel_id=1, source_target_pairs={{0,96},{16,112},{32,64},{48,80},{64,32},{80,48},{96,0},{112,16},{1... | collective-permute-start | bytes 10760 | tf_op jit(solution)/shard_map/ppermute | solution.py:87
  195.5 2.8 %collective-permute-start.32 = (f32[896]{0:T(1024)}, f32[896]{0:T(1024)S(1)}, u32[]{:S(2)}, u32[]{:S(2)}) collective-permute-start(f32[896]{0:T(1024)} %bitcast.39), channel_id=1, source_target_pairs={{0,112},{16,96},{32,80},{48,64},{64,48},{80,32},{96,16},{112,0},{1... | collective-permute-start | bytes 10760 | tf_op jit(solution)/shard_map/ppermute | solution.py:87
  198.3 5.6 %collective-permute-start.29 = (f32[896]{0:T(1024)}, f32[896]{0:T(1024)S(1)}, u32[]{:S(2)}, u32[]{:S(2)}) collective-permute-start(f32[896]{0:T(1024)} %bitcast.39), channel_id=1, source_target_pairs={{0,64},{16,80},{32,96},{48,112},{64,0},{80,16},{96,32},{112,48},{1... | collective-permute-start | bytes 10760 | tf_op jit(solution)/shard_map/ppermute | solution.py:87
  206.1 3.9 %collective-permute-start.27 = (f32[896]{0:T(1024)}, f32[896]{0:T(1024)S(1)}, u32[]{:S(2)}, u32[]{:S(2)}) collective-permute-start(f32[896]{0:T(1024)} %bitcast.39), channel_id=1, source_target_pairs={{0,32},{16,48},{32,0},{48,16},{64,96},{80,112},{96,64},{112,80},{1... | collective-permute-start | bytes 10760 | tf_op jit(solution)/shard_map/ppermute | solution.py:87
  210.8 3.2 %fusion.15 = bf16[7,128,128]{1,2,0:T(8,128)(2,1)S(1)} fusion(f32[7,128,640]{1,2,0:T(8,128)S(1)} %fusion.95, bf16[2,1,640,128]{3,2,1,0:T(8,128)(2,1)S(1)} %copy-done.18, f32[7,128,640]{1,2,0:T(8,128)} %get-tuple-element.47, f32[7,128]{1,0:T(8,128)S(1)} %copy-done.40), kind=kOutput, calls=%fused_computation.21 | convolution fusion | flops 150930944 | bytes 9576448 | tf_op jit(solution)/shard_map/gjsk,gkd->gjsd/dot_general | solution.py:242
  214.0 2.8 %collective-permute-start.28 = (f32[896]{0:T(1024)}, f32[896]{0:T(1024)S(1)}, u32[]{:S(2)}, u32[]{:S(2)}) collective-permute-start(f32[896]{0:T(1024)} %bitcast.39), channel_id=1, source_target_pairs={{0,48},{16,32},{32,16},{48,0},{64,112},{80,96},{96,80},{112,64},{1... | collective-permute-start | bytes 10760 | tf_op jit(solution)/shard_map/ppermute | solution.py:87
  223.9 12.5 %collective-permute-start.35 = (f32[896]{0:T(1024)S(1)}, f32[896]{0:T(1024)S(1)}, u32[]{:S(2)}, u32[]{:S(2)}) collective-permute-start(f32[896]{0:T(1024)S(1)} %add_add_fusion.2), channel_id=1, source_target_pairs={{0,384},{16,400},{32,416},{48,432},{64,448},{80,464},{96,480},{112... | collective-permute-start | bytes 10760 | tf_op jit(solution)/shard_map/ppermute | solution.py:87
  238.4 3.1 %fusion.19 = f32[1,1,640,128]{3,2,1,0:T(8,128)S(1)} fusion(bf16[7,128,128]{1,2,0:T(8,128)(2,1)S(1)} %bitcast.135, f32[7,128,640]{1,2,0:T(8,128)S(1)} %fusion.95, f32[7,128,640]{1,2,0:T(8,128)} %get-tuple-element.47, f32[7,128]{1,0:T(8,128)S(1)} %copy-done.40), kind=kOutput, calls=%fused_computation.24 | convolution fusion | flops 150816256 | bytes 5148160 | tf_op jit(solution)/shard_map/gjsk,gjsd->gkd/dot_general | solution.py:245
  241.5 3.2 %collective-permute-done.33 = f32[896]{0:T(1024)S(1)} collective-permute-done((f32[896]{0:T(1024)S(1)}, f32[896]{0:T(1024)S(1)}, u32[]{:S(2)}, u32[]{:S(2)}) %collective-permute-start.33) | collective-permute-done | bytes 3616 | tf_op jit(solution)/shard_map/ppermute | solution.py:87
  244.7 4.6 %collective-permute-start.37 = (f32[896]{0:T(1024)S(1)}, f32[896]{0:T(1024)S(1)}, u32[]{:S(2)}, u32[]{:S(2)}) collective-permute-start(f32[896]{0:T(1024)S(1)} %add_add_fusion.1), channel_id=1, source_target_pairs={{0,8},{4,12},{8,0},{12,4},{1,9},{5,13},{9,1},{13,5},{2,10},{6,14},... | collective-permute-start | bytes 10760 | tf_op jit(solution)/shard_map/ppermute | solution.py:87
  249.4 2.8 collective-permute-start.38
  255.0 4.3 %collective-permute-start.25 = (f32[2,1,128,128]{3,2,1,0:T(8,128)S(1)}, f32[2,1,128,128]{3,2,1,0:T(8,128)S(1)}, u32[]{:S(2)}, u32[]{:S(2)}) collective-permute-start(f32[2,1,128,128]{3,2,1,0:T(8,128)S(1)} %get-tuple-element.29), channel_id=1, source_target_pairs={{16,0},{32,16},{48,32},{64,48},{80,64},{96,80},{112,96},{128,112},... | collective-permute-start | bytes 393224 | tf_op jit(solution)/shard_map/ppermute | solution.py:21
  263.8 3.0 %collective-permute-done.24 = f32[2,1,128,128]{3,2,1,0:T(8,128)S(1)} collective-permute-done((f32[2,1,128,128]{3,2,1,0:T(8,128)S(1)}, f32[2,1,128,128]{3,2,1,0:T(8,128)S(1)}, u32[]{:S(2)}, u32[]{:S(2)}) %collective-permute-start.24) | collective-permute-done | bytes 131104 | tf_op jit(solution)/shard_map/ppermute | solution.py:21
  266.8 6.3 %collective-permute-done.23 = f32[2,1,128,128]{3,2,1,0:T(8,128)S(1)} collective-permute-done((f32[2,1,128,128]{3,2,1,0:T(8,128)S(1)}, f32[2,1,128,128]{3,2,1,0:T(8,128)S(1)}, u32[]{:S(2)}, u32[]{:S(2)}) %collective-permute-start.23) | collective-permute-done | bytes 131104 | tf_op jit(solution)/shard_map/ppermute | solution.py:21
  273.0 4.5 %collective-permute-done.22 = f32[2,1,128,128]{3,2,1,0:T(8,128)S(1)} collective-permute-done((f32[2,1,128,128]{3,2,1,0:T(8,128)S(1)}, f32[2,1,128,128]{3,2,1,0:T(8,128)S(1)}, u32[]{:S(2)}, u32[]{:S(2)}) %collective-permute-start.22) | collective-permute-done | bytes 131104 | tf_op jit(solution)/shard_map/ppermute | solution.py:21
  (208 shorter events, 68.8 us)
Async XLA Ops:
  1.4 22.0 %collective-permute-start = (bf16[2,1,128,128]{3,2,1,0:T(8,128)(2,1)S(1)}, bf16[2,1,128,128]{3,2,1,0:T(8,128)(2,1)S(1)}, u32[]{:S(2)}, u32[]{:S(2)}) collective-permute-start(bf16[2,1,128,128]{3,2,1,0:T(8,128)(2,1)S(1)} %pad_maximum_fusion.3), channel_id=1, source_target_pairs={{0,64},{16,80},{32,96},{48,112},{64,128},{80,144},{96,160},{112,17... | collective-permute-start | bytes 196616 | tf_op jit(solution)/shard_map/ppermute | solution.py:21
  7.1 16.3 %collective-permute-start.1 = (bf16[2,1,128,128]{3,2,1,0:T(8,128)(2,1)S(1)}, bf16[2,1,128,128]{3,2,1,0:T(8,128)(2,1)S(1)}, u32[]{:S(2)}, u32[]{:S(2)}) collective-permute-start(bf16[2,1,128,128]{3,2,1,0:T(8,128)(2,1)S(1)} %pad_maximum_fusion.3), channel_id=1, source_target_pairs={{0,48},{16,64},{32,80},{48,96},{64,112},{80,128},{96,144},{112,160... | collective-permute-start | bytes 196616 | tf_op jit(solution)/shard_map/ppermute | solution.py:21
  14.1 9.4 %collective-permute-start.2 = (bf16[2,1,128,128]{3,2,1,0:T(8,128)(2,1)S(1)}, bf16[2,1,128,128]{3,2,1,0:T(8,128)(2,1)S(1)}, u32[]{:S(2)}, u32[]{:S(2)}) collective-permute-start(bf16[2,1,128,128]{3,2,1,0:T(8,128)(2,1)S(1)} %pad_maximum_fusion.3), channel_id=1, source_target_pairs={{0,32},{16,48},{32,64},{48,80},{64,96},{80,112},{96,128},{112,144}... | collective-permute-start | bytes 196616 | tf_op jit(solution)/shard_map/ppermute | solution.py:21
  17.6 5.9 %collective-permute-start.3 = (bf16[2,1,128,128]{3,2,1,0:T(8,128)(2,1)S(1)}, bf16[2,1,128,128]{3,2,1,0:T(8,128)(2,1)S(1)}, u32[]{:S(2)}, u32[]{:S(2)}) collective-permute-start(bf16[2,1,128,128]{3,2,1,0:T(8,128)(2,1)S(1)} %pad_maximum_fusion.3), channel_id=1, source_target_pairs={{0,16},{16,32},{32,48},{48,64},{64,80},{80,96},{96,112},{112,128},... | collective-permute-start | bytes 196616 | tf_op jit(solution)/shard_map/ppermute | solution.py:21
  27.9 9.7 %collective-permute-start.5 = (f32[128]{0:T(128)S(1)}, f32[128]{0:T(128)S(1)}, u32[]{:S(2)}, u32[]{:S(2)}) collective-permute-start(f32[128]{0:T(128)S(1)} %get-tuple-element.48), channel_id=1, source_target_pairs={{0,2},{1,3},{2,0},{3,1},{4,6},{5,7},{6,4},{7,5},{8,10},{9,11},{10,... | collective-permute-start | bytes 1544 | tf_op jit(solution)/shard_map/ppermute | solution.py:87
  32.7 5.5 %collective-permute-start.6 = (f32[128]{0:T(128)S(1)}, f32[128]{0:T(128)S(1)}, u32[]{:S(2)}, u32[]{:S(2)}) collective-permute-start(f32[128]{0:T(128)S(1)} %get-tuple-element.48), channel_id=1, source_target_pairs={{0,3},{1,2},{2,1},{3,0},{4,7},{5,6},{6,5},{7,4},{8,11},{9,10},{10,... | collective-permute-start | bytes 1544 | tf_op jit(solution)/shard_map/ppermute | solution.py:87
  40.7 4.8 %collective-permute-start.7 = (f32[7,136,128]{2,1,0:T(8,128)S(1)}, f32[7,136,128]{2,1,0:T(8,128)S(1)}, u32[]{:S(2)}, u32[]{:S(2)}) collective-permute-start(f32[7,136,128]{2,1,0:T(8,128)S(1)} %pad_maximum_fusion.1), channel_id=1, source_target_pairs={{0,16},{32,48},{64,80},{96,112},{128,144},{160,176},{192,208},{224... | collective-permute-start | bytes 1462280 | tf_op jit(solution)/shard_map/ppermute | solution.py:35
  45.7 9.3 %collective-permute-start.8 = (f32[7,136,128]{2,1,0:T(8,128)S(1)}, f32[7,136,128]{2,1,0:T(8,128)S(1)}, u32[]{:S(2)}, u32[]{:S(2)}) collective-permute-start(f32[7,136,128]{2,1,0:T(8,128)S(1)} %multiply_select_fusion.1), channel_id=1, source_target_pairs={{16,48},{48,80},{80,112},{112,144},{144,176},{176,208},{208,240},{... | collective-permute-start | bytes 1462280 | tf_op jit(solution)/shard_map/ppermute | solution.py:35
  56.0 9.6 %collective-permute-start.9 = (bf16[7,136,128]{2,1,0:T(8,128)(2,1)}, bf16[7,136,128]{2,1,0:T(8,128)(2,1)}, u32[]{:S(2)}, u32[]{:S(2)}) collective-permute-start(bf16[7,136,128]{2,1,0:T(8,128)(2,1)} %get-tuple-element.25), channel_id=1, source_target_pairs={{16,80},{48,112},{80,144},{112,176},{144,208},{176,240},{208,272},... | collective-permute-start | bytes 731144 | tf_op jit(solution)/shard_map/ppermute | solution.py:35
  67.5 15.2 %collective-permute-start.10 = (bf16[7,136,128]{2,1,0:T(8,128)(2,1)}, bf16[7,136,128]{2,1,0:T(8,128)(2,1)}, u32[]{:S(2)}, u32[]{:S(2)}) collective-permute-start(bf16[7,136,128]{2,1,0:T(8,128)(2,1)} %get-tuple-element.23), channel_id=1, source_target_pairs={{16,144},{48,176},{80,208},{112,240},{144,272},{176,304},{208,336}... | collective-permute-start | bytes 731144 | tf_op jit(solution)/shard_map/ppermute | solution.py:35
  83.9 15.7 %collective-permute-start.11 = (bf16[7,136,128]{2,1,0:T(8,128)(2,1)S(1)}, bf16[7,136,128]{2,1,0:T(8,128)(2,1)S(1)}, u32[]{:S(2)}, u32[]{:S(2)}) collective-permute-start(bf16[7,136,128]{2,1,0:T(8,128)(2,1)S(1)} %get-tuple-element.36), channel_id=1, source_target_pairs={{16,272},{48,304},{80,336},{112,368},{144,400},{176,432},{208,464}... | collective-permute-start | bytes 731144 | tf_op jit(solution)/shard_map/ppermute | solution.py:35
  118.5 52.5 %collective-permute-start.18 = (f32[7,128,128]{2,1,0:T(8,128)S(1)}, f32[7,128,128]{2,1,0:T(8,128)}, u32[]{:S(2)}, u32[]{:S(2)}) collective-permute-start(f32[7,128,128]{2,1,0:T(8,128)S(1)} %slice.140), channel_id=1, source_target_pairs={{480,496},{448,464},{416,432},{384,400},{352,368},{320,336},{288,3... | collective-permute-start | bytes 1376264 | tf_op jit(solution)/shard_map/ppermute | solution.py:35
  173.8 24.5 %collective-permute-start.20 = (f32[128]{0:T(128)S(1)}, f32[128]{0:T(128)S(1)}, u32[]{:S(2)}, u32[]{:S(2)}) collective-permute-start(f32[128]{0:T(128)S(1)} %get-tuple-element.16), channel_id=1, source_target_pairs={{0,2},{1,3},{2,0},{3,1},{4,6},{5,7},{6,4},{7,5},{8,10},{9,11},{10,... | collective-permute-start | bytes 1544 | tf_op jit(solution)/shard_map/ppermute | solution.py:87
  177.2 26.7 %collective-permute-start.21 = (f32[128]{0:T(128)S(1)}, f32[128]{0:T(128)S(1)}, u32[]{:S(2)}, u32[]{:S(2)}) collective-permute-start(f32[128]{0:T(128)S(1)} %get-tuple-element.16), channel_id=1, source_target_pairs={{0,3},{1,2},{2,1},{3,0},{4,7},{5,6},{6,5},{7,4},{8,11},{9,10},{10,... | collective-permute-start | bytes 1544 | tf_op jit(solution)/shard_map/ppermute | solution.py:87
  180.0 26.1 %collective-permute-start.19 = (f32[128]{0:T(128)S(1)}, f32[128]{0:T(128)S(1)}, u32[]{:S(2)}, u32[]{:S(2)}) collective-permute-start(f32[128]{0:T(128)S(1)} %get-tuple-element.16), channel_id=1, source_target_pairs={{0,1},{1,0},{2,3},{3,2},{4,5},{5,4},{6,7},{7,6},{8,9},{9,8},{10,11... | collective-permute-start | bytes 1544 | tf_op jit(solution)/shard_map/ppermute | solution.py:87
  183.3 30.7 %collective-permute-start.31 = (f32[896]{0:T(1024)}, f32[896]{0:T(1024)S(1)}, u32[]{:S(2)}, u32[]{:S(2)}) collective-permute-start(f32[896]{0:T(1024)} %bitcast.39), channel_id=1, source_target_pairs={{0,96},{16,112},{32,64},{48,80},{64,32},{80,48},{96,0},{112,16},{1... | collective-permute-start | bytes 10760 | tf_op jit(solution)/shard_map/ppermute | solution.py:87
  195.5 21.3 %collective-permute-start.32 = (f32[896]{0:T(1024)}, f32[896]{0:T(1024)S(1)}, u32[]{:S(2)}, u32[]{:S(2)}) collective-permute-start(f32[896]{0:T(1024)} %bitcast.39), channel_id=1, source_target_pairs={{0,112},{16,96},{32,80},{48,64},{64,48},{80,32},{96,16},{112,0},{1... | collective-permute-start | bytes 10760 | tf_op jit(solution)/shard_map/ppermute | solution.py:87
  198.3 23.0 %collective-permute-start.29 = (f32[896]{0:T(1024)}, f32[896]{0:T(1024)S(1)}, u32[]{:S(2)}, u32[]{:S(2)}) collective-permute-start(f32[896]{0:T(1024)} %bitcast.39), channel_id=1, source_target_pairs={{0,64},{16,80},{32,96},{48,112},{64,0},{80,16},{96,32},{112,48},{1... | collective-permute-start | bytes 10760 | tf_op jit(solution)/shard_map/ppermute | solution.py:87
  203.9 17.4 %collective-permute-start.30 = (f32[896]{0:T(1024)}, f32[896]{0:T(1024)S(1)}, u32[]{:S(2)}, u32[]{:S(2)}) collective-permute-start(f32[896]{0:T(1024)} %bitcast.39), channel_id=1, source_target_pairs={{0,80},{16,64},{32,112},{48,96},{64,16},{80,0},{96,48},{112,32},{1... | collective-permute-start | bytes 10760 | tf_op jit(solution)/shard_map/ppermute | solution.py:87
  206.1 15.2 %collective-permute-start.27 = (f32[896]{0:T(1024)}, f32[896]{0:T(1024)S(1)}, u32[]{:S(2)}, u32[]{:S(2)}) collective-permute-start(f32[896]{0:T(1024)} %bitcast.39), channel_id=1, source_target_pairs={{0,32},{16,48},{32,0},{48,16},{64,96},{80,112},{96,64},{112,80},{1... | collective-permute-start | bytes 10760 | tf_op jit(solution)/shard_map/ppermute | solution.py:87
  214.0 7.3 %collective-permute-start.28 = (f32[896]{0:T(1024)}, f32[896]{0:T(1024)S(1)}, u32[]{:S(2)}, u32[]{:S(2)}) collective-permute-start(f32[896]{0:T(1024)} %bitcast.39), channel_id=1, source_target_pairs={{0,48},{16,32},{32,16},{48,0},{64,112},{80,96},{96,80},{112,64},{1... | collective-permute-start | bytes 10760 | tf_op jit(solution)/shard_map/ppermute | solution.py:87
  216.8 4.5 %collective-permute-start.26 = (f32[896]{0:T(1024)}, f32[896]{0:T(1024)S(1)}, u32[]{:S(2)}, u32[]{:S(2)}) collective-permute-start(f32[896]{0:T(1024)} %bitcast.39), channel_id=1, source_target_pairs={{0,16},{16,0},{32,48},{48,32},{64,80},{80,64},{96,112},{112,96},{1... | collective-permute-start | bytes 10760 | tf_op jit(solution)/shard_map/ppermute | solution.py:87
  222.0 19.5 %collective-permute-start.34 = (f32[896]{0:T(1024)S(1)}, f32[896]{0:T(1024)S(1)}, u32[]{:S(2)}, u32[]{:S(2)}) collective-permute-start(f32[896]{0:T(1024)S(1)} %add_add_fusion.2), channel_id=1, source_target_pairs={{0,256},{16,272},{32,288},{48,304},{64,320},{80,336},{96,352},{112... | collective-permute-start | bytes 10760 | tf_op jit(solution)/shard_map/ppermute | solution.py:87
  223.9 17.6 %collective-permute-start.35 = (f32[896]{0:T(1024)S(1)}, f32[896]{0:T(1024)S(1)}, u32[]{:S(2)}, u32[]{:S(2)}) collective-permute-start(f32[896]{0:T(1024)S(1)} %add_add_fusion.2), channel_id=1, source_target_pairs={{0,384},{16,400},{32,416},{48,432},{64,448},{80,464},{96,480},{112... | collective-permute-start | bytes 10760 | tf_op jit(solution)/shard_map/ppermute | solution.py:87
  236.5 8.3 %collective-permute-start.33 = (f32[896]{0:T(1024)S(1)}, f32[896]{0:T(1024)S(1)}, u32[]{:S(2)}, u32[]{:S(2)}) collective-permute-start(f32[896]{0:T(1024)S(1)} %add_add_fusion.2), channel_id=1, source_target_pairs={{0,128},{16,144},{32,160},{48,176},{64,192},{80,208},{96,224},{112... | collective-permute-start | bytes 10760 | tf_op jit(solution)/shard_map/ppermute | solution.py:87
  244.7 15.8 %collective-permute-start.37 = (f32[896]{0:T(1024)S(1)}, f32[896]{0:T(1024)S(1)}, u32[]{:S(2)}, u32[]{:S(2)}) collective-permute-start(f32[896]{0:T(1024)S(1)} %add_add_fusion.1), channel_id=1, source_target_pairs={{0,8},{4,12},{8,0},{12,4},{1,9},{5,13},{9,1},{13,5},{2,10},{6,14},... | collective-permute-start | bytes 10760 | tf_op jit(solution)/shard_map/ppermute | solution.py:87
  249.4 12.5 %collective-permute-start.38 = (f32[896]{0:T(1024)S(1)}, f32[896]{0:T(1024)S(1)}, u32[]{:S(2)}, u32[]{:S(2)}) collective-permute-start(f32[896]{0:T(1024)S(1)} %add_add_fusion.1), channel_id=1, source_target_pairs={{0,12},{4,8},{8,4},{12,0},{1,13},{5,9},{9,5},{13,1},{2,14},{6,10},... | collective-permute-start | bytes 10760 | tf_op jit(solution)/shard_map/ppermute | solution.py:87
  252.2 11.0 %collective-permute-start.36 = (f32[896]{0:T(1024)S(1)}, f32[896]{0:T(1024)S(1)}, u32[]{:S(2)}, u32[]{:S(2)}) collective-permute-start(f32[896]{0:T(1024)S(1)} %add_add_fusion.1), channel_id=1, source_target_pairs={{0,4},{4,0},{8,12},{12,8},{1,5},{5,1},{9,13},{13,9},{2,6},{6,2},{1... | collective-permute-start | bytes 10760 | tf_op jit(solution)/shard_map/ppermute | solution.py:87
  255.0 8.8 %collective-permute-start.25 = (f32[2,1,128,128]{3,2,1,0:T(8,128)S(1)}, f32[2,1,128,128]{3,2,1,0:T(8,128)S(1)}, u32[]{:S(2)}, u32[]{:S(2)}) collective-permute-start(f32[2,1,128,128]{3,2,1,0:T(8,128)S(1)} %get-tuple-element.29), channel_id=1, source_target_pairs={{16,0},{32,16},{48,32},{64,48},{80,64},{96,80},{112,96},{128,112},... | collective-permute-start | bytes 393224 | tf_op jit(solution)/shard_map/ppermute | solution.py:21
  259.3 7.5 %collective-permute-start.24 = (f32[2,1,128,128]{3,2,1,0:T(8,128)S(1)}, f32[2,1,128,128]{3,2,1,0:T(8,128)S(1)}, u32[]{:S(2)}, u32[]{:S(2)}) collective-permute-start(f32[2,1,128,128]{3,2,1,0:T(8,128)S(1)} %get-tuple-element.30), channel_id=1, source_target_pairs={{32,0},{48,16},{64,32},{80,48},{96,64},{112,80},{128,96},{144,112}... | collective-permute-start | bytes 393224 | tf_op jit(solution)/shard_map/ppermute | solution.py:21
  260.6 12.4 %collective-permute-start.23 = (f32[2,1,128,128]{3,2,1,0:T(8,128)S(1)}, f32[2,1,128,128]{3,2,1,0:T(8,128)S(1)}, u32[]{:S(2)}, u32[]{:S(2)}) collective-permute-start(f32[2,1,128,128]{3,2,1,0:T(8,128)S(1)} %get-tuple-element.28), channel_id=1, source_target_pairs={{48,0},{64,16},{80,32},{96,48},{112,64},{128,80},{144,96},{160,112... | collective-permute-start | bytes 393224 | tf_op jit(solution)/shard_map/ppermute | solution.py:21
  261.9 15.6 %collective-permute-start.22 = (f32[2,1,128,128]{3,2,1,0:T(8,128)S(1)}, f32[2,1,128,128]{3,2,1,0:T(8,128)S(1)}, u32[]{:S(2)}, u32[]{:S(2)}) collective-permute-start(f32[2,1,128,128]{3,2,1,0:T(8,128)S(1)} %get-tuple-element.27), channel_id=1, source_target_pairs={{64,0},{80,16},{96,32},{112,48},{128,64},{144,80},{160,96},{176,11... | collective-permute-start | bytes 393224 | tf_op jit(solution)/shard_map/ppermute | solution.py:21
  (48 other events, 880.7 us)

commit v6 on v5

--- a/solution.py
+++ b/solution.py
@@ -96,9 +96,8 @@
         if count & (count - 1):
             value = lax.psum(value, axis)
             continue
-        bits = [1 << k for k in range(count.bit_length() - 1)]
-        for low in range(0, len(bits), 3):
-            value = xor_reduced(value, axis, bits[low : low + 3])
+        for k in range(count.bit_length() - 1):
+            value = xor_reduced(value, axis, [1 << k])
     return value
 
 

time: 280 us -> 264 us (0.943)
  starting transfers between devices: 147 us -> 122 us
  waiting for transfers between devices: 85.4 us -> 94.2 us
    ppermute x19 -> x11, starting transfers between devices: 75.4 us -> 49 us  [xor_reduced(): values[c] = lax.ppermute(value, axis, [(i, i ^ c) for i in range(count)])]
    ppermute x12, waiting for transfers between devices: 66.4 us -> 76.2 us  [moved_on(): return lax.ppermute(value, axis, pairs)]
    ppermute x8, waiting for transfers between devices: 13.7 us -> 5.58 us  [passed_along(): return lax.ppermute(block, axis, route)]
    ppermute x19 -> x11, waiting for transfers between devices: 5.35 us -> 12.4 us  [xor_reduced(): values[c] = lax.ppermute(value, axis, [(i, i ^ c) for i in range(count)])]
  transfers between devices with their start and end apart: 39 -> 31, of which waited for: 13 -> 15; matrix products, arithmetic and copies ran while one was open for 7% -> 8% of each run, Pallas kernels for 0% -> 0%
where the time goes in v6:
time: 264 us; the launch traced here: 263 us
  starting transfers between devices  122 us (46%)
  waiting for transfers between devices  94.2 us (36%)
  matrix products  20.4 us (8%)
  other arithmetic  14.2 us (5%)
  local copies, waits for them, and re-layouts  9.55 us (4%)
    ppermute x12, waiting for transfers between devices, moved_on(): return lax.ppermute(value, axis, pairs)  76.2 us
    ppermute x11, starting transfers between devices, xor_reduced(): values[c] = lax.ppermute(value, axis, [(i, i ^ c) for i in range(count)])  49 us
    ppermute x12, starting transfers between devices, moved_on(): return lax.ppermute(value, axis, pairs)  45.4 us
    ppermute x8, starting transfers between devices, passed_along(): return lax.ppermute(block, axis, route)  27.9 us
    ppermute x11, waiting for transfers between devices, xor_reduced(): values[c] = lax.ppermute(value, axis, [(i, i ^ c) for i in range(count)])  12.4 us
    convert_element_type x6, other arithmetic, entering(): sent = covered.astype(jnp.bfloat16) if distance >= 4 else covered  7.12 us
    unnamed x92, local copies, waits for them, and re-layouts  5.59 us
    ppermute x8, waiting for transfers between devices, passed_along(): return lax.ppermute(block, axis, route)  5.58 us
  transfers between devices with their start and end apart: 31, of which 15 were waited for; matrix products, arithmetic and copies ran while one was open for 8% of the time, Pallas kernels for 0%

profile of v6, /device:TPU:1, one launch (start us, length us, event | category | flops | bytes accessed | tf_op | source)
XLA Modules:
  0.0 263.0 jit_solution(8911012108799421697)
XLA Ops:
  1.4 5.7 %collective-permute-start = (bf16[2,1,128,128]{3,2,1,0:T(8,128)(2,1)S(1)}, bf16[2,1,128,128]{3,2,1,0:T(8,128)(2,1)S(1)}, u32[]{:S(2)}, u32[]{:S(2)}) collective-permute-start(bf16[2,1,128,128]{3,2,1,0:T(8,128)(2,1)S(1)} %pad_maximum_fusion.3), channel_id=1, source_target_pairs={{0,64},{16,80},{32,96},{48,112},{64,128},{80,144},{96,160},{112,17... | collective-permute-start | bytes 196616 | tf_op jit(solution)/shard_map/ppermute | solution.py:21
  7.1 7.0 %collective-permute-start.1 = (bf16[2,1,128,128]{3,2,1,0:T(8,128)(2,1)S(1)}, bf16[2,1,128,128]{3,2,1,0:T(8,128)(2,1)S(1)}, u32[]{:S(2)}, u32[]{:S(2)}) collective-permute-start(bf16[2,1,128,128]{3,2,1,0:T(8,128)(2,1)S(1)} %pad_maximum_fusion.3), channel_id=1, source_target_pairs={{0,48},{16,64},{32,80},{48,96},{64,112},{80,128},{96,144},{112,160... | collective-permute-start | bytes 196616 | tf_op jit(solution)/shard_map/ppermute | solution.py:21
  14.1 3.5 %collective-permute-start.2 = (bf16[2,1,128,128]{3,2,1,0:T(8,128)(2,1)S(1)}, bf16[2,1,128,128]{3,2,1,0:T(8,128)(2,1)S(1)}, u32[]{:S(2)}, u32[]{:S(2)}) collective-permute-start(bf16[2,1,128,128]{3,2,1,0:T(8,128)(2,1)S(1)} %pad_maximum_fusion.3), channel_id=1, source_target_pairs={{0,32},{16,48},{32,64},{48,80},{64,96},{80,112},{96,128},{112,144}... | collective-permute-start | bytes 196616 | tf_op jit(solution)/shard_map/ppermute | solution.py:21
  23.7 2.2 fusion.123
  27.3 3.2 %collective-permute-start.4 = (f32[128]{0:T(128)S(1)}, f32[128]{0:T(128)S(1)}, u32[]{:S(2)}, u32[]{:S(2)}) collective-permute-start(f32[128]{0:T(128)S(1)} %get-tuple-element.48), channel_id=1, source_target_pairs={{0,1},{1,0},{2,3},{3,2},{4,5},{5,4},{6,7},{7,6},{8,9},{9,8},{10,11... | collective-permute-start | bytes 1544 | tf_op jit(solution)/shard_map/ppermute | solution.py:87
  31.6 4.8 %collective-permute-start.5 = (f32[128]{0:T(128)S(1)}, f32[128]{0:T(128)S(1)}, u32[]{:S(2)}, u32[]{:S(2)}) collective-permute-start(f32[128]{0:T(128)S(1)} %add.175), channel_id=1, source_target_pairs={{0,2},{1,3},{2,0},{3,1},{4,6},{5,7},{6,4},{7,5},{8,10},{9,11},{10,... | collective-permute-start | bytes 1544 | tf_op jit(solution)/shard_map/ppermute | solution.py:87
  39.7 4.1 %collective-permute-done.6 = f32[7,136,128]{2,1,0:T(8,128)S(1)} collective-permute-done((f32[7,136,128]{2,1,0:T(8,128)S(1)}, f32[7,136,128]{2,1,0:T(8,128)S(1)}, u32[]{:S(2)}, u32[]{:S(2)}) %collective-permute-start.6) | collective-permute-done | bytes 487456 | tf_op jit(solution)/shard_map/ppermute | solution.py:35
  43.9 3.6 %collective-permute-start.7 = (f32[7,136,128]{2,1,0:T(8,128)S(1)}, f32[7,136,128]{2,1,0:T(8,128)S(1)}, u32[]{:S(2)}, u32[]{:S(2)}) collective-permute-start(f32[7,136,128]{2,1,0:T(8,128)S(1)} %multiply_select_fusion.1), channel_id=1, source_target_pairs={{16,48},{48,80},{80,112},{112,144},{144,176},{176,208},{208,240},{... | collective-permute-start | bytes 1462280 | tf_op jit(solution)/shard_map/ppermute | solution.py:35
  47.7 5.5 %collective-permute-done.7 = f32[7,136,128]{2,1,0:T(8,128)S(1)} collective-permute-done((f32[7,136,128]{2,1,0:T(8,128)S(1)}, f32[7,136,128]{2,1,0:T(8,128)S(1)}, u32[]{:S(2)}, u32[]{:S(2)}) %collective-permute-start.7) | collective-permute-done | bytes 487456 | tf_op jit(solution)/shard_map/ppermute | solution.py:35
  54.2 6.8 %collective-permute-start.8 = (bf16[7,136,128]{2,1,0:T(8,128)(2,1)}, bf16[7,136,128]{2,1,0:T(8,128)(2,1)}, u32[]{:S(2)}, u32[]{:S(2)}) collective-permute-start(bf16[7,136,128]{2,1,0:T(8,128)(2,1)} %get-tuple-element.25), channel_id=1, source_target_pairs={{16,80},{48,112},{80,144},{112,176},{144,208},{176,240},{208,272},... | collective-permute-start | bytes 731144 | tf_op jit(solution)/shard_map/ppermute | solution.py:35
  61.3 2.5 collective-permute-done.8
  63.8 1.9 fusion.120
  65.7 12.8 %collective-permute-start.9 = (bf16[7,136,128]{2,1,0:T(8,128)(2,1)}, bf16[7,136,128]{2,1,0:T(8,128)(2,1)}, u32[]{:S(2)}, u32[]{:S(2)}) collective-permute-start(bf16[7,136,128]{2,1,0:T(8,128)(2,1)} %get-tuple-element.23), channel_id=1, source_target_pairs={{16,144},{48,176},{80,208},{112,240},{144,272},{176,304},{208,336}... | collective-permute-start | bytes 731144 | tf_op jit(solution)/shard_map/ppermute | solution.py:35
  78.8 2.4 collective-permute-done.9
  82.5 12.8 %collective-permute-start.10 = (bf16[7,136,128]{2,1,0:T(8,128)(2,1)S(1)}, bf16[7,136,128]{2,1,0:T(8,128)(2,1)S(1)}, u32[]{:S(2)}, u32[]{:S(2)}) collective-permute-start(bf16[7,136,128]{2,1,0:T(8,128)(2,1)S(1)} %get-tuple-element.36), channel_id=1, source_target_pairs={{16,272},{48,304},{80,336},{112,368},{144,400},{176,432},{208,464}... | collective-permute-start | bytes 731144 | tf_op jit(solution)/shard_map/ppermute | solution.py:35
  105.7 2.3 collective-permute-start.12
  119.6 59.5 %collective-permute-done.17 = f32[7,128,128]{2,1,0:T(8,128)} collective-permute-done((f32[7,128,128]{2,1,0:T(8,128)S(1)}, f32[7,128,128]{2,1,0:T(8,128)}, u32[]{:S(2)}, u32[]{:S(2)}) %collective-permute-start.17) | collective-permute-done | bytes 458784 | tf_op jit(solution)/shard_map/ppermute | solution.py:35
  179.1 2.2 multiply_reduce_fusion.1
  181.2 3.3 %collective-permute-start.18 = (f32[128]{0:T(128)S(1)}, f32[128]{0:T(128)S(1)}, u32[]{:S(2)}, u32[]{:S(2)}) collective-permute-start(f32[128]{0:T(128)S(1)} %get-tuple-element.16), channel_id=1, source_target_pairs={{0,1},{1,0},{2,3},{3,2},{4,5},{5,4},{6,7},{7,6},{8,9},{9,8},{10,11... | collective-permute-start | bytes 1544 | tf_op jit(solution)/shard_map/ppermute | solution.py:87
  185.7 4.8 %collective-permute-start.19 = (f32[128]{0:T(128)S(1)}, f32[128]{0:T(128)S(1)}, u32[]{:S(2)}, u32[]{:S(2)}) collective-permute-start(f32[128]{0:T(128)S(1)} %add.204), channel_id=1, source_target_pairs={{0,2},{1,3},{2,0},{3,1},{4,6},{5,7},{6,4},{7,5},{8,10},{9,11},{10,... | collective-permute-start | bytes 1544 | tf_op jit(solution)/shard_map/ppermute | solution.py:87
  191.5 3.5 %collective-permute-start.24 = (f32[896]{0:T(1024)S(1)}, f32[896]{0:T(1024)S(1)}, u32[]{:S(2)}, u32[]{:S(2)}) collective-permute-start(f32[896]{0:T(1024)S(1)} %bitcast.151), channel_id=1, source_target_pairs={{0,16},{16,0},{32,48},{48,32},{64,80},{80,64},{96,112},{112,96},{1... | collective-permute-start | bytes 10760 | tf_op jit(solution)/shard_map/ppermute | solution.py:87
  195.8 3.6 %collective-permute-start.25 = (f32[896]{0:T(1024)S(1)}, f32[896]{0:T(1024)S(1)}, u32[]{:S(2)}, u32[]{:S(2)}) collective-permute-start(f32[896]{0:T(1024)S(1)} %bitcast_add_fusion.1), channel_id=1, source_target_pairs={{0,32},{16,48},{32,0},{48,16},{64,96},{80,112},{96,64},{112,80},{1... | collective-permute-start | bytes 10760 | tf_op jit(solution)/shard_map/ppermute | solution.py:87
  200.4 6.2 %collective-permute-start.26 = (f32[896]{0:T(1024)S(1)}, f32[896]{0:T(1024)S(1)}, u32[]{:S(2)}, u32[]{:S(2)}) collective-permute-start(f32[896]{0:T(1024)S(1)} %add.211), channel_id=1, source_target_pairs={{0,64},{16,80},{32,96},{48,112},{64,0},{80,16},{96,32},{112,48},{1... | collective-permute-start | bytes 10760 | tf_op jit(solution)/shard_map/ppermute | solution.py:87
  207.6 10.1 %collective-permute-start.27 = (f32[896]{0:T(1024)S(1)}, f32[896]{0:T(1024)S(1)}, u32[]{:S(2)}, u32[]{:S(2)}) collective-permute-start(f32[896]{0:T(1024)S(1)} %add.212), channel_id=1, source_target_pairs={{0,128},{16,144},{32,160},{48,176},{64,192},{80,208},{96,224},{112... | collective-permute-start | bytes 10760 | tf_op jit(solution)/shard_map/ppermute | solution.py:87
  217.7 2.2 convolution_bitcast_fusion
  221.8 3.1 %fusion.19 = f32[1,1,640,128]{3,2,1,0:T(8,128)S(1)} fusion(bf16[7,128,128]{1,2,0:T(8,128)(2,1)S(1)} %bitcast.135, f32[7,128,640]{1,2,0:T(8,128)S(1)} %fusion.95, f32[7,128,640]{1,2,0:T(8,128)} %get-tuple-element.47, f32[7,128]{1,0:T(8,128)S(1)} %copy-done.40), kind=kOutput, calls=%fused_computation.24 | convolution fusion | flops 150816256 | bytes 5148160 | tf_op jit(solution)/shard_map/gjsk,gjsd->gkd/dot_general | solution.py:244
  224.9 8.1 %collective-permute-done.28 = f32[896]{0:T(1024)S(1)} collective-permute-done((f32[896]{0:T(1024)S(1)}, f32[896]{0:T(1024)S(1)}, u32[]{:S(2)}, u32[]{:S(2)}) %collective-permute-start.28) | collective-permute-done | bytes 3616 | tf_op jit(solution)/shard_map/ppermute | solution.py:87
  233.0 3.1 %collective-permute-start.29 = (f32[896]{0:T(1024)S(1)}, f32[896]{0:T(1024)S(1)}, u32[]{:S(2)}, u32[]{:S(2)}) collective-permute-start(f32[896]{0:T(1024)S(1)} %add.214), channel_id=1, source_target_pairs={{0,4},{4,0},{8,12},{12,8},{1,5},{5,1},{9,13},{13,9},{2,6},{6,2},{1... | collective-permute-start | bytes 10760 | tf_op jit(solution)/shard_map/ppermute | solution.py:87
  236.9 5.9 %collective-permute-start.23 = (f32[2,1,128,128]{3,2,1,0:T(8,128)}, f32[2,1,128,128]{3,2,1,0:T(8,128)S(1)}, u32[]{:S(2)}, u32[]{:S(2)}) collective-permute-start(f32[2,1,128,128]{3,2,1,0:T(8,128)} %get-tuple-element.29), channel_id=1, source_target_pairs={{16,0},{32,16},{48,32},{64,48},{80,64},{96,80},{112,96},{128,112},... | collective-permute-start | bytes 393224 | tf_op jit(solution)/shard_map/ppermute | solution.py:21
  246.8 4.4 %collective-permute-start.30 = (f32[896]{0:T(1024)S(1)}, f32[896]{0:T(1024)S(1)}, u32[]{:S(2)}, u32[]{:S(2)}) collective-permute-start(f32[896]{0:T(1024)S(1)} %add.215), channel_id=1, source_target_pairs={{0,8},{4,12},{8,0},{12,4},{1,9},{5,13},{9,1},{13,5},{2,10},{6,14},... | collective-permute-start | bytes 10760 | tf_op jit(solution)/shard_map/ppermute | solution.py:87
  251.2 3.1 %fusion.15 = bf16[7,128,128]{1,2,0:T(8,128)(2,1)S(1)} fusion(f32[7,128,640]{1,2,0:T(8,128)S(1)} %fusion.95, bf16[2,1,640,128]{3,2,1,0:T(8,128)(2,1)} %copy-done.17, f32[7,128,640]{1,2,0:T(8,128)} %get-tuple-element.47, f32[7,128]{1,0:T(8,128)S(1)} %copy-done.40), kind=kOutput, calls=%fused_computation.21 | convolution fusion | flops 150930944 | bytes 9576448 | tf_op jit(solution)/shard_map/gjsk,gkd->gjsd/dot_general | solution.py:241
  255.8 5.6 %collective-permute-done.20 = f32[2,1,128,128]{3,2,1,0:T(8,128)} collective-permute-done((f32[2,1,128,128]{3,2,1,0:T(8,128)S(1)}, f32[2,1,128,128]{3,2,1,0:T(8,128)}, u32[]{:S(2)}, u32[]{:S(2)}) %collective-permute-start.20) | collective-permute-done | bytes 131104 | tf_op jit(solution)/shard_map/ppermute | solution.py:21
  (198 shorter events, 50.8 us)
Async XLA Ops:
  1.4 21.4 %collective-permute-start = (bf16[2,1,128,128]{3,2,1,0:T(8,128)(2,1)S(1)}, bf16[2,1,128,128]{3,2,1,0:T(8,128)(2,1)S(1)}, u32[]{:S(2)}, u32[]{:S(2)}) collective-permute-start(bf16[2,1,128,128]{3,2,1,0:T(8,128)(2,1)S(1)} %pad_maximum_fusion.3), channel_id=1, source_target_pairs={{0,64},{16,80},{32,96},{48,112},{64,128},{80,144},{96,160},{112,17... | collective-permute-start | bytes 196616 | tf_op jit(solution)/shard_map/ppermute | solution.py:21
  7.1 15.7 %collective-permute-start.1 = (bf16[2,1,128,128]{3,2,1,0:T(8,128)(2,1)S(1)}, bf16[2,1,128,128]{3,2,1,0:T(8,128)(2,1)S(1)}, u32[]{:S(2)}, u32[]{:S(2)}) collective-permute-start(bf16[2,1,128,128]{3,2,1,0:T(8,128)(2,1)S(1)} %pad_maximum_fusion.3), channel_id=1, source_target_pairs={{0,48},{16,64},{32,80},{48,96},{64,112},{80,128},{96,144},{112,160... | collective-permute-start | bytes 196616 | tf_op jit(solution)/shard_map/ppermute | solution.py:21
  14.1 8.8 %collective-permute-start.2 = (bf16[2,1,128,128]{3,2,1,0:T(8,128)(2,1)S(1)}, bf16[2,1,128,128]{3,2,1,0:T(8,128)(2,1)S(1)}, u32[]{:S(2)}, u32[]{:S(2)}) collective-permute-start(bf16[2,1,128,128]{3,2,1,0:T(8,128)(2,1)S(1)} %pad_maximum_fusion.3), channel_id=1, source_target_pairs={{0,32},{16,48},{32,64},{48,80},{64,96},{80,112},{96,128},{112,144}... | collective-permute-start | bytes 196616 | tf_op jit(solution)/shard_map/ppermute | solution.py:21
  17.6 5.2 %collective-permute-start.3 = (bf16[2,1,128,128]{3,2,1,0:T(8,128)(2,1)S(1)}, bf16[2,1,128,128]{3,2,1,0:T(8,128)(2,1)S(1)}, u32[]{:S(2)}, u32[]{:S(2)}) collective-permute-start(bf16[2,1,128,128]{3,2,1,0:T(8,128)(2,1)S(1)} %pad_maximum_fusion.3), channel_id=1, source_target_pairs={{0,16},{16,32},{32,48},{48,64},{64,80},{80,96},{96,112},{112,128},... | collective-permute-start | bytes 196616 | tf_op jit(solution)/shard_map/ppermute | solution.py:21
  27.3 4.3 %collective-permute-start.4 = (f32[128]{0:T(128)S(1)}, f32[128]{0:T(128)S(1)}, u32[]{:S(2)}, u32[]{:S(2)}) collective-permute-start(f32[128]{0:T(128)S(1)} %get-tuple-element.48), channel_id=1, source_target_pairs={{0,1},{1,0},{2,3},{3,2},{4,5},{5,4},{6,7},{7,6},{8,9},{9,8},{10,11... | collective-permute-start | bytes 1544 | tf_op jit(solution)/shard_map/ppermute | solution.py:87
  31.6 5.8 %collective-permute-start.5 = (f32[128]{0:T(128)S(1)}, f32[128]{0:T(128)S(1)}, u32[]{:S(2)}, u32[]{:S(2)}) collective-permute-start(f32[128]{0:T(128)S(1)} %add.175), channel_id=1, source_target_pairs={{0,2},{1,3},{2,0},{3,1},{4,6},{5,7},{6,4},{7,5},{8,10},{9,11},{10,... | collective-permute-start | bytes 1544 | tf_op jit(solution)/shard_map/ppermute | solution.py:87
  38.3 5.4 %collective-permute-start.6 = (f32[7,136,128]{2,1,0:T(8,128)S(1)}, f32[7,136,128]{2,1,0:T(8,128)S(1)}, u32[]{:S(2)}, u32[]{:S(2)}) collective-permute-start(f32[7,136,128]{2,1,0:T(8,128)S(1)} %pad_maximum_fusion.1), channel_id=1, source_target_pairs={{0,16},{32,48},{64,80},{96,112},{128,144},{160,176},{192,208},{224... | collective-permute-start | bytes 1462280 | tf_op jit(solution)/shard_map/ppermute | solution.py:35
  43.9 9.3 %collective-permute-start.7 = (f32[7,136,128]{2,1,0:T(8,128)S(1)}, f32[7,136,128]{2,1,0:T(8,128)S(1)}, u32[]{:S(2)}, u32[]{:S(2)}) collective-permute-start(f32[7,136,128]{2,1,0:T(8,128)S(1)} %multiply_select_fusion.1), channel_id=1, source_target_pairs={{16,48},{48,80},{80,112},{112,144},{144,176},{176,208},{208,240},{... | collective-permute-start | bytes 1462280 | tf_op jit(solution)/shard_map/ppermute | solution.py:35
  54.2 9.6 %collective-permute-start.8 = (bf16[7,136,128]{2,1,0:T(8,128)(2,1)}, bf16[7,136,128]{2,1,0:T(8,128)(2,1)}, u32[]{:S(2)}, u32[]{:S(2)}) collective-permute-start(bf16[7,136,128]{2,1,0:T(8,128)(2,1)} %get-tuple-element.25), channel_id=1, source_target_pairs={{16,80},{48,112},{80,144},{112,176},{144,208},{176,240},{208,272},... | collective-permute-start | bytes 731144 | tf_op jit(solution)/shard_map/ppermute | solution.py:35
  65.7 15.5 %collective-permute-start.9 = (bf16[7,136,128]{2,1,0:T(8,128)(2,1)}, bf16[7,136,128]{2,1,0:T(8,128)(2,1)}, u32[]{:S(2)}, u32[]{:S(2)}) collective-permute-start(bf16[7,136,128]{2,1,0:T(8,128)(2,1)} %get-tuple-element.23), channel_id=1, source_target_pairs={{16,144},{48,176},{80,208},{112,240},{144,272},{176,304},{208,336}... | collective-permute-start | bytes 731144 | tf_op jit(solution)/shard_map/ppermute | solution.py:35
  82.5 15.9 %collective-permute-start.10 = (bf16[7,136,128]{2,1,0:T(8,128)(2,1)S(1)}, bf16[7,136,128]{2,1,0:T(8,128)(2,1)S(1)}, u32[]{:S(2)}, u32[]{:S(2)}) collective-permute-start(bf16[7,136,128]{2,1,0:T(8,128)(2,1)S(1)} %get-tuple-element.36), channel_id=1, source_target_pairs={{16,272},{48,304},{80,336},{112,368},{144,400},{176,432},{208,464}... | collective-permute-start | bytes 731144 | tf_op jit(solution)/shard_map/ppermute | solution.py:35
  99.3 2.9 %collective-permute-start.11 = (f32[7,128,128]{2,1,0:T(8,128)S(1)}, f32[7,128,128]{2,1,0:T(8,128)S(1)}, u32[]{:S(2)}, u32[]{:S(2)}) collective-permute-start(f32[7,128,128]{2,1,0:T(8,128)S(1)} %slice.129), channel_id=1, source_target_pairs={{16,0},{48,32},{80,64},{112,96},{144,128},{176,160},{208,192},{240... | collective-permute-start | bytes 1376264 | tf_op jit(solution)/shard_map/ppermute | solution.py:35
  105.7 3.7 %collective-permute-start.12 = (f32[7,136,128]{2,1,0:T(8,128)S(1)}, f32[7,136,128]{2,1,0:T(8,128)S(1)}, u32[]{:S(2)}, u32[]{:S(2)}) collective-permute-start(f32[7,136,128]{2,1,0:T(8,128)S(1)} %pad_maximum_fusion), channel_id=1, source_target_pairs={{496,480},{464,448},{432,416},{400,384},{368,352},{336,320},{304,2... | collective-permute-start | bytes 1462280 | tf_op jit(solution)/shard_map/ppermute | solution.py:35
  110.2 0.8 collective-permute-start.13
  112.0 1.0 collective-permute-start.14
  114.0 1.1 collective-permute-start.15
  116.0 0.9 collective-permute-start.16
  117.3 61.8 %collective-permute-start.17 = (f32[7,128,128]{2,1,0:T(8,128)S(1)}, f32[7,128,128]{2,1,0:T(8,128)}, u32[]{:S(2)}, u32[]{:S(2)}) collective-permute-start(f32[7,128,128]{2,1,0:T(8,128)S(1)} %slice.140), channel_id=1, source_target_pairs={{480,496},{448,464},{416,432},{384,400},{352,368},{320,336},{288,3... | collective-permute-start | bytes 1376264 | tf_op jit(solution)/shard_map/ppermute | solution.py:35
  119.6 79.9 %copy-start.38 = (f32[128]{0:T(128)S(1)}, f32[128]{0:T(128)}, u32[]{:S(2)}) copy-start(f32[128]{0:T(128)} %copy-done.36) | copy-start | bytes 1540
  181.2 4.4 %collective-permute-start.18 = (f32[128]{0:T(128)S(1)}, f32[128]{0:T(128)S(1)}, u32[]{:S(2)}, u32[]{:S(2)}) collective-permute-start(f32[128]{0:T(128)S(1)} %get-tuple-element.16), channel_id=1, source_target_pairs={{0,1},{1,0},{2,3},{3,2},{4,5},{5,4},{6,7},{7,6},{8,9},{9,8},{10,11... | collective-permute-start | bytes 1544 | tf_op jit(solution)/shard_map/ppermute | solution.py:87
  185.7 9.3 %collective-permute-start.19 = (f32[128]{0:T(128)S(1)}, f32[128]{0:T(128)S(1)}, u32[]{:S(2)}, u32[]{:S(2)}) collective-permute-start(f32[128]{0:T(128)S(1)} %add.204), channel_id=1, source_target_pairs={{0,2},{1,3},{2,0},{3,1},{4,6},{5,7},{6,4},{7,5},{8,10},{9,11},{10,... | collective-permute-start | bytes 1544 | tf_op jit(solution)/shard_map/ppermute | solution.py:87
  191.5 4.3 %collective-permute-start.24 = (f32[896]{0:T(1024)S(1)}, f32[896]{0:T(1024)S(1)}, u32[]{:S(2)}, u32[]{:S(2)}) collective-permute-start(f32[896]{0:T(1024)S(1)} %bitcast.151), channel_id=1, source_target_pairs={{0,16},{16,0},{32,48},{48,32},{64,80},{80,64},{96,112},{112,96},{1... | collective-permute-start | bytes 10760 | tf_op jit(solution)/shard_map/ppermute | solution.py:87
  195.8 4.6 %collective-permute-start.25 = (f32[896]{0:T(1024)S(1)}, f32[896]{0:T(1024)S(1)}, u32[]{:S(2)}, u32[]{:S(2)}) collective-permute-start(f32[896]{0:T(1024)S(1)} %bitcast_add_fusion.1), channel_id=1, source_target_pairs={{0,32},{16,48},{32,0},{48,16},{64,96},{80,112},{96,64},{112,80},{1... | collective-permute-start | bytes 10760 | tf_op jit(solution)/shard_map/ppermute | solution.py:87
  200.4 7.2 %collective-permute-start.26 = (f32[896]{0:T(1024)S(1)}, f32[896]{0:T(1024)S(1)}, u32[]{:S(2)}, u32[]{:S(2)}) collective-permute-start(f32[896]{0:T(1024)S(1)} %add.211), channel_id=1, source_target_pairs={{0,64},{16,80},{32,96},{48,112},{64,0},{80,16},{96,32},{112,48},{1... | collective-permute-start | bytes 10760 | tf_op jit(solution)/shard_map/ppermute | solution.py:87
  207.6 12.3 %collective-permute-start.27 = (f32[896]{0:T(1024)S(1)}, f32[896]{0:T(1024)S(1)}, u32[]{:S(2)}, u32[]{:S(2)}) collective-permute-start(f32[896]{0:T(1024)S(1)} %add.212), channel_id=1, source_target_pairs={{0,128},{16,144},{32,160},{48,176},{64,192},{80,208},{96,224},{112... | collective-permute-start | bytes 10760 | tf_op jit(solution)/shard_map/ppermute | solution.py:87
  219.9 13.1 %collective-permute-start.28 = (f32[896]{0:T(1024)S(1)}, f32[896]{0:T(1024)S(1)}, u32[]{:S(2)}, u32[]{:S(2)}) collective-permute-start(f32[896]{0:T(1024)S(1)} %add.213), channel_id=1, source_target_pairs={{0,256},{16,272},{32,288},{48,304},{64,320},{80,336},{96,352},{112... | collective-permute-start | bytes 10760 | tf_op jit(solution)/shard_map/ppermute | solution.py:87
  233.0 13.8 %collective-permute-start.29 = (f32[896]{0:T(1024)S(1)}, f32[896]{0:T(1024)S(1)}, u32[]{:S(2)}, u32[]{:S(2)}) collective-permute-start(f32[896]{0:T(1024)S(1)} %add.214), channel_id=1, source_target_pairs={{0,4},{4,0},{8,12},{12,8},{1,5},{5,1},{9,13},{13,9},{2,6},{6,2},{1... | collective-permute-start | bytes 10760 | tf_op jit(solution)/shard_map/ppermute | solution.py:87
  236.9 18.8 %collective-permute-start.23 = (f32[2,1,128,128]{3,2,1,0:T(8,128)}, f32[2,1,128,128]{3,2,1,0:T(8,128)S(1)}, u32[]{:S(2)}, u32[]{:S(2)}) collective-permute-start(f32[2,1,128,128]{3,2,1,0:T(8,128)} %get-tuple-element.29), channel_id=1, source_target_pairs={{16,0},{32,16},{48,32},{64,48},{80,64},{96,80},{112,96},{128,112},... | collective-permute-start | bytes 393224 | tf_op jit(solution)/shard_map/ppermute | solution.py:21
  242.9 12.9 %collective-permute-start.22 = (f32[2,1,128,128]{3,2,1,0:T(8,128)}, f32[2,1,128,128]{3,2,1,0:T(8,128)}, u32[]{:S(2)}, u32[]{:S(2)}) collective-permute-start(f32[2,1,128,128]{3,2,1,0:T(8,128)} %get-tuple-element.30), channel_id=1, source_target_pairs={{32,0},{48,16},{64,32},{80,48},{96,64},{112,80},{128,96},{144,112}... | collective-permute-start | bytes 393224 | tf_op jit(solution)/shard_map/ppermute | solution.py:21
  244.2 11.6 %collective-permute-start.21 = (f32[2,1,128,128]{3,2,1,0:T(8,128)}, f32[2,1,128,128]{3,2,1,0:T(8,128)}, u32[]{:S(2)}, u32[]{:S(2)}) collective-permute-start(f32[2,1,128,128]{3,2,1,0:T(8,128)} %get-tuple-element.28), channel_id=1, source_target_pairs={{48,0},{64,16},{80,32},{96,48},{112,64},{128,80},{144,96},{160,112... | collective-permute-start | bytes 393224 | tf_op jit(solution)/shard_map/ppermute | solution.py:21
  245.5 15.9 %collective-permute-start.20 = (f32[2,1,128,128]{3,2,1,0:T(8,128)S(1)}, f32[2,1,128,128]{3,2,1,0:T(8,128)}, u32[]{:S(2)}, u32[]{:S(2)}) collective-permute-start(f32[2,1,128,128]{3,2,1,0:T(8,128)S(1)} %get-tuple-element.27), channel_id=1, source_target_pairs={{64,0},{80,16},{96,32},{112,48},{128,64},{144,80},{160,96},{176,11... | collective-permute-start | bytes 393224 | tf_op jit(solution)/shard_map/ppermute | solution.py:21
  246.8 8.4 %collective-permute-start.30 = (f32[896]{0:T(1024)S(1)}, f32[896]{0:T(1024)S(1)}, u32[]{:S(2)}, u32[]{:S(2)}) collective-permute-start(f32[896]{0:T(1024)S(1)} %add.215), channel_id=1, source_target_pairs={{0,8},{4,12},{8,0},{12,4},{1,9},{5,13},{9,1},{13,5},{2,10},{6,14},... | collective-permute-start | bytes 10760 | tf_op jit(solution)/shard_map/ppermute | solution.py:87
  (40 other events, 794.6 us)

commit v7 on v6

--- a/solution.py
+++ b/solution.py
@@ -222,7 +222,6 @@
         grad_parts.append(part_level)
     unit_out = jnp.concatenate(unit_parts, axis=0)
     level_grad = jnp.concatenate(grad_parts, axis=0)
-    gain_grads = summed(jnp.concatenate(gain_parts, axis=0), ("seq", "dp"))
     layer_output = (
         unit_out.astype(jnp.bfloat16).transpose(1, 0, 2).reshape(1, block_rows, q_heads * HEAD_SIZE)
     )
@@ -248,6 +247,8 @@
         "gjsk,gjsd->gkd", weights, grad_rows, preferred_element_type=jnp.float32
     )
     pair_grads = jnp.stack([key_sum, value_sum])
+    gain_part, pair_grads = lax.optimization_barrier((jnp.concatenate(gain_parts, axis=0), pair_grads))
+    gain_grads = summed(gain_part, ("seq", "dp"))
     total_grads = pair_grads[:, :, key_span:]
     for distance in range(previous, 0, -1):
         offset = (previous - distance) * block_rows

time: 264 us -> 273 us (1.034)
    unnamed x92 -> x96, local copies, waits for them, and re-layouts: 5.59 us -> 6.52 us
  transfers between devices with their start and end apart: 31 -> 31, of which waited for: 15 -> 17; matrix products, arithmetic and copies ran while one was open for 8% -> 7% of each run, Pallas kernels for 0% -> 0%
where the time goes in v7:
time: 273 us; the launch traced here: 272 us
  starting transfers between devices  124 us (45%)
  waiting for transfers between devices  96.3 us (35%)
  matrix products  21.9 us (8%)
  other arithmetic  16 us (6%)
  local copies, waits for them, and re-layouts  11.3 us (4%)
    ppermute x12, waiting for transfers between devices, moved_on(): return lax.ppermute(value, axis, pairs)  76.3 us
    ppermute x11, starting transfers between devices, xor_reduced(): values[c] = lax.ppermute(value, axis, [(i, i ^ c) for i in range(count)])  49.7 us
    ppermute x12, starting transfers between devices, moved_on(): return lax.ppermute(value, axis, pairs)  45.3 us
    ppermute x8, starting transfers between devices, passed_along(): return lax.ppermute(block, axis, route)  28.6 us
    ppermute x11, waiting for transfers between devices, xor_reduced(): values[c] = lax.ppermute(value, axis, [(i, i ^ c) for i in range(count)])  14.7 us
    convert_element_type x6, other arithmetic, entering(): sent = covered.astype(jnp.bfloat16) if distance >= 4 else covered  7.06 us
    unnamed x96, local copies, waits for them, and re-layouts  6.52 us
  transfers between devices with their start and end apart: 31, of which 17 were waited for; matrix products, arithmetic and copies ran while one was open for 7% of the time, Pallas kernels for 0%

profile of v7, /device:TPU:1, one launch (start us, length us, event | category | flops | bytes accessed | tf_op | source)
XLA Modules:
  0.0 271.5 jit_solution(15765462216114782682)
XLA Ops:
  1.4 5.7 %collective-permute-start = (bf16[2,1,128,128]{3,2,1,0:T(8,128)(2,1)S(1)}, bf16[2,1,128,128]{3,2,1,0:T(8,128)(2,1)S(1)}, u32[]{:S(2)}, u32[]{:S(2)}) collective-permute-start(bf16[2,1,128,128]{3,2,1,0:T(8,128)(2,1)S(1)} %pad_maximum_fusion.3), channel_id=1, source_target_pairs={{0,64},{16,80},{32,96},{48,112},{64,128},{80,144},{96,160},{112,17... | collective-permute-start | bytes 196616 | tf_op jit(solution)/shard_map/ppermute | solution.py:21
  7.1 7.0 %collective-permute-start.1 = (bf16[2,1,128,128]{3,2,1,0:T(8,128)(2,1)S(1)}, bf16[2,1,128,128]{3,2,1,0:T(8,128)(2,1)S(1)}, u32[]{:S(2)}, u32[]{:S(2)}) collective-permute-start(bf16[2,1,128,128]{3,2,1,0:T(8,128)(2,1)S(1)} %pad_maximum_fusion.3), channel_id=1, source_target_pairs={{0,48},{16,64},{32,80},{48,96},{64,112},{80,128},{96,144},{112,160... | collective-permute-start | bytes 196616 | tf_op jit(solution)/shard_map/ppermute | solution.py:21
  14.1 3.5 %collective-permute-start.2 = (bf16[2,1,128,128]{3,2,1,0:T(8,128)(2,1)S(1)}, bf16[2,1,128,128]{3,2,1,0:T(8,128)(2,1)S(1)}, u32[]{:S(2)}, u32[]{:S(2)}) collective-permute-start(bf16[2,1,128,128]{3,2,1,0:T(8,128)(2,1)S(1)} %pad_maximum_fusion.3), channel_id=1, source_target_pairs={{0,32},{16,48},{32,64},{48,80},{64,96},{80,112},{96,128},{112,144}... | collective-permute-start | bytes 196616 | tf_op jit(solution)/shard_map/ppermute | solution.py:21
  23.7 2.2 fusion.115
  27.3 3.2 %collective-permute-start.4 = (f32[128]{0:T(128)S(1)}, f32[128]{0:T(128)S(1)}, u32[]{:S(2)}, u32[]{:S(2)}) collective-permute-start(f32[128]{0:T(128)S(1)} %get-tuple-element.52), channel_id=1, source_target_pairs={{0,1},{1,0},{2,3},{3,2},{4,5},{5,4},{6,7},{7,6},{8,9},{9,8},{10,11... | collective-permute-start | bytes 1544 | tf_op jit(solution)/shard_map/ppermute | solution.py:87
  31.6 4.8 %collective-permute-start.5 = (f32[128]{0:T(128)S(1)}, f32[128]{0:T(128)S(1)}, u32[]{:S(2)}, u32[]{:S(2)}) collective-permute-start(f32[128]{0:T(128)S(1)} %add.175), channel_id=1, source_target_pairs={{0,2},{1,3},{2,0},{3,1},{4,6},{5,7},{6,4},{7,5},{8,10},{9,11},{10,... | collective-permute-start | bytes 1544 | tf_op jit(solution)/shard_map/ppermute | solution.py:87
  39.7 4.1 %collective-permute-done.6 = f32[7,136,128]{2,1,0:T(8,128)S(1)} collective-permute-done((f32[7,136,128]{2,1,0:T(8,128)S(1)}, f32[7,136,128]{2,1,0:T(8,128)S(1)}, u32[]{:S(2)}, u32[]{:S(2)}) %collective-permute-start.6) | collective-permute-done | bytes 487456 | tf_op jit(solution)/shard_map/ppermute | solution.py:35
  43.9 3.6 %collective-permute-start.7 = (f32[7,136,128]{2,1,0:T(8,128)S(1)}, f32[7,136,128]{2,1,0:T(8,128)S(1)}, u32[]{:S(2)}, u32[]{:S(2)}) collective-permute-start(f32[7,136,128]{2,1,0:T(8,128)S(1)} %multiply_select_fusion.1), channel_id=1, source_target_pairs={{16,48},{48,80},{80,112},{112,144},{144,176},{176,208},{208,240},{... | collective-permute-start | bytes 1462280 | tf_op jit(solution)/shard_map/ppermute | solution.py:35
  47.7 5.5 %collective-permute-done.7 = f32[7,136,128]{2,1,0:T(8,128)S(1)} collective-permute-done((f32[7,136,128]{2,1,0:T(8,128)S(1)}, f32[7,136,128]{2,1,0:T(8,128)S(1)}, u32[]{:S(2)}, u32[]{:S(2)}) %collective-permute-start.7) | collective-permute-done | bytes 487456 | tf_op jit(solution)/shard_map/ppermute | solution.py:35
  54.2 6.8 %collective-permute-start.8 = (bf16[7,136,128]{2,1,0:T(8,128)(2,1)}, bf16[7,136,128]{2,1,0:T(8,128)(2,1)}, u32[]{:S(2)}, u32[]{:S(2)}) collective-permute-start(bf16[7,136,128]{2,1,0:T(8,128)(2,1)} %get-tuple-element.29), channel_id=1, source_target_pairs={{16,80},{48,112},{80,144},{112,176},{144,208},{176,240},{208,272},... | collective-permute-start | bytes 731144 | tf_op jit(solution)/shard_map/ppermute | solution.py:35
  61.3 2.5 collective-permute-done.8
  63.8 1.9 fusion.111
  65.7 12.8 %collective-permute-start.9 = (bf16[7,136,128]{2,1,0:T(8,128)(2,1)}, bf16[7,136,128]{2,1,0:T(8,128)(2,1)}, u32[]{:S(2)}, u32[]{:S(2)}) collective-permute-start(bf16[7,136,128]{2,1,0:T(8,128)(2,1)} %get-tuple-element.27), channel_id=1, source_target_pairs={{16,144},{48,176},{80,208},{112,240},{144,272},{176,304},{208,336}... | collective-permute-start | bytes 731144 | tf_op jit(solution)/shard_map/ppermute | solution.py:35
  78.8 2.5 collective-permute-done.9
  82.5 12.8 %collective-permute-start.10 = (bf16[7,136,128]{2,1,0:T(8,128)(2,1)S(1)}, bf16[7,136,128]{2,1,0:T(8,128)(2,1)S(1)}, u32[]{:S(2)}, u32[]{:S(2)}) collective-permute-start(bf16[7,136,128]{2,1,0:T(8,128)(2,1)S(1)} %get-tuple-element.40), channel_id=1, source_target_pairs={{16,272},{48,304},{80,336},{112,368},{144,400},{176,432},{208,464}... | collective-permute-start | bytes 731144 | tf_op jit(solution)/shard_map/ppermute | solution.py:35
  105.6 2.3 collective-permute-start.12
  119.4 59.5 %collective-permute-done.17 = f32[7,128,128]{2,1,0:T(8,128)} collective-permute-done((f32[7,128,128]{2,1,0:T(8,128)S(1)}, f32[7,128,128]{2,1,0:T(8,128)}, u32[]{:S(2)}, u32[]{:S(2)}) %collective-permute-start.17) | collective-permute-done | bytes 458784 | tf_op jit(solution)/shard_map/ppermute | solution.py:35
  179.0 2.2 multiply_reduce_fusion.1
  181.1 3.3 %collective-permute-start.18 = (f32[128]{0:T(128)S(1)}, f32[128]{0:T(128)S(1)}, u32[]{:S(2)}, u32[]{:S(2)}) collective-permute-start(f32[128]{0:T(128)S(1)} %get-tuple-element.20), channel_id=1, source_target_pairs={{0,1},{1,0},{2,3},{3,2},{4,5},{5,4},{6,7},{7,6},{8,9},{9,8},{10,11... | collective-permute-start | bytes 1544 | tf_op jit(solution)/shard_map/ppermute | solution.py:87
  185.6 4.8 %collective-permute-start.19 = (f32[128]{0:T(128)S(1)}, f32[128]{0:T(128)S(1)}, u32[]{:S(2)}, u32[]{:S(2)}) collective-permute-start(f32[128]{0:T(128)S(1)} %add.204), channel_id=1, source_target_pairs={{0,2},{1,3},{2,0},{3,1},{4,6},{5,7},{6,4},{7,5},{8,10},{9,11},{10,... | collective-permute-start | bytes 1544 | tf_op jit(solution)/shard_map/ppermute | solution.py:87
  192.1 2.9 %convolution_bitcast_fusion = f32[1,1,640,128]{3,2,1,0:T(8,128)} fusion(bf16[7,128,128]{1,2,0:T(8,128)(2,1)S(1)} %multiply_convert_fusion.1, f32[7,128]{1,0:T(8,128)S(1)} %copy-done.42, pred[128,640]{0,1:T(8,128)(4,1)} %copy-done.19, bf16[7,128,128]{1,2,0:T(8,128)(2,1)S(1)} %bitcast.133, bf16[2,1,640,128]{3,2,1,0:T(8,128)(2,1)} %copy-done.17), kind=kOutput, calls=%fused_computation.25 | convolution fusion | flops 296470016 | bytes 1035776 | tf_op jit(solution)/shard_map/gjsk,gjsd->gkd/dot_general | solution.py:246
  195.0 3.9 %fusion.19 = f32[1,1,640,128]{3,2,1,0:T(8,128)} fusion(bf16[7,128,128]{1,2,0:T(8,128)(2,1)S(1)} %bitcast.134, f32[7,128,640]{1,2,0:T(8,128)S(1)} %fusion.95, f32[7,128,640]{1,2,0:T(8,128)} %get-tuple-element.51, f32[7,128]{1,0:T(8,128)S(1)} %copy-done.42), kind=kOutput, calls=%fused_computation.24 | convolution fusion | flops 150816256 | bytes 5148160 | tf_op jit(solution)/shard_map/gjsk,gjsd->gkd/dot_general | solution.py:243
  200.0 4.3 %collective-permute-start.24 = (f32[896]{0:T(1024)S(1)}, f32[896]{0:T(1024)S(1)}, u32[]{:S(2)}, u32[]{:S(2)}) collective-permute-start(f32[896]{0:T(1024)S(1)} %bitcast.150), channel_id=1, source_target_pairs={{0,16},{16,0},{32,48},{48,32},{64,80},{80,64},{96,112},{112,96},{1... | collective-permute-start | bytes 10760 | tf_op jit(solution)/shard_map/ppermute | solution.py:87
  205.1 3.6 %collective-permute-start.25 = (f32[896]{0:T(1024)S(1)}, f32[896]{0:T(1024)S(1)}, u32[]{:S(2)}, u32[]{:S(2)}) collective-permute-start(f32[896]{0:T(1024)S(1)} %add.210), channel_id=1, source_target_pairs={{0,32},{16,48},{32,0},{48,16},{64,96},{80,112},{96,64},{112,80},{1... | collective-permute-start | bytes 10760 | tf_op jit(solution)/shard_map/ppermute | solution.py:87
  209.8 6.2 %collective-permute-start.26 = (f32[896]{0:T(1024)S(1)}, f32[896]{0:T(1024)S(1)}, u32[]{:S(2)}, u32[]{:S(2)}) collective-permute-start(f32[896]{0:T(1024)S(1)} %add.211), channel_id=1, source_target_pairs={{0,64},{16,80},{32,96},{48,112},{64,0},{80,16},{96,32},{112,48},{1... | collective-permute-start | bytes 10760 | tf_op jit(solution)/shard_map/ppermute | solution.py:87
  217.0 10.1 %collective-permute-start.27 = (f32[896]{0:T(1024)S(1)}, f32[896]{0:T(1024)S(1)}, u32[]{:S(2)}, u32[]{:S(2)}) collective-permute-start(f32[896]{0:T(1024)S(1)} %add.212), channel_id=1, source_target_pairs={{0,128},{16,144},{32,160},{48,176},{64,192},{80,208},{96,224},{112... | collective-permute-start | bytes 10760 | tf_op jit(solution)/shard_map/ppermute | solution.py:87
  233.5 7.7 %collective-permute-done.28 = f32[896]{0:T(1024)S(1)} collective-permute-done((f32[896]{0:T(1024)S(1)}, f32[896]{0:T(1024)S(1)}, u32[]{:S(2)}, u32[]{:S(2)}) %collective-permute-start.28) | collective-permute-done | bytes 3616 | tf_op jit(solution)/shard_map/ppermute | solution.py:87
  241.2 3.1 %collective-permute-start.29 = (f32[896]{0:T(1024)S(1)}, f32[896]{0:T(1024)S(1)}, u32[]{:S(2)}, u32[]{:S(2)}) collective-permute-start(f32[896]{0:T(1024)S(1)} %add.214), channel_id=1, source_target_pairs={{0,4},{4,0},{8,12},{12,8},{1,5},{5,1},{9,13},{13,9},{2,6},{6,2},{1... | collective-permute-start | bytes 10760 | tf_op jit(solution)/shard_map/ppermute | solution.py:87
  245.2 6.6 %collective-permute-start.23 = (f32[2,1,128,128]{3,2,1,0:T(8,128)}, f32[2,1,128,128]{3,2,1,0:T(8,128)S(1)}, u32[]{:S(2)}, u32[]{:S(2)}) collective-permute-start(f32[2,1,128,128]{3,2,1,0:T(8,128)} %get-tuple-element.32), channel_id=1, source_target_pairs={{16,0},{32,16},{48,32},{64,48},{80,64},{96,80},{112,96},{128,112},... | collective-permute-start | bytes 393224 | tf_op jit(solution)/shard_map/ppermute | solution.py:21
  255.7 4.3 %collective-permute-start.30 = (f32[896]{0:T(1024)S(1)}, f32[896]{0:T(1024)S(1)}, u32[]{:S(2)}, u32[]{:S(2)}) collective-permute-start(f32[896]{0:T(1024)S(1)} %add.215), channel_id=1, source_target_pairs={{0,8},{4,12},{8,0},{12,4},{1,9},{5,13},{9,1},{13,5},{2,10},{6,14},... | collective-permute-start | bytes 10760 | tf_op jit(solution)/shard_map/ppermute | solution.py:87
  260.0 3.1 %fusion.15 = bf16[7,128,128]{1,2,0:T(8,128)(2,1)S(1)} fusion(f32[7,128,640]{1,2,0:T(8,128)S(1)} %fusion.95, bf16[2,1,640,128]{3,2,1,0:T(8,128)(2,1)} %copy-done.17, f32[7,128,640]{1,2,0:T(8,128)} %get-tuple-element.51, f32[7,128]{1,0:T(8,128)S(1)} %copy-done.42), kind=kOutput, calls=%fused_computation.21 | convolution fusion | flops 150930944 | bytes 9576448 | tf_op jit(solution)/shard_map/gjsk,gkd->gjsd/dot_general | solution.py:240
  264.6 5.3 %collective-permute-done.20 = f32[2,1,128,128]{3,2,1,0:T(8,128)} collective-permute-done((f32[2,1,128,128]{3,2,1,0:T(8,128)}, f32[2,1,128,128]{3,2,1,0:T(8,128)}, u32[]{:S(2)}, u32[]{:S(2)}) %collective-permute-start.20) | collective-permute-done | bytes 131104 | tf_op jit(solution)/shard_map/ppermute | solution.py:21
  (203 shorter events, 57.1 us)
Async XLA Ops:
  1.4 21.4 %collective-permute-start = (bf16[2,1,128,128]{3,2,1,0:T(8,128)(2,1)S(1)}, bf16[2,1,128,128]{3,2,1,0:T(8,128)(2,1)S(1)}, u32[]{:S(2)}, u32[]{:S(2)}) collective-permute-start(bf16[2,1,128,128]{3,2,1,0:T(8,128)(2,1)S(1)} %pad_maximum_fusion.3), channel_id=1, source_target_pairs={{0,64},{16,80},{32,96},{48,112},{64,128},{80,144},{96,160},{112,17... | collective-permute-start | bytes 196616 | tf_op jit(solution)/shard_map/ppermute | solution.py:21
  7.1 15.7 %collective-permute-start.1 = (bf16[2,1,128,128]{3,2,1,0:T(8,128)(2,1)S(1)}, bf16[2,1,128,128]{3,2,1,0:T(8,128)(2,1)S(1)}, u32[]{:S(2)}, u32[]{:S(2)}) collective-permute-start(bf16[2,1,128,128]{3,2,1,0:T(8,128)(2,1)S(1)} %pad_maximum_fusion.3), channel_id=1, source_target_pairs={{0,48},{16,64},{32,80},{48,96},{64,112},{80,128},{96,144},{112,160... | collective-permute-start | bytes 196616 | tf_op jit(solution)/shard_map/ppermute | solution.py:21
  14.1 8.8 %collective-permute-start.2 = (bf16[2,1,128,128]{3,2,1,0:T(8,128)(2,1)S(1)}, bf16[2,1,128,128]{3,2,1,0:T(8,128)(2,1)S(1)}, u32[]{:S(2)}, u32[]{:S(2)}) collective-permute-start(bf16[2,1,128,128]{3,2,1,0:T(8,128)(2,1)S(1)} %pad_maximum_fusion.3), channel_id=1, source_target_pairs={{0,32},{16,48},{32,64},{48,80},{64,96},{80,112},{96,128},{112,144}... | collective-permute-start | bytes 196616 | tf_op jit(solution)/shard_map/ppermute | solution.py:21
  17.6 5.2 %collective-permute-start.3 = (bf16[2,1,128,128]{3,2,1,0:T(8,128)(2,1)S(1)}, bf16[2,1,128,128]{3,2,1,0:T(8,128)(2,1)S(1)}, u32[]{:S(2)}, u32[]{:S(2)}) collective-permute-start(bf16[2,1,128,128]{3,2,1,0:T(8,128)(2,1)S(1)} %pad_maximum_fusion.3), channel_id=1, source_target_pairs={{0,16},{16,32},{32,48},{48,64},{64,80},{80,96},{96,112},{112,128},... | collective-permute-start | bytes 196616 | tf_op jit(solution)/shard_map/ppermute | solution.py:21
  27.3 4.3 %collective-permute-start.4 = (f32[128]{0:T(128)S(1)}, f32[128]{0:T(128)S(1)}, u32[]{:S(2)}, u32[]{:S(2)}) collective-permute-start(f32[128]{0:T(128)S(1)} %get-tuple-element.52), channel_id=1, source_target_pairs={{0,1},{1,0},{2,3},{3,2},{4,5},{5,4},{6,7},{7,6},{8,9},{9,8},{10,11... | collective-permute-start | bytes 1544 | tf_op jit(solution)/shard_map/ppermute | solution.py:87
  31.6 5.8 %collective-permute-start.5 = (f32[128]{0:T(128)S(1)}, f32[128]{0:T(128)S(1)}, u32[]{:S(2)}, u32[]{:S(2)}) collective-permute-start(f32[128]{0:T(128)S(1)} %add.175), channel_id=1, source_target_pairs={{0,2},{1,3},{2,0},{3,1},{4,6},{5,7},{6,4},{7,5},{8,10},{9,11},{10,... | collective-permute-start | bytes 1544 | tf_op jit(solution)/shard_map/ppermute | solution.py:87
  38.3 5.4 %collective-permute-start.6 = (f32[7,136,128]{2,1,0:T(8,128)S(1)}, f32[7,136,128]{2,1,0:T(8,128)S(1)}, u32[]{:S(2)}, u32[]{:S(2)}) collective-permute-start(f32[7,136,128]{2,1,0:T(8,128)S(1)} %pad_maximum_fusion.1), channel_id=1, source_target_pairs={{0,16},{32,48},{64,80},{96,112},{128,144},{160,176},{192,208},{224... | collective-permute-start | bytes 1462280 | tf_op jit(solution)/shard_map/ppermute | solution.py:35
  43.9 9.3 %collective-permute-start.7 = (f32[7,136,128]{2,1,0:T(8,128)S(1)}, f32[7,136,128]{2,1,0:T(8,128)S(1)}, u32[]{:S(2)}, u32[]{:S(2)}) collective-permute-start(f32[7,136,128]{2,1,0:T(8,128)S(1)} %multiply_select_fusion.1), channel_id=1, source_target_pairs={{16,48},{48,80},{80,112},{112,144},{144,176},{176,208},{208,240},{... | collective-permute-start | bytes 1462280 | tf_op jit(solution)/shard_map/ppermute | solution.py:35
  54.2 9.6 %collective-permute-start.8 = (bf16[7,136,128]{2,1,0:T(8,128)(2,1)}, bf16[7,136,128]{2,1,0:T(8,128)(2,1)}, u32[]{:S(2)}, u32[]{:S(2)}) collective-permute-start(bf16[7,136,128]{2,1,0:T(8,128)(2,1)} %get-tuple-element.29), channel_id=1, source_target_pairs={{16,80},{48,112},{80,144},{112,176},{144,208},{176,240},{208,272},... | collective-permute-start | bytes 731144 | tf_op jit(solution)/shard_map/ppermute | solution.py:35
  65.7 15.5 %collective-permute-start.9 = (bf16[7,136,128]{2,1,0:T(8,128)(2,1)}, bf16[7,136,128]{2,1,0:T(8,128)(2,1)}, u32[]{:S(2)}, u32[]{:S(2)}) collective-permute-start(bf16[7,136,128]{2,1,0:T(8,128)(2,1)} %get-tuple-element.27), channel_id=1, source_target_pairs={{16,144},{48,176},{80,208},{112,240},{144,272},{176,304},{208,336}... | collective-permute-start | bytes 731144 | tf_op jit(solution)/shard_map/ppermute | solution.py:35
  82.5 15.9 %collective-permute-start.10 = (bf16[7,136,128]{2,1,0:T(8,128)(2,1)S(1)}, bf16[7,136,128]{2,1,0:T(8,128)(2,1)S(1)}, u32[]{:S(2)}, u32[]{:S(2)}) collective-permute-start(bf16[7,136,128]{2,1,0:T(8,128)(2,1)S(1)} %get-tuple-element.40), channel_id=1, source_target_pairs={{16,272},{48,304},{80,336},{112,368},{144,400},{176,432},{208,464}... | collective-permute-start | bytes 731144 | tf_op jit(solution)/shard_map/ppermute | solution.py:35
  99.2 2.9 %collective-permute-start.11 = (f32[7,128,128]{2,1,0:T(8,128)S(1)}, f32[7,128,128]{2,1,0:T(8,128)S(1)}, u32[]{:S(2)}, u32[]{:S(2)}) collective-permute-start(f32[7,128,128]{2,1,0:T(8,128)S(1)} %slice.129), channel_id=1, source_target_pairs={{16,0},{48,32},{80,64},{112,96},{144,128},{176,160},{208,192},{240... | collective-permute-start | bytes 1376264 | tf_op jit(solution)/shard_map/ppermute | solution.py:35
  105.6 3.7 %collective-permute-start.12 = (f32[7,136,128]{2,1,0:T(8,128)S(1)}, f32[7,136,128]{2,1,0:T(8,128)S(1)}, u32[]{:S(2)}, u32[]{:S(2)}) collective-permute-start(f32[7,136,128]{2,1,0:T(8,128)S(1)} %pad_maximum_fusion), channel_id=1, source_target_pairs={{496,480},{464,448},{432,416},{400,384},{368,352},{336,320},{304,2... | collective-permute-start | bytes 1462280 | tf_op jit(solution)/shard_map/ppermute | solution.py:35
  110.1 0.8 collective-permute-start.13
  111.9 1.0 collective-permute-start.14
  113.8 1.1 collective-permute-start.15
  115.9 1.0 collective-permute-start.16
  117.2 61.8 %collective-permute-start.17 = (f32[7,128,128]{2,1,0:T(8,128)S(1)}, f32[7,128,128]{2,1,0:T(8,128)}, u32[]{:S(2)}, u32[]{:S(2)}) collective-permute-start(f32[7,128,128]{2,1,0:T(8,128)S(1)} %slice.140), channel_id=1, source_target_pairs={{480,496},{448,464},{416,432},{384,400},{352,368},{320,336},{288,3... | collective-permute-start | bytes 1376264 | tf_op jit(solution)/shard_map/ppermute | solution.py:35
  119.4 72.2 %copy-start.18 = (bf16[2,1,640,128]{3,2,1,0:T(8,128)(2,1)S(1)}, bf16[2,1,640,128]{3,2,1,0:T(8,128)(2,1)}, u32[]{:S(2)}) copy-start(bf16[2,1,640,128]{3,2,1,0:T(8,128)(2,1)} %copy-done.17) | copy-start | bytes 983044
  181.1 4.4 %collective-permute-start.18 = (f32[128]{0:T(128)S(1)}, f32[128]{0:T(128)S(1)}, u32[]{:S(2)}, u32[]{:S(2)}) collective-permute-start(f32[128]{0:T(128)S(1)} %get-tuple-element.20), channel_id=1, source_target_pairs={{0,1},{1,0},{2,3},{3,2},{4,5},{5,4},{6,7},{7,6},{8,9},{9,8},{10,11... | collective-permute-start | bytes 1544 | tf_op jit(solution)/shard_map/ppermute | solution.py:87
  185.6 5.8 %collective-permute-start.19 = (f32[128]{0:T(128)S(1)}, f32[128]{0:T(128)S(1)}, u32[]{:S(2)}, u32[]{:S(2)}) collective-permute-start(f32[128]{0:T(128)S(1)} %add.204), channel_id=1, source_target_pairs={{0,2},{1,3},{2,0},{3,1},{4,6},{5,7},{6,4},{7,5},{8,10},{9,11},{10,... | collective-permute-start | bytes 1544 | tf_op jit(solution)/shard_map/ppermute | solution.py:87
  200.0 5.1 %collective-permute-start.24 = (f32[896]{0:T(1024)S(1)}, f32[896]{0:T(1024)S(1)}, u32[]{:S(2)}, u32[]{:S(2)}) collective-permute-start(f32[896]{0:T(1024)S(1)} %bitcast.150), channel_id=1, source_target_pairs={{0,16},{16,0},{32,48},{48,32},{64,80},{80,64},{96,112},{112,96},{1... | collective-permute-start | bytes 10760 | tf_op jit(solution)/shard_map/ppermute | solution.py:87
  205.1 4.6 %collective-permute-start.25 = (f32[896]{0:T(1024)S(1)}, f32[896]{0:T(1024)S(1)}, u32[]{:S(2)}, u32[]{:S(2)}) collective-permute-start(f32[896]{0:T(1024)S(1)} %add.210), channel_id=1, source_target_pairs={{0,32},{16,48},{32,0},{48,16},{64,96},{80,112},{96,64},{112,80},{1... | collective-permute-start | bytes 10760 | tf_op jit(solution)/shard_map/ppermute | solution.py:87
  209.8 7.2 %collective-permute-start.26 = (f32[896]{0:T(1024)S(1)}, f32[896]{0:T(1024)S(1)}, u32[]{:S(2)}, u32[]{:S(2)}) collective-permute-start(f32[896]{0:T(1024)S(1)} %add.211), channel_id=1, source_target_pairs={{0,64},{16,80},{32,96},{48,112},{64,0},{80,16},{96,32},{112,48},{1... | collective-permute-start | bytes 10760 | tf_op jit(solution)/shard_map/ppermute | solution.py:87
  217.0 11.1 %collective-permute-start.27 = (f32[896]{0:T(1024)S(1)}, f32[896]{0:T(1024)S(1)}, u32[]{:S(2)}, u32[]{:S(2)}) collective-permute-start(f32[896]{0:T(1024)S(1)} %add.212), channel_id=1, source_target_pairs={{0,128},{16,144},{32,160},{48,176},{64,192},{80,208},{96,224},{112... | collective-permute-start | bytes 10760 | tf_op jit(solution)/shard_map/ppermute | solution.py:87
  228.1 13.1 %collective-permute-start.28 = (f32[896]{0:T(1024)S(1)}, f32[896]{0:T(1024)S(1)}, u32[]{:S(2)}, u32[]{:S(2)}) collective-permute-start(f32[896]{0:T(1024)S(1)} %add.213), channel_id=1, source_target_pairs={{0,256},{16,272},{32,288},{48,304},{64,320},{80,336},{96,352},{112... | collective-permute-start | bytes 10760 | tf_op jit(solution)/shard_map/ppermute | solution.py:87
  241.2 14.4 %collective-permute-start.29 = (f32[896]{0:T(1024)S(1)}, f32[896]{0:T(1024)S(1)}, u32[]{:S(2)}, u32[]{:S(2)}) collective-permute-start(f32[896]{0:T(1024)S(1)} %add.214), channel_id=1, source_target_pairs={{0,4},{4,0},{8,12},{12,8},{1,5},{5,1},{9,13},{13,9},{2,6},{6,2},{1... | collective-permute-start | bytes 10760 | tf_op jit(solution)/shard_map/ppermute | solution.py:87
  245.2 19.4 %collective-permute-start.23 = (f32[2,1,128,128]{3,2,1,0:T(8,128)}, f32[2,1,128,128]{3,2,1,0:T(8,128)S(1)}, u32[]{:S(2)}, u32[]{:S(2)}) collective-permute-start(f32[2,1,128,128]{3,2,1,0:T(8,128)} %get-tuple-element.32), channel_id=1, source_target_pairs={{16,0},{32,16},{48,32},{64,48},{80,64},{96,80},{112,96},{128,112},... | collective-permute-start | bytes 393224 | tf_op jit(solution)/shard_map/ppermute | solution.py:21
  251.7 12.9 %collective-permute-start.22 = (f32[2,1,128,128]{3,2,1,0:T(8,128)}, f32[2,1,128,128]{3,2,1,0:T(8,128)S(1)}, u32[]{:S(2)}, u32[]{:S(2)}) collective-permute-start(f32[2,1,128,128]{3,2,1,0:T(8,128)} %get-tuple-element.33), channel_id=1, source_target_pairs={{32,0},{48,16},{64,32},{80,48},{96,64},{112,80},{128,96},{144,112}... | collective-permute-start | bytes 393224 | tf_op jit(solution)/shard_map/ppermute | solution.py:21
  253.0 11.6 %collective-permute-start.21 = (f32[2,1,128,128]{3,2,1,0:T(8,128)}, f32[2,1,128,128]{3,2,1,0:T(8,128)}, u32[]{:S(2)}, u32[]{:S(2)}) collective-permute-start(f32[2,1,128,128]{3,2,1,0:T(8,128)} %get-tuple-element.34), channel_id=1, source_target_pairs={{48,0},{64,16},{80,32},{96,48},{112,64},{128,80},{144,96},{160,112... | collective-permute-start | bytes 393224 | tf_op jit(solution)/shard_map/ppermute | solution.py:21
  254.3 15.6 %collective-permute-start.20 = (f32[2,1,128,128]{3,2,1,0:T(8,128)}, f32[2,1,128,128]{3,2,1,0:T(8,128)}, u32[]{:S(2)}, u32[]{:S(2)}) collective-permute-start(f32[2,1,128,128]{3,2,1,0:T(8,128)} %get-tuple-element.31), channel_id=1, source_target_pairs={{64,0},{80,16},{96,32},{112,48},{128,64},{144,80},{160,96},{176,11... | collective-permute-start | bytes 393224 | tf_op jit(solution)/shard_map/ppermute | solution.py:21
  255.7 8.3 %collective-permute-start.30 = (f32[896]{0:T(1024)S(1)}, f32[896]{0:T(1024)S(1)}, u32[]{:S(2)}, u32[]{:S(2)}) collective-permute-start(f32[896]{0:T(1024)S(1)} %add.215), channel_id=1, source_target_pairs={{0,8},{4,12},{8,0},{12,4},{1,9},{5,13},{9,1},{13,5},{2,10},{6,14},... | collective-permute-start | bytes 10760 | tf_op jit(solution)/shard_map/ppermute | solution.py:87
  (42 other events, 766.2 us)

commit v8 on v6

--- a/solution.py
+++ b/solution.py
@@ -61,7 +61,7 @@
     before = identity
     distance = 2
     while distance < count:
-        sent = covered.astype(jnp.bfloat16) if distance >= 4 else covered
+        sent = covered.astype(jnp.bfloat16)
         moved = moved_on(
             sent,
             axis,
@@ -158,7 +158,7 @@
     )
 
     out_float = heads_out.astype(jnp.float32)
-    square_sum = summed(jnp.sum(out_float * out_float, axis=(0, 2)), ("tensor",))
+    square_sum = lax.psum(jnp.sum(out_float * out_float, axis=(0, 2)), "tensor")
     inverse = 1.0 / jnp.sqrt(square_sum / D + epsilon)
     normed = out_float * inverse[None, :, None]
     gain_rows = norm_gain.reshape(q_heads, HEAD_SIZE)[:, None, :]
@@ -227,7 +227,7 @@
         unit_out.astype(jnp.bfloat16).transpose(1, 0, 2).reshape(1, block_rows, q_heads * HEAD_SIZE)
     )
     normed_grad = level_grad * gain_rows
-    slope_sum = summed(jnp.sum(normed_grad * normed, axis=(0, 2)), ("tensor",))
+    slope_sum = lax.psum(jnp.sum(normed_grad * normed, axis=(0, 2)), "tensor")
     output_gradient = (
         inverse[None, :, None] * (normed_grad - normed * (slope_sum / D)[None, :, None])
     ).astype(jnp.bfloat16)

time: 264 us -> 252 us (0.955)
  waiting for transfers between devices: 94.2 us -> 77 us
  blocking collectives: 0 us -> 14.9 us
  starting transfers between devices: 122 us -> 112 us
    ppermute x12, waiting for transfers between devices: 76.2 us -> 58.9 us  [moved_on(): return lax.ppermute(value, axis, pairs)]
    psum x0 -> x2, blocking collectives: none -> 14.9 us  [the longest x1 8.73 us: local(): square_sum = lax.psum(jnp.sum(out_float * out_float, axis=(0, 2)), 'tensor')]
    ppermute x11 -> x7, starting transfers between devices: 49 us -> 39 us  [xor_reduced(): values[c] = lax.ppermute(value, axis, [(i, i ^ c) for i in range(count)])]
    convert_element_type x6 -> x8, other arithmetic: 7.12 us -> 5.99 us  [entering(): sent = covered.astype(jnp.bfloat16)]
    unnamed x92 -> x64, local copies, waits for them, and re-layouts: 5.59 us -> 5.92 us
    ppermute x11 -> x7, waiting for transfers between devices: 12.4 us -> 12.5 us  [xor_reduced(): values[c] = lax.ppermute(value, axis, [(i, i ^ c) for i in range(count)])]
  transfers between devices with their start and end apart: 31 -> 27, of which waited for: 15 -> 13; matrix products, arithmetic and copies ran while one was open for 8% -> 10% of each run, Pallas kernels for 0% -> 0%
where the time goes in v8:
time: 252 us; the launch traced here: 251 us
  starting transfers between devices  112 us (44%)
  waiting for transfers between devices  77 us (31%)
  matrix products  20.5 us (8%)
  blocking collectives  14.9 us (6%)
  other arithmetic  14.5 us (6%)
  local copies, waits for them, and re-layouts  9.88 us (4%)
    ppermute x12, waiting for transfers between devices, moved_on(): return lax.ppermute(value, axis, pairs)  58.9 us
    ppermute x12, starting transfers between devices, moved_on(): return lax.ppermute(value, axis, pairs)  45.1 us
    ppermute x7, starting transfers between devices, xor_reduced(): values[c] = lax.ppermute(value, axis, [(i, i ^ c) for i in range(count)])  39 us
    ppermute x8, starting transfers between devices, passed_along(): return lax.ppermute(block, axis, route)  28 us
    ppermute x7, waiting for transfers between devices, xor_reduced(): values[c] = lax.ppermute(value, axis, [(i, i ^ c) for i in range(count)])  12.5 us
    psum x1, blocking collectives, local(): square_sum = lax.psum(jnp.sum(out_float * out_float, axis=(0, 2)), 'tensor')  8.73 us
    psum x1, blocking collectives, local(): slope_sum = lax.psum(jnp.sum(normed_grad * normed, axis=(0, 2)), 'tensor')  6.14 us
    convert_element_type x8, other arithmetic, entering(): sent = covered.astype(jnp.bfloat16)  5.99 us
  transfers between devices with their start and end apart: 27, of which 13 were waited for; matrix products, arithmetic and copies ran while one was open for 10% of the time, Pallas kernels for 0%

profile of v8, /device:TPU:1, one launch (start us, length us, event | category | flops | bytes accessed | tf_op | source)
XLA Modules:
  0.0 251.0 jit_solution(1536295636843474295)
XLA Ops:
  1.4 5.7 %collective-permute-start = (bf16[2,1,128,128]{3,2,1,0:T(8,128)(2,1)S(1)}, bf16[2,1,128,128]{3,2,1,0:T(8,128)(2,1)S(1)}, u32[]{:S(2)}, u32[]{:S(2)}) collective-permute-start(bf16[2,1,128,128]{3,2,1,0:T(8,128)(2,1)S(1)} %pad_maximum_fusion.3), channel_id=1, source_target_pairs={{0,64},{16,80},{32,96},{48,112},{64,128},{80,144},{96,160},{112,17... | collective-permute-start | bytes 196616 | tf_op jit(solution)/shard_map/ppermute | solution.py:21
  7.1 7.0 %collective-permute-start.1 = (bf16[2,1,128,128]{3,2,1,0:T(8,128)(2,1)S(1)}, bf16[2,1,128,128]{3,2,1,0:T(8,128)(2,1)S(1)}, u32[]{:S(2)}, u32[]{:S(2)}) collective-permute-start(bf16[2,1,128,128]{3,2,1,0:T(8,128)(2,1)S(1)} %pad_maximum_fusion.3), channel_id=1, source_target_pairs={{0,48},{16,64},{32,80},{48,96},{64,112},{80,128},{96,144},{112,160... | collective-permute-start | bytes 196616 | tf_op jit(solution)/shard_map/ppermute | solution.py:21
  14.1 3.5 %collective-permute-start.2 = (bf16[2,1,128,128]{3,2,1,0:T(8,128)(2,1)S(1)}, bf16[2,1,128,128]{3,2,1,0:T(8,128)(2,1)S(1)}, u32[]{:S(2)}, u32[]{:S(2)}) collective-permute-start(bf16[2,1,128,128]{3,2,1,0:T(8,128)(2,1)S(1)} %pad_maximum_fusion.3), channel_id=1, source_target_pairs={{0,32},{16,48},{32,64},{48,80},{64,96},{80,112},{96,128},{112,144}... | collective-permute-start | bytes 196616 | tf_op jit(solution)/shard_map/ppermute | solution.py:21
  17.6 1.9 collective-permute-start.3
  26.3 2.2 fusion.133
  29.8 8.7 %psum.14 = f32[128]{0:T(128)S(1)} all-reduce(f32[128]{0:T(128)S(1)} %get-tuple-element.52), channel_id=1, replica_groups=mesh['seq'=32,'dp'=4,'tensor'=4] {'tensor'}, use_global_device_ids=true, to_apply=%region_4.5 | all-reduce | flops 128 | bytes 1024 | tf_op jit(solution)/shard_map/psum | solution.py:161
  40.8 3.8 %collective-permute-done.4 = f32[7,136,128]{2,1,0:T(8,128)S(1)} collective-permute-done((f32[7,136,128]{2,1,0:T(8,128)S(1)}, f32[7,136,128]{2,1,0:T(8,128)S(1)}, u32[]{:S(2)}, u32[]{:S(2)}) %collective-permute-start.4) | collective-permute-done | bytes 487456 | tf_op jit(solution)/shard_map/ppermute | solution.py:35
  44.8 3.6 %collective-permute-start.5 = (bf16[7,136,128]{2,1,0:T(8,128)(2,1)S(1)}, bf16[7,136,128]{2,1,0:T(8,128)(2,1)S(1)}, u32[]{:S(2)}, u32[]{:S(2)}) collective-permute-start(bf16[7,136,128]{2,1,0:T(8,128)(2,1)S(1)} %get-tuple-element.29), channel_id=1, source_target_pairs={{16,48},{48,80},{80,112},{112,144},{144,176},{176,208},{208,240},{... | collective-permute-start | bytes 731144 | tf_op jit(solution)/shard_map/ppermute | solution.py:35
  48.5 2.9 %collective-permute-done.5 = bf16[7,136,128]{2,1,0:T(8,128)(2,1)S(1)} collective-permute-done((bf16[7,136,128]{2,1,0:T(8,128)(2,1)S(1)}, bf16[7,136,128]{2,1,0:T(8,128)(2,1)S(1)}, u32[]{:S(2)}, u32[]{:S(2)}) %collective-permute-start.5) | collective-permute-done | bytes 243744 | tf_op jit(solution)/shard_map/ppermute | solution.py:35
  51.8 6.8 %collective-permute-start.6 = (bf16[7,136,128]{2,1,0:T(8,128)(2,1)S(1)}, bf16[7,136,128]{2,1,0:T(8,128)(2,1)}, u32[]{:S(2)}, u32[]{:S(2)}) collective-permute-start(bf16[7,136,128]{2,1,0:T(8,128)(2,1)S(1)} %get-tuple-element.27), channel_id=1, source_target_pairs={{16,80},{48,112},{80,144},{112,176},{144,208},{176,240},{208,272},... | collective-permute-start | bytes 731144 | tf_op jit(solution)/shard_map/ppermute | solution.py:35
  58.9 2.1 collective-permute-done.6
  62.6 11.9 %collective-permute-start.7 = (bf16[7,136,128]{2,1,0:T(8,128)(2,1)S(1)}, bf16[7,136,128]{2,1,0:T(8,128)(2,1)S(1)}, u32[]{:S(2)}, u32[]{:S(2)}) collective-permute-start(bf16[7,136,128]{2,1,0:T(8,128)(2,1)S(1)} %get-tuple-element.25), channel_id=1, source_target_pairs={{16,144},{48,176},{80,208},{112,240},{144,272},{176,304},{208,336}... | collective-permute-start | bytes 731144 | tf_op jit(solution)/shard_map/ppermute | solution.py:35
  74.7 2.8 %collective-permute-done.7 = bf16[7,136,128]{2,1,0:T(8,128)(2,1)S(1)} collective-permute-done((bf16[7,136,128]{2,1,0:T(8,128)(2,1)S(1)}, bf16[7,136,128]{2,1,0:T(8,128)(2,1)S(1)}, u32[]{:S(2)}, u32[]{:S(2)}) %collective-permute-start.7) | collective-permute-done | bytes 243744 | tf_op jit(solution)/shard_map/ppermute | solution.py:35
  77.8 12.6 %collective-permute-start.8 = (bf16[7,136,128]{2,1,0:T(8,128)(2,1)S(1)}, bf16[7,136,128]{2,1,0:T(8,128)(2,1)S(1)}, u32[]{:S(2)}, u32[]{:S(2)}) collective-permute-start(bf16[7,136,128]{2,1,0:T(8,128)(2,1)S(1)} %get-tuple-element.39), channel_id=1, source_target_pairs={{16,272},{48,304},{80,336},{112,368},{144,400},{176,432},{208,464}... | collective-permute-start | bytes 731144 | tf_op jit(solution)/shard_map/ppermute | solution.py:35
  100.8 2.3 collective-permute-start.10
  107.5 2.2 fusion.123
  117.4 44.9 %collective-permute-done.15 = f32[7,128,128]{2,1,0:T(8,128)} collective-permute-done((f32[7,128,128]{2,1,0:T(8,128)S(1)}, f32[7,128,128]{2,1,0:T(8,128)}, u32[]{:S(2)}, u32[]{:S(2)}) %collective-permute-start.15) | collective-permute-done | bytes 458784 | tf_op jit(solution)/shard_map/ppermute | solution.py:35
  162.4 2.3 multiply_reduce_fusion.1
  164.7 6.1 %psum.15 = f32[128]{0:T(128)S(1)} all-reduce(f32[128]{0:T(128)S(1)} %get-tuple-element.16), channel_id=1, replica_groups=mesh['seq'=32,'dp'=4,'tensor'=4] {'tensor'}, use_global_device_ids=true, to_apply=%region_8.9 | all-reduce | flops 128 | bytes 1024 | tf_op jit(solution)/shard_map/psum | solution.py:230
  170.8 5.6 %collective-permute-start.20 = (f32[896]{0:T(1024)S(1)}, f32[896]{0:T(1024)S(1)}, u32[]{:S(2)}, u32[]{:S(2)}) collective-permute-start(f32[896]{0:T(1024)S(1)} %bitcast.151), channel_id=1, source_target_pairs={{0,16},{16,0},{32,48},{48,32},{64,80},{80,64},{96,112},{112,96},{1... | collective-permute-start | bytes 10760 | tf_op jit(solution)/shard_map/ppermute | solution.py:87
  177.2 14.7 %collective-permute-start.21 = (f32[896]{0:T(1024)S(1)}, f32[896]{0:T(1024)S(1)}, u32[]{:S(2)}, u32[]{:S(2)}) collective-permute-start(f32[896]{0:T(1024)S(1)} %bitcast_add_fusion.1), channel_id=1, source_target_pairs={{0,32},{16,48},{32,0},{48,16},{64,96},{80,112},{96,64},{112,80},{1... | collective-permute-start | bytes 10760 | tf_op jit(solution)/shard_map/ppermute | solution.py:87
  195.3 2.9 %collective-permute-done.22 = f32[896]{0:T(1024)S(1)} collective-permute-done((f32[896]{0:T(1024)S(1)}, f32[896]{0:T(1024)S(1)}, u32[]{:S(2)}, u32[]{:S(2)}) %collective-permute-start.22) | collective-permute-done | bytes 3616 | tf_op jit(solution)/shard_map/ppermute | solution.py:87
  198.1 7.4 %collective-permute-start.23 = (f32[896]{0:T(1024)S(1)}, f32[896]{0:T(1024)S(1)}, u32[]{:S(2)}, u32[]{:S(2)}) collective-permute-start(f32[896]{0:T(1024)S(1)} %add.200), channel_id=1, source_target_pairs={{0,128},{16,144},{32,160},{48,176},{64,192},{80,208},{96,224},{112... | collective-permute-start | bytes 10760 | tf_op jit(solution)/shard_map/ppermute | solution.py:87
  205.6 2.1 convolution_bitcast_fusion
  209.6 3.1 %fusion.19 = f32[1,1,640,128]{3,2,1,0:T(8,128)S(1)} fusion(bf16[7,128,128]{1,2,0:T(8,128)(2,1)S(1)} %bitcast.135, f32[7,128,640]{1,2,0:T(8,128)S(1)} %fusion.101, f32[7,128,640]{1,2,0:T(8,128)} %get-tuple-element.51, f32[7,128]{1,0:T(8,128)S(1)} %copy-done.26), kind=kOutput, calls=%fused_computation.24 | convolution fusion | flops 150816256 | bytes 5148160 | tf_op jit(solution)/shard_map/gjsk,gjsd->gkd/dot_general | solution.py:244
  212.8 8.0 %collective-permute-done.24 = f32[896]{0:T(1024)S(1)} collective-permute-done((f32[896]{0:T(1024)S(1)}, f32[896]{0:T(1024)S(1)}, u32[]{:S(2)}, u32[]{:S(2)}) %collective-permute-start.24) | collective-permute-done | bytes 3616 | tf_op jit(solution)/shard_map/ppermute | solution.py:87
  220.8 3.1 %collective-permute-start.25 = (f32[896]{0:T(1024)S(1)}, f32[896]{0:T(1024)S(1)}, u32[]{:S(2)}, u32[]{:S(2)}) collective-permute-start(f32[896]{0:T(1024)S(1)} %add.202), channel_id=1, source_target_pairs={{0,4},{4,0},{8,12},{12,8},{1,5},{5,1},{9,13},{13,9},{2,6},{6,2},{1... | collective-permute-start | bytes 10760 | tf_op jit(solution)/shard_map/ppermute | solution.py:87
  224.7 6.0 %collective-permute-start.19 = (f32[2,1,128,128]{3,2,1,0:T(8,128)}, f32[2,1,128,128]{3,2,1,0:T(8,128)}, u32[]{:S(2)}, u32[]{:S(2)}) collective-permute-start(f32[2,1,128,128]{3,2,1,0:T(8,128)} %get-tuple-element.33), channel_id=1, source_target_pairs={{16,0},{32,16},{48,32},{64,48},{80,64},{96,80},{112,96},{128,112},... | collective-permute-start | bytes 393224 | tf_op jit(solution)/shard_map/ppermute | solution.py:21
  234.6 4.4 %collective-permute-start.26 = (f32[896]{0:T(1024)S(1)}, f32[896]{0:T(1024)S(1)}, u32[]{:S(2)}, u32[]{:S(2)}) collective-permute-start(f32[896]{0:T(1024)S(1)} %add.203), channel_id=1, source_target_pairs={{0,8},{4,12},{8,0},{12,4},{1,9},{5,13},{9,1},{13,5},{2,10},{6,14},... | collective-permute-start | bytes 10760 | tf_op jit(solution)/shard_map/ppermute | solution.py:87
  239.0 3.1 %fusion.15 = bf16[7,128,128]{1,2,0:T(8,128)(2,1)S(1)} fusion(f32[7,128,640]{1,2,0:T(8,128)S(1)} %fusion.101, bf16[2,1,640,128]{3,2,1,0:T(8,128)(2,1)S(1)} %copy-done.13, f32[7,128,640]{1,2,0:T(8,128)} %get-tuple-element.51, f32[7,128]{1,0:T(8,128)S(1)} %copy-done.26), kind=kOutput, calls=%fused_computation.21 | convolution fusion | flops 150930944 | bytes 9576448 | tf_op jit(solution)/shard_map/gjsk,gkd->gjsd/dot_general | solution.py:241
  243.6 1.9 collective-permute-done.17
  245.5 3.7 %collective-permute-done.16 = f32[2,1,128,128]{3,2,1,0:T(8,128)} collective-permute-done((f32[2,1,128,128]{3,2,1,0:T(8,128)}, f32[2,1,128,128]{3,2,1,0:T(8,128)}, u32[]{:S(2)}, u32[]{:S(2)}) %collective-permute-start.16) | collective-permute-done | bytes 131104 | tf_op jit(solution)/shard_map/ppermute | solution.py:21
  (162 shorter events, 49.3 us)
Async XLA Ops:
  1.4 23.9 %collective-permute-start = (bf16[2,1,128,128]{3,2,1,0:T(8,128)(2,1)S(1)}, bf16[2,1,128,128]{3,2,1,0:T(8,128)(2,1)S(1)}, u32[]{:S(2)}, u32[]{:S(2)}) collective-permute-start(bf16[2,1,128,128]{3,2,1,0:T(8,128)(2,1)S(1)} %pad_maximum_fusion.3), channel_id=1, source_target_pairs={{0,64},{16,80},{32,96},{48,112},{64,128},{80,144},{96,160},{112,17... | collective-permute-start | bytes 196616 | tf_op jit(solution)/shard_map/ppermute | solution.py:21
  7.1 18.2 %collective-permute-start.1 = (bf16[2,1,128,128]{3,2,1,0:T(8,128)(2,1)S(1)}, bf16[2,1,128,128]{3,2,1,0:T(8,128)(2,1)S(1)}, u32[]{:S(2)}, u32[]{:S(2)}) collective-permute-start(bf16[2,1,128,128]{3,2,1,0:T(8,128)(2,1)S(1)} %pad_maximum_fusion.3), channel_id=1, source_target_pairs={{0,48},{16,64},{32,80},{48,96},{64,112},{80,128},{96,144},{112,160... | collective-permute-start | bytes 196616 | tf_op jit(solution)/shard_map/ppermute | solution.py:21
  14.1 11.3 %collective-permute-start.2 = (bf16[2,1,128,128]{3,2,1,0:T(8,128)(2,1)S(1)}, bf16[2,1,128,128]{3,2,1,0:T(8,128)(2,1)S(1)}, u32[]{:S(2)}, u32[]{:S(2)}) collective-permute-start(bf16[2,1,128,128]{3,2,1,0:T(8,128)(2,1)S(1)} %pad_maximum_fusion.3), channel_id=1, source_target_pairs={{0,32},{16,48},{32,64},{48,80},{64,96},{80,112},{96,128},{112,144}... | collective-permute-start | bytes 196616 | tf_op jit(solution)/shard_map/ppermute | solution.py:21
  17.6 7.8 %collective-permute-start.3 = (bf16[2,1,128,128]{3,2,1,0:T(8,128)(2,1)S(1)}, bf16[2,1,128,128]{3,2,1,0:T(8,128)(2,1)S(1)}, u32[]{:S(2)}, u32[]{:S(2)}) collective-permute-start(bf16[2,1,128,128]{3,2,1,0:T(8,128)(2,1)S(1)} %pad_maximum_fusion.3), channel_id=1, source_target_pairs={{0,16},{16,32},{32,48},{48,64},{64,80},{80,96},{96,112},{112,128},... | collective-permute-start | bytes 196616 | tf_op jit(solution)/shard_map/ppermute | solution.py:21
  23.0 74.4 %copy-start.19 = (f32[7,128]{1,0:T(8,128)}, f32[7,128]{1,0:T(8,128)S(1)}, u32[]{:S(2)}) copy-start(f32[7,128]{1,0:T(8,128)S(1)} %convert_bitcast_fusion) | copy-start | bytes 10756
  38.5 58.9 %copy-start.23 = (f32[128]{0:T(128)}, f32[128]{0:T(128)S(1)}, u32[]{:S(2)}) copy-start(f32[128]{0:T(128)S(1)} %add_rsqrt_fusion.1) | copy-start | bytes 1540
  39.5 5.1 %collective-permute-start.4 = (f32[7,136,128]{2,1,0:T(8,128)S(1)}, f32[7,136,128]{2,1,0:T(8,128)S(1)}, u32[]{:S(2)}, u32[]{:S(2)}) collective-permute-start(f32[7,136,128]{2,1,0:T(8,128)S(1)} %pad_maximum_fusion.1), channel_id=1, source_target_pairs={{0,16},{32,48},{64,80},{96,112},{128,144},{160,176},{192,208},{224... | collective-permute-start | bytes 1462280 | tf_op jit(solution)/shard_map/ppermute | solution.py:35
  44.8 6.7 %collective-permute-start.5 = (bf16[7,136,128]{2,1,0:T(8,128)(2,1)S(1)}, bf16[7,136,128]{2,1,0:T(8,128)(2,1)S(1)}, u32[]{:S(2)}, u32[]{:S(2)}) collective-permute-start(bf16[7,136,128]{2,1,0:T(8,128)(2,1)S(1)} %get-tuple-element.29), channel_id=1, source_target_pairs={{16,48},{48,80},{80,112},{112,144},{144,176},{176,208},{208,240},{... | collective-permute-start | bytes 731144 | tf_op jit(solution)/shard_map/ppermute | solution.py:35
  51.8 9.2 %collective-permute-start.6 = (bf16[7,136,128]{2,1,0:T(8,128)(2,1)S(1)}, bf16[7,136,128]{2,1,0:T(8,128)(2,1)}, u32[]{:S(2)}, u32[]{:S(2)}) collective-permute-start(bf16[7,136,128]{2,1,0:T(8,128)(2,1)S(1)} %get-tuple-element.27), channel_id=1, source_target_pairs={{16,80},{48,112},{80,144},{112,176},{144,208},{176,240},{208,272},... | collective-permute-start | bytes 731144 | tf_op jit(solution)/shard_map/ppermute | solution.py:35
  62.6 15.0 %collective-permute-start.7 = (bf16[7,136,128]{2,1,0:T(8,128)(2,1)S(1)}, bf16[7,136,128]{2,1,0:T(8,128)(2,1)S(1)}, u32[]{:S(2)}, u32[]{:S(2)}) collective-permute-start(bf16[7,136,128]{2,1,0:T(8,128)(2,1)S(1)} %get-tuple-element.25), channel_id=1, source_target_pairs={{16,144},{48,176},{80,208},{112,240},{144,272},{176,304},{208,336}... | collective-permute-start | bytes 731144 | tf_op jit(solution)/shard_map/ppermute | solution.py:35
  77.8 15.7 %collective-permute-start.8 = (bf16[7,136,128]{2,1,0:T(8,128)(2,1)S(1)}, bf16[7,136,128]{2,1,0:T(8,128)(2,1)S(1)}, u32[]{:S(2)}, u32[]{:S(2)}) collective-permute-start(bf16[7,136,128]{2,1,0:T(8,128)(2,1)S(1)} %get-tuple-element.39), channel_id=1, source_target_pairs={{16,272},{48,304},{80,336},{112,368},{144,400},{176,432},{208,464}... | collective-permute-start | bytes 731144 | tf_op jit(solution)/shard_map/ppermute | solution.py:35
  93.8 2.9 %collective-permute-start.9 = (f32[7,128,128]{2,1,0:T(8,128)S(1)}, f32[7,128,128]{2,1,0:T(8,128)S(1)}, u32[]{:S(2)}, u32[]{:S(2)}) collective-permute-start(f32[7,128,128]{2,1,0:T(8,128)S(1)} %slice.129), channel_id=1, source_target_pairs={{16,0},{48,32},{80,64},{112,96},{144,128},{176,160},{208,192},{240... | collective-permute-start | bytes 1376264 | tf_op jit(solution)/shard_map/ppermute | solution.py:35
  100.8 3.7 %collective-permute-start.10 = (f32[7,136,128]{2,1,0:T(8,128)S(1)}, f32[7,136,128]{2,1,0:T(8,128)S(1)}, u32[]{:S(2)}, u32[]{:S(2)}) collective-permute-start(f32[7,136,128]{2,1,0:T(8,128)S(1)} %pad_maximum_fusion), channel_id=1, source_target_pairs={{496,480},{464,448},{432,416},{400,384},{368,352},{336,320},{304,2... | collective-permute-start | bytes 1462280 | tf_op jit(solution)/shard_map/ppermute | solution.py:35
  104.7 0.8 collective-permute-start.11
  105.9 1.6 collective-permute-start.12
  109.7 1.1 collective-permute-start.13
  111.8 1.0 collective-permute-start.14
  113.0 49.4 %copy-start.18 = (f32[896]{0:T(1024)S(1)}, f32[896]{0:T(1024)}, u32[]{:S(2)}) copy-start(f32[896]{0:T(1024)} %param.14) | copy-start | bytes 10756
  113.0 49.4 %copy-start.20 = (f32[7,128]{1,0:T(8,128)S(1)}, f32[7,128]{1,0:T(8,128)}, u32[]{:S(2)}) copy-start(f32[7,128]{1,0:T(8,128)} %copy-done.19) | copy-start | bytes 10756
  113.1 49.3 %collective-permute-start.15 = (f32[7,128,128]{2,1,0:T(8,128)S(1)}, f32[7,128,128]{2,1,0:T(8,128)}, u32[]{:S(2)}, u32[]{:S(2)}) collective-permute-start(f32[7,128,128]{2,1,0:T(8,128)S(1)} %slice.140), channel_id=1, source_target_pairs={{480,496},{448,464},{416,432},{384,400},{352,368},{320,336},{288,3... | collective-permute-start | bytes 1376264 | tf_op jit(solution)/shard_map/ppermute | solution.py:35
  117.2 74.7 %copy-start.8 = (f32[7,128,128]{1,2,0:T(8,128)S(1)}, f32[7,128,128]{1,2,0:T(8,128)}, u32[]{:S(2)}) copy-start(f32[7,128,128]{1,2,0:T(8,128)} %copy-done.6) | copy-start | bytes 1376260
  170.8 6.4 %collective-permute-start.20 = (f32[896]{0:T(1024)S(1)}, f32[896]{0:T(1024)S(1)}, u32[]{:S(2)}, u32[]{:S(2)}) collective-permute-start(f32[896]{0:T(1024)S(1)} %bitcast.151), channel_id=1, source_target_pairs={{0,16},{16,0},{32,48},{48,32},{64,80},{80,64},{96,112},{112,96},{1... | collective-permute-start | bytes 10760 | tf_op jit(solution)/shard_map/ppermute | solution.py:87
  177.2 15.7 %collective-permute-start.21 = (f32[896]{0:T(1024)S(1)}, f32[896]{0:T(1024)S(1)}, u32[]{:S(2)}, u32[]{:S(2)}) collective-permute-start(f32[896]{0:T(1024)S(1)} %bitcast_add_fusion.1), channel_id=1, source_target_pairs={{0,32},{16,48},{32,0},{48,16},{64,96},{80,112},{96,64},{112,80},{1... | collective-permute-start | bytes 10760 | tf_op jit(solution)/shard_map/ppermute | solution.py:87
  192.9 5.2 %collective-permute-start.22 = (f32[896]{0:T(1024)S(1)}, f32[896]{0:T(1024)S(1)}, u32[]{:S(2)}, u32[]{:S(2)}) collective-permute-start(f32[896]{0:T(1024)S(1)} %add.199), channel_id=1, source_target_pairs={{0,64},{16,80},{32,96},{48,112},{64,0},{80,16},{96,32},{112,48},{1... | collective-permute-start | bytes 10760 | tf_op jit(solution)/shard_map/ppermute | solution.py:87
  198.1 9.6 %collective-permute-start.23 = (f32[896]{0:T(1024)S(1)}, f32[896]{0:T(1024)S(1)}, u32[]{:S(2)}, u32[]{:S(2)}) collective-permute-start(f32[896]{0:T(1024)S(1)} %add.200), channel_id=1, source_target_pairs={{0,128},{16,144},{32,160},{48,176},{64,192},{80,208},{96,224},{112... | collective-permute-start | bytes 10760 | tf_op jit(solution)/shard_map/ppermute | solution.py:87
  207.7 13.1 %collective-permute-start.24 = (f32[896]{0:T(1024)S(1)}, f32[896]{0:T(1024)S(1)}, u32[]{:S(2)}, u32[]{:S(2)}) collective-permute-start(f32[896]{0:T(1024)S(1)} %add.201), channel_id=1, source_target_pairs={{0,256},{16,272},{32,288},{48,304},{64,320},{80,336},{96,352},{112... | collective-permute-start | bytes 10760 | tf_op jit(solution)/shard_map/ppermute | solution.py:87
  220.8 13.8 %collective-permute-start.25 = (f32[896]{0:T(1024)S(1)}, f32[896]{0:T(1024)S(1)}, u32[]{:S(2)}, u32[]{:S(2)}) collective-permute-start(f32[896]{0:T(1024)S(1)} %add.202), channel_id=1, source_target_pairs={{0,4},{4,0},{8,12},{12,8},{1,5},{5,1},{9,13},{13,9},{2,6},{6,2},{1... | collective-permute-start | bytes 10760 | tf_op jit(solution)/shard_map/ppermute | solution.py:87
  224.7 18.9 %collective-permute-start.19 = (f32[2,1,128,128]{3,2,1,0:T(8,128)}, f32[2,1,128,128]{3,2,1,0:T(8,128)}, u32[]{:S(2)}, u32[]{:S(2)}) collective-permute-start(f32[2,1,128,128]{3,2,1,0:T(8,128)} %get-tuple-element.33), channel_id=1, source_target_pairs={{16,0},{32,16},{48,32},{64,48},{80,64},{96,80},{112,96},{128,112},... | collective-permute-start | bytes 393224 | tf_op jit(solution)/shard_map/ppermute | solution.py:21
  230.7 12.9 %collective-permute-start.18 = (f32[2,1,128,128]{3,2,1,0:T(8,128)}, f32[2,1,128,128]{3,2,1,0:T(8,128)}, u32[]{:S(2)}, u32[]{:S(2)}) collective-permute-start(f32[2,1,128,128]{3,2,1,0:T(8,128)} %get-tuple-element.34), channel_id=1, source_target_pairs={{32,0},{48,16},{64,32},{80,48},{96,64},{112,80},{128,96},{144,112}... | collective-permute-start | bytes 393224 | tf_op jit(solution)/shard_map/ppermute | solution.py:21
  232.0 13.5 %collective-permute-start.17 = (f32[2,1,128,128]{3,2,1,0:T(8,128)}, f32[2,1,128,128]{3,2,1,0:T(8,128)}, u32[]{:S(2)}, u32[]{:S(2)}) collective-permute-start(f32[2,1,128,128]{3,2,1,0:T(8,128)} %get-tuple-element.32), channel_id=1, source_target_pairs={{48,0},{64,16},{80,32},{96,48},{112,64},{128,80},{144,96},{160,112... | collective-permute-start | bytes 393224 | tf_op jit(solution)/shard_map/ppermute | solution.py:21
  233.3 15.9 %collective-permute-start.16 = (f32[2,1,128,128]{3,2,1,0:T(8,128)}, f32[2,1,128,128]{3,2,1,0:T(8,128)}, u32[]{:S(2)}, u32[]{:S(2)}) collective-permute-start(f32[2,1,128,128]{3,2,1,0:T(8,128)} %get-tuple-element.31), channel_id=1, source_target_pairs={{64,0},{80,16},{96,32},{112,48},{128,64},{144,80},{160,96},{176,11... | collective-permute-start | bytes 393224 | tf_op jit(solution)/shard_map/ppermute | solution.py:21
  234.6 8.3 %collective-permute-start.26 = (f32[896]{0:T(1024)S(1)}, f32[896]{0:T(1024)S(1)}, u32[]{:S(2)}, u32[]{:S(2)}) collective-permute-start(f32[896]{0:T(1024)S(1)} %add.203), channel_id=1, source_target_pairs={{0,8},{4,12},{8,0},{12,4},{1,9},{5,13},{9,1},{13,5},{2,10},{6,14},... | collective-permute-start | bytes 10760 | tf_op jit(solution)/shard_map/ppermute | solution.py:87
  (22 other events, 318.3 us)

commit v9 on v8

--- a/solution.py
+++ b/solution.py
@@ -222,7 +222,7 @@
         grad_parts.append(part_level)
     unit_out = jnp.concatenate(unit_parts, axis=0)
     level_grad = jnp.concatenate(grad_parts, axis=0)
-    gain_grads = summed(jnp.concatenate(gain_parts, axis=0), ("seq", "dp"))
+    gain_grads = lax.psum(summed(jnp.concatenate(gain_parts, axis=0), ("seq",)), "dp")
     layer_output = (
         unit_out.astype(jnp.bfloat16).transpose(1, 0, 2).reshape(1, block_rows, q_heads * HEAD_SIZE)
     )

time: 252 us -> 247 us (0.980); the launches traced: 251 us -> 243 us
  waiting for transfers between devices: 77 us -> 59.1 us
  blocking collectives: 14.9 us -> 23.9 us
    ppermute x7 -> x5, waiting for transfers between devices: 12.5 us -> 0.22 us  [xor_reduced(): values[c] = lax.ppermute(value, axis, [(i, i ^ c) for i in range(count)])]
    psum x0 -> x1, blocking collectives: none -> 9.03 us  [local(): lax.psum(summed(jnp.concatenate(gain_parts, axis=0), ('seq',)), 'dp')]
    ppermute x8, waiting for transfers between devices: 5.64 us -> 0.02 us  [passed_along(): return lax.ppermute(block, axis, route)]
    ppermute x7 -> x5, starting transfers between devices: 39 us -> 42.4 us  [xor_reduced(): values[c] = lax.ppermute(value, axis, [(i, i ^ c) for i in range(count)])]
    unnamed x64 -> x62, local copies, waits for them, and re-layouts: 5.92 us -> 5.92 us
  transfers between devices with their start and end apart: 27 -> 25, of which waited for: 13 -> 8; matrix products, arithmetic and copies ran while one was open for 10% -> 10% of each run, Pallas kernels for 0% -> 0%
where the time goes in v9:
time: 247 us; the launch traced here: 243 us
  starting transfers between devices  113 us (46%)
  waiting for transfers between devices  59.1 us (24%)
  blocking collectives  23.9 us (10%)
  matrix products  21.4 us (9%)
  other arithmetic  13.8 us (6%)
  local copies, waits for them, and re-layouts  9.88 us (4%)
    ppermute x12, waiting for transfers between devices, moved_on(): return lax.ppermute(value, axis, pairs)  58.9 us
    ppermute x12, starting transfers between devices, moved_on(): return lax.ppermute(value, axis, pairs)  45.1 us
    ppermute x5, starting transfers between devices, xor_reduced(): values[c] = lax.ppermute(value, axis, [(i, i ^ c) for i in range(count)])  42.4 us
    ppermute x8, starting transfers between devices, passed_along(): return lax.ppermute(block, axis, route)  25.6 us
    psum x1, blocking collectives, local(): lax.psum(summed(jnp.concatenate(gain_parts, axis=0), ('seq',)), 'dp')  9.03 us
    psum x1, blocking collectives, local(): square_sum = lax.psum(jnp.sum(out_float * out_float, axis=(0, 2)), 'tensor')  8.73 us
    psum x1, blocking collectives, local(): slope_sum = lax.psum(jnp.sum(normed_grad * normed, axis=(0, 2)), 'tensor')  6.14 us
    convert_element_type x8, other arithmetic, entering(): sent = covered.astype(jnp.bfloat16)  5.99 us
  transfers between devices with their start and end apart: 25, of which 8 were waited for; matrix products, arithmetic and copies ran while one was open for 10% of the time, Pallas kernels for 0%

profile of v9, /device:TPU:1, one launch (start us, length us, event | category | flops | bytes accessed | tf_op | source)
XLA Modules:
  0.0 243.4 jit_solution(2287852178424928216)
XLA Ops:
  1.4 5.7 %collective-permute-start = (bf16[2,1,128,128]{3,2,1,0:T(8,128)(2,1)S(1)}, bf16[2,1,128,128]{3,2,1,0:T(8,128)(2,1)S(1)}, u32[]{:S(2)}, u32[]{:S(2)}) collective-permute-start(bf16[2,1,128,128]{3,2,1,0:T(8,128)(2,1)S(1)} %pad_maximum_fusion.3), channel_id=1, source_target_pairs={{0,64},{16,80},{32,96},{48,112},{64,128},{80,144},{96,160},{112,17... | collective-permute-start | bytes 196616 | tf_op jit(solution)/shard_map/ppermute | solution.py:21
  7.1 7.0 %collective-permute-start.1 = (bf16[2,1,128,128]{3,2,1,0:T(8,128)(2,1)S(1)}, bf16[2,1,128,128]{3,2,1,0:T(8,128)(2,1)S(1)}, u32[]{:S(2)}, u32[]{:S(2)}) collective-permute-start(bf16[2,1,128,128]{3,2,1,0:T(8,128)(2,1)S(1)} %pad_maximum_fusion.3), channel_id=1, source_target_pairs={{0,48},{16,64},{32,80},{48,96},{64,112},{80,128},{96,144},{112,160... | collective-permute-start | bytes 196616 | tf_op jit(solution)/shard_map/ppermute | solution.py:21
  14.1 3.5 %collective-permute-start.2 = (bf16[2,1,128,128]{3,2,1,0:T(8,128)(2,1)S(1)}, bf16[2,1,128,128]{3,2,1,0:T(8,128)(2,1)S(1)}, u32[]{:S(2)}, u32[]{:S(2)}) collective-permute-start(bf16[2,1,128,128]{3,2,1,0:T(8,128)(2,1)S(1)} %pad_maximum_fusion.3), channel_id=1, source_target_pairs={{0,32},{16,48},{32,64},{48,80},{64,96},{80,112},{96,128},{112,144}... | collective-permute-start | bytes 196616 | tf_op jit(solution)/shard_map/ppermute | solution.py:21
  17.6 1.9 collective-permute-start.3
  26.3 2.2 fusion.133
  29.8 8.7 %psum.21 = f32[128]{0:T(128)S(1)} all-reduce(f32[128]{0:T(128)S(1)} %get-tuple-element.52), channel_id=1, replica_groups=mesh['seq'=32,'dp'=4,'tensor'=4] {'tensor'}, use_global_device_ids=true, to_apply=%region_4.5 | all-reduce | flops 128 | bytes 1024 | tf_op jit(solution)/shard_map/psum | solution.py:161
  40.8 3.8 %collective-permute-done.4 = f32[7,136,128]{2,1,0:T(8,128)S(1)} collective-permute-done((f32[7,136,128]{2,1,0:T(8,128)S(1)}, f32[7,136,128]{2,1,0:T(8,128)S(1)}, u32[]{:S(2)}, u32[]{:S(2)}) %collective-permute-start.4) | collective-permute-done | bytes 487456 | tf_op jit(solution)/shard_map/ppermute | solution.py:35
  44.8 3.6 %collective-permute-start.5 = (bf16[7,136,128]{2,1,0:T(8,128)(2,1)S(1)}, bf16[7,136,128]{2,1,0:T(8,128)(2,1)S(1)}, u32[]{:S(2)}, u32[]{:S(2)}) collective-permute-start(bf16[7,136,128]{2,1,0:T(8,128)(2,1)S(1)} %get-tuple-element.29), channel_id=1, source_target_pairs={{16,48},{48,80},{80,112},{112,144},{144,176},{176,208},{208,240},{... | collective-permute-start | bytes 731144 | tf_op jit(solution)/shard_map/ppermute | solution.py:35
  48.5 2.9 %collective-permute-done.5 = bf16[7,136,128]{2,1,0:T(8,128)(2,1)S(1)} collective-permute-done((bf16[7,136,128]{2,1,0:T(8,128)(2,1)S(1)}, bf16[7,136,128]{2,1,0:T(8,128)(2,1)S(1)}, u32[]{:S(2)}, u32[]{:S(2)}) %collective-permute-start.5) | collective-permute-done | bytes 243744 | tf_op jit(solution)/shard_map/ppermute | solution.py:35
  51.8 6.8 %collective-permute-start.6 = (bf16[7,136,128]{2,1,0:T(8,128)(2,1)S(1)}, bf16[7,136,128]{2,1,0:T(8,128)(2,1)}, u32[]{:S(2)}, u32[]{:S(2)}) collective-permute-start(bf16[7,136,128]{2,1,0:T(8,128)(2,1)S(1)} %get-tuple-element.27), channel_id=1, source_target_pairs={{16,80},{48,112},{80,144},{112,176},{144,208},{176,240},{208,272},... | collective-permute-start | bytes 731144 | tf_op jit(solution)/shard_map/ppermute | solution.py:35
  58.9 2.1 collective-permute-done.6
  61.1 1.5 fusion.128
  62.6 11.9 %collective-permute-start.7 = (bf16[7,136,128]{2,1,0:T(8,128)(2,1)S(1)}, bf16[7,136,128]{2,1,0:T(8,128)(2,1)S(1)}, u32[]{:S(2)}, u32[]{:S(2)}) collective-permute-start(bf16[7,136,128]{2,1,0:T(8,128)(2,1)S(1)} %get-tuple-element.25), channel_id=1, source_target_pairs={{16,144},{48,176},{80,208},{112,240},{144,272},{176,304},{208,336}... | collective-permute-start | bytes 731144 | tf_op jit(solution)/shard_map/ppermute | solution.py:35
  74.7 2.8 %collective-permute-done.7 = bf16[7,136,128]{2,1,0:T(8,128)(2,1)S(1)} collective-permute-done((bf16[7,136,128]{2,1,0:T(8,128)(2,1)S(1)}, bf16[7,136,128]{2,1,0:T(8,128)(2,1)S(1)}, u32[]{:S(2)}, u32[]{:S(2)}) %collective-permute-start.7) | collective-permute-done | bytes 243744 | tf_op jit(solution)/shard_map/ppermute | solution.py:35
  77.8 12.6 %collective-permute-start.8 = (bf16[7,136,128]{2,1,0:T(8,128)(2,1)S(1)}, bf16[7,136,128]{2,1,0:T(8,128)(2,1)S(1)}, u32[]{:S(2)}, u32[]{:S(2)}) collective-permute-start(bf16[7,136,128]{2,1,0:T(8,128)(2,1)S(1)} %get-tuple-element.39), channel_id=1, source_target_pairs={{16,272},{48,304},{80,336},{112,368},{144,400},{176,432},{208,464}... | collective-permute-start | bytes 731144 | tf_op jit(solution)/shard_map/ppermute | solution.py:35
  97.4 1.5 multiply_reduce_fusion.4
  100.8 2.3 collective-permute-start.10
  107.5 2.2 fusion.123
  113.1 1.6 collective-permute-start.15
  117.4 44.9 %collective-permute-done.15 = f32[7,128,128]{2,1,0:T(8,128)} collective-permute-done((f32[7,128,128]{2,1,0:T(8,128)S(1)}, f32[7,128,128]{2,1,0:T(8,128)}, u32[]{:S(2)}, u32[]{:S(2)}) %collective-permute-start.15) | collective-permute-done | bytes 458784 | tf_op jit(solution)/shard_map/ppermute | solution.py:35
  162.3 2.3 multiply_reduce_fusion.1
  164.6 6.1 %psum.22 = f32[128]{0:T(128)S(1)} all-reduce(f32[128]{0:T(128)S(1)} %get-tuple-element.16), channel_id=1, replica_groups=mesh['seq'=32,'dp'=4,'tensor'=4] {'tensor'}, use_global_device_ids=true, to_apply=%region_8.9 | all-reduce | flops 128 | bytes 1024 | tf_op jit(solution)/shard_map/psum | solution.py:230
  170.8 5.6 %collective-permute-start.20 = (f32[896]{0:T(1024)S(1)}, f32[896]{0:T(1024)S(1)}, u32[]{:S(2)}, u32[]{:S(2)}) collective-permute-start(f32[896]{0:T(1024)S(1)} %bitcast.151), channel_id=1, source_target_pairs={{0,16},{16,0},{32,48},{48,32},{64,80},{80,64},{96,112},{112,96},{1... | collective-permute-start | bytes 10760 | tf_op jit(solution)/shard_map/ppermute | solution.py:87
  178.0 14.7 %collective-permute-start.21 = (f32[896]{0:T(1024)S(1)}, f32[896]{0:T(1024)S(1)}, u32[]{:S(2)}, u32[]{:S(2)}) collective-permute-start(f32[896]{0:T(1024)S(1)} %bitcast_add_fusion.1), channel_id=1, source_target_pairs={{0,32},{16,48},{32,0},{48,16},{64,96},{80,112},{96,64},{112,80},{1... | collective-permute-start | bytes 10760 | tf_op jit(solution)/shard_map/ppermute | solution.py:87
  192.7 2.2 convolution_bitcast_fusion
  194.9 1.9 collective-permute-start.22
  196.8 3.1 %fusion.19 = f32[1,1,640,128]{3,2,1,0:T(8,128)S(1)} fusion(bf16[7,128,128]{1,2,0:T(8,128)(2,1)S(1)} %bitcast.135, f32[7,128,640]{1,2,0:T(8,128)S(1)} %fusion.101, f32[7,128,640]{1,2,0:T(8,128)} %get-tuple-element.51, f32[7,128]{1,0:T(8,128)S(1)} %copy-done.25), kind=kOutput, calls=%fused_computation.24 | convolution fusion | flops 150816256 | bytes 5148160 | tf_op jit(solution)/shard_map/gjsk,gjsd->gkd/dot_general | solution.py:244
  200.1 7.4 %collective-permute-start.23 = (f32[896]{0:T(1024)S(1)}, f32[896]{0:T(1024)S(1)}, u32[]{:S(2)}, u32[]{:S(2)}) collective-permute-start(f32[896]{0:T(1024)S(1)} %add.196), channel_id=1, source_target_pairs={{0,128},{16,144},{32,160},{48,176},{64,192},{80,208},{96,224},{112... | collective-permute-start | bytes 10760 | tf_op jit(solution)/shard_map/ppermute | solution.py:87
  208.3 3.6 %collective-permute-start.19 = (f32[2,1,128,128]{3,2,1,0:T(8,128)}, f32[2,1,128,128]{3,2,1,0:T(8,128)S(1)}, u32[]{:S(2)}, u32[]{:S(2)}) collective-permute-start(f32[2,1,128,128]{3,2,1,0:T(8,128)} %get-tuple-element.33), channel_id=1, source_target_pairs={{16,0},{32,16},{48,32},{64,48},{80,64},{96,80},{112,96},{128,112},... | collective-permute-start | bytes 393224 | tf_op jit(solution)/shard_map/ppermute | solution.py:21
  215.9 12.8 %collective-permute-start.24 = (f32[896]{0:T(1024)S(1)}, f32[896]{0:T(1024)S(1)}, u32[]{:S(2)}, u32[]{:S(2)}) collective-permute-start(f32[896]{0:T(1024)S(1)} %add.197), channel_id=1, source_target_pairs={{0,256},{16,272},{32,288},{48,304},{64,320},{80,336},{96,352},{112... | collective-permute-start | bytes 10760 | tf_op jit(solution)/shard_map/ppermute | solution.py:87
  228.6 3.1 %fusion.15 = bf16[7,128,128]{1,2,0:T(8,128)(2,1)S(1)} fusion(f32[7,128,640]{1,2,0:T(8,128)S(1)} %fusion.101, bf16[2,1,640,128]{3,2,1,0:T(8,128)(2,1)} %copy-done.12, f32[7,128,640]{1,2,0:T(8,128)} %get-tuple-element.51, f32[7,128]{1,0:T(8,128)S(1)} %copy-done.25), kind=kOutput, calls=%fused_computation.21 | convolution fusion | flops 150930944 | bytes 9576448 | tf_op jit(solution)/shard_map/gjsk,gkd->gjsd/dot_general | solution.py:241
  232.6 9.0 %psum.23 = f32[896]{0:T(1024)} all-reduce(f32[896]{0:T(1024)S(1)} %add.198), channel_id=1, replica_groups=mesh['seq'=32,'dp'=4,'tensor'=4] {'dp'}, use_global_device_ids=true, to_apply=%region_11.12 | all-reduce | flops 896 | bytes 7168 | tf_op jit(solution)/shard_map/psum | solution.py:225
  (155 shorter events, 39.7 us)
Async XLA Ops:
  1.4 23.9 %collective-permute-start = (bf16[2,1,128,128]{3,2,1,0:T(8,128)(2,1)S(1)}, bf16[2,1,128,128]{3,2,1,0:T(8,128)(2,1)S(1)}, u32[]{:S(2)}, u32[]{:S(2)}) collective-permute-start(bf16[2,1,128,128]{3,2,1,0:T(8,128)(2,1)S(1)} %pad_maximum_fusion.3), channel_id=1, source_target_pairs={{0,64},{16,80},{32,96},{48,112},{64,128},{80,144},{96,160},{112,17... | collective-permute-start | bytes 196616 | tf_op jit(solution)/shard_map/ppermute | solution.py:21
  7.1 18.2 %collective-permute-start.1 = (bf16[2,1,128,128]{3,2,1,0:T(8,128)(2,1)S(1)}, bf16[2,1,128,128]{3,2,1,0:T(8,128)(2,1)S(1)}, u32[]{:S(2)}, u32[]{:S(2)}) collective-permute-start(bf16[2,1,128,128]{3,2,1,0:T(8,128)(2,1)S(1)} %pad_maximum_fusion.3), channel_id=1, source_target_pairs={{0,48},{16,64},{32,80},{48,96},{64,112},{80,128},{96,144},{112,160... | collective-permute-start | bytes 196616 | tf_op jit(solution)/shard_map/ppermute | solution.py:21
  14.1 11.3 %collective-permute-start.2 = (bf16[2,1,128,128]{3,2,1,0:T(8,128)(2,1)S(1)}, bf16[2,1,128,128]{3,2,1,0:T(8,128)(2,1)S(1)}, u32[]{:S(2)}, u32[]{:S(2)}) collective-permute-start(bf16[2,1,128,128]{3,2,1,0:T(8,128)(2,1)S(1)} %pad_maximum_fusion.3), channel_id=1, source_target_pairs={{0,32},{16,48},{32,64},{48,80},{64,96},{80,112},{96,128},{112,144}... | collective-permute-start | bytes 196616 | tf_op jit(solution)/shard_map/ppermute | solution.py:21
  17.6 7.8 %collective-permute-start.3 = (bf16[2,1,128,128]{3,2,1,0:T(8,128)(2,1)S(1)}, bf16[2,1,128,128]{3,2,1,0:T(8,128)(2,1)S(1)}, u32[]{:S(2)}, u32[]{:S(2)}) collective-permute-start(bf16[2,1,128,128]{3,2,1,0:T(8,128)(2,1)S(1)} %pad_maximum_fusion.3), channel_id=1, source_target_pairs={{0,16},{16,32},{32,48},{48,64},{64,80},{80,96},{96,112},{112,128},... | collective-permute-start | bytes 196616 | tf_op jit(solution)/shard_map/ppermute | solution.py:21
  23.0 74.4 %copy-start.18 = (f32[7,128]{1,0:T(8,128)}, f32[7,128]{1,0:T(8,128)S(1)}, u32[]{:S(2)}) copy-start(f32[7,128]{1,0:T(8,128)S(1)} %convert_bitcast_fusion) | copy-start | bytes 10756
  38.5 58.9 %copy-start.22 = (f32[128]{0:T(128)}, f32[128]{0:T(128)S(1)}, u32[]{:S(2)}) copy-start(f32[128]{0:T(128)S(1)} %add_rsqrt_fusion.1) | copy-start | bytes 1540
  39.5 5.1 %collective-permute-start.4 = (f32[7,136,128]{2,1,0:T(8,128)S(1)}, f32[7,136,128]{2,1,0:T(8,128)S(1)}, u32[]{:S(2)}, u32[]{:S(2)}) collective-permute-start(f32[7,136,128]{2,1,0:T(8,128)S(1)} %pad_maximum_fusion.1), channel_id=1, source_target_pairs={{0,16},{32,48},{64,80},{96,112},{128,144},{160,176},{192,208},{224... | collective-permute-start | bytes 1462280 | tf_op jit(solution)/shard_map/ppermute | solution.py:35
  44.8 6.7 %collective-permute-start.5 = (bf16[7,136,128]{2,1,0:T(8,128)(2,1)S(1)}, bf16[7,136,128]{2,1,0:T(8,128)(2,1)S(1)}, u32[]{:S(2)}, u32[]{:S(2)}) collective-permute-start(bf16[7,136,128]{2,1,0:T(8,128)(2,1)S(1)} %get-tuple-element.29), channel_id=1, source_target_pairs={{16,48},{48,80},{80,112},{112,144},{144,176},{176,208},{208,240},{... | collective-permute-start | bytes 731144 | tf_op jit(solution)/shard_map/ppermute | solution.py:35
  51.8 9.2 %collective-permute-start.6 = (bf16[7,136,128]{2,1,0:T(8,128)(2,1)S(1)}, bf16[7,136,128]{2,1,0:T(8,128)(2,1)}, u32[]{:S(2)}, u32[]{:S(2)}) collective-permute-start(bf16[7,136,128]{2,1,0:T(8,128)(2,1)S(1)} %get-tuple-element.27), channel_id=1, source_target_pairs={{16,80},{48,112},{80,144},{112,176},{144,208},{176,240},{208,272},... | collective-permute-start | bytes 731144 | tf_op jit(solution)/shard_map/ppermute | solution.py:35
  62.6 15.0 %collective-permute-start.7 = (bf16[7,136,128]{2,1,0:T(8,128)(2,1)S(1)}, bf16[7,136,128]{2,1,0:T(8,128)(2,1)S(1)}, u32[]{:S(2)}, u32[]{:S(2)}) collective-permute-start(bf16[7,136,128]{2,1,0:T(8,128)(2,1)S(1)} %get-tuple-element.25), channel_id=1, source_target_pairs={{16,144},{48,176},{80,208},{112,240},{144,272},{176,304},{208,336}... | collective-permute-start | bytes 731144 | tf_op jit(solution)/shard_map/ppermute | solution.py:35
  77.8 15.7 %collective-permute-start.8 = (bf16[7,136,128]{2,1,0:T(8,128)(2,1)S(1)}, bf16[7,136,128]{2,1,0:T(8,128)(2,1)S(1)}, u32[]{:S(2)}, u32[]{:S(2)}) collective-permute-start(bf16[7,136,128]{2,1,0:T(8,128)(2,1)S(1)} %get-tuple-element.39), channel_id=1, source_target_pairs={{16,272},{48,304},{80,336},{112,368},{144,400},{176,432},{208,464}... | collective-permute-start | bytes 731144 | tf_op jit(solution)/shard_map/ppermute | solution.py:35
  93.8 2.9 %collective-permute-start.9 = (f32[7,128,128]{2,1,0:T(8,128)S(1)}, f32[7,128,128]{2,1,0:T(8,128)S(1)}, u32[]{:S(2)}, u32[]{:S(2)}) collective-permute-start(f32[7,128,128]{2,1,0:T(8,128)S(1)} %slice.129), channel_id=1, source_target_pairs={{16,0},{48,32},{80,64},{112,96},{144,128},{176,160},{208,192},{240... | collective-permute-start | bytes 1376264 | tf_op jit(solution)/shard_map/ppermute | solution.py:35
  100.8 3.7 %collective-permute-start.10 = (f32[7,136,128]{2,1,0:T(8,128)S(1)}, f32[7,136,128]{2,1,0:T(8,128)S(1)}, u32[]{:S(2)}, u32[]{:S(2)}) collective-permute-start(f32[7,136,128]{2,1,0:T(8,128)S(1)} %pad_maximum_fusion), channel_id=1, source_target_pairs={{496,480},{464,448},{432,416},{400,384},{368,352},{336,320},{304,2... | collective-permute-start | bytes 1462280 | tf_op jit(solution)/shard_map/ppermute | solution.py:35
  104.7 0.8 collective-permute-start.11
  105.9 1.6 collective-permute-start.12
  109.7 1.1 collective-permute-start.13
  111.8 1.0 collective-permute-start.14
  113.0 49.4 %copy-start.17 = (f32[896]{0:T(1024)S(1)}, f32[896]{0:T(1024)}, u32[]{:S(2)}) copy-start(f32[896]{0:T(1024)} %param.14) | copy-start | bytes 10756
  113.0 49.4 %copy-start.19 = (f32[7,128]{1,0:T(8,128)S(1)}, f32[7,128]{1,0:T(8,128)}, u32[]{:S(2)}) copy-start(f32[7,128]{1,0:T(8,128)} %copy-done.18) | copy-start | bytes 10756
  113.0 49.3 %copy-start.21 = (f32[7,128]{1,0:T(8,128)S(1)}, f32[7,128]{1,0:T(8,128)}, u32[]{:S(2)}) copy-start(f32[7,128]{1,0:T(8,128)} %copy-done.20) | copy-start | bytes 10756
  113.0 49.3 %copy-start.23 = (f32[128]{0:T(128)S(1)}, f32[128]{0:T(128)}, u32[]{:S(2)}) copy-start(f32[128]{0:T(128)} %copy-done.22) | copy-start | bytes 1540
  113.1 49.3 %collective-permute-start.15 = (f32[7,128,128]{2,1,0:T(8,128)S(1)}, f32[7,128,128]{2,1,0:T(8,128)}, u32[]{:S(2)}, u32[]{:S(2)}) collective-permute-start(f32[7,128,128]{2,1,0:T(8,128)S(1)} %slice.140), channel_id=1, source_target_pairs={{480,496},{448,464},{416,432},{384,400},{352,368},{320,336},{288,3... | collective-permute-start | bytes 1376264 | tf_op jit(solution)/shard_map/ppermute | solution.py:35
  117.2 59.1 %copy-start.8 = (f32[7,128,128]{1,2,0:T(8,128)S(1)}, f32[7,128,128]{1,2,0:T(8,128)}, u32[]{:S(2)}) copy-start(f32[7,128,128]{1,2,0:T(8,128)} %copy-done.6) | copy-start | bytes 1376260
  170.8 7.2 %collective-permute-start.20 = (f32[896]{0:T(1024)S(1)}, f32[896]{0:T(1024)S(1)}, u32[]{:S(2)}, u32[]{:S(2)}) collective-permute-start(f32[896]{0:T(1024)S(1)} %bitcast.151), channel_id=1, source_target_pairs={{0,16},{16,0},{32,48},{48,32},{64,80},{80,64},{96,112},{112,96},{1... | collective-permute-start | bytes 10760 | tf_op jit(solution)/shard_map/ppermute | solution.py:87
  178.0 16.9 %collective-permute-start.21 = (f32[896]{0:T(1024)S(1)}, f32[896]{0:T(1024)S(1)}, u32[]{:S(2)}, u32[]{:S(2)}) collective-permute-start(f32[896]{0:T(1024)S(1)} %bitcast_add_fusion.1), channel_id=1, source_target_pairs={{0,32},{16,48},{32,0},{48,16},{64,96},{80,112},{96,64},{112,80},{1... | collective-permute-start | bytes 10760 | tf_op jit(solution)/shard_map/ppermute | solution.py:87
  194.9 5.3 %collective-permute-start.22 = (f32[896]{0:T(1024)S(1)}, f32[896]{0:T(1024)S(1)}, u32[]{:S(2)}, u32[]{:S(2)}) collective-permute-start(f32[896]{0:T(1024)S(1)} %add.195), channel_id=1, source_target_pairs={{0,64},{16,80},{32,96},{48,112},{64,0},{80,16},{96,32},{112,48},{1... | collective-permute-start | bytes 10760 | tf_op jit(solution)/shard_map/ppermute | solution.py:87
  200.1 15.7 %collective-permute-start.23 = (f32[896]{0:T(1024)S(1)}, f32[896]{0:T(1024)S(1)}, u32[]{:S(2)}, u32[]{:S(2)}) collective-permute-start(f32[896]{0:T(1024)S(1)} %add.196), channel_id=1, source_target_pairs={{0,128},{16,144},{32,160},{48,176},{64,192},{80,208},{96,224},{112... | collective-permute-start | bytes 10760 | tf_op jit(solution)/shard_map/ppermute | solution.py:87
  208.3 33.3 %collective-permute-start.19 = (f32[2,1,128,128]{3,2,1,0:T(8,128)}, f32[2,1,128,128]{3,2,1,0:T(8,128)S(1)}, u32[]{:S(2)}, u32[]{:S(2)}) collective-permute-start(f32[2,1,128,128]{3,2,1,0:T(8,128)} %get-tuple-element.33), channel_id=1, source_target_pairs={{16,0},{32,16},{48,32},{64,48},{80,64},{96,80},{112,96},{128,112},... | collective-permute-start | bytes 393224 | tf_op jit(solution)/shard_map/ppermute | solution.py:21
  211.9 29.7 %collective-permute-start.18 = (f32[2,1,128,128]{3,2,1,0:T(8,128)}, f32[2,1,128,128]{3,2,1,0:T(8,128)}, u32[]{:S(2)}, u32[]{:S(2)}) collective-permute-start(f32[2,1,128,128]{3,2,1,0:T(8,128)} %get-tuple-element.34), channel_id=1, source_target_pairs={{32,0},{48,16},{64,32},{80,48},{96,64},{112,80},{128,96},{144,112}... | collective-permute-start | bytes 393224 | tf_op jit(solution)/shard_map/ppermute | solution.py:21
  213.2 28.4 %collective-permute-start.17 = (f32[2,1,128,128]{3,2,1,0:T(8,128)}, f32[2,1,128,128]{3,2,1,0:T(8,128)}, u32[]{:S(2)}, u32[]{:S(2)}) collective-permute-start(f32[2,1,128,128]{3,2,1,0:T(8,128)} %get-tuple-element.32), channel_id=1, source_target_pairs={{48,0},{64,16},{80,32},{96,48},{112,64},{128,80},{144,96},{160,112... | collective-permute-start | bytes 393224 | tf_op jit(solution)/shard_map/ppermute | solution.py:21
  214.6 27.1 %collective-permute-start.16 = (f32[2,1,128,128]{3,2,1,0:T(8,128)S(1)}, f32[2,1,128,128]{3,2,1,0:T(8,128)}, u32[]{:S(2)}, u32[]{:S(2)}) collective-permute-start(f32[2,1,128,128]{3,2,1,0:T(8,128)S(1)} %get-tuple-element.31), channel_id=1, source_target_pairs={{64,0},{80,16},{96,32},{112,48},{128,64},{144,80},{160,96},{176,11... | collective-permute-start | bytes 393224 | tf_op jit(solution)/shard_map/ppermute | solution.py:21
  215.9 16.8 %collective-permute-start.24 = (f32[896]{0:T(1024)S(1)}, f32[896]{0:T(1024)S(1)}, u32[]{:S(2)}, u32[]{:S(2)}) collective-permute-start(f32[896]{0:T(1024)S(1)} %add.197), channel_id=1, source_target_pairs={{0,256},{16,272},{32,288},{48,304},{64,320},{80,336},{96,352},{112... | collective-permute-start | bytes 10760 | tf_op jit(solution)/shard_map/ppermute | solution.py:87
  (19 other events, 161.4 us)

commit v10 on v9

--- a/solution.py
+++ b/solution.py
@@ -56,7 +56,9 @@
             distance *= 2
         return before[:, :rows]
     lead = place % 2 == 1
-    first = moved_on(value, axis, [(spot(p), spot(p + 1)) for p in range(0, count, 2)])
+    first = moved_on(
+        value.astype(jnp.bfloat16), axis, [(spot(p), spot(p + 1)) for p in range(0, count, 2)]
+    ).astype(jnp.float32)
     covered = chain_states(first, value)
     before = identity
     distance = 2
@@ -72,7 +74,9 @@
         if 2 * distance < count:
             covered = picked(present, chain_states(moved, covered), covered)
         distance *= 2
-    handed = moved_on(before[:, :rows], axis, [(spot(p), spot(p - 1)) for p in range(1, count, 2)])
+    handed = moved_on(
+        before[:, :rows].astype(jnp.bfloat16), axis, [(spot(p), spot(p - 1)) for p in range(1, count, 2)]
+    ).astype(jnp.float32)
     own_lead = chain_states(before, first)[:, :rows]
     return jnp.where(lead, own_lead, handed)
 

time: 247 us -> 244 us (0.988)
  starting transfers between devices: 113 us -> 110 us
    unnamed x62 -> x64, local copies, waits for them, and re-layouts: 5.92 us -> 6.51 us
where the time goes in v10:
time: 244 us; the launch traced here: 240 us
  starting transfers between devices  110 us (45%)
  waiting for transfers between devices  58.8 us (24%)
  blocking collectives  24 us (10%)
  matrix products  21.1 us (9%)
  other arithmetic  12.1 us (5%)
  local copies, waits for them, and re-layouts  11.4 us (5%)
    ppermute x12, waiting for transfers between devices, moved_on(): return lax.ppermute(value, axis, pairs)  58.6 us
    ppermute x12, starting transfers between devices, moved_on(): return lax.ppermute(value, axis, pairs)  43.7 us
    ppermute x5, starting transfers between devices, xor_reduced(): values[c] = lax.ppermute(value, axis, [(i, i ^ c) for i in range(count)])  40.7 us
    ppermute x8, starting transfers between devices, passed_along(): return lax.ppermute(block, axis, route)  25.6 us
    psum x1, blocking collectives, local(): lax.psum(summed(jnp.concatenate(gain_parts, axis=0), ('seq',)), 'dp')  9.05 us
    psum x1, blocking collectives, local(): square_sum = lax.psum(jnp.sum(out_float * out_float, axis=(0, 2)), 'tensor')  8.73 us
    unnamed x64, local copies, waits for them, and re-layouts  6.51 us
    psum x1, blocking collectives, local(): slope_sum = lax.psum(jnp.sum(normed_grad * normed, axis=(0, 2)), 'tensor')  6.26 us
  transfers between devices with their start and end apart: 25, of which 8 were waited for; matrix products, arithmetic and copies ran while one was open for 10% of the time, Pallas kernels for 0%

profile of v10, /device:TPU:1, one launch (start us, length us, event | category | flops | bytes accessed | tf_op | source)
XLA Modules:
  0.0 239.6 jit_solution(13105617951929391646)
XLA Ops:
  1.4 5.7 %collective-permute-start = (bf16[2,1,128,128]{3,2,1,0:T(8,128)(2,1)S(1)}, bf16[2,1,128,128]{3,2,1,0:T(8,128)(2,1)S(1)}, u32[]{:S(2)}, u32[]{:S(2)}) collective-permute-start(bf16[2,1,128,128]{3,2,1,0:T(8,128)(2,1)S(1)} %pad_maximum_fusion.3), channel_id=1, source_target_pairs={{0,64},{16,80},{32,96},{48,112},{64,128},{80,144},{96,160},{112,17... | collective-permute-start | bytes 196616 | tf_op jit(solution)/shard_map/ppermute | solution.py:21
  7.1 7.0 %collective-permute-start.1 = (bf16[2,1,128,128]{3,2,1,0:T(8,128)(2,1)S(1)}, bf16[2,1,128,128]{3,2,1,0:T(8,128)(2,1)S(1)}, u32[]{:S(2)}, u32[]{:S(2)}) collective-permute-start(bf16[2,1,128,128]{3,2,1,0:T(8,128)(2,1)S(1)} %pad_maximum_fusion.3), channel_id=1, source_target_pairs={{0,48},{16,64},{32,80},{48,96},{64,112},{80,128},{96,144},{112,160... | collective-permute-start | bytes 196616 | tf_op jit(solution)/shard_map/ppermute | solution.py:21
  14.1 3.5 %collective-permute-start.2 = (bf16[2,1,128,128]{3,2,1,0:T(8,128)(2,1)S(1)}, bf16[2,1,128,128]{3,2,1,0:T(8,128)(2,1)S(1)}, u32[]{:S(2)}, u32[]{:S(2)}) collective-permute-start(bf16[2,1,128,128]{3,2,1,0:T(8,128)(2,1)S(1)} %pad_maximum_fusion.3), channel_id=1, source_target_pairs={{0,32},{16,48},{32,64},{48,80},{64,96},{80,112},{96,128},{112,144}... | collective-permute-start | bytes 196616 | tf_op jit(solution)/shard_map/ppermute | solution.py:21
  17.6 1.9 collective-permute-start.3
  26.3 2.2 fusion.137
  29.8 8.7 %psum.21 = f32[128]{0:T(128)S(1)} all-reduce(f32[128]{0:T(128)S(1)} %get-tuple-element.52), channel_id=1, replica_groups=mesh['seq'=32,'dp'=4,'tensor'=4] {'tensor'}, use_global_device_ids=true, to_apply=%region_4.5 | all-reduce | flops 128 | bytes 1024 | tf_op jit(solution)/shard_map/psum | solution.py:165
  41.4 3.5 %collective-permute-done.4 = bf16[7,136,128]{2,1,0:T(8,128)(2,1)S(1)} collective-permute-done((bf16[7,136,128]{2,1,0:T(8,128)(2,1)S(1)}, bf16[7,136,128]{2,1,0:T(8,128)(2,1)S(1)}, u32[]{:S(2)}, u32[]{:S(2)}) %collective-permute-start.4) | collective-permute-done | bytes 243744 | tf_op jit(solution)/shard_map/ppermute | solution.py:35
  45.1 3.6 %collective-permute-start.5 = (bf16[7,136,128]{2,1,0:T(8,128)(2,1)S(1)}, bf16[7,136,128]{2,1,0:T(8,128)(2,1)S(1)}, u32[]{:S(2)}, u32[]{:S(2)}) collective-permute-start(bf16[7,136,128]{2,1,0:T(8,128)(2,1)S(1)} %get-tuple-element.29), channel_id=1, source_target_pairs={{16,48},{48,80},{80,112},{112,144},{144,176},{176,208},{208,240},{... | collective-permute-start | bytes 731144 | tf_op jit(solution)/shard_map/ppermute | solution.py:35
  48.8 2.9 %collective-permute-done.5 = bf16[7,136,128]{2,1,0:T(8,128)(2,1)S(1)} collective-permute-done((bf16[7,136,128]{2,1,0:T(8,128)(2,1)S(1)}, bf16[7,136,128]{2,1,0:T(8,128)(2,1)S(1)}, u32[]{:S(2)}, u32[]{:S(2)}) %collective-permute-start.5) | collective-permute-done | bytes 243744 | tf_op jit(solution)/shard_map/ppermute | solution.py:35
  52.1 6.1 %collective-permute-start.6 = (bf16[7,136,128]{2,1,0:T(8,128)(2,1)S(1)}, bf16[7,136,128]{2,1,0:T(8,128)(2,1)S(1)}, u32[]{:S(2)}, u32[]{:S(2)}) collective-permute-start(bf16[7,136,128]{2,1,0:T(8,128)(2,1)S(1)} %get-tuple-element.27), channel_id=1, source_target_pairs={{16,80},{48,112},{80,144},{112,176},{144,208},{176,240},{208,272},... | collective-permute-start | bytes 731144 | tf_op jit(solution)/shard_map/ppermute | solution.py:35
  58.5 2.8 %collective-permute-done.6 = bf16[7,136,128]{2,1,0:T(8,128)(2,1)S(1)} collective-permute-done((bf16[7,136,128]{2,1,0:T(8,128)(2,1)S(1)}, bf16[7,136,128]{2,1,0:T(8,128)(2,1)S(1)}, u32[]{:S(2)}, u32[]{:S(2)}) %collective-permute-start.6) | collective-permute-done | bytes 243744 | tf_op jit(solution)/shard_map/ppermute | solution.py:35
  61.7 11.9 %collective-permute-start.7 = (bf16[7,136,128]{2,1,0:T(8,128)(2,1)S(1)}, bf16[7,136,128]{2,1,0:T(8,128)(2,1)S(1)}, u32[]{:S(2)}, u32[]{:S(2)}) collective-permute-start(bf16[7,136,128]{2,1,0:T(8,128)(2,1)S(1)} %get-tuple-element.25), channel_id=1, source_target_pairs={{16,144},{48,176},{80,208},{112,240},{144,272},{176,304},{208,336}... | collective-permute-start | bytes 731144 | tf_op jit(solution)/shard_map/ppermute | solution.py:35
  73.9 2.8 %collective-permute-done.7 = bf16[7,136,128]{2,1,0:T(8,128)(2,1)S(1)} collective-permute-done((bf16[7,136,128]{2,1,0:T(8,128)(2,1)S(1)}, bf16[7,136,128]{2,1,0:T(8,128)(2,1)S(1)}, u32[]{:S(2)}, u32[]{:S(2)}) %collective-permute-start.7) | collective-permute-done | bytes 243744 | tf_op jit(solution)/shard_map/ppermute | solution.py:35
  77.0 12.6 %collective-permute-start.8 = (bf16[7,136,128]{2,1,0:T(8,128)(2,1)S(1)}, bf16[7,136,128]{2,1,0:T(8,128)(2,1)S(1)}, u32[]{:S(2)}, u32[]{:S(2)}) collective-permute-start(bf16[7,136,128]{2,1,0:T(8,128)(2,1)S(1)} %get-tuple-element.39), channel_id=1, source_target_pairs={{16,272},{48,304},{80,336},{112,368},{144,400},{176,432},{208,464}... | collective-permute-start | bytes 731144 | tf_op jit(solution)/shard_map/ppermute | solution.py:35
  90.9 1.8 collective-permute-done.8
  93.0 2.0 collective-permute-start.9
  96.8 1.6 fusion.82
  98.4 1.5 multiply_reduce_fusion.4
  108.8 2.3 fusion.127
  113.0 1.6 fusion.118
  117.7 43.6 %collective-permute-done.15 = bf16[7,128,128]{2,1,0:T(8,128)(2,1)S(1)} collective-permute-done((bf16[7,128,128]{2,1,0:T(8,128)(2,1)S(1)}, bf16[7,128,128]{2,1,0:T(8,128)(2,1)S(1)}, u32[]{:S(2)}, u32[]{:S(2)}) %collective-permute-start.15) | collective-permute-done | bytes 229408 | tf_op jit(solution)/shard_map/ppermute | solution.py:35
  162.4 6.3 %psum.22 = f32[128]{0:T(128)S(1)} all-reduce(f32[128]{0:T(128)S(1)} %get-tuple-element.16), channel_id=1, replica_groups=mesh['seq'=32,'dp'=4,'tensor'=4] {'tensor'}, use_global_device_ids=true, to_apply=%region_8.9 | all-reduce | flops 128 | bytes 1024 | tf_op jit(solution)/shard_map/psum | solution.py:234
  168.7 3.9 %collective-permute-start.20 = (f32[896]{0:T(1024)S(1)}, f32[896]{0:T(1024)S(1)}, u32[]{:S(2)}, u32[]{:S(2)}) collective-permute-start(f32[896]{0:T(1024)S(1)} %bitcast.151), channel_id=1, source_target_pairs={{0,16},{16,0},{32,48},{48,32},{64,80},{80,64},{96,112},{112,96},{1... | collective-permute-start | bytes 10760 | tf_op jit(solution)/shard_map/ppermute | solution.py:91
  174.1 14.7 %collective-permute-start.21 = (f32[896]{0:T(1024)S(1)}, f32[896]{0:T(1024)S(1)}, u32[]{:S(2)}, u32[]{:S(2)}) collective-permute-start(f32[896]{0:T(1024)S(1)} %bitcast_add_fusion.1), channel_id=1, source_target_pairs={{0,32},{16,48},{32,0},{48,16},{64,96},{80,112},{96,64},{112,80},{1... | collective-permute-start | bytes 10760 | tf_op jit(solution)/shard_map/ppermute | solution.py:91
  188.8 2.2 convolution_bitcast_fusion
  191.0 1.9 collective-permute-start.22
  193.0 3.1 %fusion.19 = f32[1,1,640,128]{3,2,1,0:T(8,128)S(1)} fusion(bf16[7,128,128]{1,2,0:T(8,128)(2,1)S(1)} %bitcast.135, f32[7,128,640]{1,2,0:T(8,128)S(1)} %fusion.107, f32[7,128,640]{1,2,0:T(8,128)} %get-tuple-element.51, f32[7,128]{1,0:T(8,128)S(1)} %copy-done.26), kind=kOutput, calls=%fused_computation.24 | convolution fusion | flops 150816256 | bytes 5148160 | tf_op jit(solution)/shard_map/gjsk,gjsd->gkd/dot_general | solution.py:248
  196.3 7.4 %collective-permute-start.23 = (f32[896]{0:T(1024)S(1)}, f32[896]{0:T(1024)S(1)}, u32[]{:S(2)}, u32[]{:S(2)}) collective-permute-start(f32[896]{0:T(1024)S(1)} %add.196), channel_id=1, source_target_pairs={{0,128},{16,144},{32,160},{48,176},{64,192},{80,208},{96,224},{112... | collective-permute-start | bytes 10760 | tf_op jit(solution)/shard_map/ppermute | solution.py:91
  204.5 3.6 %collective-permute-start.19 = (f32[2,1,128,128]{3,2,1,0:T(8,128)}, f32[2,1,128,128]{3,2,1,0:T(8,128)S(1)}, u32[]{:S(2)}, u32[]{:S(2)}) collective-permute-start(f32[2,1,128,128]{3,2,1,0:T(8,128)} %get-tuple-element.33), channel_id=1, source_target_pairs={{16,0},{32,16},{48,32},{64,48},{80,64},{96,80},{112,96},{128,112},... | collective-permute-start | bytes 393224 | tf_op jit(solution)/shard_map/ppermute | solution.py:21
  212.0 12.8 %collective-permute-start.24 = (f32[896]{0:T(1024)S(1)}, f32[896]{0:T(1024)S(1)}, u32[]{:S(2)}, u32[]{:S(2)}) collective-permute-start(f32[896]{0:T(1024)S(1)} %add.197), channel_id=1, source_target_pairs={{0,256},{16,272},{32,288},{48,304},{64,320},{80,336},{96,352},{112... | collective-permute-start | bytes 10760 | tf_op jit(solution)/shard_map/ppermute | solution.py:91
  224.8 3.1 %fusion.15 = bf16[7,128,128]{1,2,0:T(8,128)(2,1)S(1)} fusion(f32[7,128,640]{1,2,0:T(8,128)S(1)} %fusion.107, bf16[2,1,640,128]{3,2,1,0:T(8,128)(2,1)} %copy-done.10, f32[7,128,640]{1,2,0:T(8,128)} %get-tuple-element.51, f32[7,128]{1,0:T(8,128)S(1)} %copy-done.26), kind=kOutput, calls=%fused_computation.21 | convolution fusion | flops 150930944 | bytes 9576448 | tf_op jit(solution)/shard_map/gjsk,gkd->gjsd/dot_general | solution.py:245
  228.8 9.1 %psum.23 = f32[896]{0:T(1024)} all-reduce(f32[896]{0:T(1024)S(1)} %add.198), channel_id=1, replica_groups=mesh['seq'=32,'dp'=4,'tensor'=4] {'dp'}, use_global_device_ids=true, to_apply=%region_11.12 | all-reduce | flops 896 | bytes 7168 | tf_op jit(solution)/shard_map/psum | solution.py:229
  (159 shorter events, 39.7 us)
Async XLA Ops:
  1.4 23.9 %collective-permute-start = (bf16[2,1,128,128]{3,2,1,0:T(8,128)(2,1)S(1)}, bf16[2,1,128,128]{3,2,1,0:T(8,128)(2,1)S(1)}, u32[]{:S(2)}, u32[]{:S(2)}) collective-permute-start(bf16[2,1,128,128]{3,2,1,0:T(8,128)(2,1)S(1)} %pad_maximum_fusion.3), channel_id=1, source_target_pairs={{0,64},{16,80},{32,96},{48,112},{64,128},{80,144},{96,160},{112,17... | collective-permute-start | bytes 196616 | tf_op jit(solution)/shard_map/ppermute | solution.py:21
  7.1 18.2 %collective-permute-start.1 = (bf16[2,1,128,128]{3,2,1,0:T(8,128)(2,1)S(1)}, bf16[2,1,128,128]{3,2,1,0:T(8,128)(2,1)S(1)}, u32[]{:S(2)}, u32[]{:S(2)}) collective-permute-start(bf16[2,1,128,128]{3,2,1,0:T(8,128)(2,1)S(1)} %pad_maximum_fusion.3), channel_id=1, source_target_pairs={{0,48},{16,64},{32,80},{48,96},{64,112},{80,128},{96,144},{112,160... | collective-permute-start | bytes 196616 | tf_op jit(solution)/shard_map/ppermute | solution.py:21
  14.1 11.3 %collective-permute-start.2 = (bf16[2,1,128,128]{3,2,1,0:T(8,128)(2,1)S(1)}, bf16[2,1,128,128]{3,2,1,0:T(8,128)(2,1)S(1)}, u32[]{:S(2)}, u32[]{:S(2)}) collective-permute-start(bf16[2,1,128,128]{3,2,1,0:T(8,128)(2,1)S(1)} %pad_maximum_fusion.3), channel_id=1, source_target_pairs={{0,32},{16,48},{32,64},{48,80},{64,96},{80,112},{96,128},{112,144}... | collective-permute-start | bytes 196616 | tf_op jit(solution)/shard_map/ppermute | solution.py:21
  17.6 7.8 %collective-permute-start.3 = (bf16[2,1,128,128]{3,2,1,0:T(8,128)(2,1)S(1)}, bf16[2,1,128,128]{3,2,1,0:T(8,128)(2,1)S(1)}, u32[]{:S(2)}, u32[]{:S(2)}) collective-permute-start(bf16[2,1,128,128]{3,2,1,0:T(8,128)(2,1)S(1)} %pad_maximum_fusion.3), channel_id=1, source_target_pairs={{0,16},{16,32},{32,48},{48,64},{64,80},{80,96},{96,112},{112,128},... | collective-permute-start | bytes 196616 | tf_op jit(solution)/shard_map/ppermute | solution.py:21
  23.0 75.4 %copy-start.18 = (f32[7,128]{1,0:T(8,128)}, f32[7,128]{1,0:T(8,128)S(1)}, u32[]{:S(2)}) copy-start(f32[7,128]{1,0:T(8,128)S(1)} %convert_bitcast_fusion) | copy-start | bytes 10756
  29.8 68.6 %copy-start.3 = (f32[7,128,128]{1,2,0:T(8,128)}, f32[7,128,128]{1,2,0:T(8,128)S(1)}, u32[]{:S(2)}) copy-start(f32[7,128,128]{1,2,0:T(8,128)S(1)} %get-tuple-element.53) | copy-start | bytes 1376260
  40.0 4.8 %collective-permute-start.4 = (bf16[7,136,128]{2,1,0:T(8,128)(2,1)S(1)}, bf16[7,136,128]{2,1,0:T(8,128)(2,1)S(1)}, u32[]{:S(2)}, u32[]{:S(2)}) collective-permute-start(bf16[7,136,128]{2,1,0:T(8,128)(2,1)S(1)} %fusion.95), channel_id=1, source_target_pairs={{0,16},{32,48},{64,80},{96,112},{128,144},{160,176},{192,208},{224... | collective-permute-start | bytes 731144 | tf_op jit(solution)/shard_map/ppermute | solution.py:35
  45.1 6.7 %collective-permute-start.5 = (bf16[7,136,128]{2,1,0:T(8,128)(2,1)S(1)}, bf16[7,136,128]{2,1,0:T(8,128)(2,1)S(1)}, u32[]{:S(2)}, u32[]{:S(2)}) collective-permute-start(bf16[7,136,128]{2,1,0:T(8,128)(2,1)S(1)} %get-tuple-element.29), channel_id=1, source_target_pairs={{16,48},{48,80},{80,112},{112,144},{144,176},{176,208},{208,240},{... | collective-permute-start | bytes 731144 | tf_op jit(solution)/shard_map/ppermute | solution.py:35
  52.1 9.2 %collective-permute-start.6 = (bf16[7,136,128]{2,1,0:T(8,128)(2,1)S(1)}, bf16[7,136,128]{2,1,0:T(8,128)(2,1)S(1)}, u32[]{:S(2)}, u32[]{:S(2)}) collective-permute-start(bf16[7,136,128]{2,1,0:T(8,128)(2,1)S(1)} %get-tuple-element.27), channel_id=1, source_target_pairs={{16,80},{48,112},{80,144},{112,176},{144,208},{176,240},{208,272},... | collective-permute-start | bytes 731144 | tf_op jit(solution)/shard_map/ppermute | solution.py:35
  61.7 15.0 %collective-permute-start.7 = (bf16[7,136,128]{2,1,0:T(8,128)(2,1)S(1)}, bf16[7,136,128]{2,1,0:T(8,128)(2,1)S(1)}, u32[]{:S(2)}, u32[]{:S(2)}) collective-permute-start(bf16[7,136,128]{2,1,0:T(8,128)(2,1)S(1)} %get-tuple-element.25), channel_id=1, source_target_pairs={{16,144},{48,176},{80,208},{112,240},{144,272},{176,304},{208,336}... | collective-permute-start | bytes 731144 | tf_op jit(solution)/shard_map/ppermute | solution.py:35
  77.0 15.7 %collective-permute-start.8 = (bf16[7,136,128]{2,1,0:T(8,128)(2,1)S(1)}, bf16[7,136,128]{2,1,0:T(8,128)(2,1)S(1)}, u32[]{:S(2)}, u32[]{:S(2)}) collective-permute-start(bf16[7,136,128]{2,1,0:T(8,128)(2,1)S(1)} %get-tuple-element.39), channel_id=1, source_target_pairs={{16,272},{48,304},{80,336},{112,368},{144,400},{176,432},{208,464}... | collective-permute-start | bytes 731144 | tf_op jit(solution)/shard_map/ppermute | solution.py:35
  93.0 3.8 %collective-permute-start.9 = (bf16[7,128,128]{2,1,0:T(8,128)(2,1)S(1)}, bf16[7,128,128]{2,1,0:T(8,128)(2,1)}, u32[]{:S(2)}, u32[]{:S(2)}) collective-permute-start(bf16[7,128,128]{2,1,0:T(8,128)(2,1)S(1)} %slice.244), channel_id=1, source_target_pairs={{16,0},{48,32},{80,64},{112,96},{144,128},{176,160},{208,192},{240... | collective-permute-start | bytes 688136 | tf_op jit(solution)/shard_map/ppermute | solution.py:35
  101.7 2.4 %collective-permute-start.10 = (bf16[7,136,128]{2,1,0:T(8,128)(2,1)S(1)}, bf16[7,136,128]{2,1,0:T(8,128)(2,1)S(1)}, u32[]{:S(2)}, u32[]{:S(2)}) collective-permute-start(bf16[7,136,128]{2,1,0:T(8,128)(2,1)S(1)} %fusion.96), channel_id=1, source_target_pairs={{496,480},{464,448},{432,416},{400,384},{368,352},{336,320},{304,2... | collective-permute-start | bytes 731144 | tf_op jit(solution)/shard_map/ppermute | solution.py:35
  104.4 0.8 collective-permute-start.11
  106.4 2.4 collective-permute-start.12
  111.1 1.0 collective-permute-start.13
  112.4 2.5 %collective-permute-start.14 = (bf16[7,136,128]{2,1,0:T(8,128)(2,1)S(1)}, bf16[7,136,128]{2,1,0:T(8,128)(2,1)S(1)}, u32[]{:S(2)}, u32[]{:S(2)}) collective-permute-start(bf16[7,136,128]{2,1,0:T(8,128)(2,1)S(1)} %get-tuple-element.35), channel_id=1, source_target_pairs={{480,224},{448,192},{416,160},{384,128},{352,96},{320,64},{288,32}... | collective-permute-start | bytes 731144 | tf_op jit(solution)/shard_map/ppermute | solution.py:35
  114.7 46.7 %copy-start.4 = (f32[7,128,128]{1,2,0:T(8,128)S(1)}, f32[7,128,128]{1,2,0:T(8,128)}, u32[]{:S(2)}) copy-start(f32[7,128,128]{1,2,0:T(8,128)} %copy-done.3) | copy-start | bytes 1376260
  114.7 46.7 %copy-start.9 = (bf16[1,128,896]{1,2,0:T(8,128)(2,1)S(1)}, bf16[1,128,896]{1,2,0:T(8,128)(2,1)}, u32[]{:S(2)}) copy-start(bf16[1,128,896]{1,2,0:T(8,128)(2,1)} %copy-done.7) | copy-start | bytes 688132
  114.7 46.7 %copy-start.17 = (f32[896]{0:T(1024)S(1)}, f32[896]{0:T(1024)}, u32[]{:S(2)}) copy-start(f32[896]{0:T(1024)} %param.14) | copy-start | bytes 10756
  114.7 46.7 %copy-start.19 = (f32[7,128]{1,0:T(8,128)S(1)}, f32[7,128]{1,0:T(8,128)}, u32[]{:S(2)}) copy-start(f32[7,128]{1,0:T(8,128)} %copy-done.18) | copy-start | bytes 10756
  114.7 46.6 %copy-start.21 = (f32[7,128]{1,0:T(8,128)S(1)}, f32[7,128]{1,0:T(8,128)}, u32[]{:S(2)}) copy-start(f32[7,128]{1,0:T(8,128)} %copy-done.20) | copy-start | bytes 10756
  115.1 46.2 %collective-permute-start.15 = (bf16[7,128,128]{2,1,0:T(8,128)(2,1)S(1)}, bf16[7,128,128]{2,1,0:T(8,128)(2,1)S(1)}, u32[]{:S(2)}, u32[]{:S(2)}) collective-permute-start(bf16[7,128,128]{2,1,0:T(8,128)(2,1)S(1)} %slice.243), channel_id=1, source_target_pairs={{480,496},{448,464},{416,432},{384,400},{352,368},{320,336},{288,3... | collective-permute-start | bytes 688136 | tf_op jit(solution)/shard_map/ppermute | solution.py:35
  168.7 5.5 %collective-permute-start.20 = (f32[896]{0:T(1024)S(1)}, f32[896]{0:T(1024)S(1)}, u32[]{:S(2)}, u32[]{:S(2)}) collective-permute-start(f32[896]{0:T(1024)S(1)} %bitcast.151), channel_id=1, source_target_pairs={{0,16},{16,0},{32,48},{48,32},{64,80},{80,64},{96,112},{112,96},{1... | collective-permute-start | bytes 10760 | tf_op jit(solution)/shard_map/ppermute | solution.py:91
  174.1 16.9 %collective-permute-start.21 = (f32[896]{0:T(1024)S(1)}, f32[896]{0:T(1024)S(1)}, u32[]{:S(2)}, u32[]{:S(2)}) collective-permute-start(f32[896]{0:T(1024)S(1)} %bitcast_add_fusion.1), channel_id=1, source_target_pairs={{0,32},{16,48},{32,0},{48,16},{64,96},{80,112},{96,64},{112,80},{1... | collective-permute-start | bytes 10760 | tf_op jit(solution)/shard_map/ppermute | solution.py:91
  191.0 5.3 %collective-permute-start.22 = (f32[896]{0:T(1024)S(1)}, f32[896]{0:T(1024)S(1)}, u32[]{:S(2)}, u32[]{:S(2)}) collective-permute-start(f32[896]{0:T(1024)S(1)} %add.195), channel_id=1, source_target_pairs={{0,64},{16,80},{32,96},{48,112},{64,0},{80,16},{96,32},{112,48},{1... | collective-permute-start | bytes 10760 | tf_op jit(solution)/shard_map/ppermute | solution.py:91
  196.3 15.7 %collective-permute-start.23 = (f32[896]{0:T(1024)S(1)}, f32[896]{0:T(1024)S(1)}, u32[]{:S(2)}, u32[]{:S(2)}) collective-permute-start(f32[896]{0:T(1024)S(1)} %add.196), channel_id=1, source_target_pairs={{0,128},{16,144},{32,160},{48,176},{64,192},{80,208},{96,224},{112... | collective-permute-start | bytes 10760 | tf_op jit(solution)/shard_map/ppermute | solution.py:91
  204.5 33.4 %collective-permute-start.19 = (f32[2,1,128,128]{3,2,1,0:T(8,128)}, f32[2,1,128,128]{3,2,1,0:T(8,128)S(1)}, u32[]{:S(2)}, u32[]{:S(2)}) collective-permute-start(f32[2,1,128,128]{3,2,1,0:T(8,128)} %get-tuple-element.33), channel_id=1, source_target_pairs={{16,0},{32,16},{48,32},{64,48},{80,64},{96,80},{112,96},{128,112},... | collective-permute-start | bytes 393224 | tf_op jit(solution)/shard_map/ppermute | solution.py:21
  208.1 29.7 %collective-permute-start.18 = (f32[2,1,128,128]{3,2,1,0:T(8,128)}, f32[2,1,128,128]{3,2,1,0:T(8,128)}, u32[]{:S(2)}, u32[]{:S(2)}) collective-permute-start(f32[2,1,128,128]{3,2,1,0:T(8,128)} %get-tuple-element.34), channel_id=1, source_target_pairs={{32,0},{48,16},{64,32},{80,48},{96,64},{112,80},{128,96},{144,112}... | collective-permute-start | bytes 393224 | tf_op jit(solution)/shard_map/ppermute | solution.py:21
  209.4 28.4 %collective-permute-start.17 = (f32[2,1,128,128]{3,2,1,0:T(8,128)}, f32[2,1,128,128]{3,2,1,0:T(8,128)}, u32[]{:S(2)}, u32[]{:S(2)}) collective-permute-start(f32[2,1,128,128]{3,2,1,0:T(8,128)} %get-tuple-element.32), channel_id=1, source_target_pairs={{48,0},{64,16},{80,32},{96,48},{112,64},{128,80},{144,96},{160,112... | collective-permute-start | bytes 393224 | tf_op jit(solution)/shard_map/ppermute | solution.py:21
  210.7 27.1 %collective-permute-start.16 = (f32[2,1,128,128]{3,2,1,0:T(8,128)S(1)}, f32[2,1,128,128]{3,2,1,0:T(8,128)}, u32[]{:S(2)}, u32[]{:S(2)}) collective-permute-start(f32[2,1,128,128]{3,2,1,0:T(8,128)S(1)} %get-tuple-element.31), channel_id=1, source_target_pairs={{64,0},{80,16},{96,32},{112,48},{128,64},{144,80},{160,96},{176,11... | collective-permute-start | bytes 393224 | tf_op jit(solution)/shard_map/ppermute | solution.py:21
  212.0 16.8 %collective-permute-start.24 = (f32[896]{0:T(1024)S(1)}, f32[896]{0:T(1024)S(1)}, u32[]{:S(2)}, u32[]{:S(2)}) collective-permute-start(f32[896]{0:T(1024)S(1)} %add.197), channel_id=1, source_target_pairs={{0,256},{16,272},{32,288},{48,304},{64,320},{80,336},{96,352},{112... | collective-permute-start | bytes 10760 | tf_op jit(solution)/shard_map/ppermute | solution.py:91
  (20 other events, 247.9 us)

commit v11 on v10

--- a/solution.py
+++ b/solution.py
@@ -226,7 +226,7 @@
         grad_parts.append(part_level)
     unit_out = jnp.concatenate(unit_parts, axis=0)
     level_grad = jnp.concatenate(grad_parts, axis=0)
-    gain_grads = lax.psum(summed(jnp.concatenate(gain_parts, axis=0), ("seq",)), "dp")
+    gain_grads = lax.psum(lax.psum(jnp.concatenate(gain_parts, axis=0), "seq"), "dp")
     layer_output = (
         unit_out.astype(jnp.bfloat16).transpose(1, 0, 2).reshape(1, block_rows, q_heads * HEAD_SIZE)
     )

time: 244 us -> 263 us (1.078)
  the two profiles are of different devices: /device:TPU:1 before, /device:TPU:8 now
where the time goes in v11:
time: 263 us; the launch traced here: 262 us
  blocking collectives  91.5 us (35%)
  waiting for transfers between devices  86.7 us (33%)
  starting transfers between devices  36.3 us (14%)
  matrix products  22 us (8%)
  other arithmetic  12.1 us (5%)
  local copies, waits for them, and re-layouts  11.4 us (4%)
    ppermute x12, waiting for transfers between devices, moved_on(): return lax.ppermute(value, axis, pairs)  86.7 us
    psum x1, blocking collectives, local(): lax.psum(jnp.concatenate(gain_parts, axis=0), 'seq')  61.4 us
    ppermute x8, starting transfers between devices, passed_along(): return lax.ppermute(block, axis, route)  22.3 us
    ppermute x12, starting transfers between devices, moved_on(): return lax.ppermute(value, axis, pairs)  14 us
    psum x1, blocking collectives, local(): lax.psum(lax.psum(jnp.concatenate(gain_parts, axis=0), 'seq'), 'dp')  11.1 us
    psum x1, blocking collectives, local(): slope_sum = lax.psum(jnp.sum(normed_grad * normed, axis=(0, 2)), 'tensor')  10.4 us
    psum x1, blocking collectives, local(): square_sum = lax.psum(jnp.sum(out_float * out_float, axis=(0, 2)), 'tensor')  8.71 us
    unnamed x64, local copies, waits for them, and re-layouts  6.51 us
  transfers between devices with their start and end apart: 20, of which 7 were waited for; matrix products, arithmetic and copies ran while one was open for 6% of the time, Pallas kernels for 0%

profile of v11, /device:TPU:8, one launch (start us, length us, event | category | flops | bytes accessed | tf_op | source)
XLA Modules:
  0.0 262.1 jit_solution(4495802880578286435)
XLA Ops:
  1.4 5.2 %collective-permute-start = (bf16[2,1,128,128]{3,2,1,0:T(8,128)(2,1)S(1)}, bf16[2,1,128,128]{3,2,1,0:T(8,128)(2,1)S(1)}, u32[]{:S(2)}, u32[]{:S(2)}) collective-permute-start(bf16[2,1,128,128]{3,2,1,0:T(8,128)(2,1)S(1)} %pad_maximum_fusion.3), channel_id=1, source_target_pairs={{0,64},{16,80},{32,96},{48,112},{64,128},{80,144},{96,160},{112,17... | collective-permute-start | bytes 196616 | tf_op jit(solution)/shard_map/ppermute | solution.py:21
  6.6 3.0 %collective-permute-start.1 = (bf16[2,1,128,128]{3,2,1,0:T(8,128)(2,1)S(1)}, bf16[2,1,128,128]{3,2,1,0:T(8,128)(2,1)S(1)}, u32[]{:S(2)}, u32[]{:S(2)}) collective-permute-start(bf16[2,1,128,128]{3,2,1,0:T(8,128)(2,1)S(1)} %pad_maximum_fusion.3), channel_id=1, source_target_pairs={{0,48},{16,64},{32,80},{48,96},{64,112},{80,128},{96,144},{112,160... | collective-permute-start | bytes 196616 | tf_op jit(solution)/shard_map/ppermute | solution.py:21
  9.6 5.0 %collective-permute-start.2 = (bf16[2,1,128,128]{3,2,1,0:T(8,128)(2,1)S(1)}, bf16[2,1,128,128]{3,2,1,0:T(8,128)(2,1)S(1)}, u32[]{:S(2)}, u32[]{:S(2)}) collective-permute-start(bf16[2,1,128,128]{3,2,1,0:T(8,128)(2,1)S(1)} %pad_maximum_fusion.3), channel_id=1, source_target_pairs={{0,32},{16,48},{32,64},{48,80},{64,96},{80,112},{96,128},{112,144}... | collective-permute-start | bytes 196616 | tf_op jit(solution)/shard_map/ppermute | solution.py:21
  14.6 3.9 %collective-permute-start.3 = (bf16[2,1,128,128]{3,2,1,0:T(8,128)(2,1)S(1)}, bf16[2,1,128,128]{3,2,1,0:T(8,128)(2,1)S(1)}, u32[]{:S(2)}, u32[]{:S(2)}) collective-permute-start(bf16[2,1,128,128]{3,2,1,0:T(8,128)(2,1)S(1)} %pad_maximum_fusion.3), channel_id=1, source_target_pairs={{0,16},{16,32},{32,48},{48,64},{64,80},{80,96},{96,112},{112,128},... | collective-permute-start | bytes 196616 | tf_op jit(solution)/shard_map/ppermute | solution.py:21
  25.3 2.2 fusion.137
  27.5 1.3 multiply_reduce_fusion.5
  28.8 8.7 %psum.28 = f32[128]{0:T(128)S(1)} all-reduce(f32[128]{0:T(128)S(1)} %get-tuple-element.52), channel_id=1, replica_groups=mesh['seq'=32,'dp'=4,'tensor'=4] {'tensor'}, use_global_device_ids=true, to_apply=%region_4.5 | all-reduce | flops 128 | bytes 1024 | tf_op jit(solution)/shard_map/psum | solution.py:165
  39.0 1.3 collective-permute-start.4
  47.9 1.3 collective-permute-start.9
  51.0 41.4 %collective-permute-done.9 = bf16[7,128,128]{2,1,0:T(8,128)(2,1)} collective-permute-done((bf16[7,128,128]{2,1,0:T(8,128)(2,1)S(1)}, bf16[7,128,128]{2,1,0:T(8,128)(2,1)}, u32[]{:S(2)}, u32[]{:S(2)}) %collective-permute-start.9) | collective-permute-done | bytes 229408 | tf_op jit(solution)/shard_map/ppermute | solution.py:35
  92.4 1.6 fusion.82
  94.0 1.5 multiply_reduce_fusion.4
  98.6 2.3 collective-permute-done.10
  101.2 1.3 collective-permute-start.11
  102.6 9.5 %collective-permute-done.11 = bf16[7,136,128]{2,1,0:T(8,128)(2,1)S(1)} collective-permute-done((bf16[7,136,128]{2,1,0:T(8,128)(2,1)S(1)}, bf16[7,136,128]{2,1,0:T(8,128)(2,1)S(1)}, u32[]{:S(2)}, u32[]{:S(2)}) %collective-permute-start.11) | collective-permute-done | bytes 243744 | tf_op jit(solution)/shard_map/ppermute | solution.py:35
  115.6 7.2 %collective-permute-done.12 = bf16[7,136,128]{2,1,0:T(8,128)(2,1)} collective-permute-done((bf16[7,136,128]{2,1,0:T(8,128)(2,1)}, bf16[7,136,128]{2,1,0:T(8,128)(2,1)}, u32[]{:S(2)}, u32[]{:S(2)}) %collective-permute-start.12) | collective-permute-done | bytes 243744 | tf_op jit(solution)/shard_map/ppermute | solution.py:35
  122.9 2.3 fusion.127
  126.8 11.3 %collective-permute-done.13 = bf16[7,136,128]{2,1,0:T(8,128)(2,1)S(1)} collective-permute-done((bf16[7,136,128]{2,1,0:T(8,128)(2,1)}, bf16[7,136,128]{2,1,0:T(8,128)(2,1)S(1)}, u32[]{:S(2)}, u32[]{:S(2)}) %collective-permute-start.13) | collective-permute-done | bytes 243744 | tf_op jit(solution)/shard_map/ppermute | solution.py:35
  139.7 1.6 fusion.118
  141.5 13.8 %collective-permute-done.14 = bf16[7,136,128]{2,1,0:T(8,128)(2,1)S(1)} collective-permute-done((bf16[7,136,128]{2,1,0:T(8,128)(2,1)S(1)}, bf16[7,136,128]{2,1,0:T(8,128)(2,1)S(1)}, u32[]{:S(2)}, u32[]{:S(2)}) %collective-permute-start.14) | collective-permute-done | bytes 243744 | tf_op jit(solution)/shard_map/ppermute | solution.py:35
  155.5 2.2 collective-permute-start.15
  158.8 1.9 multiply_reduce_fusion.1
  160.8 10.4 %psum.29 = f32[128]{0:T(128)S(1)} all-reduce(f32[128]{0:T(128)S(1)} %get-tuple-element.16), channel_id=1, replica_groups=mesh['seq'=32,'dp'=4,'tensor'=4] {'tensor'}, use_global_device_ids=true, to_apply=%region_8.9 | all-reduce | flops 128 | bytes 1024 | tf_op jit(solution)/shard_map/psum | solution.py:234
  171.3 1.4 fusion.107
  172.7 2.2 convolution_bitcast_fusion
  174.9 3.1 %fusion.19 = f32[1,1,640,128]{3,2,1,0:T(8,128)S(1)} fusion(bf16[7,128,128]{1,2,0:T(8,128)(2,1)S(1)} %bitcast.134, f32[7,128,640]{1,2,0:T(8,128)S(1)} %fusion.107, f32[7,128,640]{1,2,0:T(8,128)} %get-tuple-element.51, f32[7,128]{1,0:T(8,128)S(1)} %copy-done.26), kind=kOutput, calls=%fused_computation.24 | convolution fusion | flops 150816256 | bytes 5148160 | tf_op jit(solution)/shard_map/gjsk,gjsd->gkd/dot_general | solution.py:248
  180.0 1.3 collective-permute-start.18
  181.3 1.3 collective-permute-start.17
  182.6 1.3 collective-permute-start.16
  183.9 3.1 %fusion.15 = bf16[7,128,128]{1,2,0:T(8,128)(2,1)S(1)} fusion(f32[7,128,640]{1,2,0:T(8,128)S(1)} %fusion.107, bf16[2,1,640,128]{3,2,1,0:T(8,128)(2,1)} %copy-done.10, f32[7,128,640]{1,2,0:T(8,128)} %get-tuple-element.51, f32[7,128]{1,0:T(8,128)S(1)} %copy-done.26), kind=kOutput, calls=%fused_computation.21 | convolution fusion | flops 150930944 | bytes 9576448 | tf_op jit(solution)/shard_map/gjsk,gkd->gjsd/dot_general | solution.py:245
  187.9 61.4 %psum.30 = f32[896]{0:T(1024)S(1)} all-reduce(f32[896]{0:T(1024)S(1)} %bitcast.150), channel_id=1, replica_groups=mesh['seq'=32,'dp'=4,'tensor'=4] {'seq'}, use_global_device_ids=true, to_apply=%region_11.12 | all-reduce | flops 896 | bytes 7168 | tf_op jit(solution)/shard_map/psum | solution.py:229
  249.3 11.1 %psum.31 = f32[896]{0:T(1024)} all-reduce(f32[896]{0:T(1024)S(1)} %psum.30), channel_id=1, replica_groups=mesh['seq'=32,'dp'=4,'tensor'=4] {'dp'}, use_global_device_ids=true, to_apply=%region_12.13 | all-reduce | flops 896 | bytes 7168 | tf_op jit(solution)/shard_map/psum | solution.py:229
  (145 shorter events, 33.7 us)
Async XLA Ops:
  1.4 22.9 %collective-permute-start = (bf16[2,1,128,128]{3,2,1,0:T(8,128)(2,1)S(1)}, bf16[2,1,128,128]{3,2,1,0:T(8,128)(2,1)S(1)}, u32[]{:S(2)}, u32[]{:S(2)}) collective-permute-start(bf16[2,1,128,128]{3,2,1,0:T(8,128)(2,1)S(1)} %pad_maximum_fusion.3), channel_id=1, source_target_pairs={{0,64},{16,80},{32,96},{48,112},{64,128},{80,144},{96,160},{112,17... | collective-permute-start | bytes 196616 | tf_op jit(solution)/shard_map/ppermute | solution.py:21
  6.6 17.8 %collective-permute-start.1 = (bf16[2,1,128,128]{3,2,1,0:T(8,128)(2,1)S(1)}, bf16[2,1,128,128]{3,2,1,0:T(8,128)(2,1)S(1)}, u32[]{:S(2)}, u32[]{:S(2)}) collective-permute-start(bf16[2,1,128,128]{3,2,1,0:T(8,128)(2,1)S(1)} %pad_maximum_fusion.3), channel_id=1, source_target_pairs={{0,48},{16,64},{32,80},{48,96},{64,112},{80,128},{96,144},{112,160... | collective-permute-start | bytes 196616 | tf_op jit(solution)/shard_map/ppermute | solution.py:21
  9.6 14.8 %collective-permute-start.2 = (bf16[2,1,128,128]{3,2,1,0:T(8,128)(2,1)S(1)}, bf16[2,1,128,128]{3,2,1,0:T(8,128)(2,1)S(1)}, u32[]{:S(2)}, u32[]{:S(2)}) collective-permute-start(bf16[2,1,128,128]{3,2,1,0:T(8,128)(2,1)S(1)} %pad_maximum_fusion.3), channel_id=1, source_target_pairs={{0,32},{16,48},{32,64},{48,80},{64,96},{80,112},{96,128},{112,144}... | collective-permute-start | bytes 196616 | tf_op jit(solution)/shard_map/ppermute | solution.py:21
  14.6 9.8 %collective-permute-start.3 = (bf16[2,1,128,128]{3,2,1,0:T(8,128)(2,1)S(1)}, bf16[2,1,128,128]{3,2,1,0:T(8,128)(2,1)S(1)}, u32[]{:S(2)}, u32[]{:S(2)}) collective-permute-start(bf16[2,1,128,128]{3,2,1,0:T(8,128)(2,1)S(1)} %pad_maximum_fusion.3), channel_id=1, source_target_pairs={{0,16},{16,32},{32,48},{48,64},{64,80},{80,96},{96,112},{112,128},... | collective-permute-start | bytes 196616 | tf_op jit(solution)/shard_map/ppermute | solution.py:21
  22.0 72.0 %copy-start.18 = (f32[7,128]{1,0:T(8,128)}, f32[7,128]{1,0:T(8,128)S(1)}, u32[]{:S(2)}) copy-start(f32[7,128]{1,0:T(8,128)S(1)} %convert_bitcast_fusion) | copy-start | bytes 10756
  22.0 19.4 %copy-start.14 = (f32[7]{0:T(128)}, f32[7]{0:T(128)S(1)}, u32[]{:S(2)}) copy-start(f32[7]{0:T(128)S(1)} %exp.37) | copy-start | bytes 88
  28.8 65.2 %copy-start.3 = (f32[7,128,128]{1,2,0:T(8,128)}, f32[7,128,128]{1,2,0:T(8,128)S(1)}, u32[]{:S(2)}) copy-start(f32[7,128,128]{1,2,0:T(8,128)S(1)} %get-tuple-element.53) | copy-start | bytes 1376260
  39.0 2.4 collective-permute-start.4
  41.7 0.8 collective-permute-start.5
  42.8 1.0 collective-permute-start.6
  44.2 1.1 collective-permute-start.7
  45.6 2.0 collective-permute-start.8
  47.9 46.1 %copy-start.23 = (f32[128]{0:T(128)S(1)}, f32[128]{0:T(128)}, u32[]{:S(2)}) copy-start(f32[128]{0:T(128)} %copy-done.22) | copy-start | bytes 1540
  47.9 44.5 %collective-permute-start.9 = (bf16[7,128,128]{2,1,0:T(8,128)(2,1)S(1)}, bf16[7,128,128]{2,1,0:T(8,128)(2,1)}, u32[]{:S(2)}, u32[]{:S(2)}) collective-permute-start(bf16[7,128,128]{2,1,0:T(8,128)(2,1)S(1)} %slice.244), channel_id=1, source_target_pairs={{16,0},{48,32},{80,64},{112,96},{144,128},{176,160},{208,192},{240... | collective-permute-start | bytes 688136 | tf_op jit(solution)/shard_map/ppermute | solution.py:35
  49.5 49.1 %copy-start.1 = (f32[7,128,128]{2,1,0:T(8,128)}, f32[7,128,128]{2,1,0:T(8,128)S(1)}, u32[]{:S(2)}) copy-start(f32[7,128,128]{2,1,0:T(8,128)S(1)} %convolution_multiply_fusion.1) | copy-start | bytes 1376260
  97.3 3.6 %collective-permute-start.10 = (bf16[7,136,128]{2,1,0:T(8,128)(2,1)S(1)}, bf16[7,136,128]{2,1,0:T(8,128)(2,1)S(1)}, u32[]{:S(2)}, u32[]{:S(2)}) collective-permute-start(bf16[7,136,128]{2,1,0:T(8,128)(2,1)S(1)} %fusion.96), channel_id=1, source_target_pairs={{496,480},{464,448},{432,416},{400,384},{368,352},{336,320},{304,2... | collective-permute-start | bytes 731144 | tf_op jit(solution)/shard_map/ppermute | solution.py:35
  101.2 11.0 %collective-permute-start.11 = (bf16[7,136,128]{2,1,0:T(8,128)(2,1)S(1)}, bf16[7,136,128]{2,1,0:T(8,128)(2,1)S(1)}, u32[]{:S(2)}, u32[]{:S(2)}) collective-permute-start(bf16[7,136,128]{2,1,0:T(8,128)(2,1)S(1)} %get-tuple-element.21), channel_id=1, source_target_pairs={{480,448},{448,416},{416,384},{384,352},{352,320},{320,288},{288,2... | collective-permute-start | bytes 731144 | tf_op jit(solution)/shard_map/ppermute | solution.py:35
  113.3 9.6 %collective-permute-start.12 = (bf16[7,136,128]{2,1,0:T(8,128)(2,1)}, bf16[7,136,128]{2,1,0:T(8,128)(2,1)}, u32[]{:S(2)}, u32[]{:S(2)}) collective-permute-start(bf16[7,136,128]{2,1,0:T(8,128)(2,1)} %get-tuple-element.19), channel_id=1, source_target_pairs={{480,416},{448,384},{416,352},{384,320},{352,288},{320,256},{288,2... | collective-permute-start | bytes 731144 | tf_op jit(solution)/shard_map/ppermute | solution.py:35
  125.2 12.9 %collective-permute-start.13 = (bf16[7,136,128]{2,1,0:T(8,128)(2,1)}, bf16[7,136,128]{2,1,0:T(8,128)(2,1)S(1)}, u32[]{:S(2)}, u32[]{:S(2)}) collective-permute-start(bf16[7,136,128]{2,1,0:T(8,128)(2,1)} %get-tuple-element.17), channel_id=1, source_target_pairs={{480,352},{448,320},{416,288},{384,256},{352,224},{320,192},{288,1... | collective-permute-start | bytes 731144 | tf_op jit(solution)/shard_map/ppermute | solution.py:35
  126.8 30.9 %copy-start.2 = (f32[7,128,128]{1,2,0:T(8,128)S(1)}, f32[7,128,128]{1,2,0:T(8,128)}, u32[]{:S(2)}) copy-start(f32[7,128,128]{1,2,0:T(8,128)} %get-tuple-element.54) | copy-start | bytes 1376260
  126.8 30.9 %copy-start.12 = (f32[128,7]{0,1:T(8,128)S(1)}, f32[128,7]{0,1:T(8,128)}, u32[]{:S(2)}) copy-start(f32[128,7]{0,1:T(8,128)} %get-tuple-element.46) | copy-start | bytes 10756
  126.8 30.9 %copy-start.13 = (f32[128,7]{0,1:T(8,128)S(1)}, f32[128,7]{0,1:T(8,128)}, u32[]{:S(2)}) copy-start(f32[128,7]{0,1:T(8,128)} %get-tuple-element.47) | copy-start | bytes 10756
  138.4 16.9 %collective-permute-start.14 = (bf16[7,136,128]{2,1,0:T(8,128)(2,1)S(1)}, bf16[7,136,128]{2,1,0:T(8,128)(2,1)S(1)}, u32[]{:S(2)}, u32[]{:S(2)}) collective-permute-start(bf16[7,136,128]{2,1,0:T(8,128)(2,1)S(1)} %get-tuple-element.35), channel_id=1, source_target_pairs={{480,224},{448,192},{416,160},{384,128},{352,96},{320,64},{288,32}... | collective-permute-start | bytes 731144 | tf_op jit(solution)/shard_map/ppermute | solution.py:35
  141.3 17.5 %copy-start.4 = (f32[7,128,128]{1,2,0:T(8,128)S(1)}, f32[7,128,128]{1,2,0:T(8,128)}, u32[]{:S(2)}) copy-start(f32[7,128,128]{1,2,0:T(8,128)} %copy-done.3) | copy-start | bytes 1376260
  141.3 17.5 %copy-start.9 = (bf16[1,128,896]{1,2,0:T(8,128)(2,1)S(1)}, bf16[1,128,896]{1,2,0:T(8,128)(2,1)}, u32[]{:S(2)}) copy-start(bf16[1,128,896]{1,2,0:T(8,128)(2,1)} %copy-done.7) | copy-start | bytes 688132
  141.3 17.5 %copy-start.17 = (f32[896]{0:T(1024)S(1)}, f32[896]{0:T(1024)}, u32[]{:S(2)}) copy-start(f32[896]{0:T(1024)} %param.14) | copy-start | bytes 10756
  141.3 17.5 %copy-start.19 = (f32[7,128]{1,0:T(8,128)S(1)}, f32[7,128]{1,0:T(8,128)}, u32[]{:S(2)}) copy-start(f32[7,128]{1,0:T(8,128)} %copy-done.18) | copy-start | bytes 10756
  155.5 3.3 %collective-permute-start.15 = (bf16[7,128,128]{2,1,0:T(8,128)(2,1)S(1)}, bf16[7,128,128]{2,1,0:T(8,128)(2,1)}, u32[]{:S(2)}, u32[]{:S(2)}) collective-permute-start(bf16[7,128,128]{2,1,0:T(8,128)(2,1)S(1)} %slice.243), channel_id=1, source_target_pairs={{480,496},{448,464},{416,432},{384,400},{352,368},{320,336},{288,3... | collective-permute-start | bytes 688136 | tf_op jit(solution)/shard_map/ppermute | solution.py:35
  178.8 81.6 %collective-permute-start.19 = (f32[2,1,128,128]{3,2,1,0:T(8,128)}, f32[2,1,128,128]{3,2,1,0:T(8,128)S(1)}, u32[]{:S(2)}, u32[]{:S(2)}) collective-permute-start(f32[2,1,128,128]{3,2,1,0:T(8,128)} %get-tuple-element.33), channel_id=1, source_target_pairs={{16,0},{32,16},{48,32},{64,48},{80,64},{96,80},{112,96},{128,112},... | collective-permute-start | bytes 393224 | tf_op jit(solution)/shard_map/ppermute | solution.py:21
  180.0 80.3 %collective-permute-start.18 = (f32[2,1,128,128]{3,2,1,0:T(8,128)}, f32[2,1,128,128]{3,2,1,0:T(8,128)}, u32[]{:S(2)}, u32[]{:S(2)}) collective-permute-start(f32[2,1,128,128]{3,2,1,0:T(8,128)} %get-tuple-element.34), channel_id=1, source_target_pairs={{32,0},{48,16},{64,32},{80,48},{96,64},{112,80},{128,96},{144,112}... | collective-permute-start | bytes 393224 | tf_op jit(solution)/shard_map/ppermute | solution.py:21
  181.3 79.0 %collective-permute-start.17 = (f32[2,1,128,128]{3,2,1,0:T(8,128)}, f32[2,1,128,128]{3,2,1,0:T(8,128)}, u32[]{:S(2)}, u32[]{:S(2)}) collective-permute-start(f32[2,1,128,128]{3,2,1,0:T(8,128)} %get-tuple-element.32), channel_id=1, source_target_pairs={{48,0},{64,16},{80,32},{96,48},{112,64},{128,80},{144,96},{160,112... | collective-permute-start | bytes 393224 | tf_op jit(solution)/shard_map/ppermute | solution.py:21
  182.6 77.7 %collective-permute-start.16 = (f32[2,1,128,128]{3,2,1,0:T(8,128)S(1)}, f32[2,1,128,128]{3,2,1,0:T(8,128)}, u32[]{:S(2)}, u32[]{:S(2)}) collective-permute-start(f32[2,1,128,128]{3,2,1,0:T(8,128)S(1)} %get-tuple-element.31), channel_id=1, source_target_pairs={{64,0},{80,16},{96,32},{112,48},{128,64},{144,80},{160,96},{176,11... | collective-permute-start | bytes 393224 | tf_op jit(solution)/shard_map/ppermute | solution.py:21
  (15 other events, 131.2 us)
